TPU v7x, 32 devices: a whole 2x2x4 slice. The times are simulated.
32 devices in a mesh: inner: 2 (over y), outer: 16 (over z, x, core).
Axes of the slice: x: 2, y: 2, z: 4, core: 2. Of those that a mesh axis runs over, the one named last changes fastest.
Arguments:
- propagator_matrices: bfloat16 [16, 48, 256, 256], P('outer', 'inner')
- smoothed_adjoints: float32 [16, 48, 256], P('outer', 'inner'), may hold values from -0.4330127 to 0.4330127
- station_loadings: float32 [16, 48, 2, 128], P('outer', 'inner'), may hold values from -0.21650635 to 0.21650635
- offset_response: float32 [16, 48, 256], P('outer', 'inner'), may hold values from -0.021650635 to 0.021650635
Outputs:
- adjoint: float32 [16, 48, 256], P('outer', 'inner')
- spatial_matrix_derivative: float32 [128, 128], replicated
- variance_derivative: float32 [], replicated
All inputs are finite; a program needn't handle non-finite values.
Results may differ from a plain program's by a relative error of at most 0.0003.
Values sent between devices are 32-bit elements; how exact they have to be, the bound alone decides.
No kernel may reach another device: no remote copies, remote signals or barrier semaphores. Data moves between devices by JAX's collectives and lax.ppermute only.
A program may use at most 128 MiB of HBM per device.

v0:
```python
import jax
import jax.numpy as jnp
from jax import lax
from jax.sharding import PartitionSpec as P


def entering(value, axis, join, neutral):
    count, mine = (lax.axis_size(axis), lax.axis_index(axis))
    pieces = jax.tree.map(lambda part: lax.all_gather(part, axis), value)
    pieces = jax.tree.map(lambda part: part[::-1], pieces)
    mine = count - 1 - mine
    subtotal = jax.tree.map(
        lambda part, zero: jnp.full_like(part, 0) + jnp.asarray(zero, part.dtype), value, neutral
    )

    def turn(position, subtotal):
        longer = join(subtotal, jax.tree.map(lambda part: part[position], pieces))
        return jax.tree.map(lambda new, old: jnp.where(position < mine, new, old), longer, subtotal)

    return lax.fori_loop(0, count - 1, turn, subtotal)


def spread(block, axis, source):
    block = jnp.where(lax.axis_index(axis) == source, block, jnp.zeros_like(block))
    return lax.psum(block, axis)


def compose(earlier, later):
    return (
        jnp.dot(later[0], earlier[0], precision=lax.Precision.HIGHEST),
        jnp.dot(later[0], earlier[1], precision=lax.Precision.HIGHEST) + later[1],
    )


def body(propagator_matrices, smoothed_adjoints, station_loadings, offset_response):
    blocks = propagator_matrices[0]
    derivative_results = smoothed_adjoints[0]
    width = derivative_results.shape[1]
    stations = station_loadings.shape[3]
    unit = jnp.eye(width, dtype=jnp.float32)
    nothing = jnp.zeros((width,), jnp.float32)

    def summarize(carry, items):
        matrix, grad_row = items
        wide = matrix.astype(jnp.float32)
        new_mat = jnp.dot(wide.T, carry[0], precision=lax.Precision.HIGHEST)
        new_vec = jnp.dot(grad_row + carry[1], wide, precision=lax.Precision.HIGHEST)
        return ((new_mat, new_vec), None)

    (own_mat, own_vec), _ = lax.scan(
        summarize, (unit, nothing), (blocks, derivative_results), reverse=True
    )
    suf_mat, suf_vec = entering((own_mat, own_vec), "inner", compose, (unit, nothing))
    whole_mat, whole_vec = compose((suf_mat, suf_vec), (own_mat, own_vec))
    packed = jnp.concatenate([whole_mat, whole_vec[None, :]], axis=0)
    shared = spread(packed, "inner", 0)
    total_mat = shared[:width]
    total_vec = shared[width]
    beyond_mat, beyond_vec = entering((total_mat, total_vec), "outer", compose, (unit, nothing))
    incoming = jnp.dot(suf_mat, beyond_vec, precision=lax.Precision.HIGHEST) + suf_vec

    def backward(carry, items):
        matrix, grad_row = items
        lam = grad_row + carry
        message = jnp.dot(lam, matrix.astype(jnp.float32), precision=lax.Precision.HIGHEST)
        return (message, lam)

    _, length_rates = lax.scan(backward, incoming, (blocks, derivative_results), reverse=True)
    argument_values = station_loadings[0]
    local_kernel = jnp.dot(
        length_rates[:, :stations].T, argument_values[:, 0, :], precision=lax.Precision.HIGHEST
    )
    local_kernel = local_kernel + jnp.dot(
        length_rates[:, stations:].T, argument_values[:, 1, :], precision=lax.Precision.HIGHEST
    )
    local_noise = -jnp.sum(length_rates * offset_response[0])
    spatial_matrix_derivative, variance_derivative = lax.psum(
        (local_kernel, local_noise), ("inner", "outer")
    )
    return (length_rates[None], spatial_matrix_derivative, variance_derivative)


def solution(mesh):
    return jax.shard_map(
        body,
        mesh=mesh,
        in_specs=(
            P("outer", "inner", None, None),
            P("outer", "inner", None),
            P("outer", "inner", None, None),
            P("outer", "inner", None),
        ),
        out_specs=(P("outer", "inner", None), P(), P()),
        check_vma=False,
    )
```

profile of v0, /device:TPU:0, one launch (start us, length us, event | category | flops | bytes accessed | tf_op | source)
XLA Modules:
  0.0 368.7 jit_solution(7613051268337838645)
XLA Ops:
  7.3 73.5 %while.52 = (s32[]{:T(128)}, f32[256,256]{1,0:T(8,128)S(1)}, f32[256]{0:T(256)S(1)}, bf16[24,256,256]{2,1,0:T(8,128)(2,1)}, f32[24,256]{1,0:T(8,128)}, /*index=5*/s32[]{:T(128)}, s32[]{:T(128)}) while((s32[]{:T(128)}, f32[256,256]{1,0:T(8,128)S(1)}, f32[256]{0:T(256)S(1)}, bf16[24,256,256]{2,1,0:T(8,128)(2,1)}, f32[24,256]{1,0:T(8,128)}, ...), condition=%wide.region_1.2_spmd, body=%wide.region_0.1_spmd.sunk | while | flops 202113280 | bytes 1317989 | solution.py:50
  8.0 1.0 fusion.59
  9.1 1.3 fusion.58
  11.1 1.0 fusion.59
  12.1 1.3 fusion.58
  15.2 1.3 fusion.58
  17.2 1.0 fusion.59
  18.2 1.3 fusion.58
  20.3 1.0 fusion.59
  21.3 1.3 fusion.58
  23.3 1.0 fusion.59
  24.4 1.3 fusion.58
  26.4 1.0 fusion.59
  27.4 1.3 fusion.58
  30.5 1.3 fusion.58
  32.5 1.0 fusion.59
  33.6 1.3 fusion.58
  35.6 1.0 fusion.59
  36.6 1.3 fusion.58
  38.6 1.0 fusion.59
  39.7 1.3 fusion.58
  41.7 1.0 fusion.59
  42.7 1.3 fusion.58
  44.8 1.0 fusion.59
  45.8 1.3 fusion.58
  47.8 1.0 fusion.59
  48.9 1.3 fusion.58
  51.9 1.3 fusion.58
  55.0 1.3 fusion.58
  58.1 1.3 fusion.58
  61.1 1.3 fusion.58
  64.2 1.3 fusion.58
  67.3 1.3 fusion.58
  70.3 1.3 fusion.58
  73.4 1.3 fusion.58
  76.4 1.3 fusion.58
  79.5 1.3 fusion.58
  80.8 5.2 %all-gather.3 = f32[2,1,256]{2,1,0:T(1,128)S(1)} all-gather(f32[1,1,256]{2,1,0:T(1,128)S(1)} %bitcast.107), channel_id=3, replica_groups=mesh['inner'=2,'outer'=16] {'inner'}, dimensions={0}, use_global_device_ids=true | all-gather | bytes 3072 | tf_op jit(solution)/shard_map/all_gather | solution.py:9
  86.0 7.9 %all-gather = f32[512,256]{1,0:T(8,128)S(1)} all-gather(f32[256,256]{1,0:T(8,128)S(1)} %get-tuple-element.325), channel_id=2, replica_groups=mesh['inner'=2,'outer'=16] {'inner'}, dimensions={0}, use_global_device_ids=true | all-gather | bytes 786432 | tf_op jit(solution)/shard_map/all_gather | solution.py:9
  96.0 24.9 %all-reduce.3.cloned.1.call-done = f32[257,256]{1,0:T(8,128)} async-done(((f32[257,256]{1,0:T(8,128)}), f32[257,256]{1,0:T(8,128)}) %all-reduce.3.cloned.1.call-update) | async-done | bytes 263184 | tf_op jit(solution)/shard_map/psum | solution.py:25
  120.9 1.7 slice.33
  123.4 21.3 %all-gather.4 = f32[16,1,256]{2,1,0:T(1,128)S(1)} all-gather(f32[1,1,256]{2,1,0:T(1,128)S(1)} %slice_bitcast_fusion), channel_id=1, replica_groups=mesh['inner'=2,'outer'=16] {'outer'}, dimensions={0}, use_global_device_ids=true | all-gather | bytes 17408 | tf_op jit(solution)/shard_map/all_gather | solution.py:9
  144.8 29.2 %all-gather.7.cloned.1.call-done = f32[4096,256]{1,0:T(8,128)} async-done(((f32[256,256]{1,0:T(8,128)}), f32[4096,256]{1,0:T(8,128)}) %all-gather.7.cloned.1.call-update) | async-done | bytes 4194320 | tf_op jit(solution)/shard_map/all_gather | solution.py:9
  174.0 4.6 %rev.8 = f32[16,256,256]{2,1,0:T(8,128)} reverse(f32[16,256,256]{2,1,0:T(8,128)} %bitcast.93), dimensions={0} | reverse | bytes 8388608 | tf_op jit(solution)/shard_map/rev | solution.py:10
  178.6 20.1 %while.54 = (s32[]{:T(128)}, f32[256]{0:T(256)S(1)}, s32[]{:T(128)}, f32[16,256,256]{2,1,0:T(8,128)}, f32[16,256]{1,0:T(8,128)S(1)}, /*index=5*/s32[]{:T(128)}, s32[]{:T(128)}) while((s32[]{:T(128)}, f32[256]{0:T(256)S(1)}, s32[]{:T(128)}, f32[16,256,256]{2,1,0:T(8,128)}, f32[16,256]{1,0:T(8,128)S(1)}, /*index=5*/s32[]{:T(128)}, ...), condition=%wide.region_4.5_spmd.clone, body=%wide.region_3.4_spmd.clone.sunk | while | flops 787460 | bytes 272498 | solution.py:20
  178.6 1.2 fusion.65
  179.9 1.2 fusion.65
  181.3 1.2 fusion.65
  182.6 1.2 fusion.65
  183.9 1.2 fusion.65
  185.3 1.2 fusion.65
  186.6 1.2 fusion.65
  188.0 1.2 fusion.65
  189.3 1.2 fusion.65
  190.7 1.2 fusion.65
  192.0 1.2 fusion.65
  193.4 1.2 fusion.65
  194.7 1.2 fusion.65
  196.1 1.2 fusion.65
  197.4 1.2 fusion.65
  199.0 44.2 %while.53 = (s32[]{:T(128)}, f32[256]{0:T(256)S(1)}, f32[24,256]{1,0:T(8,128)S(1)}, f32[24,256]{1,0:T(8,128)}, bf16[24,256,256]{2,1,0:T(8,128)(2,1)}, /*index=5*/s32[]{:T(128)}, s32[]{:T(128)}, s32[]{:T(128)}) while((s32[]{:T(128)}, f32[256]{0:T(256)S(1)}, f32[24,256]{1,0:T(8,128)S(1)}, f32[24,256]{1,0:T(8,128)}, ...), condition=%wide.region_6.7_spmd, body=%wide.region_5.6_spmd.sunk | while | flops 786691 | bytes 140397 | solution.py:68
  245.8 39.3 %psum.23 = f32[]{:T(128)} all-reduce(f32[]{:T(128)S(6)} %neg.3), channel_id=1, replica_groups=mesh['inner'=2,'outer'=16] {'inner','outer'}, use_global_device_ids=true, to_apply=%region_9.10 | all-reduce | flops 1 | bytes 8 | tf_op jit(solution)/shard_map/psum | solution.py:77
  285.0 75.7 %all-reduce.5.cloned.1.call-done = f32[128,128]{1,0:T(8,128)} async-done(((f32[128,128]{1,0:T(8,128)}), f32[128,128]{1,0:T(8,128)}) %all-reduce.5.cloned.1.call-update) | async-done | bytes 65552 | tf_op jit(solution)/shard_map/psum | solution.py:77
  360.7 1.5 copy.39
  (258 shorter events, 80.0 us)
Async XLA Ops:
  7.2 113.7 %all-reduce.3.cloned.1.call-start = ((), (), s32[]{:S(2)}) async-start(), calls=%async_computation | async-start | bytes 540672 | tf_op jit(solution)/shard_map/psum | solution.py:25
  80.8 41.9 %copy-start.1 = (f32[1,24,2,128]{3,2,1,0:T(2,128)S(1)}, f32[1,24,2,128]{3,2,1,0:T(2,128)}, u32[]{:S(2)}) copy-start(f32[1,24,2,128]{3,2,1,0:T(2,128)} %param.12) | copy-start | bytes 73732
  95.9 78.1 %all-gather.7.cloned.1.call-start = ((), (), s32[]{:S(2)}) async-start(), calls=%async_computation.2 | async-start | bytes 4456448 | tf_op jit(solution)/shard_map/all_gather | solution.py:9
  122.6 238.1 %all-reduce.5.cloned.1.call-start = ((), (), s32[]{:S(2)}) async-start(), calls=%async_computation.1 | async-start | bytes 131072 | tf_op jit(solution)/shard_map/psum | solution.py:77
  174.0 70.5 %copy-start.2 = (f32[1,24,256]{2,1,0:T(8,128)S(1)}, f32[1,24,256]{2,1,0:T(8,128)}, u32[]{:S(2)}) copy-start(f32[1,24,256]{2,1,0:T(8,128)} %param.13) | copy-start | bytes 73732
  243.2 119.0 %copy-start = (f32[24,256]{1,0:T(8,128)}, f32[24,256]{1,0:T(8,128)S(1)}, u32[]{:S(2)}) copy-start(f32[24,256]{1,0:T(8,128)S(1)} %get-tuple-element.328) | copy-start | bytes 73732
Sparse Core Ops, SparseCore 0:
  96.1 24.7 all-reduce.2
  123.3 50.6 all-gather.6
  244.6 116.0 all-reduce.4
where the time goes:
time: 374 us; the launch traced here: 369 us
  waiting for transfers between devices  130 us (35%)
  matrix products  101 us (27%)
  blocking collectives  73.6 us (20%)
  local copies, waits for them, and re-layouts  44.7 us (12%)
  between operations  14.6 us (4%)
    psum x1, waiting for transfers between devices, body(): lax.psum((local_kernel, local_noise), ('inner', 'outer'))  75.7 us
    psum x1, blocking collectives, body(): lax.psum((local_kernel, local_noise), ('inner', 'outer'))  39.3 us
    all_gather x3, blocking collectives, entering(): pieces = jax.tree.map(lambda part: lax.all_gather(part, axis), value)  34.4 us
    dynamic_slice x48, local copies, waits for them, and re-layouts, body(): lax.scan(summarize, (unit, nothing), (blocks, derivative_results), revers...  33.9 us
    dot_general x24, matrix products, summarize(): new_mat = jnp.dot(wide.T, carry[0], precision=lax.Precision.HIGHEST)  30.3 us
    all_gather x1, waiting for transfers between devices, entering(): pieces = jax.tree.map(lambda part: lax.all_gather(part, axis), value)  29.2 us
    psum x1, waiting for transfers between devices, spread(): return lax.psum(block, axis)  24.9 us
    dot_general x24, matrix products, summarize(): jnp.dot(grad_row + carry[1], wide, precision=lax.Precision.HIGHEST)  24.9 us
  transfers between devices with their start and end apart: 3, of which 3 were waited for; matrix products, arithmetic and copies ran while one was open for 0% of the time, Pallas kernels for 0%

commit v1 on v0

v1 whole, which is shorter than its diff:
```python
import jax
import jax.numpy as jnp
from jax import lax
from jax.sharding import PartitionSpec as P

EXACT = lax.Precision.HIGHEST
AXES = ("inner", "outer")


def vecmat(v, q):
    return jnp.einsum("nj,njk->nk", v, q.astype(jnp.float32), precision=EXACT)


def matmat(later, earlier):
    if later.dtype == jnp.bfloat16 and earlier.dtype == jnp.bfloat16:
        return jnp.einsum("nij,njk->nik", later, earlier, preferred_element_type=jnp.float32)
    return jnp.einsum(
        "nij,njk->nik", later.astype(jnp.float32), earlier.astype(jnp.float32), precision=EXACT
    )


def upsweep(q, v):
    levels = [(q, v)]
    while q.shape[0] > 1:
        n = q.shape[0]
        half = n // 2
        qa, qb = q[0 : 2 * half : 2], q[1 : 2 * half : 2]
        va, vb = v[0 : 2 * half : 2], v[1 : 2 * half : 2]
        nq = matmat(qb, qa)
        nv = vecmat(vb, qa) + va
        if n % 2:
            nq = jnp.concatenate([nq, q[-1:].astype(jnp.float32)], axis=0)
            nv = jnp.concatenate([nv, v[-1:]], axis=0)
        q, v = nq, nv
        levels.append((q, v))
    return levels


def downsweep(levels, incoming):
    m = incoming
    for q, v in reversed(levels[:-1]):
        n = q.shape[0]
        half = n // 2
        top = m[:half]
        left = vecmat(top, q[1 : 2 * half : 2]) + v[1 : 2 * half : 2]
        m_new = jnp.stack([left, top], axis=1).reshape(2 * half, -1)
        if n % 2:
            m_new = jnp.concatenate([m_new, m[-1:]], axis=0)
        m = m_new
    return m


def place(b):
    inner = lax.axis_size("inner")
    return (b % inner) * lax.axis_size("outer") + b // inner


def shift_from_later(x, d, count):
    return lax.ppermute(x, AXES, [(place(j + d), place(j)) for j in range(count - d)])


def body(propagator_matrices, smoothed_adjoints, station_loadings, offset_response):
    blocks = propagator_matrices[0]
    grads = smoothed_adjoints[0]
    stations = station_loadings.shape[3]
    count = lax.axis_size("outer") * lax.axis_size("inner")
    me = lax.axis_index("outer") * lax.axis_size("inner") + lax.axis_index("inner")

    leaf_v = vecmat(grads, blocks)
    levels = upsweep(blocks, leaf_v)
    q, v = levels[-1]
    q, v = q[0].astype(jnp.float32), v[0]

    span = 1
    while 2 * span < count:
        rq, rv = shift_from_later((q, v), span, count)
        valid = me + span < count
        nq = jnp.dot(rq, q, precision=EXACT)
        nv = jnp.dot(rv, q, precision=EXACT) + v
        q = jnp.where(valid, nq, q)
        v = jnp.where(valid, nv, v)
        span *= 2
    rv = shift_from_later(v, span, count)
    w = jnp.where(me + span < count, jnp.dot(rv, q, precision=EXACT) + v, v)
    incoming = shift_from_later(w, 1, count)
    incoming = jnp.where(me + 1 < count, incoming, jnp.zeros_like(incoming))

    after = downsweep(levels, incoming[None, :])
    length_rates = grads + after
    argument_values = station_loadings[0]
    local_kernel = jnp.dot(
        length_rates[:, :stations].T, argument_values[:, 0, :], precision=EXACT
    )
    local_kernel = local_kernel + jnp.dot(
        length_rates[:, stations:].T, argument_values[:, 1, :], precision=EXACT
    )
    local_noise = -jnp.sum(length_rates * offset_response[0])
    noise_row = jnp.zeros((1, local_kernel.shape[1]), jnp.float32).at[0, 0].set(local_noise)
    packed = jnp.concatenate([local_kernel, noise_row], axis=0)
    d = 1
    while d < count:
        packed = packed + lax.ppermute(packed, AXES, [(place(j), place(j ^ d)) for j in range(count)])
        d *= 2
    return (length_rates[None], packed[:stations], packed[stations, 0])


def solution(mesh):
    return jax.shard_map(
        body,
        mesh=mesh,
        in_specs=(
            P("outer", "inner", None, None),
            P("outer", "inner", None),
            P("outer", "inner", None, None),
            P("outer", "inner", None),
        ),
        out_specs=(P("outer", "inner", None), P(), P()),
        check_vma=False,
    )
```

time: 374 us -> 96.9 us (0.26); the launches traced: 369 us -> 96.5 us
  waiting for transfers between devices: 130 us -> 48 us
  matrix products: 101 us -> 23.9 us
  blocking collectives: 73.6 us -> 0 us
  local copies, waits for them, and re-layouts: 44.7 us -> 1.46 us
  starting transfers between devices: 0.12 us -> 18.4 us
  between operations: 14.6 us -> 2.45 us
    psum x2 -> x0, waiting for transfers between devices: 101 us -> none  [the longest x1 75.7 us: body(): lax.psum((local_kernel, local_noise), ('inner', 'outer'))]
    dot_general x92 -> x25, matrix products: 100 us -> 23.3 us  [the longest x11 9.72 us: vecmat(): return jnp.einsum('nj,njk->nk', v, q.astype(jnp.float32), precision=EXACT)]
    ppermute x0 -> x15, waiting for transfers between devices: none -> 48 us  [the longest x10 34 us: shift_from_later(): lax.ppermute(x, AXES, [(place(j + d), place(j)) for j in range(count - d)])]
    psum x1 -> x0, blocking collectives: 39.3 us -> none  [body(): lax.psum((local_kernel, local_noise), ('inner', 'outer'))]
    all_gather x3 -> x0, blocking collectives: 34.4 us -> none  [entering(): pieces = jax.tree.map(lambda part: lax.all_gather(part, axis), value)]
    dynamic_slice x64 -> x0, local copies, waits for them, and re-layouts: 34.1 us -> none  [the longest x48 33.9 us: body(): lax.scan(summarize, (unit, nothing), (blocks, derivative_results), revers...]
    all_gather x1 -> x0, waiting for transfers between devices: 29.2 us -> none  [entering(): pieces = jax.tree.map(lambda part: lax.all_gather(part, axis), value)]
    ppermute x0 -> x15, starting transfers between devices: none -> 18.4 us  [the longest x10 13.4 us: shift_from_later(): lax.ppermute(x, AXES, [(place(j + d), place(j)) for j in range(count - d)])]
  transfers between devices with their start and end apart: 3 -> 15, of which waited for: 3 -> 14; matrix products, arithmetic and copies ran while one was open for 0% -> 5% of each run, Pallas kernels for 0% -> 0%
where the time goes in v1:
time: 96.9 us; the launch traced here: 96.5 us
  waiting for transfers between devices  48 us (50%)
  matrix products  23.9 us (25%)
  starting transfers between devices  18.4 us (19%)
  between operations  2.45 us (3%)
  other arithmetic  2.26 us (2%)
  local copies, waits for them, and re-layouts  1.46 us (2%)
    ppermute x10, waiting for transfers between devices, shift_from_later(): lax.ppermute(x, AXES, [(place(j + d), place(j)) for j in range(count - d)])  34 us
    ppermute x5, waiting for transfers between devices, body(): lax.ppermute(packed, AXES, [(place(j), place(j ^ d)) for j in range(count)])  14 us
    ppermute x10, starting transfers between devices, shift_from_later(): lax.ppermute(x, AXES, [(place(j + d), place(j)) for j in range(count - d)])  13.4 us
    dot_general x11, matrix products, vecmat(): return jnp.einsum('nj,njk->nk', v, q.astype(jnp.float32), precision=EXACT)  9.72 us
    dot_general x4, matrix products, matmat(): jnp.einsum('nij,njk->nik', later.astype(jnp.float32), earlier.astype(jnp....  7.94 us
    ppermute x5, starting transfers between devices, body(): lax.ppermute(packed, AXES, [(place(j), place(j ^ d)) for j in range(count)])  5.05 us
    dot_general x4, matrix products, body(): nq = jnp.dot(rq, q, precision=EXACT)  2.47 us
    dot_general x1, matrix products, matmat(): jnp.einsum('nij,njk->nik', later, earlier, preferred_element_type=jnp.flo...  2.24 us
  transfers between devices with their start and end apart: 15, of which 14 were waited for; matrix products, arithmetic and copies ran while one was open for 5% of the time, Pallas kernels for 0%

profile of v1, /device:TPU:0, one launch (start us, length us, event | category | flops | bytes accessed | tf_op | source)
XLA Modules:
  0.0 96.5 jit_solution(1994618842511407475)
XLA Ops:
  0.6 3.4 %fusion.26 = f32[24,1,256]{2,1,0:T(1,128)S(1)} fusion(f32[24,256,1]{1,0,2:T(8,128)} %bitcast.124, bf16[1,24,256,256]{3,2,1,0:T(8,128)(2,1)} %param.6), kind=kOutput, calls=%fused_computation.43 | convolution fusion | flops 18874368 | bytes 3194880 | tf_op jit(solution)/shard_map/nj,njk->nk/dot_general | solution.py:11
  4.1 2.2 %fusion.9 = f32[12,256,256]{2,1,0:T(8,128)} fusion(bf16[24,256,256]{2,1,0:T(8,128)(2,1)S(1)} %bitcast.121), kind=kOutput, calls=%fused_computation.9 | convolution fusion | flops 402653184 | bytes 6291456 | tf_op jit(solution)/shard_map/nij,njk->nik/dot_general | solution.py:16
  6.3 0.7 fusion.12
  7.1 4.8 %fusion.2 = f32[6,256,256]{2,1,0:T(8,128)} fusion(f32[12,256,256]{2,1,0:T(8,128)} %fusion.9), kind=kOutput, calls=%fused_computation.2 | convolution fusion | flops 1207959552 | bytes 4718592 | tf_op jit(solution)/shard_map/nij,njk->nik/dot_general | solution.py:17
  11.9 0.9 fusion.5
  12.8 2.4 %fusion.18 = f32[3,256,256]{2,1,0:T(8,128)S(1)} fusion(f32[6,256,256]{2,1,0:T(8,128)} %fusion.2), kind=kOutput, calls=%fused_computation.26 | convolution fusion | flops 603979776 | bytes 2359296 | tf_op jit(solution)/shard_map/nij,njk->nik/dot_general | solution.py:17
  15.2 0.4 fusion.23
  15.6 0.5 fusion.21
  16.1 0.2 fusion.42
  16.3 0.2 fusion.15
  16.5 1.3 %collective-permute-start = (f32[256]{0:T(256)S(1)}, f32[256]{0:T(256)S(1)}, u32[]{:S(2)}, u32[]{:S(2)}) collective-permute-start(f32[256]{0:T(256)S(1)} %bitcast.136), channel_id=1, source_target_pairs={{16,0},{1,16},{17,1},{2,17},{18,2},{3,18},{19,3},{4,19},{20,4},{5,... | collective-permute-start | bytes 3080 | tf_op jit(solution)/shard_map/ppermute | solution.py:59
  17.9 0.4 fusion.24
  18.2 1.3 %collective-permute-start.2 = (f32[256,256]{1,0:T(8,128)S(1)}, f32[256,256]{1,0:T(8,128)}, u32[]{:S(2)}, u32[]{:S(2)}) collective-permute-start(f32[256,256]{1,0:T(8,128)S(1)} %fusion.24), channel_id=1, source_target_pairs={{16,0},{1,16},{17,1},{2,17},{18,2},{3,18},{19,3},{4,19},{20,4},{5,... | collective-permute-start | bytes 786440 | tf_op jit(solution)/shard_map/ppermute | solution.py:59
  19.6 3.4 %collective-permute-done = f32[256]{0:T(256)S(1)} collective-permute-done((f32[256]{0:T(256)S(1)}, f32[256]{0:T(256)S(1)}, u32[]{:S(2)}, u32[]{:S(2)}) %collective-permute-start) | collective-permute-done | bytes 1056 | tf_op jit(solution)/shard_map/ppermute | solution.py:59
  23.0 0.2 fusion.49
  23.2 1.3 %collective-permute-start.1 = (f32[256]{0:T(256)S(1)}, f32[256]{0:T(256)S(1)}, u32[]{:S(2)}, u32[]{:S(2)}) collective-permute-start(f32[256]{0:T(256)S(1)} %add_select_fusion.4), channel_id=1, source_target_pairs={{1,0},{17,16},{2,1},{18,17},{3,2},{19,18},{4,3},{20,19},{5,4},{21,... | collective-permute-start | bytes 3080 | tf_op jit(solution)/shard_map/ppermute | solution.py:59
  24.5 5.3 %collective-permute-done.2 = f32[256,256]{1,0:T(8,128)} collective-permute-done((f32[256,256]{1,0:T(8,128)S(1)}, f32[256,256]{1,0:T(8,128)}, u32[]{:S(2)}, u32[]{:S(2)}) %collective-permute-start.2) | collective-permute-done | bytes 262176 | tf_op jit(solution)/shard_map/ppermute | solution.py:59
  29.8 1.3 %convolution_select_fusion.3 = f32[256,256]{1,0:T(8,128)S(1)} fusion(f32[256,256]{1,0:T(8,128)S(1)} %fusion.24, f32[256,256]{1,0:T(8,128)} %collective-permute-done.2, pred[]{:T(512)S(6)} %lt.16), kind=kOutput, calls=%fused_computation.17 | convolution fusion | flops 201392128 | bytes 786433 | tf_op jit(solution)/shard_map/dot_general | solution.py:78
  31.2 1.3 %collective-permute-start.4 = (f32[256,256]{1,0:T(8,128)S(1)}, f32[256,256]{1,0:T(8,128)S(1)}, u32[]{:S(2)}, u32[]{:S(2)}) collective-permute-start(f32[256,256]{1,0:T(8,128)S(1)} %convolution_select_fusion.3), channel_id=1, source_target_pairs={{1,0},{17,16},{2,1},{18,17},{3,2},{19,18},{4,3},{20,19},{5,4},{21,... | collective-permute-start | bytes 786440 | tf_op jit(solution)/shard_map/ppermute | solution.py:59
  32.5 0.2 fusion.50
  32.7 0.0 copy-start.7
  32.8 1.4 %collective-permute-start.3 = (f32[256]{0:T(256)S(1)}, f32[256]{0:T(256)S(1)}, u32[]{:S(2)}, u32[]{:S(2)}) collective-permute-start(f32[256]{0:T(256)S(1)} %add_select_fusion.3), channel_id=1, source_target_pairs={{2,0},{18,16},{3,1},{19,17},{4,2},{20,18},{5,3},{21,19},{6,4},{22,... | collective-permute-start | bytes 3080 | tf_op jit(solution)/shard_map/ppermute | solution.py:59
  34.2 0.9 collective-permute-done.4
  35.1 0.4 convolution_select_fusion.2
  35.5 1.4 %collective-permute-start.6 = (f32[256,256]{1,0:T(8,128)S(1)}, f32[256,256]{1,0:T(8,128)S(1)}, u32[]{:S(2)}, u32[]{:S(2)}) collective-permute-start(f32[256,256]{1,0:T(8,128)S(1)} %convolution_select_fusion.2), channel_id=1, source_target_pairs={{2,0},{18,16},{3,1},{19,17},{4,2},{20,18},{5,3},{21,19},{6,4},{22,... | collective-permute-start | bytes 786440 | tf_op jit(solution)/shard_map/ppermute | solution.py:59
  36.9 4.3 %collective-permute-done.3 = f32[256]{0:T(256)S(1)} collective-permute-done((f32[256]{0:T(256)S(1)}, f32[256]{0:T(256)S(1)}, u32[]{:S(2)}, u32[]{:S(2)}) %collective-permute-start.3) | collective-permute-done | bytes 1056 | tf_op jit(solution)/shard_map/ppermute | solution.py:59
  41.3 0.2 fusion.51
  41.5 1.3 %collective-permute-start.5 = (f32[256]{0:T(256)S(1)}, f32[256]{0:T(256)S(1)}, u32[]{:S(2)}, u32[]{:S(2)}) collective-permute-start(f32[256]{0:T(256)S(1)} %add_select_fusion.2), channel_id=1, source_target_pairs={{4,0},{20,16},{5,1},{21,17},{6,2},{22,18},{7,3},{23,19},{8,4},{24,... | collective-permute-start | bytes 3080 | tf_op jit(solution)/shard_map/ppermute | solution.py:59
  42.8 5.6 %collective-permute-done.6 = f32[256,256]{1,0:T(8,128)S(1)} collective-permute-done((f32[256,256]{1,0:T(8,128)S(1)}, f32[256,256]{1,0:T(8,128)S(1)}, u32[]{:S(2)}, u32[]{:S(2)}) %collective-permute-start.6) | collective-permute-done | bytes 262176 | tf_op jit(solution)/shard_map/ppermute | solution.py:59
  48.4 0.4 convolution_select_fusion.1
  48.8 1.3 %collective-permute-start.8 = (f32[256,256]{1,0:T(8,128)S(1)}, f32[256,256]{1,0:T(8,128)S(1)}, u32[]{:S(2)}, u32[]{:S(2)}) collective-permute-start(f32[256,256]{1,0:T(8,128)S(1)} %convolution_select_fusion.1), channel_id=1, source_target_pairs={{4,0},{20,16},{5,1},{21,17},{6,2},{22,18},{7,3},{23,19},{8,4},{24,... | collective-permute-start | bytes 786440 | tf_op jit(solution)/shard_map/ppermute | solution.py:59
  50.1 0.1 collective-permute-done.5
  50.1 0.2 fusion.52
  50.4 1.3 %collective-permute-start.7 = (f32[256]{0:T(256)S(1)}, f32[256]{0:T(256)S(1)}, u32[]{:S(2)}, u32[]{:S(2)}) collective-permute-start(f32[256]{0:T(256)S(1)} %add_select_fusion.1), channel_id=1, source_target_pairs={{8,0},{24,16},{9,1},{25,17},{10,2},{26,18},{11,3},{27,19},{12,4},{... | collective-permute-start | bytes 3080 | tf_op jit(solution)/shard_map/ppermute | solution.py:59
  51.7 10.2 %collective-permute-done.8 = f32[256,256]{1,0:T(8,128)S(1)} collective-permute-done((f32[256,256]{1,0:T(8,128)S(1)}, f32[256,256]{1,0:T(8,128)S(1)}, u32[]{:S(2)}, u32[]{:S(2)}) %collective-permute-start.8) | collective-permute-done | bytes 262176 | tf_op jit(solution)/shard_map/ppermute | solution.py:59
  61.9 0.4 convolution_select_fusion
  62.3 0.8 collective-permute-done.7
  63.1 0.2 fusion.53
  63.3 1.5 %collective-permute-start.9 = (f32[256]{0:T(256)S(1)}, f32[256]{0:T(256)S(1)}, u32[]{:S(2)}, u32[]{:S(2)}) collective-permute-start(f32[256]{0:T(256)S(1)} %add_select_fusion), channel_id=1, source_target_pairs={{16,0},{1,16},{17,1},{2,17},{18,2},{3,18},{19,3},{4,19},{20,4},{5,... | collective-permute-start | bytes 3080 | tf_op jit(solution)/shard_map/ppermute | solution.py:59
  64.8 0.6 compare_reduce_fusion
  65.5 3.3 %collective-permute-done.9 = f32[256]{0:T(256)S(1)} collective-permute-done((f32[256]{0:T(256)S(1)}, f32[256]{0:T(256)S(1)}, u32[]{:S(2)}, u32[]{:S(2)}) %collective-permute-start.9) | collective-permute-done | bytes 1056 | tf_op jit(solution)/shard_map/ppermute | solution.py:59
  68.8 0.2 convolution_add_fusion.2
  69.0 0.2 fusion.14
  69.3 0.5 fusion.16
  69.8 0.0 copy-start.6
  69.8 0.0 copy-start.8
  69.8 2.3 %fusion = f32[6,1,256]{2,1,0:T(1,128)S(1)} fusion(f32[6,256,1]{1,2,0:T(1,128)S(1)} %reshape.140, f32[12,256,256]{2,1,0:T(8,128)} %fusion.9), kind=kOutput, calls=%fused_computation | convolution fusion | flops 4718592 | bytes 1585152 | tf_op jit(solution)/shard_map/nj,njk->nk/dot_general | solution.py:11
  72.2 0.7 fusion.7
  73.0 0.6 fusion.25
  74.3 0.3 fusion.30
  74.6 0.3 convolution_add_fusion
  75.5 0.1 collective-permute-start.10
  75.6 4.3 %collective-permute-done.10 = f32[129,128]{1,0:T(8,128)S(1)} collective-permute-done((f32[129,128]{1,0:T(8,128)S(1)}, f32[129,128]{1,0:T(8,128)S(1)}, u32[]{:S(2)}, u32[]{:S(2)}) %collective-permute-start.10) | collective-permute-done | bytes 66080 | tf_op jit(solution)/shard_map/ppermute | solution.py:102
  79.9 0.1 collective-permute-start.11
  80.0 1.2 %collective-permute-done.11 = f32[129,128]{1,0:T(8,128)S(1)} collective-permute-done((f32[129,128]{1,0:T(8,128)S(1)}, f32[129,128]{1,0:T(8,128)S(1)}, u32[]{:S(2)}, u32[]{:S(2)}) %collective-permute-start.11) | collective-permute-done | bytes 66080 | tf_op jit(solution)/shard_map/ppermute | solution.py:102
  81.2 1.2 %collective-permute-start.12 = (f32[129,128]{1,0:T(8,128)S(1)}, f32[129,128]{1,0:T(8,128)S(1)}, u32[]{:S(2)}, u32[]{:S(2)}) collective-permute-start(f32[129,128]{1,0:T(8,128)S(1)} %add.117), channel_id=1, source_target_pairs={{0,2},{16,18},{1,3},{17,19},{2,0},{18,16},{3,1},{19,17},{4,6},{20,... | collective-permute-start | bytes 198152 | tf_op jit(solution)/shard_map/ppermute | solution.py:102
  82.5 3.2 %collective-permute-done.12 = f32[129,128]{1,0:T(8,128)S(1)} collective-permute-done((f32[129,128]{1,0:T(8,128)S(1)}, f32[129,128]{1,0:T(8,128)S(1)}, u32[]{:S(2)}, u32[]{:S(2)}) %collective-permute-start.12) | collective-permute-done | bytes 66080 | tf_op jit(solution)/shard_map/ppermute | solution.py:102
  85.6 1.7 %collective-permute-start.13 = (f32[129,128]{1,0:T(8,128)S(1)}, f32[129,128]{1,0:T(8,128)S(1)}, u32[]{:S(2)}, u32[]{:S(2)}) collective-permute-start(f32[129,128]{1,0:T(8,128)S(1)} %add.118), channel_id=1, source_target_pairs={{0,4},{16,20},{1,5},{17,21},{2,6},{18,22},{3,7},{19,23},{4,0},{20,... | collective-permute-start | bytes 198152 | tf_op jit(solution)/shard_map/ppermute | solution.py:102
  87.3 2.7 %collective-permute-done.13 = f32[129,128]{1,0:T(8,128)S(1)} collective-permute-done((f32[129,128]{1,0:T(8,128)S(1)}, f32[129,128]{1,0:T(8,128)S(1)}, u32[]{:S(2)}, u32[]{:S(2)}) %collective-permute-start.13) | collective-permute-done | bytes 66080 | tf_op jit(solution)/shard_map/ppermute | solution.py:102
  90.0 2.0 %collective-permute-start.14 = (f32[129,128]{1,0:T(8,128)S(1)}, f32[129,128]{1,0:T(8,128)S(1)}, u32[]{:S(2)}, u32[]{:S(2)}) collective-permute-start(f32[129,128]{1,0:T(8,128)S(1)} %add.119), channel_id=1, source_target_pairs={{0,8},{16,24},{1,9},{17,25},{2,10},{18,26},{3,11},{19,27},{4,12},{... | collective-permute-start | bytes 198152 | tf_op jit(solution)/shard_map/ppermute | solution.py:102
  92.1 0.6 add.113
  92.7 2.6 %collective-permute-done.14 = f32[129,128]{1,0:T(8,128)S(1)} collective-permute-done((f32[129,128]{1,0:T(8,128)S(1)}, f32[129,128]{1,0:T(8,128)S(1)}, u32[]{:S(2)}, u32[]{:S(2)}) %collective-permute-start.14) | collective-permute-done | bytes 66080 | tf_op jit(solution)/shard_map/ppermute | solution.py:102
  95.3 0.6 slice.145
  95.9 0.5 slice.146
  (56 shorter events, 0.7 us)
Async XLA Ops:
  0.6 3.4 %copy-start = (bf16[1,24,256,256]{3,2,1,0:T(8,128)(2,1)S(1)}, bf16[1,24,256,256]{3,2,1,0:T(8,128)(2,1)}, u32[]{:S(2)}) copy-start(bf16[1,24,256,256]{3,2,1,0:T(8,128)(2,1)} %param.6) | copy-start | bytes 9437188
  7.1 4.8 %copy-start.1 = (f32[12,256,256]{2,1,0:T(8,128)S(1)}, f32[12,256,256]{2,1,0:T(8,128)}, u32[]{:S(2)}) copy-start(f32[12,256,256]{2,1,0:T(8,128)} %fusion.9) | copy-start | bytes 9437188
  12.8 2.8 %copy-start.2 = (f32[6,256,256]{2,1,0:T(8,128)S(1)}, f32[6,256,256]{2,1,0:T(8,128)}, u32[]{:S(2)}) copy-start(f32[6,256,256]{2,1,0:T(8,128)} %fusion.2) | copy-start | bytes 4718596
  15.2 2.7 %copy-start.4 = (f32[3,256,256]{2,1,0:T(8,128)}, f32[3,256,256]{2,1,0:T(8,128)S(1)}, u32[]{:S(2)}) copy-start(f32[3,256,256]{2,1,0:T(8,128)S(1)} %fusion.18) | copy-start | bytes 2359300
  16.5 6.4 %collective-permute-start = (f32[256]{0:T(256)S(1)}, f32[256]{0:T(256)S(1)}, u32[]{:S(2)}, u32[]{:S(2)}) collective-permute-start(f32[256]{0:T(256)S(1)} %bitcast.136), channel_id=1, source_target_pairs={{16,0},{1,16},{17,1},{2,17},{18,2},{3,18},{19,3},{4,19},{20,4},{5,... | collective-permute-start | bytes 3080 | tf_op jit(solution)/shard_map/ppermute | solution.py:59
  18.2 11.6 %collective-permute-start.2 = (f32[256,256]{1,0:T(8,128)S(1)}, f32[256,256]{1,0:T(8,128)}, u32[]{:S(2)}, u32[]{:S(2)}) collective-permute-start(f32[256,256]{1,0:T(8,128)S(1)} %fusion.24), channel_id=1, source_target_pairs={{16,0},{1,16},{17,1},{2,17},{18,2},{3,18},{19,3},{4,19},{20,4},{5,... | collective-permute-start | bytes 786440 | tf_op jit(solution)/shard_map/ppermute | solution.py:59
  23.2 9.3 %collective-permute-start.1 = (f32[256]{0:T(256)S(1)}, f32[256]{0:T(256)S(1)}, u32[]{:S(2)}, u32[]{:S(2)}) collective-permute-start(f32[256]{0:T(256)S(1)} %add_select_fusion.4), channel_id=1, source_target_pairs={{1,0},{17,16},{2,1},{18,17},{3,2},{19,18},{4,3},{20,19},{5,4},{21,... | collective-permute-start | bytes 3080 | tf_op jit(solution)/shard_map/ppermute | solution.py:59
  31.2 3.9 %collective-permute-start.4 = (f32[256,256]{1,0:T(8,128)S(1)}, f32[256,256]{1,0:T(8,128)S(1)}, u32[]{:S(2)}, u32[]{:S(2)}) collective-permute-start(f32[256,256]{1,0:T(8,128)S(1)} %convolution_select_fusion.3), channel_id=1, source_target_pairs={{1,0},{17,16},{2,1},{18,17},{3,2},{19,18},{4,3},{20,19},{5,4},{21,... | collective-permute-start | bytes 786440 | tf_op jit(solution)/shard_map/ppermute | solution.py:59
  32.7 32.0 %copy-start.7 = (f32[1,24,2,128]{3,2,1,0:T(2,128)S(1)}, f32[1,24,2,128]{3,2,1,0:T(2,128)}, u32[]{:S(2)}) copy-start(f32[1,24,2,128]{3,2,1,0:T(2,128)} %param.8) | copy-start | bytes 73732
  32.7 36.0 %copy-start.5 = (f32[3,256,256]{2,1,0:T(8,128)S(1)}, f32[3,256,256]{2,1,0:T(8,128)}, u32[]{:S(2)}) copy-start(f32[3,256,256]{2,1,0:T(8,128)} %copy-done.4) | copy-start | bytes 2359300
  32.8 8.5 %collective-permute-start.3 = (f32[256]{0:T(256)S(1)}, f32[256]{0:T(256)S(1)}, u32[]{:S(2)}, u32[]{:S(2)}) collective-permute-start(f32[256]{0:T(256)S(1)} %add_select_fusion.3), channel_id=1, source_target_pairs={{2,0},{18,16},{3,1},{19,17},{4,2},{20,18},{5,3},{21,19},{6,4},{22,... | collective-permute-start | bytes 3080 | tf_op jit(solution)/shard_map/ppermute | solution.py:59
  35.5 33.8 %copy-start.3 = (f32[6,256,256]{2,1,0:T(8,128)S(1)}, f32[6,256,256]{2,1,0:T(8,128)}, u32[]{:S(2)}) copy-start(f32[6,256,256]{2,1,0:T(8,128)} %fusion.2) | copy-start | bytes 4718596
  35.5 12.9 %collective-permute-start.6 = (f32[256,256]{1,0:T(8,128)S(1)}, f32[256,256]{1,0:T(8,128)S(1)}, u32[]{:S(2)}, u32[]{:S(2)}) collective-permute-start(f32[256,256]{1,0:T(8,128)S(1)} %convolution_select_fusion.2), channel_id=1, source_target_pairs={{2,0},{18,16},{3,1},{19,17},{4,2},{20,18},{5,3},{21,19},{6,4},{22,... | collective-permute-start | bytes 786440 | tf_op jit(solution)/shard_map/ppermute | solution.py:59
  41.5 8.6 %collective-permute-start.5 = (f32[256]{0:T(256)S(1)}, f32[256]{0:T(256)S(1)}, u32[]{:S(2)}, u32[]{:S(2)}) collective-permute-start(f32[256]{0:T(256)S(1)} %add_select_fusion.2), channel_id=1, source_target_pairs={{4,0},{20,16},{5,1},{21,17},{6,2},{22,18},{7,3},{23,19},{8,4},{24,... | collective-permute-start | bytes 3080 | tf_op jit(solution)/shard_map/ppermute | solution.py:59
  48.8 13.1 %collective-permute-start.8 = (f32[256,256]{1,0:T(8,128)S(1)}, f32[256,256]{1,0:T(8,128)S(1)}, u32[]{:S(2)}, u32[]{:S(2)}) collective-permute-start(f32[256,256]{1,0:T(8,128)S(1)} %convolution_select_fusion.1), channel_id=1, source_target_pairs={{4,0},{20,16},{5,1},{21,17},{6,2},{22,18},{7,3},{23,19},{8,4},{24,... | collective-permute-start | bytes 786440 | tf_op jit(solution)/shard_map/ppermute | solution.py:59
  50.4 12.7 %collective-permute-start.7 = (f32[256]{0:T(256)S(1)}, f32[256]{0:T(256)S(1)}, u32[]{:S(2)}, u32[]{:S(2)}) collective-permute-start(f32[256]{0:T(256)S(1)} %add_select_fusion.1), channel_id=1, source_target_pairs={{8,0},{24,16},{9,1},{25,17},{10,2},{26,18},{11,3},{27,19},{12,4},{... | collective-permute-start | bytes 3080 | tf_op jit(solution)/shard_map/ppermute | solution.py:59
  63.3 5.5 %collective-permute-start.9 = (f32[256]{0:T(256)S(1)}, f32[256]{0:T(256)S(1)}, u32[]{:S(2)}, u32[]{:S(2)}) collective-permute-start(f32[256]{0:T(256)S(1)} %add_select_fusion), channel_id=1, source_target_pairs={{16,0},{1,16},{17,1},{2,17},{18,2},{3,18},{19,3},{4,19},{20,4},{5,... | collective-permute-start | bytes 3080 | tf_op jit(solution)/shard_map/ppermute | solution.py:59
  69.8 3.2 %copy-start.6 = (f32[1,24,256]{2,1,0:T(8,128)S(1)}, f32[1,24,256]{2,1,0:T(8,128)}, u32[]{:S(2)}) copy-start(f32[1,24,256]{2,1,0:T(8,128)} %param.7) | copy-start | bytes 73732
  69.8 3.2 %copy-start.8 = (f32[1,24,256]{2,1,0:T(8,128)S(1)}, f32[1,24,256]{2,1,0:T(8,128)}, u32[]{:S(2)}) copy-start(f32[1,24,256]{2,1,0:T(8,128)} %param.9) | copy-start | bytes 73732
  75.5 4.4 %collective-permute-start.10 = (f32[129,128]{1,0:T(8,128)S(1)}, f32[129,128]{1,0:T(8,128)S(1)}, u32[]{:S(2)}, u32[]{:S(2)}) collective-permute-start(f32[129,128]{1,0:T(8,128)S(1)} %select_maximum_fusion), channel_id=1, source_target_pairs={{0,16},{16,0},{1,17},{17,1},{2,18},{18,2},{3,19},{19,3},{4,20},{20... | collective-permute-start | bytes 198152 | tf_op jit(solution)/shard_map/ppermute | solution.py:102
  79.9 1.3 %collective-permute-start.11 = (f32[129,128]{1,0:T(8,128)S(1)}, f32[129,128]{1,0:T(8,128)S(1)}, u32[]{:S(2)}, u32[]{:S(2)}) collective-permute-start(f32[129,128]{1,0:T(8,128)S(1)} %fusion.47), channel_id=1, source_target_pairs={{0,1},{16,17},{1,0},{17,16},{2,3},{18,19},{3,2},{19,18},{4,5},{20,... | collective-permute-start | bytes 198152 | tf_op jit(solution)/shard_map/ppermute | solution.py:102
  81.2 4.4 %collective-permute-start.12 = (f32[129,128]{1,0:T(8,128)S(1)}, f32[129,128]{1,0:T(8,128)S(1)}, u32[]{:S(2)}, u32[]{:S(2)}) collective-permute-start(f32[129,128]{1,0:T(8,128)S(1)} %add.117), channel_id=1, source_target_pairs={{0,2},{16,18},{1,3},{17,19},{2,0},{18,16},{3,1},{19,17},{4,6},{20,... | collective-permute-start | bytes 198152 | tf_op jit(solution)/shard_map/ppermute | solution.py:102
  85.6 4.4 %collective-permute-start.13 = (f32[129,128]{1,0:T(8,128)S(1)}, f32[129,128]{1,0:T(8,128)S(1)}, u32[]{:S(2)}, u32[]{:S(2)}) collective-permute-start(f32[129,128]{1,0:T(8,128)S(1)} %add.118), channel_id=1, source_target_pairs={{0,4},{16,20},{1,5},{17,21},{2,6},{18,22},{3,7},{19,23},{4,0},{20,... | collective-permute-start | bytes 198152 | tf_op jit(solution)/shard_map/ppermute | solution.py:102
  90.0 5.3 %collective-permute-start.14 = (f32[129,128]{1,0:T(8,128)S(1)}, f32[129,128]{1,0:T(8,128)S(1)}, u32[]{:S(2)}, u32[]{:S(2)}) collective-permute-start(f32[129,128]{1,0:T(8,128)S(1)} %add.119), channel_id=1, source_target_pairs={{0,8},{16,24},{1,9},{17,25},{2,10},{18,26},{3,11},{19,27},{4,12},{... | collective-permute-start | bytes 198152 | tf_op jit(solution)/shard_map/ppermute | solution.py:102

commit v2 on v1

--- a/solution.py
+++ b/solution.py
@@ -8,7 +8,7 @@
 
 
 def vecmat(v, q):
-    return jnp.einsum("nj,njk->nk", v, q.astype(jnp.float32), precision=EXACT)
+    return jnp.sum(v[:, :, None] * q.astype(jnp.float32), axis=1)
 
 
 def matmat(later, earlier):
@@ -36,17 +36,21 @@
     return levels
 
 
-def downsweep(levels, incoming):
-    m = incoming
+def downsweep(levels, top):
+    m = top
+    width = top.shape[2]
+    offset_row = jnp.zeros((1, width), jnp.float32)
     for q, v in reversed(levels[:-1]):
         n = q.shape[0]
         half = n // 2
-        top = m[:half]
-        left = vecmat(top, q[1 : 2 * half : 2]) + v[1 : 2 * half : 2]
-        m_new = jnp.stack([left, top], axis=1).reshape(2 * half, -1)
+        upper = m[:half]
+        shift = jnp.concatenate([jnp.zeros((half, top.shape[1] - 1, width), jnp.float32), v[1 : 2 * half : 2, None, :]], axis=1)
+        left = matmat(upper, q[1 : 2 * half : 2]) + shift
+        m_new = jnp.stack([left, upper], axis=1).reshape((2 * half,) + upper.shape[1:])
         if n % 2:
             m_new = jnp.concatenate([m_new, m[-1:]], axis=0)
         m = m_new
+    del offset_row
     return m
 
 
@@ -55,37 +59,48 @@
     return (b % inner) * lax.axis_size("outer") + b // inner
 
 
-def shift_from_later(x, d, count):
-    return lax.ppermute(x, AXES, [(place(j + d), place(j)) for j in range(count - d)])
+def exchange(x, d, count):
+    return lax.ppermute(x, AXES, [(place(j), place(j ^ d)) for j in range(count)])
 
 
 def body(propagator_matrices, smoothed_adjoints, station_loadings, offset_response):
     blocks = propagator_matrices[0]
     grads = smoothed_adjoints[0]
+    width = grads.shape[1]
     stations = station_loadings.shape[3]
     count = lax.axis_size("outer") * lax.axis_size("inner")
     me = lax.axis_index("outer") * lax.axis_size("inner") + lax.axis_index("inner")
 
     leaf_v = vecmat(grads, blocks)
     levels = upsweep(blocks, leaf_v)
-    q, v = levels[-1]
-    q, v = q[0].astype(jnp.float32), v[0]
+    tq, tv = levels[-1]
+    tq, tv = tq[0].astype(jnp.float32), tv[0]
+    sq = jnp.eye(width, dtype=jnp.float32)
+    sv = jnp.zeros((width,), jnp.float32)
 
-    span = 1
-    while 2 * span < count:
-        rq, rv = shift_from_later((q, v), span, count)
-        valid = me + span < count
-        nq = jnp.dot(rq, q, precision=EXACT)
-        nv = jnp.dot(rv, q, precision=EXACT) + v
-        q = jnp.where(valid, nq, q)
-        v = jnp.where(valid, nv, v)
-        span *= 2
-    rv = shift_from_later(v, span, count)
-    w = jnp.where(me + span < count, jnp.dot(rv, q, precision=EXACT) + v, v)
-    incoming = shift_from_later(w, 1, count)
-    incoming = jnp.where(me + 1 < count, incoming, jnp.zeros_like(incoming))
+    d = 1
+    while 2 * d < count:
+        lower = (me // d) % 2 == 0
+        got = exchange(jnp.concatenate([tq, tv[None, :]], axis=0), d, count)
+        rq, rv = got[:width], got[width]
+        q_up = jnp.where(lower, rq, tq)
+        q_low = jnp.where(lower, tq, rq)
+        v_up = jnp.where(lower, rv, tv)
+        v_low = jnp.where(lower, tv, rv)
+        both = jnp.dot(q_up, jnp.concatenate([q_low, sq], axis=1), precision=EXACT)
+        new_sv = jnp.sum(rv[:, None] * sq, axis=0) + sv
+        tv = jnp.sum(v_up[:, None] * q_low, axis=0) + v_low
+        tq = both[:, :width]
+        sq = jnp.where(lower, both[:, width:], sq)
+        sv = jnp.where(lower, new_sv, sv)
+        d *= 2
+    lower = (me // d) % 2 == 0
+    rv = exchange(tv, d, count)
+    incoming = jnp.where(lower, jnp.sum(rv[:, None] * sq, axis=0) + sv, sv)
 
-    after = downsweep(levels, incoming[None, :])
+    top = jnp.concatenate([jnp.eye(width, dtype=jnp.float32), jnp.zeros((1, width), jnp.float32)], axis=0)
+    maps = downsweep(levels, top[None])
+    after = jnp.sum(incoming[None, :, None] * maps[:, :width, :], axis=1) + maps[:, width, :]
     length_rates = grads + after
     argument_values = station_loadings[0]
     local_kernel = jnp.dot(
@@ -99,7 +114,7 @@
     packed = jnp.concatenate([local_kernel, noise_row], axis=0)
     d = 1
     while d < count:
-        packed = packed + lax.ppermute(packed, AXES, [(place(j), place(j ^ d)) for j in range(count)])
+        packed = packed + exchange(packed, d, count)
         d *= 2
     return (length_rates[None], packed[:stations], packed[stations, 0])
 

time: 96.9 us -> 95.3 us (0.983)
  waiting for transfers between devices: 48 us -> 21.8 us
  other arithmetic: 2.26 us -> 19.8 us
  local copies, waits for them, and re-layouts: 1.46 us -> 16.8 us
  matrix products: 23.9 us -> 19.1 us
  starting transfers between devices: 18.4 us -> 14.9 us
    ppermute x15 -> x10, waiting for transfers between devices: 48 us -> 21.8 us  [exchange(): lax.ppermute(x, AXES, [(place(j), place(j ^ d)) for j in range(count)])]
    another operation x5, local copies, waits for them, and re-layouts: 0.06 us -> 11.8 us  [downsweep(): jnp.stack([left, upper], axis=1).reshape((2 * half,) + upper.shape[1:])]
    dot_general x20 -> x4, matrix products: 13.1 us -> 3.23 us  [body(): both = jnp.dot(q_up, jnp.concatenate([q_low, sq], axis=1), precision=EXACT)]
    another operation x7 -> x9, other arithmetic: 0.69 us -> 9.79 us  [the longest x8 9.16 us: downsweep(): jnp.stack([left, upper], axis=1).reshape((2 * half,) + upper.shape[1:])]
    reduce_sum x0 -> x11, other arithmetic: none -> 5.82 us  [the longest x5 3.66 us: vecmat(): return jnp.sum(v[:, :, None] * q.astype(jnp.float32), axis=1)]
    dot_general x4 -> x9, matrix products: 7.94 us -> 13 us  [matmat(): jnp.einsum('nij,njk->nik', later.astype(jnp.float32), earlier.astype(jnp....]
    ppermute x15 -> x10, starting transfers between devices: 18.4 us -> 14.9 us  [exchange(): lax.ppermute(x, AXES, [(place(j), place(j ^ d)) for j in range(count)])]
    unnamed x18 -> x22, local copies, waits for them, and re-layouts: 0.04 us -> 2.61 us
  transfers between devices with their start and end apart: 15 -> 10, of which waited for: 14 -> 7; matrix products, arithmetic and copies ran while one was open for 5% -> 31% of each run, Pallas kernels for 0% -> 0%
where the time goes in v2:
time: 95.3 us; the launch traced here: 94.9 us
  waiting for transfers between devices  21.8 us (23%)
  other arithmetic  19.8 us (21%)
  matrix products  19.1 us (20%)
  local copies, waits for them, and re-layouts  16.8 us (18%)
  starting transfers between devices  14.9 us (16%)
  between operations  2.51 us (3%)
    ppermute x10, waiting for transfers between devices, exchange(): lax.ppermute(x, AXES, [(place(j), place(j ^ d)) for j in range(count)])  21.8 us
    ppermute x10, starting transfers between devices, exchange(): lax.ppermute(x, AXES, [(place(j), place(j ^ d)) for j in range(count)])  14.9 us
    dot_general x9, matrix products, matmat(): jnp.einsum('nij,njk->nik', later.astype(jnp.float32), earlier.astype(jnp....  13 us
    another operation x5, local copies, waits for them, and re-layouts, downsweep(): jnp.stack([left, upper], axis=1).reshape((2 * half,) + upper.shape[1:])  11.8 us
    another operation x8, other arithmetic, downsweep(): jnp.stack([left, upper], axis=1).reshape((2 * half,) + upper.shape[1:])  9.16 us
    reduce_sum x5, other arithmetic, vecmat(): return jnp.sum(v[:, :, None] * q.astype(jnp.float32), axis=1)  3.66 us
    dot_general x4, matrix products, body(): both = jnp.dot(q_up, jnp.concatenate([q_low, sq], axis=1), precision=EXACT)  3.23 us
    unnamed x22, local copies, waits for them, and re-layouts  2.61 us
  transfers between devices with their start and end apart: 10, of which 7 were waited for; matrix products, arithmetic and copies ran while one was open for 31% of the time, Pallas kernels for 0%

profile of v2, /device:TPU:0, one launch (start us, length us, event | category | flops | bytes accessed | tf_op | source)
XLA Modules:
  0.0 94.9 jit_solution(9018120351503754669)
XLA Ops:
  0.6 2.6 %multiply_reduce_fusion = f32[24,256]{1,0:T(8,128)S(1)} fusion(f32[24,256]{1,0:T(8,128)} %bitcast.97, bf16[1,24,256,256]{3,2,1,0:T(8,128)(2,1)} %param.6), kind=kLoop, calls=%fused_computation.3 | loop fusion | flops 4712448 | bytes 3194880 | tf_op jit(solution)/shard_map/reduce_sum | solution.py:11
  3.3 0.2 copy-done
  3.5 2.3 %fusion.8 = f32[12,256,256]{2,1,0:T(8,128)} fusion(bf16[24,256,256]{2,1,0:T(8,128)(2,1)S(1)} %bitcast.90), kind=kOutput, calls=%fused_computation.17 | convolution fusion | flops 402653184 | bytes 6291456 | tf_op jit(solution)/shard_map/nij,njk->nik/dot_general | solution.py:16
  5.8 0.5 multiply_reduce_fusion.1
  6.3 4.8 %fusion.3 = f32[6,256,256]{2,1,0:T(8,128)} fusion(f32[12,256,256]{2,1,0:T(8,128)} %fusion.8), kind=kOutput, calls=%fused_computation.12 | convolution fusion | flops 1207959552 | bytes 4718592 | tf_op jit(solution)/shard_map/nij,njk->nik/dot_general | solution.py:17
  11.1 0.3 multiply_reduce_fusion.2
  11.4 2.4 %fusion.16 = f32[3,256,256]{2,1,0:T(8,128)S(1)} fusion(f32[6,256,256]{2,1,0:T(8,128)} %fusion.3), kind=kOutput, calls=%fused_computation.30 | convolution fusion | flops 603979776 | bytes 2359296 | tf_op jit(solution)/shard_map/nij,njk->nik/dot_general | solution.py:17
  14.0 0.4 multiply_reduce_fusion.13
  14.6 0.4 fusion.45
  15.0 0.8 pad_maximum_fusion.4
  15.8 3.0 %collective-permute-start = (f32[257,256]{1,0:T(8,128)}, f32[257,256]{1,0:T(8,128)}, u32[]{:S(2)}, u32[]{:S(2)}) collective-permute-start(f32[257,256]{1,0:T(8,128)} %pad_maximum_fusion.4), channel_id=1, source_target_pairs={{0,16},{16,0},{1,17},{17,1},{2,18},{18,2},{3,19},{19,3},{4,20},{20... | collective-permute-start | bytes 789512 | tf_op jit(solution)/shard_map/ppermute | solution.py:63
  18.8 0.4 fusion.43
  19.2 0.2 pad_add_fusion
  19.4 0.2 fusion.85
  19.6 0.4 fusion.32
  20.0 0.3 copy.12
  20.3 0.2 add_bitcast_fusion
  20.4 0.5 maximum_bitcast_fusion
  20.9 0.5 pad_maximum_fusion.3
  21.5 1.0 %fusion.14 = f32[3,257,256]{2,1,0:T(8,128)S(1)} fusion(f32[3,257,256]{2,0,1:T(4,128)S(1)} %get-tuple-element.37, f32[6,256,256]{2,1,0:T(8,128)S(1)} %copy-done.4), kind=kOutput, calls=%fused_computation.27 | convolution fusion | flops 606339072 | bytes 2628608 | tf_op jit(solution)/shard_map/nij,njk->nik/dot_general | solution.py:17
  22.5 0.4 fusion.13
  22.9 0.6 pad_maximum_fusion.2
  23.5 0.3 copy.15
  23.9 2.1 %copy-done.2 = f32[12,256,256]{2,1,0:T(8,128)S(1)} copy-done((f32[12,256,256]{2,1,0:T(8,128)S(1)}, f32[12,256,256]{2,1,0:T(8,128)}, u32[]{:S(2)}) %copy-start.2) | copy-done | bytes 3145752
  26.0 1.7 %fusion.5 = f32[6,257,256]{2,1,0:T(8,128)S(1)} fusion(f32[6,257,256]{2,1,0:T(8,128)S(1)} %bitcast.95, f32[12,256,256]{2,1,0:T(8,128)S(1)} %copy-done.2), kind=kOutput, calls=%fused_computation.14 | convolution fusion | flops 1212678144 | bytes 4773888 | tf_op jit(solution)/shard_map/nij,njk->nik/dot_general | solution.py:17
  27.7 2.0 %fusion.2 = f32[6,1,257,256]{3,0,2,1:T(8,128)} fusion(f32[6,257,256]{2,1,0:T(8,128)S(1)} %fusion.5, f32[6,1,256]{2,0,1:T(8,128)S(1)} %bitcast.99), kind=kLoop, calls=%fused_computation.10 | loop fusion | flops 394752 | bytes 3164160 | tf_op jit(solution)/shard_map/stack | solution.py:49
  29.7 2.1 %copy.18 = f32[6,1,257,256]{3,0,2,1:T(8,128)S(1)} copy(f32[6,1,257,256]{3,2,0,1:T(8,128)} %bitcast.96) | data formatting | bytes 3158016 | tf_op jit(solution)/shard_map/stack;reshape | solution.py:49
  31.9 0.4 pad_maximum_fusion.1
  32.3 1.0 %copy.19 = f32[6,2,257,256]{3,2,1,0:T(8,128)S(1)} copy(f32[6,2,257,256]{3,0,2,1:T(8,128)S(1)} %pad_maximum_fusion.1) | data formatting | bytes 6316032 | tf_op jit(solution)/shard_map/stack | solution.py:49
  33.3 1.1 %copy.22 = f32[12,1,257,256]{3,0,2,1:T(8,128)S(1)} copy(f32[12,1,257,256]{3,2,0,1:T(8,128)S(1)} %bitcast.88) | data formatting | bytes 6316032 | tf_op jit(solution)/shard_map/stack;reshape | solution.py:49
  34.4 0.7 slice.212
  35.1 1.1 %multiply_reduce_fusion.11 = (f32[256]{0:T(256)S(1)}, f32[256,256]{1,0:T(8,128)S(1)}) fusion(f32[256]{0:T(256)S(1)} %broadcast_select_fusion.5, f32[256,256]{1,0:T(8,128)S(1)} %copy-done.7, f32[257,256]{1,0:T(8,128)} %collective-permute-done, pred[]{:T(512)S(6)} %eq.35), kind=kLoop, calls=%fused_computation.76 | loop fusion | flops 196352 | bytes 788481 | tf_op jit(solution)/shard_map/reduce_sum | solution.py:92
  36.2 1.6 %fusion.20 = f32[256,512]{1,0:T(8,128)S(1)} fusion(f32[256,256]{1,0:T(8,128)S(1)} %fusion.41, f32[256,256]{1,0:T(8,128)S(1)} %get-tuple-element.36, f32[256,256]{1,0:T(8,128)S(1)} %copy-done.7, f32[257,256]{1,0:T(8,128)} %collective-permute-done, pred[]{:T(512)S(6)} %eq.35), kind=kOutput, calls=%fused_computation.35 | convolution fusion | flops 402849792 | bytes 1572865 | tf_op jit(solution)/shard_map/dot_general | solution.py:90
  37.8 0.7 fusion.63
  38.7 1.7 %fusion.10 = f32[12,257,256]{2,1,0:T(8,128)S(1)} fusion(f32[12,257,256]{2,1,0:T(8,128)S(1)} %bitcast.89, bf16[24,256,256]{2,1,0:T(8,128)(2,1)S(1)} %bitcast.92), kind=kOutput, calls=%fused_computation.19 | convolution fusion | flops 2425356288 | bytes 7974912 | tf_op jit(solution)/shard_map/nij,njk->nik/dot_general | solution.py:17
  40.5 0.6 fusion.24
  41.2 1.6 %collective-permute-start.2 = (f32[257,256]{1,0:T(8,128)S(1)}, f32[257,256]{1,0:T(8,128)S(1)}, u32[]{:S(2)}, u32[]{:S(2)}) collective-permute-start(f32[257,256]{1,0:T(8,128)S(1)} %pad_maximum_fusion.6), channel_id=1, source_target_pairs={{0,2},{16,18},{1,3},{17,19},{2,0},{18,16},{3,1},{19,17},{4,6},{20,... | collective-permute-start | bytes 789512 | tf_op jit(solution)/shard_map/ppermute | solution.py:63
  42.8 1.1 %fusion.1 = f32[12,1,257,256]{3,0,2,1:T(8,128)S(1)} fusion(f32[12,257,256]{2,1,0:T(8,128)S(1)} %fusion.10, f32[12,1,256]{2,0,1:T(8,128)S(1)} %bitcast.98), kind=kLoop, calls=%fused_computation.6 | loop fusion | flops 789504 | bytes 6328320 | tf_op jit(solution)/shard_map/stack | solution.py:49
  43.8 6.3 %collective-permute-done.2 = f32[257,256]{1,0:T(8,128)S(1)} collective-permute-done((f32[257,256]{1,0:T(8,128)S(1)}, f32[257,256]{1,0:T(8,128)S(1)}, u32[]{:S(2)}, u32[]{:S(2)}) %collective-permute-start.2) | collective-permute-done | bytes 263200 | tf_op jit(solution)/shard_map/ppermute | solution.py:63
  50.3 0.6 fusion.28
  51.0 1.6 %collective-permute-start.3 = (f32[257,256]{1,0:T(8,128)S(1)}, f32[257,256]{1,0:T(8,128)S(1)}, u32[]{:S(2)}, u32[]{:S(2)}) collective-permute-start(f32[257,256]{1,0:T(8,128)S(1)} %pad_maximum_fusion.7), channel_id=1, source_target_pairs={{0,4},{16,20},{1,5},{17,21},{2,6},{18,22},{3,7},{19,23},{4,0},{20,... | collective-permute-start | bytes 789512 | tf_op jit(solution)/shard_map/ppermute | solution.py:63
  52.7 4.2 %pad_maximum_fusion = f32[12,2,257,256]{3,0,2,1:T(8,128)} fusion(f32[12,1,257,256]{3,0,2,1:T(8,128)S(1)} %copy.22, f32[12,1,257,256]{3,0,2,1:T(8,128)S(1)} %fusion.1), kind=kLoop, calls=%fused_computation | loop fusion | flops 1579008 | bytes 12632064 | tf_op jit(solution)/shard_map/stack | solution.py:49
  56.9 7.3 %copy.23 = f32[12,2,257,256]{3,2,1,0:T(8,128)S(1)} copy(f32[12,2,257,256]{3,0,2,1:T(8,128)} %pad_maximum_fusion) | data formatting | bytes 12632064 | tf_op jit(solution)/shard_map/stack | solution.py:49
  64.2 0.6 compare_reduce_fusion
  65.1 2.7 %collective-permute-start.4 = (f32[256]{0:T(256)S(1)}, f32[256]{0:T(256)S(1)}, u32[]{:S(2)}, u32[]{:S(2)}) collective-permute-start(f32[256]{0:T(256)S(1)} %select_add_fusion), channel_id=1, source_target_pairs={{0,8},{16,24},{1,9},{17,25},{2,10},{18,26},{3,11},{19,27},{4,12},{... | collective-permute-start | bytes 3080 | tf_op jit(solution)/shard_map/ppermute | solution.py:63
  67.8 1.8 %collective-permute-done.4 = f32[256]{0:T(256)S(1)} collective-permute-done((f32[256]{0:T(256)S(1)}, f32[256]{0:T(256)S(1)}, u32[]{:S(2)}, u32[]{:S(2)}) %collective-permute-start.4) | collective-permute-done | bytes 1056 | tf_op jit(solution)/shard_map/ppermute | solution.py:63
  69.6 0.4 multiply_reduce_fusion.7
  70.0 0.5 fusion
  70.6 0.2 copy-done.8
  70.8 0.6 fusion.59
  72.0 0.3 fusion.61
  72.3 0.3 convolution_add_fusion
  73.3 0.6 collective-permute-start.5
  73.9 3.8 %collective-permute-done.5 = f32[129,128]{1,0:T(8,128)S(1)} collective-permute-done((f32[129,128]{1,0:T(8,128)S(1)}, f32[129,128]{1,0:T(8,128)S(1)}, u32[]{:S(2)}, u32[]{:S(2)}) %collective-permute-start.5) | collective-permute-done | bytes 66080 | tf_op jit(solution)/shard_map/ppermute | solution.py:63
  77.8 1.2 %collective-permute-done.6 = f32[129,128]{1,0:T(8,128)S(1)} collective-permute-done((f32[129,128]{1,0:T(8,128)S(1)}, f32[129,128]{1,0:T(8,128)S(1)}, u32[]{:S(2)}, u32[]{:S(2)}) %collective-permute-start.6) | collective-permute-done | bytes 66080 | tf_op jit(solution)/shard_map/ppermute | solution.py:63
  79.0 1.6 %collective-permute-start.7 = (f32[129,128]{1,0:T(8,128)S(1)}, f32[129,128]{1,0:T(8,128)S(1)}, u32[]{:S(2)}, u32[]{:S(2)}) collective-permute-start(f32[129,128]{1,0:T(8,128)S(1)} %add.212), channel_id=1, source_target_pairs={{0,2},{16,18},{1,3},{17,19},{2,0},{18,16},{3,1},{19,17},{4,6},{20,... | collective-permute-start | bytes 198152 | tf_op jit(solution)/shard_map/ppermute | solution.py:63
  80.6 2.8 %collective-permute-done.7 = f32[129,128]{1,0:T(8,128)S(1)} collective-permute-done((f32[129,128]{1,0:T(8,128)S(1)}, f32[129,128]{1,0:T(8,128)S(1)}, u32[]{:S(2)}, u32[]{:S(2)}) %collective-permute-start.7) | collective-permute-done | bytes 66080 | tf_op jit(solution)/shard_map/ppermute | solution.py:63
  83.4 0.5 collective-permute-start.8
  83.9 3.9 %collective-permute-done.8 = f32[129,128]{1,0:T(8,128)S(1)} collective-permute-done((f32[129,128]{1,0:T(8,128)S(1)}, f32[129,128]{1,0:T(8,128)S(1)}, u32[]{:S(2)}, u32[]{:S(2)}) %collective-permute-start.8) | collective-permute-done | bytes 66080 | tf_op jit(solution)/shard_map/ppermute | solution.py:63
  87.8 3.4 %collective-permute-start.9 = (f32[129,128]{1,0:T(8,128)S(1)}, f32[129,128]{1,0:T(8,128)S(1)}, u32[]{:S(2)}, u32[]{:S(2)}) collective-permute-start(f32[129,128]{1,0:T(8,128)S(1)} %add.214), channel_id=1, source_target_pairs={{0,8},{16,24},{1,9},{17,25},{2,10},{18,26},{3,11},{19,27},{4,12},{... | collective-permute-start | bytes 198152 | tf_op jit(solution)/shard_map/ppermute | solution.py:63
  91.2 0.6 fusion.58
  91.8 1.9 %collective-permute-done.9 = f32[129,128]{1,0:T(8,128)S(1)} collective-permute-done((f32[129,128]{1,0:T(8,128)S(1)}, f32[129,128]{1,0:T(8,128)S(1)}, u32[]{:S(2)}, u32[]{:S(2)}) %collective-permute-start.9) | collective-permute-done | bytes 66080 | tf_op jit(solution)/shard_map/ppermute | solution.py:63
  93.7 0.6 slice.230
  94.4 0.5 slice.231
  (68 shorter events, 1.5 us)
Async XLA Ops:
  0.6 2.9 %copy-start = (bf16[1,24,256,256]{3,2,1,0:T(8,128)(2,1)S(1)}, bf16[1,24,256,256]{3,2,1,0:T(8,128)(2,1)}, u32[]{:S(2)}) copy-start(bf16[1,24,256,256]{3,2,1,0:T(8,128)(2,1)} %param.6) | copy-start | bytes 9437188
  6.3 4.8 %copy-start.1 = (f32[12,256,256]{2,1,0:T(8,128)S(1)}, f32[12,256,256]{2,1,0:T(8,128)}, u32[]{:S(2)}) copy-start(f32[12,256,256]{2,1,0:T(8,128)} %fusion.8) | copy-start | bytes 9437188
  11.4 2.4 %copy-start.4 = (f32[6,256,256]{2,1,0:T(8,128)S(1)}, f32[6,256,256]{2,1,0:T(8,128)}, u32[]{:S(2)}) copy-start(f32[6,256,256]{2,1,0:T(8,128)} %fusion.3) | copy-start | bytes 4718596
  14.9 5.3 %copy-start.6 = (f32[256,256]{1,0:T(8,128)}, f32[256,256]{1,0:T(8,128)S(1)}, u32[]{:S(2)}) copy-start(f32[256,256]{1,0:T(8,128)S(1)} %fusion.45) | copy-start | bytes 786436
  15.8 18.6 %collective-permute-start = (f32[257,256]{1,0:T(8,128)}, f32[257,256]{1,0:T(8,128)}, u32[]{:S(2)}, u32[]{:S(2)}) collective-permute-start(f32[257,256]{1,0:T(8,128)} %pad_maximum_fusion.4), channel_id=1, source_target_pairs={{0,16},{16,0},{1,17},{17,1},{2,18},{18,2},{3,19},{19,3},{4,20},{20... | collective-permute-start | bytes 789512 | tf_op jit(solution)/shard_map/ppermute | solution.py:63
  23.5 2.5 %copy-start.2 = (f32[12,256,256]{2,1,0:T(8,128)S(1)}, f32[12,256,256]{2,1,0:T(8,128)}, u32[]{:S(2)}) copy-start(f32[12,256,256]{2,1,0:T(8,128)} %fusion.8) | copy-start | bytes 9437188
  23.8 3.8 %copy-start.3 = (f32[3,2,257,256]{3,2,1,0:T(8,128)}, f32[3,2,257,256]{3,2,1,0:T(8,128)S(1)}, u32[]{:S(2)}) copy-start(f32[3,2,257,256]{3,2,1,0:T(8,128)S(1)} %copy.15) | copy-start | bytes 4737028
  29.7 2.1 %copy-start.5 = (f32[6,1,257,256]{3,0,2,1:T(8,128)S(1)}, f32[6,1,257,256]{3,0,2,1:T(8,128)}, u32[]{:S(2)}) copy-start(f32[6,1,257,256]{3,0,2,1:T(8,128)} %fusion.2) | copy-start | bytes 4737028
  33.3 1.8 %copy-start.7 = (f32[256,256]{1,0:T(8,128)S(1)}, f32[256,256]{1,0:T(8,128)}, u32[]{:S(2)}) copy-start(f32[256,256]{1,0:T(8,128)} %copy-done.6) | copy-start | bytes 786436
  38.6 1.8 %collective-permute-start.1 = (f32[257,256]{1,0:T(8,128)S(1)}, f32[257,256]{1,0:T(8,128)S(1)}, u32[]{:S(2)}, u32[]{:S(2)}) collective-permute-start(f32[257,256]{1,0:T(8,128)S(1)} %pad_maximum_fusion.5), channel_id=1, source_target_pairs={{0,1},{16,17},{1,0},{17,16},{2,3},{18,19},{3,2},{19,18},{4,5},{20,... | collective-permute-start | bytes 789512 | tf_op jit(solution)/shard_map/ppermute | solution.py:63
  41.2 8.9 %collective-permute-start.2 = (f32[257,256]{1,0:T(8,128)S(1)}, f32[257,256]{1,0:T(8,128)S(1)}, u32[]{:S(2)}, u32[]{:S(2)}) collective-permute-start(f32[257,256]{1,0:T(8,128)S(1)} %pad_maximum_fusion.6), channel_id=1, source_target_pairs={{0,2},{16,18},{1,3},{17,19},{2,0},{18,16},{3,1},{19,17},{4,6},{20,... | collective-permute-start | bytes 789512 | tf_op jit(solution)/shard_map/ppermute | solution.py:63
  51.0 13.9 %collective-permute-start.3 = (f32[257,256]{1,0:T(8,128)S(1)}, f32[257,256]{1,0:T(8,128)S(1)}, u32[]{:S(2)}, u32[]{:S(2)}) collective-permute-start(f32[257,256]{1,0:T(8,128)S(1)} %pad_maximum_fusion.7), channel_id=1, source_target_pairs={{0,4},{16,20},{1,5},{17,21},{2,6},{18,22},{3,7},{19,23},{4,0},{20,... | collective-permute-start | bytes 789512 | tf_op jit(solution)/shard_map/ppermute | solution.py:63
  56.9 8.0 %copy-start.9 = (f32[1,24,2,128]{3,2,1,0:T(2,128)S(1)}, f32[1,24,2,128]{3,2,1,0:T(2,128)}, u32[]{:S(2)}) copy-start(f32[1,24,2,128]{3,2,1,0:T(2,128)} %param.8) | copy-start | bytes 73732
  65.1 4.5 %collective-permute-start.4 = (f32[256]{0:T(256)S(1)}, f32[256]{0:T(256)S(1)}, u32[]{:S(2)}, u32[]{:S(2)}) collective-permute-start(f32[256]{0:T(256)S(1)} %select_add_fusion), channel_id=1, source_target_pairs={{0,8},{16,24},{1,9},{17,25},{2,10},{18,26},{3,11},{19,27},{4,12},{... | collective-permute-start | bytes 3080 | tf_op jit(solution)/shard_map/ppermute | solution.py:63
  70.0 0.7 copy-start.8
  70.0 0.7 copy-start.10
  73.3 4.4 %collective-permute-start.5 = (f32[129,128]{1,0:T(8,128)S(1)}, f32[129,128]{1,0:T(8,128)S(1)}, u32[]{:S(2)}, u32[]{:S(2)}) collective-permute-start(f32[129,128]{1,0:T(8,128)S(1)} %select_maximum_fusion), channel_id=1, source_target_pairs={{0,16},{16,0},{1,17},{17,1},{2,18},{18,2},{3,19},{19,3},{4,20},{20... | collective-permute-start | bytes 198152 | tf_op jit(solution)/shard_map/ppermute | solution.py:63
  77.7 1.3 %collective-permute-start.6 = (f32[129,128]{1,0:T(8,128)S(1)}, f32[129,128]{1,0:T(8,128)S(1)}, u32[]{:S(2)}, u32[]{:S(2)}) collective-permute-start(f32[129,128]{1,0:T(8,128)S(1)} %fusion.72), channel_id=1, source_target_pairs={{0,1},{16,17},{1,0},{17,16},{2,3},{18,19},{3,2},{19,18},{4,5},{20,... | collective-permute-start | bytes 198152 | tf_op jit(solution)/shard_map/ppermute | solution.py:63
  79.0 4.4 %collective-permute-start.7 = (f32[129,128]{1,0:T(8,128)S(1)}, f32[129,128]{1,0:T(8,128)S(1)}, u32[]{:S(2)}, u32[]{:S(2)}) collective-permute-start(f32[129,128]{1,0:T(8,128)S(1)} %add.212), channel_id=1, source_target_pairs={{0,2},{16,18},{1,3},{17,19},{2,0},{18,16},{3,1},{19,17},{4,6},{20,... | collective-permute-start | bytes 198152 | tf_op jit(solution)/shard_map/ppermute | solution.py:63
  83.4 4.4 %collective-permute-start.8 = (f32[129,128]{1,0:T(8,128)S(1)}, f32[129,128]{1,0:T(8,128)S(1)}, u32[]{:S(2)}, u32[]{:S(2)}) collective-permute-start(f32[129,128]{1,0:T(8,128)S(1)} %add.213), channel_id=1, source_target_pairs={{0,4},{16,20},{1,5},{17,21},{2,6},{18,22},{3,7},{19,23},{4,0},{20,... | collective-permute-start | bytes 198152 | tf_op jit(solution)/shard_map/ppermute | solution.py:63
  87.8 5.9 %collective-permute-start.9 = (f32[129,128]{1,0:T(8,128)S(1)}, f32[129,128]{1,0:T(8,128)S(1)}, u32[]{:S(2)}, u32[]{:S(2)}) collective-permute-start(f32[129,128]{1,0:T(8,128)S(1)} %add.214), channel_id=1, source_target_pairs={{0,8},{16,24},{1,9},{17,25},{2,10},{18,26},{3,11},{19,27},{4,12},{... | collective-permute-start | bytes 198152 | tf_op jit(solution)/shard_map/ppermute | solution.py:63

commit v3 on v2

--- a/solution.py
+++ b/solution.py
@@ -36,21 +36,17 @@
     return levels
 
 
-def downsweep(levels, top):
-    m = top
-    width = top.shape[2]
-    offset_row = jnp.zeros((1, width), jnp.float32)
+def downsweep(levels, incoming):
+    m = incoming
     for q, v in reversed(levels[:-1]):
         n = q.shape[0]
         half = n // 2
         upper = m[:half]
-        shift = jnp.concatenate([jnp.zeros((half, top.shape[1] - 1, width), jnp.float32), v[1 : 2 * half : 2, None, :]], axis=1)
-        left = matmat(upper, q[1 : 2 * half : 2]) + shift
-        m_new = jnp.stack([left, upper], axis=1).reshape((2 * half,) + upper.shape[1:])
+        left = vecmat(upper, q[1 : 2 * half : 2]) + v[1 : 2 * half : 2]
+        m_new = jnp.stack([left, upper], axis=1).reshape(2 * half, -1)
         if n % 2:
             m_new = jnp.concatenate([m_new, m[-1:]], axis=0)
         m = m_new
-    del offset_row
     return m
 
 
@@ -59,8 +55,8 @@
     return (b % inner) * lax.axis_size("outer") + b // inner
 
 
-def exchange(x, d, count):
-    return lax.ppermute(x, AXES, [(place(j), place(j ^ d)) for j in range(count)])
+def exchange(x, mask, count):
+    return lax.ppermute(x, AXES, [(place(j), place(j ^ mask)) for j in range(count)])
 
 
 def body(propagator_matrices, smoothed_adjoints, station_loadings, offset_response):
@@ -98,9 +94,7 @@
     rv = exchange(tv, d, count)
     incoming = jnp.where(lower, jnp.sum(rv[:, None] * sq, axis=0) + sv, sv)
 
-    top = jnp.concatenate([jnp.eye(width, dtype=jnp.float32), jnp.zeros((1, width), jnp.float32)], axis=0)
-    maps = downsweep(levels, top[None])
-    after = jnp.sum(incoming[None, :, None] * maps[:, :width, :], axis=1) + maps[:, width, :]
+    after = downsweep(levels, incoming[None, :])
     length_rates = grads + after
     argument_values = station_loadings[0]
     local_kernel = jnp.dot(
@@ -112,10 +106,14 @@
     local_noise = -jnp.sum(length_rates * offset_response[0])
     noise_row = jnp.zeros((1, local_kernel.shape[1]), jnp.float32).at[0, 0].set(local_noise)
     packed = jnp.concatenate([local_kernel, noise_row], axis=0)
-    d = 1
-    while d < count:
-        packed = packed + exchange(packed, d, count)
-        d *= 2
+    low = 1
+    while low < count:
+        high = min(low * 8, count)
+        vals = [packed] + [exchange(packed, m, count) for m in range(low, high, low)]
+        while len(vals) > 1:
+            vals = [vals[i] + vals[i + 1] for i in range(0, len(vals), 2)]
+        packed = vals[0]
+        low = high
     return (length_rates[None], packed[:stations], packed[stations, 0])
 
 

time: 95.3 us -> 99.3 us (1.042)
  waiting for transfers between devices: 21.8 us -> 33 us
  local copies, waits for them, and re-layouts: 16.8 us -> 6.28 us
  starting transfers between devices: 14.9 us -> 21 us
  matrix products: 19.1 us -> 17 us
    another operation x5, local copies, waits for them, and re-layouts: 11.8 us -> 0.06 us  [downsweep(): m_new = jnp.stack([left, upper], axis=1).reshape(2 * half, -1)]
    ppermute x10 -> x15, waiting for transfers between devices: 21.8 us -> 33 us  [exchange(): lax.ppermute(x, AXES, [(place(j), place(j ^ mask)) for j in range(count)])]
    another operation x9 -> x8, other arithmetic: 9.79 us -> 0.68 us  [the longest x8 9.16 us: downsweep(): jnp.stack([left, upper], axis=1).reshape((2 * half,) + upper.shape[1:])]
    ppermute x10 -> x15, starting transfers between devices: 14.9 us -> 21 us  [exchange(): lax.ppermute(x, AXES, [(place(j), place(j ^ mask)) for j in range(count)])]
    dot_general x9 -> x4, matrix products: 13 us -> 7.82 us  [matmat(): jnp.einsum('nij,njk->nik', later.astype(jnp.float32), earlier.astype(jnp....]
    reduce_sum x5 -> x10, other arithmetic: 3.66 us -> 7.69 us  [vecmat(): return jnp.sum(v[:, :, None] * q.astype(jnp.float32), axis=1)]
    reduce_sum x4, other arithmetic: 0.56 us -> 3.79 us  [body(): new_sv = jnp.sum(rv[:, None] * sq, axis=0) + sv]
    dot_general x4, matrix products: 3.23 us -> 6.34 us  [body(): both = jnp.dot(q_up, jnp.concatenate([q_low, sq], axis=1), precision=EXACT)]
  transfers between devices with their start and end apart: 10 -> 15, of which waited for: 7 -> 11; matrix products, arithmetic and copies ran while one was open for 31% -> 1% of each run, Pallas kernels for 0% -> 0%
where the time goes in v3:
time: 99.3 us; the launch traced here: 98.7 us
  waiting for transfers between devices  33 us (33%)
  starting transfers between devices  21 us (21%)
  other arithmetic  19 us (19%)
  matrix products  17 us (17%)
  local copies, waits for them, and re-layouts  6.28 us (6%)
  between operations  2.41 us (2%)
    ppermute x15, waiting for transfers between devices, exchange(): lax.ppermute(x, AXES, [(place(j), place(j ^ mask)) for j in range(count)])  33 us
    ppermute x15, starting transfers between devices, exchange(): lax.ppermute(x, AXES, [(place(j), place(j ^ mask)) for j in range(count)])  21 us
    dot_general x4, matrix products, matmat(): jnp.einsum('nij,njk->nik', later.astype(jnp.float32), earlier.astype(jnp....  7.82 us
    reduce_sum x10, other arithmetic, vecmat(): return jnp.sum(v[:, :, None] * q.astype(jnp.float32), axis=1)  7.69 us
    dot_general x4, matrix products, body(): both = jnp.dot(q_up, jnp.concatenate([q_low, sq], axis=1), precision=EXACT)  6.34 us
    reduce_sum x4, other arithmetic, body(): new_sv = jnp.sum(rv[:, None] * sq, axis=0) + sv  3.79 us
    unnamed x26, local copies, waits for them, and re-layouts  3.44 us
    concatenate x4, other arithmetic, body(): got = exchange(jnp.concatenate([tq, tv[None, :]], axis=0), d, count)  2.97 us
  transfers between devices with their start and end apart: 15, of which 11 were waited for; matrix products, arithmetic and copies ran while one was open for 1% of the time, Pallas kernels for 0%

profile of v3, /device:TPU:0, one launch (start us, length us, event | category | flops | bytes accessed | tf_op | source)
XLA Modules:
  0.0 98.7 jit_solution(13724624392173331739)
XLA Ops:
  0.6 2.6 %multiply_reduce_fusion = f32[24,256]{1,0:T(8,128)S(1)} fusion(f32[24,256]{1,0:T(8,128)} %bitcast.66, bf16[1,24,256,256]{3,2,1,0:T(8,128)(2,1)} %param.6), kind=kLoop, calls=%fused_computation | loop fusion | flops 4712448 | bytes 3194880 | tf_op jit(solution)/shard_map/reduce_sum | solution.py:11
  3.3 0.2 copy-done
  3.5 2.3 %fusion.3 = f32[12,256,256]{2,1,0:T(8,128)} fusion(bf16[24,256,256]{2,1,0:T(8,128)(2,1)S(1)} %bitcast.63), kind=kOutput, calls=%fused_computation.8 | convolution fusion | flops 402653184 | bytes 6291456 | tf_op jit(solution)/shard_map/nij,njk->nik/dot_general | solution.py:16
  5.8 0.5 multiply_reduce_fusion.2
  6.3 4.8 %fusion = f32[6,256,256]{2,1,0:T(8,128)} fusion(f32[12,256,256]{2,1,0:T(8,128)} %fusion.3), kind=kOutput, calls=%fused_computation.5 | convolution fusion | flops 1207959552 | bytes 4718592 | tf_op jit(solution)/shard_map/nij,njk->nik/dot_general | solution.py:17
  11.1 0.3 multiply_reduce_fusion.4
  11.4 2.3 %fusion.6 = f32[3,256,256]{2,1,0:T(8,128)S(1)} fusion(f32[6,256,256]{2,1,0:T(8,128)} %fusion), kind=kOutput, calls=%fused_computation.15 | convolution fusion | flops 603979776 | bytes 2359296 | tf_op jit(solution)/shard_map/nij,njk->nik/dot_general | solution.py:17
  13.7 1.6 %multiply_reduce_fusion.6 = f32[3,256]{1,0:T(4,128)S(1)} fusion(f32[6,256,256]{2,1,0:T(8,128)} %fusion, f32[3,256]{1,0:T(4,128)S(1)} %slice.166), kind=kLoop, calls=%fused_computation.14 | loop fusion | flops 392448 | bytes 792576 | tf_op jit(solution)/shard_map/reduce_sum | solution.py:11
  15.3 0.4 multiply_reduce_fusion.18
  15.9 0.4 fusion.25
  16.3 0.7 pad_maximum_fusion
  17.0 3.0 %collective-permute-start = (f32[257,256]{1,0:T(8,128)}, f32[257,256]{1,0:T(8,128)}, u32[]{:S(2)}, u32[]{:S(2)}) collective-permute-start(f32[257,256]{1,0:T(8,128)} %pad_maximum_fusion), channel_id=1, source_target_pairs={{0,16},{16,0},{1,17},{17,1},{2,18},{18,2},{3,19},{19,3},{4,20},{20... | collective-permute-start | bytes 789512 | tf_op jit(solution)/shard_map/ppermute | solution.py:59
  20.0 6.8 %collective-permute-done = f32[257,256]{1,0:T(8,128)} collective-permute-done((f32[257,256]{1,0:T(8,128)}, f32[257,256]{1,0:T(8,128)}, u32[]{:S(2)}, u32[]{:S(2)}) %collective-permute-start) | collective-permute-done | bytes 263200 | tf_op jit(solution)/shard_map/ppermute | solution.py:59
  26.8 0.7 slice.201
  27.5 1.1 %multiply_reduce_fusion.16 = (f32[256]{0:T(256)S(1)}, f32[256,256]{1,0:T(8,128)S(1)}) fusion(f32[256]{0:T(256)S(1)} %broadcast_select_fusion.10, f32[256,256]{1,0:T(8,128)S(1)} %fusion.25, f32[257,256]{1,0:T(8,128)} %collective-permute-done, pred[]{:T(512)S(6)} %eq.32), kind=kLoop, calls=%fused_computation.57 | loop fusion | flops 196352 | bytes 788481 | tf_op jit(solution)/shard_map/reduce_sum | solution.py:88
  28.5 1.6 %fusion.9 = f32[256,512]{1,0:T(8,128)S(1)} fusion(f32[256,256]{1,0:T(8,128)S(1)} %fusion.30, f32[256,256]{1,0:T(8,128)S(1)} %get-tuple-element.38, f32[256,256]{1,0:T(8,128)S(1)} %fusion.25, f32[257,256]{1,0:T(8,128)} %collective-permute-done, pred[]{:T(512)S(6)} %eq.32), kind=kOutput, calls=%fused_computation.18 | convolution fusion | flops 402849792 | bytes 1572865 | tf_op jit(solution)/shard_map/dot_general | solution.py:86
  30.1 0.8 copy-done.5
  31.0 0.7 fusion.49
  31.7 0.7 pad_maximum_fusion.1
  32.4 1.8 %collective-permute-done.1 = f32[257,256]{1,0:T(8,128)S(1)} collective-permute-done((f32[257,256]{1,0:T(8,128)}, f32[257,256]{1,0:T(8,128)S(1)}, u32[]{:S(2)}, u32[]{:S(2)}) %collective-permute-start.1) | collective-permute-done | bytes 263200 | tf_op jit(solution)/shard_map/ppermute | solution.py:59
  34.2 1.2 %multiply_reduce_fusion.9 = (f32[256]{0:T(256)S(1)}, f32[256,256]{1,0:T(8,128)S(1)}, f32[256]{0:T(256)S(1)}, f32[256,256]{1,0:T(8,128)S(1)}) fusion(f32[256]{0:T(256)S(1)} %bitcast.79, f32[256,512]{1,0:T(8,128)} %copy-done.5, pred[]{:T(512)S(6)} %eq.32, f32[257,256]{1,0:T(8,128)S(1)} %collective-permute-done.1, pred[]{:T(512)S(6)} %eq.31, ...), kind=kLoop, calls=%fused_computation.47 | loop fusion | flops 523776 | bytes 1314818 | tf_op jit(solution)/shard_map/reduce_sum | solution.py:87
  35.4 1.7 %fusion.13 = f32[256,512]{1,0:T(8,128)S(1)} fusion(f32[256,256]{1,0:T(8,128)S(1)} %get-tuple-element.20, f32[256,256]{1,0:T(8,128)S(1)} %get-tuple-element.44, f32[257,256]{1,0:T(8,128)S(1)} %collective-permute-done.1, pred[]{:T(512)S(6)} %eq.31, f32[256,512]{1,0:T(8,128)} %copy-done.5), kind=kOutput, calls=%fused_computation.22 | convolution fusion | flops 402849792 | bytes 1572865 | tf_op jit(solution)/shard_map/dot_general | solution.py:86
  37.1 0.8 copy-done.7
  38.0 0.7 pad_maximum_fusion.2
  38.7 1.7 %collective-permute-start.2 = (f32[257,256]{1,0:T(8,128)}, f32[257,256]{1,0:T(8,128)S(1)}, u32[]{:S(2)}, u32[]{:S(2)}) collective-permute-start(f32[257,256]{1,0:T(8,128)} %pad_maximum_fusion.2), channel_id=1, source_target_pairs={{0,2},{16,18},{1,3},{17,19},{2,0},{18,16},{3,1},{19,17},{4,6},{20,... | collective-permute-start | bytes 789512 | tf_op jit(solution)/shard_map/ppermute | solution.py:59
  40.4 7.0 %collective-permute-done.2 = f32[257,256]{1,0:T(8,128)S(1)} collective-permute-done((f32[257,256]{1,0:T(8,128)}, f32[257,256]{1,0:T(8,128)S(1)}, u32[]{:S(2)}, u32[]{:S(2)}) %collective-permute-start.2) | collective-permute-done | bytes 263200 | tf_op jit(solution)/shard_map/ppermute | solution.py:59
  47.4 0.7 copy-done.9
  48.2 1.3 %multiply_reduce_fusion.10 = (f32[256]{0:T(256)S(1)}, f32[256,256]{1,0:T(8,128)S(1)}, f32[256]{0:T(256)S(1)}, f32[256,256]{1,0:T(8,128)S(1)}) fusion(f32[256]{0:T(256)S(1)} %bitcast.76, f32[256,256]{1,0:T(8,128)} %copy-done.8, f32[256,512]{1,0:T(8,128)} %copy-done.7, pred[]{:T(512)S(6)} %eq.31, f32[257,256]{1,0:T(8,128)} %copy-done.9, pred[]{:T(512)S(6)} %eq.30, ...), kind=kLoop, calls=%fused_computation.48 | loop fusion | flops 392704 | bytes 1576962 | tf_op jit(solution)/shard_map/reduce_sum | solution.py:87
  49.4 1.7 %fusion.17 = f32[256,512]{1,0:T(8,128)S(1)} fusion(f32[256,256]{1,0:T(8,128)S(1)} %get-tuple-element.22, f32[256,256]{1,0:T(8,128)S(1)} %get-tuple-element.42, f32[257,256]{1,0:T(8,128)} %copy-done.9, pred[]{:T(512)S(6)} %eq.30, f32[256,512]{1,0:T(8,128)} %copy-done.7), kind=kOutput, calls=%fused_computation.26 | convolution fusion | flops 402849792 | bytes 1572865 | tf_op jit(solution)/shard_map/dot_general | solution.py:86
  51.1 0.8 copy-done.6
  51.9 0.7 fusion.51
  52.6 0.7 pad_maximum_fusion.3
  53.4 1.8 %collective-permute-start.3 = (f32[257,256]{1,0:T(8,128)}, f32[257,256]{1,0:T(8,128)}, u32[]{:S(2)}, u32[]{:S(2)}) collective-permute-start(f32[257,256]{1,0:T(8,128)} %pad_maximum_fusion.3), channel_id=1, source_target_pairs={{0,4},{16,20},{1,5},{17,21},{2,6},{18,22},{3,7},{19,23},{4,0},{20,... | collective-permute-start | bytes 789512 | tf_op jit(solution)/shard_map/ppermute | solution.py:59
  55.2 0.6 compare_reduce_fusion
  55.9 5.7 %collective-permute-done.3 = f32[257,256]{1,0:T(8,128)} collective-permute-done((f32[257,256]{1,0:T(8,128)}, f32[257,256]{1,0:T(8,128)}, u32[]{:S(2)}, u32[]{:S(2)}) %collective-permute-start.3) | collective-permute-done | bytes 263200 | tf_op jit(solution)/shard_map/ppermute | solution.py:59
  61.5 0.7 slice.210
  62.2 1.3 %multiply_reduce_fusion.11 = (f32[256]{0:T(256)S(1)}, f32[256,256]{1,0:T(8,128)S(1)}, f32[256]{0:T(256)S(1)}, f32[256,256]{1,0:T(8,128)S(1)}) fusion(f32[256]{0:T(256)S(1)} %bitcast.82, f32[256,256]{1,0:T(8,128)S(1)} %get-tuple-element.22, f32[256,512]{1,0:T(8,128)} %copy-done.6, pred[]{:T(512)S(6)} %eq.30, f32[257,256]{1,0:T(8,128)} %collective-permute-done.3, ...), kind=kLoop, calls=%fused_computation.49 | loop fusion | flops 392704 | bytes 1576962 | tf_op jit(solution)/shard_map/reduce_sum | solution.py:87
  63.5 2.8 %collective-permute-start.4 = (f32[256]{0:T(256)S(1)}, f32[256]{0:T(256)S(1)}, u32[]{:S(2)}, u32[]{:S(2)}) collective-permute-start(f32[256]{0:T(256)S(1)} %select_add_fusion), channel_id=1, source_target_pairs={{0,8},{16,24},{1,9},{17,25},{2,10},{18,26},{3,11},{19,27},{4,12},{... | collective-permute-start | bytes 3080 | tf_op jit(solution)/shard_map/ppermute | solution.py:59
  66.4 1.6 %collective-permute-done.4 = f32[256]{0:T(256)S(1)} collective-permute-done((f32[256]{0:T(256)S(1)}, f32[256]{0:T(256)S(1)}, u32[]{:S(2)}, u32[]{:S(2)}) %collective-permute-start.4) | collective-permute-done | bytes 1056 | tf_op jit(solution)/shard_map/ppermute | solution.py:59
  68.0 1.4 %multiply_reduce_fusion.12 = f32[256]{0:T(256)S(1)} fusion(f32[256]{0:T(256)S(1)} %collective-permute-done.4, f32[256,256]{1,0:T(8,128)S(1)} %get-tuple-element.24, f32[256,256]{1,0:T(8,128)S(1)} %get-tuple-element.40, f32[257,256]{1,0:T(8,128)} %collective-permute-done.3, pred[]{:T(512)S(6)} %eq.29, f32[256,512]{1,0:T(8,128)} %copy-done.6), kind=kOutput, calls=%fused_computation.50 | convolution fusion | flops 201654016 | bytes 1313792 | tf_op jit(solution)/shard_map/dot_general | solution.py:86
  69.6 0.1 multiply_reduce_fusion.7
  69.8 0.2 multiply_reduce_fusion.5
  70.1 1.7 %multiply_reduce_fusion.3 = f32[6,256]{1,0:T(8,128)S(1)} fusion(f32[12,256,256]{2,1,0:T(8,128)} %fusion.3, f32[6,256]{1,0:T(8,128)S(1)} %mul.220), kind=kLoop, calls=%fused_computation.3 | loop fusion | flops 784896 | bytes 1585152 | tf_op jit(solution)/shard_map/reduce_sum | solution.py:11
  71.9 0.5 multiply_reduce_fusion.1
  72.5 0.6 fusion.45
  73.7 0.3 fusion.47
  74.0 0.3 convolution_add_fusion
  75.1 2.9 %collective-permute-start.11 = (f32[129,128]{1,0:T(8,128)S(1)}, f32[129,128]{1,0:T(8,128)S(1)}, u32[]{:S(2)}, u32[]{:S(2)}) collective-permute-start(f32[129,128]{1,0:T(8,128)S(1)} %select_maximum_fusion), channel_id=1, source_target_pairs={{0,19},{16,3},{1,18},{17,2},{2,17},{18,1},{3,16},{19,0},{4,23},{20... | collective-permute-start | bytes 198152 | tf_op jit(solution)/shard_map/ppermute | solution.py:59
  77.9 0.4 collective-permute-start.5
  78.3 1.8 %collective-permute-start.7 = (f32[129,128]{1,0:T(8,128)S(1)}, f32[129,128]{1,0:T(8,128)S(1)}, u32[]{:S(2)}, u32[]{:S(2)}) collective-permute-start(f32[129,128]{1,0:T(8,128)S(1)} %select_maximum_fusion), channel_id=1, source_target_pairs={{0,17},{16,1},{1,16},{17,0},{2,19},{18,3},{3,18},{19,2},{4,21},{20... | collective-permute-start | bytes 198152 | tf_op jit(solution)/shard_map/ppermute | solution.py:59
  80.1 1.5 %collective-permute-start.8 = (f32[129,128]{1,0:T(8,128)S(1)}, f32[129,128]{1,0:T(8,128)S(1)}, u32[]{:S(2)}, u32[]{:S(2)}) collective-permute-start(f32[129,128]{1,0:T(8,128)S(1)} %select_maximum_fusion), channel_id=1, source_target_pairs={{0,2},{16,18},{1,3},{17,19},{2,0},{18,16},{3,1},{19,17},{4,6},{20,... | collective-permute-start | bytes 198152 | tf_op jit(solution)/shard_map/ppermute | solution.py:59
  81.5 0.4 collective-permute-done.11
  81.9 0.7 collective-permute-start.9
  82.6 1.1 %collective-permute-done.5 = f32[129,128]{1,0:T(8,128)S(1)} collective-permute-done((f32[129,128]{1,0:T(8,128)S(1)}, f32[129,128]{1,0:T(8,128)S(1)}, u32[]{:S(2)}, u32[]{:S(2)}) %collective-permute-start.5) | collective-permute-done | bytes 66080 | tf_op jit(solution)/shard_map/ppermute | solution.py:59
  83.7 0.9 collective-permute-done.7
  84.6 2.5 %collective-permute-done.9 = f32[129,128]{1,0:T(8,128)S(1)} collective-permute-done((f32[129,128]{1,0:T(8,128)S(1)}, f32[129,128]{1,0:T(8,128)S(1)}, u32[]{:S(2)}, u32[]{:S(2)}) %collective-permute-start.9) | collective-permute-done | bytes 66080 | tf_op jit(solution)/shard_map/ppermute | solution.py:59
  87.2 1.7 %collective-permute-start.12 = (f32[129,128]{1,0:T(8,128)S(1)}, f32[129,128]{1,0:T(8,128)S(1)}, u32[]{:S(2)}, u32[]{:S(2)}) collective-permute-start(f32[129,128]{1,0:T(8,128)S(1)} %add_add_fusion.1), channel_id=1, source_target_pairs={{0,4},{16,20},{1,5},{17,21},{2,6},{18,22},{3,7},{19,23},{4,0},{20,... | collective-permute-start | bytes 198152 | tf_op jit(solution)/shard_map/ppermute | solution.py:59
  88.8 2.6 %collective-permute-start.13 = (f32[129,128]{1,0:T(8,128)S(1)}, f32[129,128]{1,0:T(8,128)S(1)}, u32[]{:S(2)}, u32[]{:S(2)}) collective-permute-start(f32[129,128]{1,0:T(8,128)S(1)} %add_add_fusion.1), channel_id=1, source_target_pairs={{0,8},{16,24},{1,9},{17,25},{2,10},{18,26},{3,11},{19,27},{4,12},{... | collective-permute-start | bytes 198152 | tf_op jit(solution)/shard_map/ppermute | solution.py:59
  91.4 0.2 collective-permute-start.14
  91.7 0.6 add.241
  92.3 3.3 %collective-permute-done.13 = f32[129,128]{1,0:T(8,128)S(1)} collective-permute-done((f32[129,128]{1,0:T(8,128)S(1)}, f32[129,128]{1,0:T(8,128)S(1)}, u32[]{:S(2)}, u32[]{:S(2)}) %collective-permute-start.13) | collective-permute-done | bytes 66080 | tf_op jit(solution)/shard_map/ppermute | solution.py:59
  95.5 2.0 %collective-permute-done.14 = f32[129,128]{1,0:T(8,128)S(1)} collective-permute-done((f32[129,128]{1,0:T(8,128)S(1)}, f32[129,128]{1,0:T(8,128)S(1)}, u32[]{:S(2)}, u32[]{:S(2)}) %collective-permute-start.14) | collective-permute-done | bytes 66080 | tf_op jit(solution)/shard_map/ppermute | solution.py:59
  97.6 0.6 slice.217
  98.2 0.5 slice.218
  (79 shorter events, 1.0 us)
Async XLA Ops:
  0.6 2.9 %copy-start = (bf16[1,24,256,256]{3,2,1,0:T(8,128)(2,1)S(1)}, bf16[1,24,256,256]{3,2,1,0:T(8,128)(2,1)}, u32[]{:S(2)}) copy-start(bf16[1,24,256,256]{3,2,1,0:T(8,128)(2,1)} %param.6) | copy-start | bytes 9437188
  6.3 4.8 %copy-start.1 = (f32[12,256,256]{2,1,0:T(8,128)S(1)}, f32[12,256,256]{2,1,0:T(8,128)}, u32[]{:S(2)}) copy-start(f32[12,256,256]{2,1,0:T(8,128)} %fusion.3) | copy-start | bytes 9437188
  13.7 2.2 %copy-start.3 = (f32[3,256,256]{2,1,0:T(8,128)}, f32[3,256,256]{2,1,0:T(8,128)S(1)}, u32[]{:S(2)}) copy-start(f32[3,256,256]{2,1,0:T(8,128)S(1)} %fusion.6) | copy-start | bytes 2359300
  17.0 9.8 %collective-permute-start = (f32[257,256]{1,0:T(8,128)}, f32[257,256]{1,0:T(8,128)}, u32[]{:S(2)}, u32[]{:S(2)}) collective-permute-start(f32[257,256]{1,0:T(8,128)} %pad_maximum_fusion), channel_id=1, source_target_pairs={{0,16},{16,0},{1,17},{17,1},{2,18},{18,2},{3,19},{19,3},{4,20},{20... | collective-permute-start | bytes 789512 | tf_op jit(solution)/shard_map/ppermute | solution.py:59
  30.1 0.8 copy-start.5
  32.4 1.8 %collective-permute-start.1 = (f32[257,256]{1,0:T(8,128)}, f32[257,256]{1,0:T(8,128)S(1)}, u32[]{:S(2)}, u32[]{:S(2)}) collective-permute-start(f32[257,256]{1,0:T(8,128)} %pad_maximum_fusion.1), channel_id=1, source_target_pairs={{0,1},{16,17},{1,0},{17,16},{2,3},{18,19},{3,2},{19,18},{4,5},{20,... | collective-permute-start | bytes 789512 | tf_op jit(solution)/shard_map/ppermute | solution.py:59
  35.4 2.6 %copy-start.8 = (f32[256,256]{1,0:T(8,128)}, f32[256,256]{1,0:T(8,128)S(1)}, u32[]{:S(2)}) copy-start(f32[256,256]{1,0:T(8,128)S(1)} %get-tuple-element.20) | copy-start | bytes 786436
  35.4 20.4 %copy-start.11 = (f32[1,24,2,128]{3,2,1,0:T(2,128)S(1)}, f32[1,24,2,128]{3,2,1,0:T(2,128)}, u32[]{:S(2)}) copy-start(f32[1,24,2,128]{3,2,1,0:T(2,128)} %param.8) | copy-start | bytes 73732
  37.1 0.8 copy-start.7
  38.7 8.7 %collective-permute-start.2 = (f32[257,256]{1,0:T(8,128)}, f32[257,256]{1,0:T(8,128)S(1)}, u32[]{:S(2)}, u32[]{:S(2)}) collective-permute-start(f32[257,256]{1,0:T(8,128)} %pad_maximum_fusion.2), channel_id=1, source_target_pairs={{0,2},{16,18},{1,3},{17,19},{2,0},{18,16},{3,1},{19,17},{4,6},{20,... | collective-permute-start | bytes 789512 | tf_op jit(solution)/shard_map/ppermute | solution.py:59
  47.4 0.7 copy-start.9
  51.1 0.8 copy-start.6
  53.4 8.1 %collective-permute-start.3 = (f32[257,256]{1,0:T(8,128)}, f32[257,256]{1,0:T(8,128)}, u32[]{:S(2)}, u32[]{:S(2)}) collective-permute-start(f32[257,256]{1,0:T(8,128)} %pad_maximum_fusion.3), channel_id=1, source_target_pairs={{0,4},{16,20},{1,5},{17,21},{2,6},{18,22},{3,7},{19,23},{4,0},{20,... | collective-permute-start | bytes 789512 | tf_op jit(solution)/shard_map/ppermute | solution.py:59
  55.2 14.3 %copy-start.4 = (f32[3,256,256]{2,1,0:T(8,128)S(1)}, f32[3,256,256]{2,1,0:T(8,128)}, u32[]{:S(2)}) copy-start(f32[3,256,256]{2,1,0:T(8,128)} %copy-done.3) | copy-start | bytes 2359300
  55.2 14.6 %copy-start.2 = (f32[6,256,256]{2,1,0:T(8,128)S(1)}, f32[6,256,256]{2,1,0:T(8,128)}, u32[]{:S(2)}) copy-start(f32[6,256,256]{2,1,0:T(8,128)} %fusion) | copy-start | bytes 4718596
  63.5 4.5 %collective-permute-start.4 = (f32[256]{0:T(256)S(1)}, f32[256]{0:T(256)S(1)}, u32[]{:S(2)}, u32[]{:S(2)}) collective-permute-start(f32[256]{0:T(256)S(1)} %select_add_fusion), channel_id=1, source_target_pairs={{0,8},{16,24},{1,9},{17,25},{2,10},{18,26},{3,11},{19,27},{4,12},{... | collective-permute-start | bytes 3080 | tf_op jit(solution)/shard_map/ppermute | solution.py:59
  68.0 4.4 %copy-start.10 = (f32[1,24,256]{2,1,0:T(8,128)S(1)}, f32[1,24,256]{2,1,0:T(8,128)}, u32[]{:S(2)}) copy-start(f32[1,24,256]{2,1,0:T(8,128)} %param.7) | copy-start | bytes 73732
  68.0 4.4 %copy-start.12 = (f32[1,24,256]{2,1,0:T(8,128)S(1)}, f32[1,24,256]{2,1,0:T(8,128)}, u32[]{:S(2)}) copy-start(f32[1,24,256]{2,1,0:T(8,128)} %param.9) | copy-start | bytes 73732
  75.0 5.1 %collective-permute-start.10 = (f32[129,128]{1,0:T(8,128)S(1)}, f32[129,128]{1,0:T(8,128)S(1)}, u32[]{:S(2)}, u32[]{:S(2)}) collective-permute-start(f32[129,128]{1,0:T(8,128)S(1)} %select_maximum_fusion), channel_id=1, source_target_pairs={{0,3},{16,19},{1,2},{17,18},{2,1},{18,17},{3,0},{19,16},{4,7},{20,... | collective-permute-start | bytes 198152 | tf_op jit(solution)/shard_map/ppermute | solution.py:59
  75.1 6.9 %collective-permute-start.11 = (f32[129,128]{1,0:T(8,128)S(1)}, f32[129,128]{1,0:T(8,128)S(1)}, u32[]{:S(2)}, u32[]{:S(2)}) collective-permute-start(f32[129,128]{1,0:T(8,128)S(1)} %select_maximum_fusion), channel_id=1, source_target_pairs={{0,19},{16,3},{1,18},{17,2},{2,17},{18,1},{3,16},{19,0},{4,23},{20... | collective-permute-start | bytes 198152 | tf_op jit(solution)/shard_map/ppermute | solution.py:59
  77.9 5.8 %collective-permute-start.5 = (f32[129,128]{1,0:T(8,128)S(1)}, f32[129,128]{1,0:T(8,128)S(1)}, u32[]{:S(2)}, u32[]{:S(2)}) collective-permute-start(f32[129,128]{1,0:T(8,128)S(1)} %select_maximum_fusion), channel_id=1, source_target_pairs={{0,16},{16,0},{1,17},{17,1},{2,18},{18,2},{3,19},{19,3},{4,20},{20... | collective-permute-start | bytes 198152 | tf_op jit(solution)/shard_map/ppermute | solution.py:59
  78.3 5.4 %collective-permute-start.6 = (f32[129,128]{1,0:T(8,128)S(1)}, f32[129,128]{1,0:T(8,128)S(1)}, u32[]{:S(2)}, u32[]{:S(2)}) collective-permute-start(f32[129,128]{1,0:T(8,128)S(1)} %select_maximum_fusion), channel_id=1, source_target_pairs={{0,1},{16,17},{1,0},{17,16},{2,3},{18,19},{3,2},{19,18},{4,5},{20,... | collective-permute-start | bytes 198152 | tf_op jit(solution)/shard_map/ppermute | solution.py:59
  78.3 6.3 %collective-permute-start.7 = (f32[129,128]{1,0:T(8,128)S(1)}, f32[129,128]{1,0:T(8,128)S(1)}, u32[]{:S(2)}, u32[]{:S(2)}) collective-permute-start(f32[129,128]{1,0:T(8,128)S(1)} %select_maximum_fusion), channel_id=1, source_target_pairs={{0,17},{16,1},{1,16},{17,0},{2,19},{18,3},{3,18},{19,2},{4,21},{20... | collective-permute-start | bytes 198152 | tf_op jit(solution)/shard_map/ppermute | solution.py:59
  80.1 4.6 %collective-permute-start.8 = (f32[129,128]{1,0:T(8,128)S(1)}, f32[129,128]{1,0:T(8,128)S(1)}, u32[]{:S(2)}, u32[]{:S(2)}) collective-permute-start(f32[129,128]{1,0:T(8,128)S(1)} %select_maximum_fusion), channel_id=1, source_target_pairs={{0,2},{16,18},{1,3},{17,19},{2,0},{18,16},{3,1},{19,17},{4,6},{20,... | collective-permute-start | bytes 198152 | tf_op jit(solution)/shard_map/ppermute | solution.py:59
  81.9 5.2 %collective-permute-start.9 = (f32[129,128]{1,0:T(8,128)S(1)}, f32[129,128]{1,0:T(8,128)S(1)}, u32[]{:S(2)}, u32[]{:S(2)}) collective-permute-start(f32[129,128]{1,0:T(8,128)S(1)} %select_maximum_fusion), channel_id=1, source_target_pairs={{0,18},{16,2},{1,19},{17,3},{2,16},{18,0},{3,17},{19,1},{4,22},{20... | collective-permute-start | bytes 198152 | tf_op jit(solution)/shard_map/ppermute | solution.py:59
  87.2 5.1 %collective-permute-start.12 = (f32[129,128]{1,0:T(8,128)S(1)}, f32[129,128]{1,0:T(8,128)S(1)}, u32[]{:S(2)}, u32[]{:S(2)}) collective-permute-start(f32[129,128]{1,0:T(8,128)S(1)} %add_add_fusion.1), channel_id=1, source_target_pairs={{0,4},{16,20},{1,5},{17,21},{2,6},{18,22},{3,7},{19,23},{4,0},{20,... | collective-permute-start | bytes 198152 | tf_op jit(solution)/shard_map/ppermute | solution.py:59
  88.8 6.7 %collective-permute-start.13 = (f32[129,128]{1,0:T(8,128)S(1)}, f32[129,128]{1,0:T(8,128)S(1)}, u32[]{:S(2)}, u32[]{:S(2)}) collective-permute-start(f32[129,128]{1,0:T(8,128)S(1)} %add_add_fusion.1), channel_id=1, source_target_pairs={{0,8},{16,24},{1,9},{17,25},{2,10},{18,26},{3,11},{19,27},{4,12},{... | collective-permute-start | bytes 198152 | tf_op jit(solution)/shard_map/ppermute | solution.py:59
  91.4 6.1 %collective-permute-start.14 = (f32[129,128]{1,0:T(8,128)S(1)}, f32[129,128]{1,0:T(8,128)S(1)}, u32[]{:S(2)}, u32[]{:S(2)}) collective-permute-start(f32[129,128]{1,0:T(8,128)S(1)} %add_add_fusion.1), channel_id=1, source_target_pairs={{0,12},{16,28},{1,13},{17,29},{2,14},{18,30},{3,15},{19,31},{4,8},... | collective-permute-start | bytes 198152 | tf_op jit(solution)/shard_map/ppermute | solution.py:59

commit v4 on v3

--- a/solution.py
+++ b/solution.py
@@ -74,24 +74,22 @@
     sq = jnp.eye(width, dtype=jnp.float32)
     sv = jnp.zeros((width,), jnp.float32)
 
+    packed = jnp.concatenate([tq, tv[None, :]], axis=0)
     d = 1
     while 2 * d < count:
         lower = (me // d) % 2 == 0
-        got = exchange(jnp.concatenate([tq, tv[None, :]], axis=0), d, count)
-        rq, rv = got[:width], got[width]
-        q_up = jnp.where(lower, rq, tq)
-        q_low = jnp.where(lower, tq, rq)
-        v_up = jnp.where(lower, rv, tv)
-        v_low = jnp.where(lower, tv, rv)
-        both = jnp.dot(q_up, jnp.concatenate([q_low, sq], axis=1), precision=EXACT)
-        new_sv = jnp.sum(rv[:, None] * sq, axis=0) + sv
-        tv = jnp.sum(v_up[:, None] * q_low, axis=0) + v_low
-        tq = both[:, :width]
-        sq = jnp.where(lower, both[:, width:], sq)
-        sv = jnp.where(lower, new_sv, sv)
+        got = exchange(packed, d, count)
+        later = jnp.where(lower, got, packed)
+        earlier_q = jnp.where(lower, packed[:width], got[:width])
+        earlier_v = jnp.where(lower, packed[width], got[width])
+        both = jnp.dot(later, jnp.concatenate([earlier_q, sq], axis=1), precision=EXACT)
+        offset = jnp.zeros((width + 1, width), jnp.float32).at[width].set(earlier_v)
+        packed = both[:, :width] + offset
+        sq = jnp.where(lower, both[:width, width:], sq)
+        sv = jnp.where(lower, both[width, width:] + sv, sv)
         d *= 2
     lower = (me // d) % 2 == 0
-    rv = exchange(tv, d, count)
+    rv = exchange(packed[width], d, count)
     incoming = jnp.where(lower, jnp.sum(rv[:, None] * sq, axis=0) + sv, sv)
 
     after = downsweep(levels, incoming[None, :])
@@ -106,14 +104,10 @@
     local_noise = -jnp.sum(length_rates * offset_response[0])
     noise_row = jnp.zeros((1, local_kernel.shape[1]), jnp.float32).at[0, 0].set(local_noise)
     packed = jnp.concatenate([local_kernel, noise_row], axis=0)
-    low = 1
-    while low < count:
-        high = min(low * 8, count)
-        vals = [packed] + [exchange(packed, m, count) for m in range(low, high, low)]
-        while len(vals) > 1:
-            vals = [vals[i] + vals[i + 1] for i in range(0, len(vals), 2)]
-        packed = vals[0]
-        low = high
+    d = 1
+    while d < count:
+        packed = packed + exchange(packed, d, count)
+        d *= 2
     return (length_rates[None], packed[:stations], packed[stations, 0])
 
 

time: 99.3 us -> 96.7 us (0.974)
  other arithmetic: 19 us -> 25.2 us
  starting transfers between devices: 21 us -> 15.3 us
  local copies, waits for them, and re-layouts: 6.28 us -> 4.12 us
  waiting for transfers between devices: 33 us -> 31.6 us
    select_n x4 -> x7, other arithmetic: 0.03 us -> 6.97 us  [the longest x4 3.93 us: body(): earlier_q = jnp.where(lower, packed[:width], got[:width])]
    ppermute x15 -> x10, starting transfers between devices: 21 us -> 15.3 us  [exchange(): lax.ppermute(x, AXES, [(place(j), place(j ^ mask)) for j in range(count)])]
    reduce_sum x5 -> x1, other arithmetic: 4.86 us -> 1.06 us  [body(): incoming = jnp.where(lower, jnp.sum(rv[:, None] * sq, axis=0) + sv, sv)]
    reduce_sum x10, other arithmetic: 7.69 us -> 10.7 us  [vecmat(): return jnp.sum(v[:, :, None] * q.astype(jnp.float32), axis=1)]
    scatter x0 -> x4, other arithmetic: none -> 2.91 us  [body(): offset = jnp.zeros((width + 1, width), jnp.float32).at[width].set(earlier_v)]
    concatenate x4 -> x1, other arithmetic: 2.97 us -> 0.74 us  [body(): packed = jnp.concatenate([tq, tv[None, :]], axis=0)]
    add x6 -> x5, other arithmetic: 1.48 us -> 0.05 us  [body(): packed = packed + exchange(packed, d, count)]
    slice x7 -> x3, local copies, waits for them, and re-layouts: 1.45 us -> 0.06 us  [body(): packed = both[:, :width] + offset]
  transfers between devices with their start and end apart: 15 -> 10, of which waited for: 11 -> 10; matrix products, arithmetic and copies ran while one was open for 1% -> 5% of each run, Pallas kernels for 0% -> 0%
where the time goes in v4:
time: 96.7 us; the launch traced here: 95.8 us
  waiting for transfers between devices  31.6 us (33%)
  other arithmetic  25.2 us (26%)
  matrix products  17 us (18%)
  starting transfers between devices  15.3 us (16%)
  local copies, waits for them, and re-layouts  4.12 us (4%)
  between operations  2.52 us (3%)
    ppermute x10, waiting for transfers between devices, exchange(): lax.ppermute(x, AXES, [(place(j), place(j ^ mask)) for j in range(count)])  31.6 us
    ppermute x10, starting transfers between devices, exchange(): lax.ppermute(x, AXES, [(place(j), place(j ^ mask)) for j in range(count)])  15.3 us
    reduce_sum x10, other arithmetic, vecmat(): return jnp.sum(v[:, :, None] * q.astype(jnp.float32), axis=1)  10.7 us
    dot_general x4, matrix products, matmat(): jnp.einsum('nij,njk->nik', later.astype(jnp.float32), earlier.astype(jnp....  7.82 us
    dot_general x4, matrix products, body(): jnp.dot(later, jnp.concatenate([earlier_q, sq], axis=1), precision=EXACT)  6.4 us
    select_n x4, other arithmetic, body(): earlier_q = jnp.where(lower, packed[:width], got[:width])  3.93 us
    select_n x3, other arithmetic, body(): sq = jnp.where(lower, both[:width, width:], sq)  3.04 us
    scatter x4, other arithmetic, body(): offset = jnp.zeros((width + 1, width), jnp.float32).at[width].set(earlier_v)  2.91 us
  transfers between devices with their start and end apart: 10, of which 10 were waited for; matrix products, arithmetic and copies ran while one was open for 5% of the time, Pallas kernels for 0%

profile of v4, /device:TPU:0, one launch (start us, length us, event | category | flops | bytes accessed | tf_op | source)
XLA Modules:
  0.0 95.8 jit_solution(7544454407805383523)
XLA Ops:
  0.6 2.6 %multiply_reduce_fusion = f32[24,256]{1,0:T(8,128)S(1)} fusion(f32[24,256]{1,0:T(8,128)} %bitcast.59, bf16[1,24,256,256]{3,2,1,0:T(8,128)(2,1)} %param.14), kind=kLoop, calls=%fused_computation | loop fusion | flops 4712448 | bytes 3194880 | tf_op jit(solution)/shard_map/reduce_sum | solution.py:11
  3.3 0.2 copy-done
  3.5 2.3 %fusion.3 = f32[12,256,256]{2,1,0:T(8,128)} fusion(bf16[24,256,256]{2,1,0:T(8,128)(2,1)S(1)} %bitcast.56), kind=kOutput, calls=%fused_computation.8 | convolution fusion | flops 402653184 | bytes 6291456 | tf_op jit(solution)/shard_map/nij,njk->nik/dot_general | solution.py:16
  5.8 0.5 multiply_reduce_fusion.2
  6.3 4.8 %fusion = f32[6,256,256]{2,1,0:T(8,128)} fusion(f32[12,256,256]{2,1,0:T(8,128)} %fusion.3), kind=kOutput, calls=%fused_computation.5 | convolution fusion | flops 1207959552 | bytes 4718592 | tf_op jit(solution)/shard_map/nij,njk->nik/dot_general | solution.py:17
  11.1 0.3 multiply_reduce_fusion.4
  11.4 2.3 %fusion.6 = f32[3,256,256]{2,1,0:T(8,128)S(1)} fusion(f32[6,256,256]{2,1,0:T(8,128)} %fusion), kind=kOutput, calls=%fused_computation.14 | convolution fusion | flops 603979776 | bytes 2359296 | tf_op jit(solution)/shard_map/nij,njk->nik/dot_general | solution.py:17
  13.7 1.6 %multiply_reduce_fusion.6 = f32[3,256]{1,0:T(4,128)S(1)} fusion(f32[6,256,256]{2,1,0:T(8,128)} %fusion, f32[3,256]{1,0:T(4,128)S(1)} %slice.264), kind=kLoop, calls=%fused_computation.13 | loop fusion | flops 392448 | bytes 792576 | tf_op jit(solution)/shard_map/reduce_sum | solution.py:11
  15.3 0.4 multiply_reduce_fusion.10
  15.7 0.4 fusion.34
  16.1 0.1 multiply_reduce_fusion.9
  16.3 0.7 pad_maximum_fusion
  17.0 3.0 %collective-permute-start = (f32[257,256]{1,0:T(8,128)}, f32[257,256]{1,0:T(8,128)}, u32[]{:S(2)}, u32[]{:S(2)}) collective-permute-start(f32[257,256]{1,0:T(8,128)} %pad_maximum_fusion), channel_id=1, source_target_pairs={{0,16},{16,0},{1,17},{17,1},{2,18},{18,2},{3,19},{19,3},{4,20},{20... | collective-permute-start | bytes 789512 | tf_op jit(solution)/shard_map/ppermute | solution.py:59
  20.0 6.8 %collective-permute-done = f32[257,256]{1,0:T(8,128)} collective-permute-done((f32[257,256]{1,0:T(8,128)}, f32[257,256]{1,0:T(8,128)}, u32[]{:S(2)}, u32[]{:S(2)}) %collective-permute-start) | collective-permute-done | bytes 263200 | tf_op jit(solution)/shard_map/ppermute | solution.py:59
  26.8 1.0 %slice_select_fusion.7 = f32[256,256]{1,0:T(8,128)S(1)} fusion(f32[256,256]{1,0:T(8,128)S(1)} %fusion.34, f32[257,256]{1,0:T(8,128)} %collective-permute-done, pred[]{:T(512)S(6)} %eq.30), kind=kLoop, calls=%fused_computation.47 | loop fusion | flops 65536 | bytes 786433 | tf_op jit(solution)/shard_map/jit(_where)/select_n | solution.py:83
  27.8 1.6 %fusion.9 = f32[257,512]{1,0:T(8,128)S(1)} fusion(f32[256,256]{1,0:T(8,128)S(1)} %fusion.36, f32[256,256]{1,0:T(8,128)S(1)} %slice_select_fusion.7, f32[257,256]{1,0:T(8,128)} %collective-permute-done, pred[]{:T(512)S(6)} %eq.30, f32[1,256]{1,0:T(1,128)S(1)} %fusion.52, f32[256,256]{1,0:T(8,128)S(1)} %fusion.34), kind=kOutput, calls=%fused_computation.17 | convolution fusion | flops 404488704 | bytes 1576961 | tf_op jit(solution)/shard_map/dot_general | solution.py:85
  29.4 0.8 copy-done.3
  30.2 0.7 fusion.48
  30.9 0.1 collective-permute-start.1
  31.0 1.0 %slice_select_fusion.5 = f32[256,256]{1,0:T(8,128)S(1)} fusion(f32[257,512]{1,0:T(8,128)} %copy-done.3, pred[]{:T(512)S(6)} %eq.30), kind=kLoop, calls=%fused_computation.45 | loop fusion | flops 196608 | bytes 524289 | tf_op jit(solution)/shard_map/jit(_where)/select_n | solution.py:88
  32.0 0.7 collective-permute-done.1
  32.7 1.0 %slice_select_fusion.6 = f32[256,256]{1,0:T(8,128)S(1)} fusion(f32[257,256]{1,0:T(8,128)} %collective-permute-done.1, f32[257,256]{1,0:T(8,128)S(1)} %add.167, pred[]{:T(512)S(6)} %eq.29), kind=kLoop, calls=%fused_computation.46 | loop fusion | flops 65536 | bytes 786433 | tf_op jit(solution)/shard_map/jit(_where)/select_n | solution.py:83
  33.7 1.6 %fusion.13 = f32[257,512]{1,0:T(8,128)S(1)} fusion(f32[256,256]{1,0:T(8,128)S(1)} %slice_select_fusion.5, f32[256,256]{1,0:T(8,128)S(1)} %slice_select_fusion.6, f32[257,256]{1,0:T(8,128)} %collective-permute-done.1, f32[257,256]{1,0:T(8,128)S(1)} %add.167, pred[]{:T(512)S(6)} %eq.29), kind=kOutput, calls=%fused_computation.21 | convolution fusion | flops 404422912 | bytes 1576961 | tf_op jit(solution)/shard_map/dot_general | solution.py:85
  35.3 0.8 copy-done.6
  36.1 0.7 fusion.49
  36.8 1.8 %collective-permute-start.2 = (f32[257,256]{1,0:T(8,128)S(1)}, f32[257,256]{1,0:T(8,128)}, u32[]{:S(2)}, u32[]{:S(2)}) collective-permute-start(f32[257,256]{1,0:T(8,128)S(1)} %add.168), channel_id=1, source_target_pairs={{0,2},{16,18},{1,3},{17,19},{2,0},{18,16},{3,1},{19,17},{4,6},{20,... | collective-permute-start | bytes 789512 | tf_op jit(solution)/shard_map/ppermute | solution.py:59
  38.6 1.1 %slice_select_fusion.3 = f32[256,256]{1,0:T(8,128)S(1)} fusion(f32[257,512]{1,0:T(8,128)} %copy-done.6, pred[]{:T(512)S(6)} %eq.29, f32[257,512]{1,0:T(8,128)} %copy-done.3, pred[]{:T(512)S(6)} %eq.30), kind=kLoop, calls=%fused_computation.43 | loop fusion | flops 262144 | bytes 786434 | tf_op jit(solution)/shard_map/jit(_where)/select_n | solution.py:88
  39.7 4.9 %collective-permute-done.2 = f32[257,256]{1,0:T(8,128)} collective-permute-done((f32[257,256]{1,0:T(8,128)S(1)}, f32[257,256]{1,0:T(8,128)}, u32[]{:S(2)}, u32[]{:S(2)}) %collective-permute-start.2) | collective-permute-done | bytes 263200 | tf_op jit(solution)/shard_map/ppermute | solution.py:59
  44.6 1.0 %slice_select_fusion.4 = f32[256,256]{1,0:T(8,128)S(1)} fusion(f32[257,256]{1,0:T(8,128)} %collective-permute-done.2, f32[257,256]{1,0:T(8,128)S(1)} %add.168, pred[]{:T(512)S(6)} %eq.28), kind=kLoop, calls=%fused_computation.44 | loop fusion | flops 65536 | bytes 786433 | tf_op jit(solution)/shard_map/jit(_where)/select_n | solution.py:83
  45.6 1.6 %fusion.17 = f32[257,512]{1,0:T(8,128)S(1)} fusion(f32[256,256]{1,0:T(8,128)S(1)} %slice_select_fusion.3, f32[256,256]{1,0:T(8,128)S(1)} %slice_select_fusion.4, f32[257,256]{1,0:T(8,128)} %collective-permute-done.2, f32[257,256]{1,0:T(8,128)S(1)} %add.168, pred[]{:T(512)S(6)} %eq.28), kind=kOutput, calls=%fused_computation.25 | convolution fusion | flops 404422912 | bytes 1576961 | tf_op jit(solution)/shard_map/dot_general | solution.py:85
  47.2 0.8 copy-done.7
  48.0 0.7 fusion.50
  48.7 1.9 %collective-permute-start.3 = (f32[257,256]{1,0:T(8,128)S(1)}, f32[257,256]{1,0:T(8,128)}, u32[]{:S(2)}, u32[]{:S(2)}) collective-permute-start(f32[257,256]{1,0:T(8,128)S(1)} %add.169), channel_id=1, source_target_pairs={{0,4},{16,20},{1,5},{17,21},{2,6},{18,22},{3,7},{19,23},{4,0},{20,... | collective-permute-start | bytes 789512 | tf_op jit(solution)/shard_map/ppermute | solution.py:59
  50.6 1.0 %slice_select_fusion.1 = f32[256,256]{1,0:T(8,128)S(1)} fusion(f32[256,256]{1,0:T(8,128)} %copy-done.5, f32[257,512]{1,0:T(8,128)} %copy-done.7, pred[]{:T(512)S(6)} %eq.28), kind=kLoop, calls=%fused_computation.41 | loop fusion | flops 65536 | bytes 786433 | tf_op jit(solution)/shard_map/jit(_where)/select_n | solution.py:88
  51.6 4.0 %collective-permute-done.3 = f32[257,256]{1,0:T(8,128)} collective-permute-done((f32[257,256]{1,0:T(8,128)S(1)}, f32[257,256]{1,0:T(8,128)}, u32[]{:S(2)}, u32[]{:S(2)}) %collective-permute-start.3) | collective-permute-done | bytes 263200 | tf_op jit(solution)/shard_map/ppermute | solution.py:59
  55.6 1.0 %slice_select_fusion.2 = f32[256,256]{1,0:T(8,128)S(1)} fusion(f32[257,256]{1,0:T(8,128)} %collective-permute-done.3, f32[257,256]{1,0:T(8,128)S(1)} %add.169, pred[]{:T(512)S(6)} %eq.27), kind=kLoop, calls=%fused_computation.42 | loop fusion | flops 65536 | bytes 786433 | tf_op jit(solution)/shard_map/jit(_where)/select_n | solution.py:83
  56.6 1.6 %fusion.21 = f32[257,512]{1,0:T(8,128)S(1)} fusion(f32[256,256]{1,0:T(8,128)S(1)} %slice_select_fusion.1, f32[256,256]{1,0:T(8,128)S(1)} %slice_select_fusion.2, f32[257,256]{1,0:T(8,128)} %collective-permute-done.3, f32[257,256]{1,0:T(8,128)S(1)} %add.169, pred[]{:T(512)S(6)} %eq.27), kind=kOutput, calls=%fused_computation.29 | convolution fusion | flops 404422912 | bytes 1576961 | tf_op jit(solution)/shard_map/dot_general | solution.py:85
  58.2 0.8 fusion.51
  59.0 2.8 %collective-permute-start.4 = (f32[256]{0:T(256)S(1)}, f32[256]{0:T(256)S(1)}, u32[]{:S(2)}, u32[]{:S(2)}) collective-permute-start(f32[256]{0:T(256)S(1)} %bitcast.76), channel_id=1, source_target_pairs={{0,8},{16,24},{1,9},{17,25},{2,10},{18,26},{3,11},{19,27},{4,12},{... | collective-permute-start | bytes 3080 | tf_op jit(solution)/shard_map/ppermute | solution.py:59
  61.8 0.6 compare_reduce_fusion
  62.4 1.1 %collective-permute-done.4 = f32[256]{0:T(256)S(1)} collective-permute-done((f32[256]{0:T(256)S(1)}, f32[256]{0:T(256)S(1)}, u32[]{:S(2)}, u32[]{:S(2)}) %collective-permute-start.4) | collective-permute-done | bytes 1056 | tf_op jit(solution)/shard_map/ppermute | solution.py:59
  63.5 1.1 %fusion.30 = f32[256]{0:T(256)S(1)} fusion(f32[256,256]{1,0:T(8,128)} %copy-done.4, f32[257,512]{1,0:T(8,128)} %copy-done.8, f32[256]{0:T(256)S(1)} %collective-permute-done.4, pred[]{:T(512)S(6)} %eq.27), kind=kLoop, calls=%fused_computation.40 | loop fusion | flops 196352 | bytes 526337 | tf_op jit(solution)/shard_map/reduce_sum | solution.py:93
  64.6 0.8 broadcast_select_fusion
  65.3 1.1 %multiply_reduce_fusion.8 = f32[256]{0:T(256)S(1)} fusion(f32[3,256,256]{2,1,0:T(8,128)} %copy-done.2, f32[256]{0:T(256)S(1)} %add_select_fusion), kind=kLoop, calls=%fused_computation.54 | loop fusion | flops 130816 | bytes 264192 | tf_op jit(solution)/shard_map/reduce_sum | solution.py:11
  66.4 1.1 %multiply_reduce_fusion.7 = f32[256]{0:T(256)S(1)} fusion(f32[3,256,256]{2,1,0:T(8,128)} %copy-done.2, f32[256]{0:T(256)S(1)} %bitcast.63), kind=kLoop, calls=%fused_computation.53 | loop fusion | flops 130816 | bytes 264192 | tf_op jit(solution)/shard_map/reduce_sum | solution.py:11
  67.5 1.3 %multiply_reduce_fusion.5 = f32[3,256]{1,0:T(4,128)S(1)} fusion(f32[6,256,256]{2,1,0:T(8,128)} %fusion, f32[3,256]{1,0:T(4,128)S(1)} %get-tuple-element.74), kind=kLoop, calls=%fused_computation.12 | loop fusion | flops 392448 | bytes 792576 | tf_op jit(solution)/shard_map/reduce_sum | solution.py:11
  68.9 1.7 %multiply_reduce_fusion.3 = f32[6,256]{1,0:T(8,128)S(1)} fusion(f32[12,256,256]{2,1,0:T(8,128)} %fusion.3, f32[6,256]{1,0:T(8,128)S(1)} %mul.140), kind=kLoop, calls=%fused_computation.3 | loop fusion | flops 784896 | bytes 1585152 | tf_op jit(solution)/shard_map/reduce_sum | solution.py:11
  70.7 0.5 multiply_reduce_fusion.1
  71.3 0.6 fusion.44
  72.6 0.3 fusion.46
  72.9 0.3 convolution_add_fusion
  73.8 0.8 collective-permute-start.5
  74.6 3.6 %collective-permute-done.5 = f32[129,128]{1,0:T(8,128)S(1)} collective-permute-done((f32[129,128]{1,0:T(8,128)S(1)}, f32[129,128]{1,0:T(8,128)S(1)}, u32[]{:S(2)}, u32[]{:S(2)}) %collective-permute-start.5) | collective-permute-done | bytes 66080 | tf_op jit(solution)/shard_map/ppermute | solution.py:59
  78.2 0.1 collective-permute-start.6
  78.3 1.2 %collective-permute-done.6 = f32[129,128]{1,0:T(8,128)S(1)} collective-permute-done((f32[129,128]{1,0:T(8,128)S(1)}, f32[129,128]{1,0:T(8,128)S(1)}, u32[]{:S(2)}, u32[]{:S(2)}) %collective-permute-start.6) | collective-permute-done | bytes 66080 | tf_op jit(solution)/shard_map/ppermute | solution.py:59
  79.5 0.8 collective-permute-start.7
  80.3 3.6 %collective-permute-done.7 = f32[129,128]{1,0:T(8,128)S(1)} collective-permute-done((f32[129,128]{1,0:T(8,128)S(1)}, f32[129,128]{1,0:T(8,128)S(1)}, u32[]{:S(2)}, u32[]{:S(2)}) %collective-permute-start.7) | collective-permute-done | bytes 66080 | tf_op jit(solution)/shard_map/ppermute | solution.py:59
  83.9 0.9 collective-permute-start.8
  84.9 3.4 %collective-permute-done.8 = f32[129,128]{1,0:T(8,128)S(1)} collective-permute-done((f32[129,128]{1,0:T(8,128)S(1)}, f32[129,128]{1,0:T(8,128)S(1)}, u32[]{:S(2)}, u32[]{:S(2)}) %collective-permute-start.8) | collective-permute-done | bytes 66080 | tf_op jit(solution)/shard_map/ppermute | solution.py:59
  88.3 3.3 %collective-permute-start.9 = (f32[129,128]{1,0:T(8,128)S(1)}, f32[129,128]{1,0:T(8,128)S(1)}, u32[]{:S(2)}, u32[]{:S(2)}) collective-permute-start(f32[129,128]{1,0:T(8,128)S(1)} %add.189), channel_id=1, source_target_pairs={{0,8},{16,24},{1,9},{17,25},{2,10},{18,26},{3,11},{19,27},{4,12},{... | collective-permute-start | bytes 198152 | tf_op jit(solution)/shard_map/ppermute | solution.py:59
  91.6 0.6 add.183
  92.2 2.4 %collective-permute-done.9 = f32[129,128]{1,0:T(8,128)S(1)} collective-permute-done((f32[129,128]{1,0:T(8,128)S(1)}, f32[129,128]{1,0:T(8,128)S(1)}, u32[]{:S(2)}, u32[]{:S(2)}) %collective-permute-start.9) | collective-permute-done | bytes 66080 | tf_op jit(solution)/shard_map/ppermute | solution.py:59
  94.6 0.6 slice.337
  95.3 0.5 slice.338
  (65 shorter events, 0.6 us)
Async XLA Ops:
  0.6 2.9 %copy-start = (bf16[1,24,256,256]{3,2,1,0:T(8,128)(2,1)S(1)}, bf16[1,24,256,256]{3,2,1,0:T(8,128)(2,1)}, u32[]{:S(2)}) copy-start(bf16[1,24,256,256]{3,2,1,0:T(8,128)(2,1)} %param.14) | copy-start | bytes 9437188
  6.3 4.8 %copy-start.1 = (f32[12,256,256]{2,1,0:T(8,128)S(1)}, f32[12,256,256]{2,1,0:T(8,128)}, u32[]{:S(2)}) copy-start(f32[12,256,256]{2,1,0:T(8,128)} %fusion.3) | copy-start | bytes 9437188
  13.7 2.4 %copy-start.2 = (f32[3,256,256]{2,1,0:T(8,128)}, f32[3,256,256]{2,1,0:T(8,128)S(1)}, u32[]{:S(2)}) copy-start(f32[3,256,256]{2,1,0:T(8,128)S(1)} %fusion.6) | copy-start | bytes 2359300
  17.0 9.8 %collective-permute-start = (f32[257,256]{1,0:T(8,128)}, f32[257,256]{1,0:T(8,128)}, u32[]{:S(2)}, u32[]{:S(2)}) collective-permute-start(f32[257,256]{1,0:T(8,128)} %pad_maximum_fusion), channel_id=1, source_target_pairs={{0,16},{16,0},{1,17},{17,1},{2,18},{18,2},{3,19},{19,3},{4,20},{20... | collective-permute-start | bytes 789512 | tf_op jit(solution)/shard_map/ppermute | solution.py:59
  29.4 0.8 copy-start.3
  30.9 1.7 %collective-permute-start.1 = (f32[257,256]{1,0:T(8,128)S(1)}, f32[257,256]{1,0:T(8,128)}, u32[]{:S(2)}, u32[]{:S(2)}) collective-permute-start(f32[257,256]{1,0:T(8,128)S(1)} %add.167), channel_id=1, source_target_pairs={{0,1},{16,17},{1,0},{17,16},{2,3},{18,19},{3,2},{19,18},{4,5},{20,... | collective-permute-start | bytes 789512 | tf_op jit(solution)/shard_map/ppermute | solution.py:59
  33.7 16.9 %copy-start.10 = (f32[1,24,2,128]{3,2,1,0:T(2,128)S(1)}, f32[1,24,2,128]{3,2,1,0:T(2,128)}, u32[]{:S(2)}) copy-start(f32[1,24,2,128]{3,2,1,0:T(2,128)} %param.16) | copy-start | bytes 73732
  35.3 0.8 copy-start.6
  36.8 7.7 %collective-permute-start.2 = (f32[257,256]{1,0:T(8,128)S(1)}, f32[257,256]{1,0:T(8,128)}, u32[]{:S(2)}, u32[]{:S(2)}) collective-permute-start(f32[257,256]{1,0:T(8,128)S(1)} %add.168), channel_id=1, source_target_pairs={{0,2},{16,18},{1,3},{17,19},{2,0},{18,16},{3,1},{19,17},{4,6},{20,... | collective-permute-start | bytes 789512 | tf_op jit(solution)/shard_map/ppermute | solution.py:59
  39.7 7.5 %copy-start.5 = (f32[256,256]{1,0:T(8,128)}, f32[256,256]{1,0:T(8,128)S(1)}, u32[]{:S(2)}) copy-start(f32[256,256]{1,0:T(8,128)S(1)} %slice_select_fusion.3) | copy-start | bytes 786436
  47.2 0.8 copy-start.7
  48.7 6.9 %collective-permute-start.3 = (f32[257,256]{1,0:T(8,128)S(1)}, f32[257,256]{1,0:T(8,128)}, u32[]{:S(2)}, u32[]{:S(2)}) collective-permute-start(f32[257,256]{1,0:T(8,128)S(1)} %add.169), channel_id=1, source_target_pairs={{0,4},{16,20},{1,5},{17,21},{2,6},{18,22},{3,7},{19,23},{4,0},{20,... | collective-permute-start | bytes 789512 | tf_op jit(solution)/shard_map/ppermute | solution.py:59
  51.6 6.6 %copy-start.4 = (f32[256,256]{1,0:T(8,128)}, f32[256,256]{1,0:T(8,128)S(1)}, u32[]{:S(2)}) copy-start(f32[256,256]{1,0:T(8,128)S(1)} %slice_select_fusion.1) | copy-start | bytes 786436
  58.2 0.8 copy-start.8
  58.2 13.1 %copy-start.9 = (f32[1,24,256]{2,1,0:T(8,128)S(1)}, f32[1,24,256]{2,1,0:T(8,128)}, u32[]{:S(2)}) copy-start(f32[1,24,256]{2,1,0:T(8,128)} %param.15) | copy-start | bytes 73732
  58.2 13.1 %copy-start.11 = (f32[1,24,256]{2,1,0:T(8,128)S(1)}, f32[1,24,256]{2,1,0:T(8,128)}, u32[]{:S(2)}) copy-start(f32[1,24,256]{2,1,0:T(8,128)} %param.17) | copy-start | bytes 73732
  59.0 4.5 %collective-permute-start.4 = (f32[256]{0:T(256)S(1)}, f32[256]{0:T(256)S(1)}, u32[]{:S(2)}, u32[]{:S(2)}) collective-permute-start(f32[256]{0:T(256)S(1)} %bitcast.76), channel_id=1, source_target_pairs={{0,8},{16,24},{1,9},{17,25},{2,10},{18,26},{3,11},{19,27},{4,12},{... | collective-permute-start | bytes 3080 | tf_op jit(solution)/shard_map/ppermute | solution.py:59
  73.8 4.4 %collective-permute-start.5 = (f32[129,128]{1,0:T(8,128)S(1)}, f32[129,128]{1,0:T(8,128)S(1)}, u32[]{:S(2)}, u32[]{:S(2)}) collective-permute-start(f32[129,128]{1,0:T(8,128)S(1)} %select_maximum_fusion), channel_id=1, source_target_pairs={{0,16},{16,0},{1,17},{17,1},{2,18},{18,2},{3,19},{19,3},{4,20},{20... | collective-permute-start | bytes 198152 | tf_op jit(solution)/shard_map/ppermute | solution.py:59
  78.2 1.3 %collective-permute-start.6 = (f32[129,128]{1,0:T(8,128)S(1)}, f32[129,128]{1,0:T(8,128)S(1)}, u32[]{:S(2)}, u32[]{:S(2)}) collective-permute-start(f32[129,128]{1,0:T(8,128)S(1)} %fusion.58), channel_id=1, source_target_pairs={{0,1},{16,17},{1,0},{17,16},{2,3},{18,19},{3,2},{19,18},{4,5},{20,... | collective-permute-start | bytes 198152 | tf_op jit(solution)/shard_map/ppermute | solution.py:59
  79.5 4.4 %collective-permute-start.7 = (f32[129,128]{1,0:T(8,128)S(1)}, f32[129,128]{1,0:T(8,128)S(1)}, u32[]{:S(2)}, u32[]{:S(2)}) collective-permute-start(f32[129,128]{1,0:T(8,128)S(1)} %add.187), channel_id=1, source_target_pairs={{0,2},{16,18},{1,3},{17,19},{2,0},{18,16},{3,1},{19,17},{4,6},{20,... | collective-permute-start | bytes 198152 | tf_op jit(solution)/shard_map/ppermute | solution.py:59
  83.9 4.4 %collective-permute-start.8 = (f32[129,128]{1,0:T(8,128)S(1)}, f32[129,128]{1,0:T(8,128)S(1)}, u32[]{:S(2)}, u32[]{:S(2)}) collective-permute-start(f32[129,128]{1,0:T(8,128)S(1)} %add.188), channel_id=1, source_target_pairs={{0,4},{16,20},{1,5},{17,21},{2,6},{18,22},{3,7},{19,23},{4,0},{20,... | collective-permute-start | bytes 198152 | tf_op jit(solution)/shard_map/ppermute | solution.py:59
  88.3 6.3 %collective-permute-start.9 = (f32[129,128]{1,0:T(8,128)S(1)}, f32[129,128]{1,0:T(8,128)S(1)}, u32[]{:S(2)}, u32[]{:S(2)}) collective-permute-start(f32[129,128]{1,0:T(8,128)S(1)} %add.189), channel_id=1, source_target_pairs={{0,8},{16,24},{1,9},{17,25},{2,10},{18,26},{3,11},{19,27},{4,12},{... | collective-permute-start | bytes 198152 | tf_op jit(solution)/shard_map/ppermute | solution.py:59

commit v5 on v4

--- a/solution.py
+++ b/solution.py
@@ -9,6 +9,10 @@
 
 def vecmat(v, q):
     return jnp.sum(v[:, :, None] * q.astype(jnp.float32), axis=1)
+
+
+def vecmat_mxu(v, q):
+    return jnp.einsum("nj,njk->nk", v, q.astype(jnp.float32), precision=EXACT)
 
 
 def matmat(later, earlier):
@@ -42,7 +46,7 @@
         n = q.shape[0]
         half = n // 2
         upper = m[:half]
-        left = vecmat(upper, q[1 : 2 * half : 2]) + v[1 : 2 * half : 2]
+        left = vecmat_mxu(upper, q[1 : 2 * half : 2]) + v[1 : 2 * half : 2]
         m_new = jnp.stack([left, upper], axis=1).reshape(2 * half, -1)
         if n % 2:
             m_new = jnp.concatenate([m_new, m[-1:]], axis=0)
@@ -77,16 +81,19 @@
     packed = jnp.concatenate([tq, tv[None, :]], axis=0)
     d = 1
     while 2 * d < count:
-        lower = (me // d) % 2 == 0
         got = exchange(packed, d, count)
-        later = jnp.where(lower, got, packed)
-        earlier_q = jnp.where(lower, packed[:width], got[:width])
-        earlier_v = jnp.where(lower, packed[width], got[width])
-        both = jnp.dot(later, jnp.concatenate([earlier_q, sq], axis=1), precision=EXACT)
-        offset = jnp.zeros((width + 1, width), jnp.float32).at[width].set(earlier_v)
-        packed = both[:, :width] + offset
-        sq = jnp.where(lower, both[:width, width:], sq)
-        sv = jnp.where(lower, both[width, width:] + sv, sv)
+
+        def as_lower(packed, got, sq, sv):
+            both = jnp.dot(got, jnp.concatenate([packed[:width], sq], axis=1), precision=EXACT)
+            offset = jnp.zeros((width + 1, width), jnp.float32).at[width].set(packed[width])
+            return both[:, :width] + offset, both[:width, width:], both[width, width:] + sv
+
+        def as_upper(packed, got, sq, sv):
+            new = jnp.dot(packed, got[:width], precision=EXACT)
+            offset = jnp.zeros((width + 1, width), jnp.float32).at[width].set(got[width])
+            return new + offset, sq, sv
+
+        packed, sq, sv = lax.cond((me // d) % 2 == 0, as_lower, as_upper, packed, got, sq, sv)
         d *= 2
     lower = (me // d) % 2 == 0
     rv = exchange(packed[width], d, count)

time: 96.7 us -> 101 us (1.044)
  other arithmetic: 25.2 us -> 9.55 us
  local copies, waits for them, and re-layouts: 4.12 us -> 15.9 us
  matrix products: 17 us -> 24.1 us
  waiting for transfers between devices: 31.6 us -> 33.5 us
    reduce_sum x10 -> x5, other arithmetic: 10.7 us -> 3.66 us  [vecmat(): return jnp.sum(v[:, :, None] * q.astype(jnp.float32), axis=1)]
    dot_general x4 -> x9, matrix products: 6.4 us -> 13.4 us  [the longest x5 6.9 us: vecmat_mxu(): return jnp.einsum('nj,njk->nk', v, q.astype(jnp.float32), precision=EXACT)]
    select_n x7 -> x0, other arithmetic: 6.97 us -> none  [the longest x4 3.93 us: body(): earlier_q = jnp.where(lower, packed[:width], got[:width])]
    slice x3 -> x16, local copies, waits for them, and re-layouts: 0.06 us -> 6.85 us  [the longest x3 3.12 us: as_lower(): packed[:width]]
    add x3 -> x4, local copies, waits for them, and re-layouts: 0.07 us -> 5.21 us  [as_upper(): return (new + offset, sq, sv)]
    unnamed x24 -> x16, local copies, waits for them, and re-layouts: 2.6 us -> 0.26 us
    cond x0 -> x9, local copies, waits for them, and re-layouts: none -> 2.2 us
    ppermute x10, waiting for transfers between devices: 31.6 us -> 33.5 us  [exchange(): lax.ppermute(x, AXES, [(place(j), place(j ^ mask)) for j in range(count)])]
  transfers between devices with their start and end apart: 10 -> 10, of which waited for: 10 -> 10; matrix products, arithmetic and copies ran while one was open for 5% -> 1% of each run, Pallas kernels for 0% -> 0%
where the time goes in v5:
time: 101 us
  waiting for transfers between devices  33.5 us (33%)
  matrix products  24.1 us (24%)
  local copies, waits for them, and re-layouts  15.9 us (16%)
  starting transfers between devices  15 us (15%)
  other arithmetic  9.55 us (9%)
  between operations  2.29 us (2%)
    ppermute x10, waiting for transfers between devices, exchange(): lax.ppermute(x, AXES, [(place(j), place(j ^ mask)) for j in range(count)])  33.5 us
    ppermute x10, starting transfers between devices, exchange(): lax.ppermute(x, AXES, [(place(j), place(j ^ mask)) for j in range(count)])  15 us
    dot_general x4, matrix products, matmat(): jnp.einsum('nij,njk->nik', later.astype(jnp.float32), earlier.astype(jnp....  7.96 us
    dot_general x5, matrix products, vecmat_mxu(): return jnp.einsum('nj,njk->nk', v, q.astype(jnp.float32), precision=EXACT)  6.9 us
    dot_general x4, matrix products, as_lower(): jnp.dot(got, jnp.concatenate([packed[:width], sq], axis=1), precision=EXACT)  6.5 us
    add x4, local copies, waits for them, and re-layouts, as_upper(): return (new + offset, sq, sv)  5.21 us
    reduce_sum x5, other arithmetic, vecmat(): return jnp.sum(v[:, :, None] * q.astype(jnp.float32), axis=1)  3.66 us
    slice x3, local copies, waits for them, and re-layouts, as_lower(): packed[:width]  3.12 us
  transfers between devices with their start and end apart: 10, of which 10 were waited for; matrix products, arithmetic and copies ran while one was open for 1% of the time, Pallas kernels for 0%

profile of v5, /device:TPU:0, one launch (start us, length us, event | category | flops | bytes accessed | tf_op | source)
XLA Modules:
  0.0 100.5 jit_solution(16250828918497466346)
XLA Ops:
  0.6 2.6 %multiply_reduce_fusion = f32[24,256]{1,0:T(8,128)S(1)} fusion(f32[24,256]{1,0:T(8,128)} %bitcast.98, bf16[1,24,256,256]{3,2,1,0:T(8,128)(2,1)} %param.30), kind=kLoop, calls=%fused_computation.28 | loop fusion | flops 4712448 | bytes 3194880 | tf_op jit(solution)/shard_map/reduce_sum | solution.py:11
  3.5 2.2 %fusion.29 = f32[12,256,256]{2,1,0:T(8,128)} fusion(bf16[24,256,256]{2,1,0:T(8,128)(2,1)S(1)} %bitcast.95), kind=kOutput, calls=%fused_computation.36 | convolution fusion | flops 402653184 | bytes 6291456 | tf_op jit(solution)/shard_map/nij,njk->nik/dot_general | solution.py:20
  5.7 0.5 multiply_reduce_fusion.1
  6.3 4.8 %fusion.24 = f32[6,256,256]{2,1,0:T(8,128)} fusion(f32[12,256,256]{2,1,0:T(8,128)} %fusion.29), kind=kOutput, calls=%fused_computation.31 | convolution fusion | flops 1207959552 | bytes 4718592 | tf_op jit(solution)/shard_map/nij,njk->nik/dot_general | solution.py:21
  11.1 0.3 multiply_reduce_fusion.2
  11.4 2.4 %fusion.35 = f32[3,256,256]{2,1,0:T(8,128)S(1)} fusion(f32[6,256,256]{2,1,0:T(8,128)} %fusion.24), kind=kOutput, calls=%fused_computation.46 | convolution fusion | flops 603979776 | bytes 2359296 | tf_op jit(solution)/shard_map/nij,njk->nik/dot_general | solution.py:21
  14.0 0.4 multiply_reduce_fusion.6
  14.5 0.4 fusion.43
  15.0 0.8 pad_maximum_fusion
  15.8 3.0 %collective-permute-start = (f32[257,256]{1,0:T(8,128)}, f32[257,256]{1,0:T(8,128)}, u32[]{:S(2)}, u32[]{:S(2)}) collective-permute-start(f32[257,256]{1,0:T(8,128)} %pad_maximum_fusion), channel_id=1, source_target_pairs={{0,16},{16,0},{1,17},{17,1},{2,18},{18,2},{3,19},{19,3},{4,20},{20... | collective-permute-start | bytes 789512 | tf_op jit(solution)/shard_map/ppermute | solution.py:63
  18.8 6.8 %collective-permute-done = f32[257,256]{1,0:T(8,128)} collective-permute-done((f32[257,256]{1,0:T(8,128)}, f32[257,256]{1,0:T(8,128)}, u32[]{:S(2)}, u32[]{:S(2)}) %collective-permute-start) | collective-permute-done | bytes 263200 | tf_op jit(solution)/shard_map/ppermute | solution.py:63
  25.5 2.5 %conditional.4 = (f32[256,256]{1,0:T(8,128)S(1)}, f32[256]{0:T(256)S(1)}, f32[257,256]{1,0:T(8,128)}, s32[]{:T(128)}, f32[1,256]{1,0:T(1,128)S(1)}) conditional(s32[]{:T(128)} %convert_element_type.27, (f32[257,256]{1,0:T(8,128)}, f32[257,256]{1,0:T(8,128)}, f32[256,256]{1,0:T(8,128)S(1)}) %tuple.120, (f32[256,256]{1,0:T(8,128)}, ...), branch_computations={%region_6.7_spmd, %region_7.8_spmd} | conditional | flops 404357120 | bytes 2366512 | solution.py:96
  25.5 1.7 %convolution_bitcast_fusion = f32[257,512]{1,0:T(8,128)S(1)} fusion(f32[257,256]{1,0:T(8,128)} %get-tuple-element.361, f32[256,256]{1,0:T(8,128)S(1)} %get-tuple-element.360, f32[256,256]{1,0:T(8,128)} %get-tuple-element.359), kind=kOutput, calls=%fused_computation.2 | convolution fusion | flops 404357120 | bytes 1313792 | tf_op jit(solution)/shard_map/cond/branch_1_fun/dot_general | solution.py:87
  27.2 0.7 slice.371
  28.0 0.7 dynamic-slice_add_fusion
  28.7 1.3 %add.155 = f32[257,256]{1,0:T(8,128)} dynamic-update-slice(f32[257,256]{1,0:T(8,128)} %get-tuple-element.410, f32[1,256]{1,0:T(1,128)S(1)} %dynamic-slice_add_fusion, s32[]{:T(128)} %get-tuple-element.411, s32[]{:T(128)} %constant.391.clone.1) | dynamic-update-slice | bytes 2052 | tf_op jit(solution)/shard_map/cond/branch_0_fun/add | solution.py:94
  30.0 1.9 %collective-permute-done.1 = f32[257,256]{1,0:T(8,128)} collective-permute-done((f32[257,256]{1,0:T(8,128)}, f32[257,256]{1,0:T(8,128)}, u32[]{:S(2)}, u32[]{:S(2)}) %collective-permute-start.1) | collective-permute-done | bytes 263200 | tf_op jit(solution)/shard_map/ppermute | solution.py:63
  31.9 4.2 %conditional.5 = (f32[256,256]{1,0:T(8,128)S(1)}, f32[256]{0:T(256)S(1)}, f32[257,256]{1,0:T(8,128)}, s32[]{:T(128)}, f32[257,256]{1,0:T(8,128)}) conditional(s32[]{:T(128)} %convert_element_type.26, (f32[257,256]{1,0:T(8,128)}, f32[257,256]{1,0:T(8,128)}, f32[256,256]{1,0:T(8,128)S(1)}, f32[256]{0:T(256)S(1)}) %tuple.122, (f32[257,256]{1,0:T(8,128)}, ...), branch_computations={%region_8.9_spmd, %region_9.10_spmd} | conditional | flops 404357376 | bytes 4472908 | solution.py:96
  31.9 1.0 %slice.297 = f32[256,256]{1,0:T(8,128)S(1)} slice(f32[257,256]{1,0:T(8,128)} %get-tuple-element.459), slice={[0:256], [0:256]} | slice | bytes 524288 | tf_op jit(solution)/shard_map/cond/branch_1_fun/slice | solution.py:87
  32.9 1.6 %convolution_bitcast_fusion.1 = f32[257,512]{1,0:T(8,128)S(1)} fusion(f32[257,256]{1,0:T(8,128)} %get-tuple-element.369, f32[256,256]{1,0:T(8,128)S(1)} %get-tuple-element.368, f32[256,256]{1,0:T(8,128)S(1)} %slice.297), kind=kOutput, calls=%fused_computation.9 | convolution fusion | flops 404357120 | bytes 1313792 | tf_op jit(solution)/shard_map/cond/branch_1_fun/dot_general | solution.py:87
  34.5 0.7 slice.374
  35.3 0.7 copy.44
  36.1 0.7 slice_add_fusion.3
  36.8 1.3 %add.156 = f32[257,256]{1,0:T(8,128)} dynamic-update-slice(f32[257,256]{1,0:T(8,128)} %get-tuple-element.415, f32[1,256]{1,0:T(1,128)S(1)} %slice_add_fusion.3, s32[]{:T(128)} %get-tuple-element.416, s32[]{:T(128)} %constant.391.clone.1) | dynamic-update-slice | bytes 2052 | tf_op jit(solution)/shard_map/cond/branch_0_fun/add | solution.py:94
  38.1 1.7 %collective-permute-start.2 = (f32[257,256]{1,0:T(8,128)}, f32[257,256]{1,0:T(8,128)}, u32[]{:S(2)}, u32[]{:S(2)}) collective-permute-start(f32[257,256]{1,0:T(8,128)} %add.156), channel_id=1, source_target_pairs={{0,2},{16,18},{1,3},{17,19},{2,0},{18,16},{3,1},{19,17},{4,6},{20,... | collective-permute-start | bytes 789512 | tf_op jit(solution)/shard_map/ppermute | solution.py:63
  39.8 5.1 %collective-permute-done.2 = f32[257,256]{1,0:T(8,128)} collective-permute-done((f32[257,256]{1,0:T(8,128)}, f32[257,256]{1,0:T(8,128)}, u32[]{:S(2)}, u32[]{:S(2)}) %collective-permute-start.2) | collective-permute-done | bytes 263200 | tf_op jit(solution)/shard_map/ppermute | solution.py:63
  44.9 4.2 %conditional.6 = (f32[256,256]{1,0:T(8,128)S(1)}, f32[256]{0:T(256)S(1)}, f32[257,256]{1,0:T(8,128)}, s32[]{:T(128)}, f32[257,256]{1,0:T(8,128)}) conditional(s32[]{:T(128)} %convert_element_type.25, (f32[257,256]{1,0:T(8,128)}, f32[257,256]{1,0:T(8,128)}, f32[256,256]{1,0:T(8,128)S(1)}, f32[256]{0:T(256)S(1)}) %tuple.124, (f32[257,256]{1,0:T(8,128)}, ...), branch_computations={%region_10.11_spmd, %region_11.12_spmd} | conditional | flops 404357376 | bytes 4472908 | solution.py:96
  44.9 1.0 %slice.302 = f32[256,256]{1,0:T(8,128)S(1)} slice(f32[257,256]{1,0:T(8,128)} %get-tuple-element.469), slice={[0:256], [0:256]} | slice | bytes 524288 | tf_op jit(solution)/shard_map/cond/branch_1_fun/slice | solution.py:87
  45.9 1.6 %convolution_bitcast_fusion.2 = f32[257,512]{1,0:T(8,128)S(1)} fusion(f32[257,256]{1,0:T(8,128)} %get-tuple-element.377, f32[256,256]{1,0:T(8,128)S(1)} %get-tuple-element.376, f32[256,256]{1,0:T(8,128)S(1)} %slice.302), kind=kOutput, calls=%fused_computation.16 | convolution fusion | flops 404357120 | bytes 1313792 | tf_op jit(solution)/shard_map/cond/branch_1_fun/dot_general | solution.py:87
  47.6 0.7 slice.377
  48.3 0.7 copy.55
  49.1 0.7 slice_add_fusion.2
  49.8 1.3 %add.157 = f32[257,256]{1,0:T(8,128)} dynamic-update-slice(f32[257,256]{1,0:T(8,128)} %get-tuple-element.420, f32[1,256]{1,0:T(1,128)S(1)} %slice_add_fusion.2, s32[]{:T(128)} %get-tuple-element.421, s32[]{:T(128)} %constant.391.clone.1) | dynamic-update-slice | bytes 2052 | tf_op jit(solution)/shard_map/cond/branch_0_fun/add | solution.py:94
  51.1 1.8 %collective-permute-start.3 = (f32[257,256]{1,0:T(8,128)}, f32[257,256]{1,0:T(8,128)}, u32[]{:S(2)}, u32[]{:S(2)}) collective-permute-start(f32[257,256]{1,0:T(8,128)} %add.157), channel_id=1, source_target_pairs={{0,4},{16,20},{1,5},{17,21},{2,6},{18,22},{3,7},{19,23},{4,0},{20,... | collective-permute-start | bytes 789512 | tf_op jit(solution)/shard_map/ppermute | solution.py:63
  52.9 4.9 %collective-permute-done.3 = f32[257,256]{1,0:T(8,128)} collective-permute-done((f32[257,256]{1,0:T(8,128)}, f32[257,256]{1,0:T(8,128)}, u32[]{:S(2)}, u32[]{:S(2)}) %collective-permute-start.3) | collective-permute-done | bytes 263200 | tf_op jit(solution)/shard_map/ppermute | solution.py:63
  57.9 4.2 %conditional.7 = (f32[256,256]{1,0:T(8,128)S(1)}, f32[256]{0:T(256)S(1)}, f32[257,256]{1,0:T(8,128)}, s32[]{:T(128)}, f32[257,256]{1,0:T(8,128)}) conditional(s32[]{:T(128)} %convert_element_type.24, (f32[257,256]{1,0:T(8,128)}, f32[257,256]{1,0:T(8,128)}, f32[256,256]{1,0:T(8,128)S(1)}, f32[256]{0:T(256)S(1)}) %tuple.126, (f32[257,256]{1,0:T(8,128)}, ...), branch_computations={%region_12.13_spmd, %region_13.14_spmd} | conditional | flops 404357376 | bytes 4472908 | solution.py:96
  57.9 1.0 %slice.307 = f32[256,256]{1,0:T(8,128)S(1)} slice(f32[257,256]{1,0:T(8,128)} %get-tuple-element.479), slice={[0:256], [0:256]} | slice | bytes 524288 | tf_op jit(solution)/shard_map/cond/branch_1_fun/slice | solution.py:87
  58.9 1.6 %convolution_bitcast_fusion.3 = f32[257,512]{1,0:T(8,128)S(1)} fusion(f32[257,256]{1,0:T(8,128)} %get-tuple-element.385, f32[256,256]{1,0:T(8,128)S(1)} %get-tuple-element.384, f32[256,256]{1,0:T(8,128)S(1)} %slice.307), kind=kOutput, calls=%fused_computation.23 | convolution fusion | flops 404357120 | bytes 1313792 | tf_op jit(solution)/shard_map/cond/branch_1_fun/dot_general | solution.py:87
  60.5 0.7 slice.380
  61.3 0.7 copy.66
  62.1 0.7 slice_add_fusion.1
  62.8 1.3 %add.158 = f32[257,256]{1,0:T(8,128)} dynamic-update-slice(f32[257,256]{1,0:T(8,128)} %get-tuple-element.425, f32[1,256]{1,0:T(1,128)S(1)} %slice_add_fusion.1, s32[]{:T(128)} %get-tuple-element.426, s32[]{:T(128)} %constant.391.clone.1) | dynamic-update-slice | bytes 2052 | tf_op jit(solution)/shard_map/cond/branch_0_fun/add | solution.py:94
  64.1 0.7 slice.387
  64.8 2.8 %collective-permute-start.4 = (f32[256]{0:T(256)S(1)}, f32[256]{0:T(256)S(1)}, u32[]{:S(2)}, u32[]{:S(2)}) collective-permute-start(f32[256]{0:T(256)S(1)} %bitcast.113), channel_id=1, source_target_pairs={{0,8},{16,24},{1,9},{17,25},{2,10},{18,26},{3,11},{19,27},{4,12},{... | collective-permute-start | bytes 3080 | tf_op jit(solution)/shard_map/ppermute | solution.py:63
  67.6 0.6 compare_reduce_fusion
  68.2 1.0 %collective-permute-done.4 = f32[256]{0:T(256)S(1)} collective-permute-done((f32[256]{0:T(256)S(1)}, f32[256]{0:T(256)S(1)}, u32[]{:S(2)}, u32[]{:S(2)}) %collective-permute-start.4) | collective-permute-done | bytes 1056 | tf_op jit(solution)/shard_map/ppermute | solution.py:63
  69.4 1.1 %convolution_add_fusion.2 = f32[1,256]{1,0:T(1,128)S(1)} fusion(f32[256,1]{0,1:T(1,128)S(1)} %bitcast.104, f32[3,256,256]{2,1,0:T(8,128)} %copy-done.3, f32[3,256]{1,0:T(4,128)S(1)} %add.152), kind=kOutput, calls=%fused_computation.44 | convolution fusion | flops 786688 | bytes 265216 | tf_op jit(solution)/shard_map/nj,njk->nk/dot_general | solution.py:15
  70.5 1.2 %fusion.34 = f32[1,1,256]{2,1,0:T(1,128)S(1)} fusion(f32[3,256,256]{2,1,0:T(8,128)} %copy-done.3, f32[1,256]{1,0:T(1,128)S(1)} %convolution_add_fusion.2, f32[3,256]{1,0:T(4,128)S(1)} %add.152), kind=kOutput, calls=%fused_computation.43 | convolution fusion | flops 786688 | bytes 265216 | tf_op jit(solution)/shard_map/nj,njk->nk/dot_general | solution.py:15
  71.8 1.6 %fusion.37 = f32[3,1,256]{2,1,0:T(1,128)S(1)} fusion(f32[6,256,256]{2,1,0:T(8,128)} %fusion.24, f32[3,256,1]{1,0,2:T(4,128)S(1)} %get-tuple-element.436), kind=kOutput, calls=%fused_computation.48 | convolution fusion | flops 2359296 | bytes 792576 | tf_op jit(solution)/shard_map/nj,njk->nk/dot_general | solution.py:15
  73.5 2.3 %fusion.26 = f32[6,1,256]{2,1,0:T(1,128)S(1)} fusion(f32[6,256,1]{1,2,0:T(1,128)S(1)} %reshape.335, f32[12,256,256]{2,1,0:T(8,128)} %fusion.29), kind=kOutput, calls=%fused_computation.33 | convolution fusion | flops 4718592 | bytes 1585152 | tf_op jit(solution)/shard_map/nj,njk->nk/dot_general | solution.py:15
  75.8 0.7 fusion.31
  76.6 0.6 fusion.45
  77.9 0.3 fusion.48
  78.2 0.3 convolution_add_fusion
  79.2 2.2 %collective-permute-start.5 = (f32[129,128]{1,0:T(8,128)S(1)}, f32[129,128]{1,0:T(8,128)S(1)}, u32[]{:S(2)}, u32[]{:S(2)}) collective-permute-start(f32[129,128]{1,0:T(8,128)S(1)} %select_maximum_fusion), channel_id=1, source_target_pairs={{0,16},{16,0},{1,17},{17,1},{2,18},{18,2},{3,19},{19,3},{4,20},{20... | collective-permute-start | bytes 198152 | tf_op jit(solution)/shard_map/ppermute | solution.py:63
  81.3 2.3 %collective-permute-done.5 = f32[129,128]{1,0:T(8,128)S(1)} collective-permute-done((f32[129,128]{1,0:T(8,128)S(1)}, f32[129,128]{1,0:T(8,128)S(1)}, u32[]{:S(2)}, u32[]{:S(2)}) %collective-permute-start.5) | collective-permute-done | bytes 66080 | tf_op jit(solution)/shard_map/ppermute | solution.py:63
  83.7 1.2 %collective-permute-done.6 = f32[129,128]{1,0:T(8,128)S(1)} collective-permute-done((f32[129,128]{1,0:T(8,128)S(1)}, f32[129,128]{1,0:T(8,128)S(1)}, u32[]{:S(2)}, u32[]{:S(2)}) %collective-permute-start.6) | collective-permute-done | bytes 66080 | tf_op jit(solution)/shard_map/ppermute | solution.py:63
  85.1 4.3 %collective-permute-done.7 = f32[129,128]{1,0:T(8,128)S(1)} collective-permute-done((f32[129,128]{1,0:T(8,128)S(1)}, f32[129,128]{1,0:T(8,128)S(1)}, u32[]{:S(2)}, u32[]{:S(2)}) %collective-permute-start.7) | collective-permute-done | bytes 66080 | tf_op jit(solution)/shard_map/ppermute | solution.py:63
  89.4 4.3 %collective-permute-done.8 = f32[129,128]{1,0:T(8,128)S(1)} collective-permute-done((f32[129,128]{1,0:T(8,128)S(1)}, f32[129,128]{1,0:T(8,128)S(1)}, u32[]{:S(2)}, u32[]{:S(2)}) %collective-permute-start.8) | collective-permute-done | bytes 66080 | tf_op jit(solution)/shard_map/ppermute | solution.py:63
  93.8 3.3 %collective-permute-start.9 = (f32[129,128]{1,0:T(8,128)S(1)}, f32[129,128]{1,0:T(8,128)S(1)}, u32[]{:S(2)}, u32[]{:S(2)}) collective-permute-start(f32[129,128]{1,0:T(8,128)S(1)} %add.171), channel_id=1, source_target_pairs={{0,8},{16,24},{1,9},{17,25},{2,10},{18,26},{3,11},{19,27},{4,12},{... | collective-permute-start | bytes 198152 | tf_op jit(solution)/shard_map/ppermute | solution.py:63
  97.1 0.6 add.165
  97.7 1.7 %collective-permute-done.9 = f32[129,128]{1,0:T(8,128)S(1)} collective-permute-done((f32[129,128]{1,0:T(8,128)S(1)}, f32[129,128]{1,0:T(8,128)S(1)}, u32[]{:S(2)}, u32[]{:S(2)}) %collective-permute-start.9) | collective-permute-done | bytes 66080 | tf_op jit(solution)/shard_map/ppermute | solution.py:63
  99.4 0.6 slice.392
  100.0 0.5 slice.393
  (77 shorter events, 1.5 us)
Async XLA Ops:
  0.6 2.9 %copy-start = (bf16[1,24,256,256]{3,2,1,0:T(8,128)(2,1)S(1)}, bf16[1,24,256,256]{3,2,1,0:T(8,128)(2,1)}, u32[]{:S(2)}) copy-start(bf16[1,24,256,256]{3,2,1,0:T(8,128)(2,1)} %param.30) | copy-start | bytes 9437188
  6.2 4.8 %copy-start.1 = (f32[12,256,256]{2,1,0:T(8,128)S(1)}, f32[12,256,256]{2,1,0:T(8,128)}, u32[]{:S(2)}) copy-start(f32[12,256,256]{2,1,0:T(8,128)} %fusion.29) | copy-start | bytes 9437188
  11.4 2.4 %copy-start.2 = (f32[6,256,256]{2,1,0:T(8,128)S(1)}, f32[6,256,256]{2,1,0:T(8,128)}, u32[]{:S(2)}) copy-start(f32[6,256,256]{2,1,0:T(8,128)} %fusion.24) | copy-start | bytes 4718596
  13.8 2.0 %copy-start.3 = (f32[3,256,256]{2,1,0:T(8,128)}, f32[3,256,256]{2,1,0:T(8,128)S(1)}, u32[]{:S(2)}) copy-start(f32[3,256,256]{2,1,0:T(8,128)S(1)} %fusion.35) | copy-start | bytes 2359300
  14.9 3.8 %copy-start.7 = (f32[256,256]{1,0:T(8,128)}, f32[256,256]{1,0:T(8,128)S(1)}, u32[]{:S(2)}) copy-start(f32[256,256]{1,0:T(8,128)S(1)} %fusion.43) | copy-start | bytes 786436
  15.8 9.8 %collective-permute-start = (f32[257,256]{1,0:T(8,128)}, f32[257,256]{1,0:T(8,128)}, u32[]{:S(2)}, u32[]{:S(2)}) collective-permute-start(f32[257,256]{1,0:T(8,128)} %pad_maximum_fusion), channel_id=1, source_target_pairs={{0,16},{16,0},{1,17},{17,1},{2,18},{18,2},{3,19},{19,3},{4,20},{20... | collective-permute-start | bytes 789512 | tf_op jit(solution)/shard_map/ppermute | solution.py:63
  30.0 1.9 %collective-permute-start.1 = (f32[257,256]{1,0:T(8,128)}, f32[257,256]{1,0:T(8,128)}, u32[]{:S(2)}, u32[]{:S(2)}) collective-permute-start(f32[257,256]{1,0:T(8,128)} %add.155), channel_id=1, source_target_pairs={{0,1},{16,17},{1,0},{17,16},{2,3},{18,19},{3,2},{19,18},{4,5},{20,... | collective-permute-start | bytes 789512 | tf_op jit(solution)/shard_map/ppermute | solution.py:63
  31.9 3.5 %copy-start.4 = (f32[257,256]{1,0:T(8,128)S(1)}, f32[257,256]{1,0:T(8,128)}, u32[]{:S(2)}) copy-start(f32[257,256]{1,0:T(8,128)} %get-tuple-element.459) | copy-start | bytes 789508 | tf_op jit(solution)/shard_map/cond
  38.1 6.8 %collective-permute-start.2 = (f32[257,256]{1,0:T(8,128)}, f32[257,256]{1,0:T(8,128)}, u32[]{:S(2)}, u32[]{:S(2)}) collective-permute-start(f32[257,256]{1,0:T(8,128)} %add.156), channel_id=1, source_target_pairs={{0,2},{16,18},{1,3},{17,19},{2,0},{18,16},{3,1},{19,17},{4,6},{20,... | collective-permute-start | bytes 789512 | tf_op jit(solution)/shard_map/ppermute | solution.py:63
  44.9 8.0 %copy-start.9 = (f32[1,24,2,128]{3,2,1,0:T(2,128)S(1)}, f32[1,24,2,128]{3,2,1,0:T(2,128)}, u32[]{:S(2)}) copy-start(f32[1,24,2,128]{3,2,1,0:T(2,128)} %param.32) | copy-start | bytes 73732
  44.9 3.4 %copy-start.5 = (f32[257,256]{1,0:T(8,128)S(1)}, f32[257,256]{1,0:T(8,128)}, u32[]{:S(2)}) copy-start(f32[257,256]{1,0:T(8,128)} %get-tuple-element.469) | copy-start | bytes 789508 | tf_op jit(solution)/shard_map/cond
  51.1 6.8 %collective-permute-start.3 = (f32[257,256]{1,0:T(8,128)}, f32[257,256]{1,0:T(8,128)}, u32[]{:S(2)}, u32[]{:S(2)}) collective-permute-start(f32[257,256]{1,0:T(8,128)} %add.157), channel_id=1, source_target_pairs={{0,4},{16,20},{1,5},{17,21},{2,6},{18,22},{3,7},{19,23},{4,0},{20,... | collective-permute-start | bytes 789512 | tf_op jit(solution)/shard_map/ppermute | solution.py:63
  57.9 3.4 %copy-start.6 = (f32[257,256]{1,0:T(8,128)S(1)}, f32[257,256]{1,0:T(8,128)}, u32[]{:S(2)}) copy-start(f32[257,256]{1,0:T(8,128)} %get-tuple-element.479) | copy-start | bytes 789508 | tf_op jit(solution)/shard_map/cond
  64.8 4.5 %collective-permute-start.4 = (f32[256]{0:T(256)S(1)}, f32[256]{0:T(256)S(1)}, u32[]{:S(2)}, u32[]{:S(2)}) collective-permute-start(f32[256]{0:T(256)S(1)} %bitcast.113), channel_id=1, source_target_pairs={{0,8},{16,24},{1,9},{17,25},{2,10},{18,26},{3,11},{19,27},{4,12},{... | collective-permute-start | bytes 3080 | tf_op jit(solution)/shard_map/ppermute | solution.py:63
  73.4 3.2 %copy-start.8 = (f32[1,24,256]{2,1,0:T(8,128)S(1)}, f32[1,24,256]{2,1,0:T(8,128)}, u32[]{:S(2)}) copy-start(f32[1,24,256]{2,1,0:T(8,128)} %param.31) | copy-start | bytes 73732
  73.5 3.2 %copy-start.10 = (f32[1,24,256]{2,1,0:T(8,128)S(1)}, f32[1,24,256]{2,1,0:T(8,128)}, u32[]{:S(2)}) copy-start(f32[1,24,256]{2,1,0:T(8,128)} %param.33) | copy-start | bytes 73732
  79.2 4.5 %collective-permute-start.5 = (f32[129,128]{1,0:T(8,128)S(1)}, f32[129,128]{1,0:T(8,128)S(1)}, u32[]{:S(2)}, u32[]{:S(2)}) collective-permute-start(f32[129,128]{1,0:T(8,128)S(1)} %select_maximum_fusion), channel_id=1, source_target_pairs={{0,16},{16,0},{1,17},{17,1},{2,18},{18,2},{3,19},{19,3},{4,20},{20... | collective-permute-start | bytes 198152 | tf_op jit(solution)/shard_map/ppermute | solution.py:63
  83.6 1.3 %collective-permute-start.6 = (f32[129,128]{1,0:T(8,128)S(1)}, f32[129,128]{1,0:T(8,128)S(1)}, u32[]{:S(2)}, u32[]{:S(2)}) collective-permute-start(f32[129,128]{1,0:T(8,128)S(1)} %fusion.57), channel_id=1, source_target_pairs={{0,1},{16,17},{1,0},{17,16},{2,3},{18,19},{3,2},{19,18},{4,5},{20,... | collective-permute-start | bytes 198152 | tf_op jit(solution)/shard_map/ppermute | solution.py:63
  85.0 4.4 %collective-permute-start.7 = (f32[129,128]{1,0:T(8,128)S(1)}, f32[129,128]{1,0:T(8,128)S(1)}, u32[]{:S(2)}, u32[]{:S(2)}) collective-permute-start(f32[129,128]{1,0:T(8,128)S(1)} %add.169), channel_id=1, source_target_pairs={{0,2},{16,18},{1,3},{17,19},{2,0},{18,16},{3,1},{19,17},{4,6},{20,... | collective-permute-start | bytes 198152 | tf_op jit(solution)/shard_map/ppermute | solution.py:63
  89.4 4.4 %collective-permute-start.8 = (f32[129,128]{1,0:T(8,128)S(1)}, f32[129,128]{1,0:T(8,128)S(1)}, u32[]{:S(2)}, u32[]{:S(2)}) collective-permute-start(f32[129,128]{1,0:T(8,128)S(1)} %add.170), channel_id=1, source_target_pairs={{0,4},{16,20},{1,5},{17,21},{2,6},{18,22},{3,7},{19,23},{4,0},{20,... | collective-permute-start | bytes 198152 | tf_op jit(solution)/shard_map/ppermute | solution.py:63
  93.8 5.6 %collective-permute-start.9 = (f32[129,128]{1,0:T(8,128)S(1)}, f32[129,128]{1,0:T(8,128)S(1)}, u32[]{:S(2)}, u32[]{:S(2)}) collective-permute-start(f32[129,128]{1,0:T(8,128)S(1)} %add.171), channel_id=1, source_target_pairs={{0,8},{16,24},{1,9},{17,25},{2,10},{18,26},{3,11},{19,27},{4,12},{... | collective-permute-start | bytes 198152 | tf_op jit(solution)/shard_map/ppermute | solution.py:63

commit v6 on v4

--- a/solution.py
+++ b/solution.py
@@ -9,6 +9,10 @@
 
 def vecmat(v, q):
     return jnp.sum(v[:, :, None] * q.astype(jnp.float32), axis=1)
+
+
+def vecmat_mxu(v, q):
+    return jnp.einsum("nj,njk->nk", v, q.astype(jnp.float32), precision=EXACT)
 
 
 def matmat(later, earlier):
@@ -42,7 +46,7 @@
         n = q.shape[0]
         half = n // 2
         upper = m[:half]
-        left = vecmat(upper, q[1 : 2 * half : 2]) + v[1 : 2 * half : 2]
+        left = vecmat_mxu(upper, q[1 : 2 * half : 2]) + v[1 : 2 * half : 2]
         m_new = jnp.stack([left, upper], axis=1).reshape(2 * half, -1)
         if n % 2:
             m_new = jnp.concatenate([m_new, m[-1:]], axis=0)

time: 96.7 us -> 96.7 us (level)
  matrix products: 17 us -> 24.1 us
  other arithmetic: 25.2 us -> 18.1 us
    reduce_sum x10 -> x5, other arithmetic: 10.7 us -> 3.66 us  [vecmat(): return jnp.sum(v[:, :, None] * q.astype(jnp.float32), axis=1)]
    dot_general x0 -> x5, matrix products: none -> 6.9 us  [vecmat_mxu(): return jnp.einsum('nj,njk->nk', v, q.astype(jnp.float32), precision=EXACT)]
    unnamed x24 -> x26, local copies, waits for them, and re-layouts: 2.6 us -> 2.67 us
where the time goes in v6:
time: 96.7 us; the launch traced here: 95.9 us
  waiting for transfers between devices  31.6 us (33%)
  matrix products  24.1 us (25%)
  other arithmetic  18.1 us (19%)
  starting transfers between devices  15.2 us (16%)
  local copies, waits for them, and re-layouts  4.38 us (5%)
  between operations  2.48 us (3%)
    ppermute x10, waiting for transfers between devices, exchange(): lax.ppermute(x, AXES, [(place(j), place(j ^ mask)) for j in range(count)])  31.6 us
    ppermute x10, starting transfers between devices, exchange(): lax.ppermute(x, AXES, [(place(j), place(j ^ mask)) for j in range(count)])  15.2 us
    dot_general x4, matrix products, matmat(): jnp.einsum('nij,njk->nik', later.astype(jnp.float32), earlier.astype(jnp....  7.95 us
    dot_general x5, matrix products, vecmat_mxu(): return jnp.einsum('nj,njk->nk', v, q.astype(jnp.float32), precision=EXACT)  6.9 us
    dot_general x4, matrix products, body(): jnp.dot(later, jnp.concatenate([earlier_q, sq], axis=1), precision=EXACT)  6.4 us
    select_n x4, other arithmetic, body(): earlier_q = jnp.where(lower, packed[:width], got[:width])  3.93 us
    reduce_sum x5, other arithmetic, vecmat(): return jnp.sum(v[:, :, None] * q.astype(jnp.float32), axis=1)  3.66 us
    select_n x3, other arithmetic, body(): sq = jnp.where(lower, both[:width, width:], sq)  3.04 us
  transfers between devices with their start and end apart: 10, of which 10 were waited for; matrix products, arithmetic and copies ran while one was open for 5% of the time, Pallas kernels for 0%

profile of v6, /device:TPU:0, one launch (start us, length us, event | category | flops | bytes accessed | tf_op | source)
XLA Modules:
  0.0 95.9 jit_solution(9277941530638175100)
XLA Ops:
  0.6 2.6 %multiply_reduce_fusion = f32[24,256]{1,0:T(8,128)S(1)} fusion(f32[24,256]{1,0:T(8,128)} %bitcast.80, bf16[1,24,256,256]{3,2,1,0:T(8,128)(2,1)} %param.14), kind=kLoop, calls=%fused_computation | loop fusion | flops 4712448 | bytes 3194880 | tf_op jit(solution)/shard_map/reduce_sum | solution.py:11
  3.3 0.2 copy-done
  3.5 2.2 %fusion.5 = f32[12,256,256]{2,1,0:T(8,128)} fusion(bf16[24,256,256]{2,1,0:T(8,128)(2,1)S(1)} %bitcast.77), kind=kOutput, calls=%fused_computation.8 | convolution fusion | flops 402653184 | bytes 6291456 | tf_op jit(solution)/shard_map/nij,njk->nik/dot_general | solution.py:20
  5.7 0.5 multiply_reduce_fusion.1
  6.3 4.8 %fusion = f32[6,256,256]{2,1,0:T(8,128)} fusion(f32[12,256,256]{2,1,0:T(8,128)} %fusion.5), kind=kOutput, calls=%fused_computation.3 | convolution fusion | flops 1207959552 | bytes 4718592 | tf_op jit(solution)/shard_map/nij,njk->nik/dot_general | solution.py:21
  11.1 0.3 multiply_reduce_fusion.2
  11.4 2.4 %fusion.11 = f32[3,256,256]{2,1,0:T(8,128)S(1)} fusion(f32[6,256,256]{2,1,0:T(8,128)} %fusion), kind=kOutput, calls=%fused_computation.18 | convolution fusion | flops 603979776 | bytes 2359296 | tf_op jit(solution)/shard_map/nij,njk->nik/dot_general | solution.py:21
  13.8 0.2 multiply_reduce_fusion.3
  14.0 0.4 multiply_reduce_fusion.5
  14.4 0.4 fusion.41
  14.8 0.1 multiply_reduce_fusion.4
  15.0 0.7 pad_maximum_fusion
  15.7 3.0 %collective-permute-start = (f32[257,256]{1,0:T(8,128)}, f32[257,256]{1,0:T(8,128)}, u32[]{:S(2)}, u32[]{:S(2)}) collective-permute-start(f32[257,256]{1,0:T(8,128)} %pad_maximum_fusion), channel_id=1, source_target_pairs={{0,16},{16,0},{1,17},{17,1},{2,18},{18,2},{3,19},{19,3},{4,20},{20... | collective-permute-start | bytes 789512 | tf_op jit(solution)/shard_map/ppermute | solution.py:63
  18.7 6.8 %collective-permute-done = f32[257,256]{1,0:T(8,128)} collective-permute-done((f32[257,256]{1,0:T(8,128)}, f32[257,256]{1,0:T(8,128)}, u32[]{:S(2)}, u32[]{:S(2)}) %collective-permute-start) | collective-permute-done | bytes 263200 | tf_op jit(solution)/shard_map/ppermute | solution.py:63
  25.5 1.0 %slice_select_fusion.7 = f32[256,256]{1,0:T(8,128)S(1)} fusion(f32[256,256]{1,0:T(8,128)S(1)} %fusion.41, f32[257,256]{1,0:T(8,128)} %collective-permute-done, pred[]{:T(512)S(6)} %eq.30), kind=kLoop, calls=%fused_computation.53 | loop fusion | flops 65536 | bytes 786433 | tf_op jit(solution)/shard_map/jit(_where)/select_n | solution.py:87
  26.5 1.6 %fusion.16 = f32[257,512]{1,0:T(8,128)S(1)} fusion(f32[256,256]{1,0:T(8,128)S(1)} %fusion.40, f32[256,256]{1,0:T(8,128)S(1)} %slice_select_fusion.7, f32[257,256]{1,0:T(8,128)} %collective-permute-done, pred[]{:T(512)S(6)} %eq.30, f32[1,256]{1,0:T(1,128)S(1)} %fusion.61, f32[256,256]{1,0:T(8,128)S(1)} %fusion.41), kind=kOutput, calls=%fused_computation.23 | convolution fusion | flops 404488704 | bytes 1576961 | tf_op jit(solution)/shard_map/dot_general | solution.py:89
  28.1 0.8 copy-done.4
  28.9 0.7 fusion.57
  29.7 1.0 %slice_select_fusion.5 = f32[256,256]{1,0:T(8,128)S(1)} fusion(f32[257,512]{1,0:T(8,128)} %copy-done.4, pred[]{:T(512)S(6)} %eq.30), kind=kLoop, calls=%fused_computation.51 | loop fusion | flops 196608 | bytes 524289 | tf_op jit(solution)/shard_map/jit(_where)/select_n | solution.py:92
  30.7 0.7 collective-permute-done.1
  31.4 1.0 %slice_select_fusion.6 = f32[256,256]{1,0:T(8,128)S(1)} fusion(f32[257,256]{1,0:T(8,128)} %collective-permute-done.1, f32[257,256]{1,0:T(8,128)S(1)} %add.147, pred[]{:T(512)S(6)} %eq.29), kind=kLoop, calls=%fused_computation.52 | loop fusion | flops 65536 | bytes 786433 | tf_op jit(solution)/shard_map/jit(_where)/select_n | solution.py:87
  32.4 1.6 %fusion.20 = f32[257,512]{1,0:T(8,128)S(1)} fusion(f32[256,256]{1,0:T(8,128)S(1)} %slice_select_fusion.5, f32[256,256]{1,0:T(8,128)S(1)} %slice_select_fusion.6, f32[257,256]{1,0:T(8,128)} %collective-permute-done.1, f32[257,256]{1,0:T(8,128)S(1)} %add.147, pred[]{:T(512)S(6)} %eq.29), kind=kOutput, calls=%fused_computation.27 | convolution fusion | flops 404422912 | bytes 1576961 | tf_op jit(solution)/shard_map/dot_general | solution.py:89
  34.0 0.8 copy-done.7
  34.8 0.7 fusion.58
  35.5 1.8 %collective-permute-start.2 = (f32[257,256]{1,0:T(8,128)S(1)}, f32[257,256]{1,0:T(8,128)}, u32[]{:S(2)}, u32[]{:S(2)}) collective-permute-start(f32[257,256]{1,0:T(8,128)S(1)} %add.148), channel_id=1, source_target_pairs={{0,2},{16,18},{1,3},{17,19},{2,0},{18,16},{3,1},{19,17},{4,6},{20,... | collective-permute-start | bytes 789512 | tf_op jit(solution)/shard_map/ppermute | solution.py:63
  37.3 1.1 %slice_select_fusion.3 = f32[256,256]{1,0:T(8,128)S(1)} fusion(f32[257,512]{1,0:T(8,128)} %copy-done.7, pred[]{:T(512)S(6)} %eq.29, f32[257,512]{1,0:T(8,128)} %copy-done.4, pred[]{:T(512)S(6)} %eq.30), kind=kLoop, calls=%fused_computation.49 | loop fusion | flops 262144 | bytes 786434 | tf_op jit(solution)/shard_map/jit(_where)/select_n | solution.py:92
  38.4 4.9 %collective-permute-done.2 = f32[257,256]{1,0:T(8,128)} collective-permute-done((f32[257,256]{1,0:T(8,128)S(1)}, f32[257,256]{1,0:T(8,128)}, u32[]{:S(2)}, u32[]{:S(2)}) %collective-permute-start.2) | collective-permute-done | bytes 263200 | tf_op jit(solution)/shard_map/ppermute | solution.py:63
  43.3 1.0 %slice_select_fusion.4 = f32[256,256]{1,0:T(8,128)S(1)} fusion(f32[257,256]{1,0:T(8,128)} %collective-permute-done.2, f32[257,256]{1,0:T(8,128)S(1)} %add.148, pred[]{:T(512)S(6)} %eq.28), kind=kLoop, calls=%fused_computation.50 | loop fusion | flops 65536 | bytes 786433 | tf_op jit(solution)/shard_map/jit(_where)/select_n | solution.py:87
  44.2 1.6 %fusion.24 = f32[257,512]{1,0:T(8,128)S(1)} fusion(f32[256,256]{1,0:T(8,128)S(1)} %slice_select_fusion.3, f32[256,256]{1,0:T(8,128)S(1)} %slice_select_fusion.4, f32[257,256]{1,0:T(8,128)} %collective-permute-done.2, f32[257,256]{1,0:T(8,128)S(1)} %add.148, pred[]{:T(512)S(6)} %eq.28), kind=kOutput, calls=%fused_computation.31 | convolution fusion | flops 404422912 | bytes 1576961 | tf_op jit(solution)/shard_map/dot_general | solution.py:89
  45.9 0.8 copy-done.8
  46.7 0.7 fusion.59
  47.4 0.2 add.149
  47.6 1.9 %collective-permute-start.3 = (f32[257,256]{1,0:T(8,128)S(1)}, f32[257,256]{1,0:T(8,128)}, u32[]{:S(2)}, u32[]{:S(2)}) collective-permute-start(f32[257,256]{1,0:T(8,128)S(1)} %add.149), channel_id=1, source_target_pairs={{0,4},{16,20},{1,5},{17,21},{2,6},{18,22},{3,7},{19,23},{4,0},{20,... | collective-permute-start | bytes 789512 | tf_op jit(solution)/shard_map/ppermute | solution.py:63
  49.5 1.0 %slice_select_fusion.1 = f32[256,256]{1,0:T(8,128)S(1)} fusion(f32[256,256]{1,0:T(8,128)} %copy-done.6, f32[257,512]{1,0:T(8,128)} %copy-done.8, pred[]{:T(512)S(6)} %eq.28), kind=kLoop, calls=%fused_computation.47 | loop fusion | flops 65536 | bytes 786433 | tf_op jit(solution)/shard_map/jit(_where)/select_n | solution.py:92
  50.5 4.0 %collective-permute-done.3 = f32[257,256]{1,0:T(8,128)} collective-permute-done((f32[257,256]{1,0:T(8,128)S(1)}, f32[257,256]{1,0:T(8,128)}, u32[]{:S(2)}, u32[]{:S(2)}) %collective-permute-start.3) | collective-permute-done | bytes 263200 | tf_op jit(solution)/shard_map/ppermute | solution.py:63
  54.4 1.0 %slice_select_fusion.2 = f32[256,256]{1,0:T(8,128)S(1)} fusion(f32[257,256]{1,0:T(8,128)} %collective-permute-done.3, f32[257,256]{1,0:T(8,128)S(1)} %add.149, pred[]{:T(512)S(6)} %eq.27), kind=kLoop, calls=%fused_computation.48 | loop fusion | flops 65536 | bytes 786433 | tf_op jit(solution)/shard_map/jit(_where)/select_n | solution.py:87
  55.4 1.6 %fusion.28 = f32[257,512]{1,0:T(8,128)S(1)} fusion(f32[256,256]{1,0:T(8,128)S(1)} %slice_select_fusion.1, f32[256,256]{1,0:T(8,128)S(1)} %slice_select_fusion.2, f32[257,256]{1,0:T(8,128)} %collective-permute-done.3, f32[257,256]{1,0:T(8,128)S(1)} %add.149, pred[]{:T(512)S(6)} %eq.27), kind=kOutput, calls=%fused_computation.35 | convolution fusion | flops 404422912 | bytes 1576961 | tf_op jit(solution)/shard_map/dot_general | solution.py:89
  57.1 0.7 fusion.60
  57.9 2.7 %collective-permute-start.4 = (f32[256]{0:T(256)S(1)}, f32[256]{0:T(256)S(1)}, u32[]{:S(2)}, u32[]{:S(2)}) collective-permute-start(f32[256]{0:T(256)S(1)} %bitcast.90), channel_id=1, source_target_pairs={{0,8},{16,24},{1,9},{17,25},{2,10},{18,26},{3,11},{19,27},{4,12},{... | collective-permute-start | bytes 3080 | tf_op jit(solution)/shard_map/ppermute | solution.py:63
  60.6 0.6 compare_reduce_fusion
  61.2 1.1 %collective-permute-done.4 = f32[256]{0:T(256)S(1)} collective-permute-done((f32[256]{0:T(256)S(1)}, f32[256]{0:T(256)S(1)}, u32[]{:S(2)}, u32[]{:S(2)}) %collective-permute-start.4) | collective-permute-done | bytes 1056 | tf_op jit(solution)/shard_map/ppermute | solution.py:63
  62.3 1.1 %fusion.37 = f32[256]{0:T(256)S(1)} fusion(f32[256,256]{1,0:T(8,128)} %copy-done.5, f32[257,512]{1,0:T(8,128)} %copy-done.9, f32[256]{0:T(256)S(1)} %collective-permute-done.4, pred[]{:T(512)S(6)} %eq.27), kind=kLoop, calls=%fused_computation.46 | loop fusion | flops 196352 | bytes 526337 | tf_op jit(solution)/shard_map/reduce_sum | solution.py:97
  63.4 0.8 broadcast_select_fusion.8
  64.2 1.1 %convolution_add_fusion.2 = f32[1,256]{1,0:T(1,128)S(1)} fusion(f32[3,256,256]{2,1,0:T(8,128)} %copy-done.3, f32[1,256]{1,0:T(1,128)S(1)} %broadcast_select_fusion.8, f32[3,256]{1,0:T(4,128)S(1)} %add.144), kind=kOutput, calls=%fused_computation.16 | convolution fusion | flops 786688 | bytes 265216 | tf_op jit(solution)/shard_map/nj,njk->nk/dot_general | solution.py:15
  65.3 1.2 %fusion.10 = f32[1,1,256]{2,1,0:T(1,128)S(1)} fusion(f32[3,256,256]{2,1,0:T(8,128)} %copy-done.3, f32[1,256]{1,0:T(1,128)S(1)} %convolution_add_fusion.2, f32[3,256]{1,0:T(4,128)S(1)} %add.144), kind=kOutput, calls=%fused_computation.15 | convolution fusion | flops 786688 | bytes 265216 | tf_op jit(solution)/shard_map/nj,njk->nk/dot_general | solution.py:15
  66.5 1.6 %fusion.13 = f32[3,1,256]{2,1,0:T(1,128)S(1)} fusion(f32[6,256,256]{2,1,0:T(8,128)} %fusion, f32[3,256,1]{1,0,2:T(4,128)S(1)} %get-tuple-element.69), kind=kOutput, calls=%fused_computation.20 | convolution fusion | flops 2359296 | bytes 792576 | tf_op jit(solution)/shard_map/nj,njk->nk/dot_general | solution.py:15
  68.2 2.3 %fusion.2 = f32[6,1,256]{2,1,0:T(1,128)S(1)} fusion(f32[6,256,1]{1,2,0:T(1,128)S(1)} %reshape.238, f32[12,256,256]{2,1,0:T(8,128)} %fusion.5), kind=kOutput, calls=%fused_computation.5 | convolution fusion | flops 4718592 | bytes 1585152 | tf_op jit(solution)/shard_map/nj,njk->nk/dot_general | solution.py:15
  70.6 0.7 fusion.7
  71.4 0.6 fusion.47
  72.7 0.3 fusion.50
  73.0 0.3 convolution_add_fusion
  73.9 0.8 collective-permute-start.5
  74.7 3.6 %collective-permute-done.5 = f32[129,128]{1,0:T(8,128)S(1)} collective-permute-done((f32[129,128]{1,0:T(8,128)S(1)}, f32[129,128]{1,0:T(8,128)S(1)}, u32[]{:S(2)}, u32[]{:S(2)}) %collective-permute-start.5) | collective-permute-done | bytes 66080 | tf_op jit(solution)/shard_map/ppermute | solution.py:63
  78.3 0.1 collective-permute-start.6
  78.4 1.2 %collective-permute-done.6 = f32[129,128]{1,0:T(8,128)S(1)} collective-permute-done((f32[129,128]{1,0:T(8,128)S(1)}, f32[129,128]{1,0:T(8,128)S(1)}, u32[]{:S(2)}, u32[]{:S(2)}) %collective-permute-start.6) | collective-permute-done | bytes 66080 | tf_op jit(solution)/shard_map/ppermute | solution.py:63
  79.7 0.8 collective-permute-start.7
  80.4 3.6 %collective-permute-done.7 = f32[129,128]{1,0:T(8,128)S(1)} collective-permute-done((f32[129,128]{1,0:T(8,128)S(1)}, f32[129,128]{1,0:T(8,128)S(1)}, u32[]{:S(2)}, u32[]{:S(2)}) %collective-permute-start.7) | collective-permute-done | bytes 66080 | tf_op jit(solution)/shard_map/ppermute | solution.py:63
  84.0 0.9 collective-permute-start.8
  85.0 3.4 %collective-permute-done.8 = f32[129,128]{1,0:T(8,128)S(1)} collective-permute-done((f32[129,128]{1,0:T(8,128)S(1)}, f32[129,128]{1,0:T(8,128)S(1)}, u32[]{:S(2)}, u32[]{:S(2)}) %collective-permute-start.8) | collective-permute-done | bytes 66080 | tf_op jit(solution)/shard_map/ppermute | solution.py:63
  88.4 3.3 %collective-permute-start.9 = (f32[129,128]{1,0:T(8,128)S(1)}, f32[129,128]{1,0:T(8,128)S(1)}, u32[]{:S(2)}, u32[]{:S(2)}) collective-permute-start(f32[129,128]{1,0:T(8,128)S(1)} %add.165), channel_id=1, source_target_pairs={{0,8},{16,24},{1,9},{17,25},{2,10},{18,26},{3,11},{19,27},{4,12},{... | collective-permute-start | bytes 198152 | tf_op jit(solution)/shard_map/ppermute | solution.py:63
  91.7 0.6 add.159
  92.3 2.4 %collective-permute-done.9 = f32[129,128]{1,0:T(8,128)S(1)} collective-permute-done((f32[129,128]{1,0:T(8,128)S(1)}, f32[129,128]{1,0:T(8,128)S(1)}, u32[]{:S(2)}, u32[]{:S(2)}) %collective-permute-start.9) | collective-permute-done | bytes 66080 | tf_op jit(solution)/shard_map/ppermute | solution.py:63
  94.7 0.6 slice.337
  95.4 0.5 slice.338
  (64 shorter events, 0.8 us)
Async XLA Ops:
  0.6 2.9 %copy-start = (bf16[1,24,256,256]{3,2,1,0:T(8,128)(2,1)S(1)}, bf16[1,24,256,256]{3,2,1,0:T(8,128)(2,1)}, u32[]{:S(2)}) copy-start(bf16[1,24,256,256]{3,2,1,0:T(8,128)(2,1)} %param.14) | copy-start | bytes 9437188
  6.3 4.8 %copy-start.1 = (f32[12,256,256]{2,1,0:T(8,128)S(1)}, f32[12,256,256]{2,1,0:T(8,128)}, u32[]{:S(2)}) copy-start(f32[12,256,256]{2,1,0:T(8,128)} %fusion.5) | copy-start | bytes 9437188
  11.4 2.4 %copy-start.2 = (f32[6,256,256]{2,1,0:T(8,128)S(1)}, f32[6,256,256]{2,1,0:T(8,128)}, u32[]{:S(2)}) copy-start(f32[6,256,256]{2,1,0:T(8,128)} %fusion) | copy-start | bytes 4718596
  13.8 1.9 %copy-start.3 = (f32[3,256,256]{2,1,0:T(8,128)}, f32[3,256,256]{2,1,0:T(8,128)S(1)}, u32[]{:S(2)}) copy-start(f32[3,256,256]{2,1,0:T(8,128)S(1)} %fusion.11) | copy-start | bytes 2359300
  15.7 9.8 %collective-permute-start = (f32[257,256]{1,0:T(8,128)}, f32[257,256]{1,0:T(8,128)}, u32[]{:S(2)}, u32[]{:S(2)}) collective-permute-start(f32[257,256]{1,0:T(8,128)} %pad_maximum_fusion), channel_id=1, source_target_pairs={{0,16},{16,0},{1,17},{17,1},{2,18},{18,2},{3,19},{19,3},{4,20},{20... | collective-permute-start | bytes 789512 | tf_op jit(solution)/shard_map/ppermute | solution.py:63
  28.1 0.8 copy-start.4
  29.6 1.7 %collective-permute-start.1 = (f32[257,256]{1,0:T(8,128)S(1)}, f32[257,256]{1,0:T(8,128)}, u32[]{:S(2)}, u32[]{:S(2)}) collective-permute-start(f32[257,256]{1,0:T(8,128)S(1)} %add.147), channel_id=1, source_target_pairs={{0,1},{16,17},{1,0},{17,16},{2,3},{18,19},{3,2},{19,18},{4,5},{20,... | collective-permute-start | bytes 789512 | tf_op jit(solution)/shard_map/ppermute | solution.py:63
  34.0 0.8 copy-start.7
  35.5 7.7 %collective-permute-start.2 = (f32[257,256]{1,0:T(8,128)S(1)}, f32[257,256]{1,0:T(8,128)}, u32[]{:S(2)}, u32[]{:S(2)}) collective-permute-start(f32[257,256]{1,0:T(8,128)S(1)} %add.148), channel_id=1, source_target_pairs={{0,2},{16,18},{1,3},{17,19},{2,0},{18,16},{3,1},{19,17},{4,6},{20,... | collective-permute-start | bytes 789512 | tf_op jit(solution)/shard_map/ppermute | solution.py:63
  38.4 7.5 %copy-start.6 = (f32[256,256]{1,0:T(8,128)}, f32[256,256]{1,0:T(8,128)S(1)}, u32[]{:S(2)}) copy-start(f32[256,256]{1,0:T(8,128)S(1)} %slice_select_fusion.3) | copy-start | bytes 786436
  38.4 11.1 %copy-start.11 = (f32[1,24,2,128]{3,2,1,0:T(2,128)S(1)}, f32[1,24,2,128]{3,2,1,0:T(2,128)}, u32[]{:S(2)}) copy-start(f32[1,24,2,128]{3,2,1,0:T(2,128)} %param.16) | copy-start | bytes 73732
  45.8 0.8 copy-start.8
  47.6 6.9 %collective-permute-start.3 = (f32[257,256]{1,0:T(8,128)S(1)}, f32[257,256]{1,0:T(8,128)}, u32[]{:S(2)}, u32[]{:S(2)}) collective-permute-start(f32[257,256]{1,0:T(8,128)S(1)} %add.149), channel_id=1, source_target_pairs={{0,4},{16,20},{1,5},{17,21},{2,6},{18,22},{3,7},{19,23},{4,0},{20,... | collective-permute-start | bytes 789512 | tf_op jit(solution)/shard_map/ppermute | solution.py:63
  50.5 6.6 %copy-start.5 = (f32[256,256]{1,0:T(8,128)}, f32[256,256]{1,0:T(8,128)S(1)}, u32[]{:S(2)}) copy-start(f32[256,256]{1,0:T(8,128)S(1)} %slice_select_fusion.1) | copy-start | bytes 786436
  57.0 0.8 copy-start.9
  57.9 4.5 %collective-permute-start.4 = (f32[256]{0:T(256)S(1)}, f32[256]{0:T(256)S(1)}, u32[]{:S(2)}, u32[]{:S(2)}) collective-permute-start(f32[256]{0:T(256)S(1)} %bitcast.90), channel_id=1, source_target_pairs={{0,8},{16,24},{1,9},{17,25},{2,10},{18,26},{3,11},{19,27},{4,12},{... | collective-permute-start | bytes 3080 | tf_op jit(solution)/shard_map/ppermute | solution.py:63
  68.2 3.2 %copy-start.10 = (f32[1,24,256]{2,1,0:T(8,128)S(1)}, f32[1,24,256]{2,1,0:T(8,128)}, u32[]{:S(2)}) copy-start(f32[1,24,256]{2,1,0:T(8,128)} %param.15) | copy-start | bytes 73732
  68.2 3.2 %copy-start.12 = (f32[1,24,256]{2,1,0:T(8,128)S(1)}, f32[1,24,256]{2,1,0:T(8,128)}, u32[]{:S(2)}) copy-start(f32[1,24,256]{2,1,0:T(8,128)} %param.17) | copy-start | bytes 73732
  73.9 4.4 %collective-permute-start.5 = (f32[129,128]{1,0:T(8,128)S(1)}, f32[129,128]{1,0:T(8,128)S(1)}, u32[]{:S(2)}, u32[]{:S(2)}) collective-permute-start(f32[129,128]{1,0:T(8,128)S(1)} %select_maximum_fusion), channel_id=1, source_target_pairs={{0,16},{16,0},{1,17},{17,1},{2,18},{18,2},{3,19},{19,3},{4,20},{20... | collective-permute-start | bytes 198152 | tf_op jit(solution)/shard_map/ppermute | solution.py:63
  78.3 1.3 %collective-permute-start.6 = (f32[129,128]{1,0:T(8,128)S(1)}, f32[129,128]{1,0:T(8,128)S(1)}, u32[]{:S(2)}, u32[]{:S(2)}) collective-permute-start(f32[129,128]{1,0:T(8,128)S(1)} %fusion.68), channel_id=1, source_target_pairs={{0,1},{16,17},{1,0},{17,16},{2,3},{18,19},{3,2},{19,18},{4,5},{20,... | collective-permute-start | bytes 198152 | tf_op jit(solution)/shard_map/ppermute | solution.py:63
  79.7 4.4 %collective-permute-start.7 = (f32[129,128]{1,0:T(8,128)S(1)}, f32[129,128]{1,0:T(8,128)S(1)}, u32[]{:S(2)}, u32[]{:S(2)}) collective-permute-start(f32[129,128]{1,0:T(8,128)S(1)} %add.163), channel_id=1, source_target_pairs={{0,2},{16,18},{1,3},{17,19},{2,0},{18,16},{3,1},{19,17},{4,6},{20,... | collective-permute-start | bytes 198152 | tf_op jit(solution)/shard_map/ppermute | solution.py:63
  84.0 4.4 %collective-permute-start.8 = (f32[129,128]{1,0:T(8,128)S(1)}, f32[129,128]{1,0:T(8,128)S(1)}, u32[]{:S(2)}, u32[]{:S(2)}) collective-permute-start(f32[129,128]{1,0:T(8,128)S(1)} %add.164), channel_id=1, source_target_pairs={{0,4},{16,20},{1,5},{17,21},{2,6},{18,22},{3,7},{19,23},{4,0},{20,... | collective-permute-start | bytes 198152 | tf_op jit(solution)/shard_map/ppermute | solution.py:63
  88.4 6.3 %collective-permute-start.9 = (f32[129,128]{1,0:T(8,128)S(1)}, f32[129,128]{1,0:T(8,128)S(1)}, u32[]{:S(2)}, u32[]{:S(2)}) collective-permute-start(f32[129,128]{1,0:T(8,128)S(1)} %add.165), channel_id=1, source_target_pairs={{0,8},{16,24},{1,9},{17,25},{2,10},{18,26},{3,11},{19,27},{4,12},{... | collective-permute-start | bytes 198152 | tf_op jit(solution)/shard_map/ppermute | solution.py:63

commit v7 on v6

--- a/solution.py
+++ b/solution.py
@@ -1,6 +1,7 @@
 import jax
 import jax.numpy as jnp
 from jax import lax
+from jax.experimental import pallas as pl
 from jax.sharding import PartitionSpec as P
 
 EXACT = lax.Precision.HIGHEST
@@ -54,6 +55,33 @@
     return m
 
 
+def scan_round(d, width):
+    def kernel(own_ref, got_ref, sq_ref, sv_ref, own_out, sq_out, sv_out):
+        me = lax.axis_index("outer") * lax.axis_size("inner") + lax.axis_index("inner")
+        lower = (me // d) % 2 == 0
+        later = jnp.where(lower, got_ref[...], own_ref[...])
+        early_q = jnp.where(lower, own_ref[0:width, :], got_ref[0:width, :])
+        early_v = jnp.where(lower, own_ref[width:, :], got_ref[width:, :])
+        new_q = jnp.dot(later, early_q, precision=EXACT, preferred_element_type=jnp.float32)
+        new_s = jnp.dot(later, sq_ref[...], precision=EXACT, preferred_element_type=jnp.float32)
+        own_out[0:width, :] = new_q[0:width]
+        own_out[width:, :] = new_q[width:] + early_v
+        sq_out[...] = jnp.where(lower, new_s[0:width], sq_ref[...])
+        sv_out[...] = jnp.where(lower, new_s[width:] + sv_ref[...], sv_ref[...])
+
+    def run(own, got, sq, sv):
+        return pl.pallas_call(
+            kernel,
+            out_shape=(
+                jax.ShapeDtypeStruct(own.shape, jnp.float32),
+                jax.ShapeDtypeStruct(sq.shape, jnp.float32),
+                jax.ShapeDtypeStruct(sv.shape, jnp.float32),
+            ),
+        )(own, got, sq, sv)
+
+    return run
+
+
 def place(b):
     inner = lax.axis_size("inner")
     return (b % inner) * lax.axis_size("outer") + b // inner
@@ -78,23 +106,16 @@
     sq = jnp.eye(width, dtype=jnp.float32)
     sv = jnp.zeros((width,), jnp.float32)
 
-    packed = jnp.concatenate([tq, tv[None, :]], axis=0)
+    packed = jnp.concatenate([tq, tv[None, :], jnp.zeros((7, width), jnp.float32)], axis=0)
+    sv = jnp.zeros((8, width), jnp.float32)
     d = 1
     while 2 * d < count:
-        lower = (me // d) % 2 == 0
         got = exchange(packed, d, count)
-        later = jnp.where(lower, got, packed)
-        earlier_q = jnp.where(lower, packed[:width], got[:width])
-        earlier_v = jnp.where(lower, packed[width], got[width])
-        both = jnp.dot(later, jnp.concatenate([earlier_q, sq], axis=1), precision=EXACT)
-        offset = jnp.zeros((width + 1, width), jnp.float32).at[width].set(earlier_v)
-        packed = both[:, :width] + offset
-        sq = jnp.where(lower, both[:width, width:], sq)
-        sv = jnp.where(lower, both[width, width:] + sv, sv)
+        packed, sq, sv = scan_round(d, width)(packed, got, sq, sv)
         d *= 2
     lower = (me // d) % 2 == 0
     rv = exchange(packed[width], d, count)
-    incoming = jnp.where(lower, jnp.sum(rv[:, None] * sq, axis=0) + sv, sv)
+    incoming = jnp.where(lower, jnp.sum(rv[:, None] * sq, axis=0) + sv[0], sv[0])
 
     after = downsweep(levels, incoming[None, :])
     length_rates = grads + after

time: 96.7 us -> 94.8 us (0.980)
  Pallas kernels: 0 us -> 10.2 us
  other arithmetic: 18.1 us -> 8.3 us
  matrix products: 24.1 us -> 17.6 us
  starting transfers between devices: 15.2 us -> 17.5 us
  local copies, waits for them, and re-layouts: 4.38 us -> 5.82 us
  waiting for transfers between devices: 31.6 us -> 32.6 us
    pallas_call x0 -> x4, Pallas kernels: none -> 10.2 us  [run(): pl.pallas_call(kernel, out_shape=(jax.ShapeDtypeStruct(own.shape, jnp.flo...]
    select_n x8 -> x1, other arithmetic: 7.74 us -> 0.71 us  [body(): jnp.where(lower, jnp.sum(rv[:, None] * sq, axis=0) + sv[0], sv[0])]
    dot_general x4 -> x0, matrix products: 6.4 us -> none  [body(): jnp.dot(later, jnp.concatenate([earlier_q, sq], axis=1), precision=EXACT)]
    scatter x4 -> x0, other arithmetic: 2.83 us -> none  [body(): offset = jnp.zeros((width + 1, width), jnp.float32).at[width].set(earlier_v)]
    ppermute x10, starting transfers between devices: 15.2 us -> 17.5 us  [exchange(): lax.ppermute(x, AXES, [(place(j), place(j ^ mask)) for j in range(count)])]
    ppermute x10, waiting for transfers between devices: 31.6 us -> 32.6 us  [exchange(): lax.ppermute(x, AXES, [(place(j), place(j ^ mask)) for j in range(count)])]
    unnamed x26 -> x24, local copies, waits for them, and re-layouts: 2.67 us -> 3.03 us
  transfers between devices with their start and end apart: 10 -> 10, of which waited for: 10 -> 10; matrix products, arithmetic and copies ran while one was open for 5% -> 2% of each run, Pallas kernels for 0% -> 0%
where the time goes in v7:
time: 94.8 us; the launch traced here: 94.3 us
  waiting for transfers between devices  32.6 us (34%)
  matrix products  17.6 us (19%)
  starting transfers between devices  17.5 us (18%)
  Pallas kernels  10.2 us (11%)
  other arithmetic  8.3 us (9%)
  local copies, waits for them, and re-layouts  5.82 us (6%)
  between operations  2.28 us (2%)
    ppermute x10, waiting for transfers between devices, exchange(): lax.ppermute(x, AXES, [(place(j), place(j ^ mask)) for j in range(count)])  32.6 us
    ppermute x10, starting transfers between devices, exchange(): lax.ppermute(x, AXES, [(place(j), place(j ^ mask)) for j in range(count)])  17.5 us
    pallas_call x4, Pallas kernels, run(): pl.pallas_call(kernel, out_shape=(jax.ShapeDtypeStruct(own.shape, jnp.flo...  10.2 us
    dot_general x4, matrix products, matmat(): jnp.einsum('nij,njk->nik', later.astype(jnp.float32), earlier.astype(jnp....  7.95 us
    dot_general x5, matrix products, vecmat_mxu(): return jnp.einsum('nj,njk->nk', v, q.astype(jnp.float32), precision=EXACT)  6.89 us
    reduce_sum x5, other arithmetic, vecmat(): return jnp.sum(v[:, :, None] * q.astype(jnp.float32), axis=1)  3.66 us
    unnamed x24, local copies, waits for them, and re-layouts  3.03 us
    dot_general x1, matrix products, matmat(): jnp.einsum('nij,njk->nik', later, earlier, preferred_element_type=jnp.flo...  2.23 us
  transfers between devices with their start and end apart: 10, of which 10 were waited for; matrix products, arithmetic and copies ran while one was open for 2% of the time, Pallas kernels for 0%

profile of v7, /device:TPU:0, one launch (start us, length us, event | category | flops | bytes accessed | tf_op | source)
XLA Modules:
  0.0 94.3 jit_solution(4776888925714331505)
XLA Ops:
  0.6 0.0 copy-start
  0.6 2.6 %multiply_reduce_fusion = f32[24,256]{1,0:T(8,128)S(1)} fusion(f32[24,256]{1,0:T(8,128)} %bitcast.80, bf16[1,24,256,256]{3,2,1,0:T(8,128)(2,1)} %param.6), kind=kLoop, calls=%fused_computation | loop fusion | flops 4712448 | bytes 3194880 | tf_op jit(solution)/shard_map/reduce_sum | solution.py:12
  3.3 0.2 copy-done
  3.5 2.2 %fusion.5 = f32[12,256,256]{2,1,0:T(8,128)} fusion(bf16[24,256,256]{2,1,0:T(8,128)(2,1)S(1)} %bitcast.77), kind=kOutput, calls=%fused_computation.8 | convolution fusion | flops 402653184 | bytes 6291456 | tf_op jit(solution)/shard_map/nij,njk->nik/dot_general | solution.py:21
  5.7 0.5 multiply_reduce_fusion.1
  6.3 4.8 %fusion = f32[6,256,256]{2,1,0:T(8,128)} fusion(f32[12,256,256]{2,1,0:T(8,128)} %fusion.5), kind=kOutput, calls=%fused_computation.3 | convolution fusion | flops 1207959552 | bytes 4718592 | tf_op jit(solution)/shard_map/nij,njk->nik/dot_general | solution.py:22
  11.1 0.0 copy-done.1
  11.1 0.3 multiply_reduce_fusion.2
  11.4 2.4 %fusion.11 = f32[3,256,256]{2,1,0:T(8,128)S(1)} fusion(f32[6,256,256]{2,1,0:T(8,128)} %fusion), kind=kOutput, calls=%fused_computation.18 | convolution fusion | flops 603979776 | bytes 2359296 | tf_op jit(solution)/shard_map/nij,njk->nik/dot_general | solution.py:22
  13.8 0.2 multiply_reduce_fusion.3
  14.0 0.4 multiply_reduce_fusion.6
  14.4 0.1 multiply_reduce_fusion.5
  14.5 0.4 fusion.19
  15.0 0.1 pad.20.clone
  15.0 0.1 maximum_maximum_fusion.own_ref
  15.2 3.0 %collective-permute-start = (f32[264,256]{1,0:T(8,128)S(1)}, f32[264,256]{1,0:T(8,128)S(1)}, u32[]{:S(2)}, u32[]{:S(2)}) collective-permute-start(f32[264,256]{1,0:T(8,128)S(1)} %maximum_maximum_fusion.own_ref), channel_id=1, source_target_pairs={{0,16},{16,0},{1,17},{17,1},{2,18},{18,2},{3,19},{19,3},{4,20},{20... | collective-permute-start | bytes 811016 | tf_op jit(solution)/shard_map/ppermute | solution.py:91
  18.2 0.7 fusion.18.sq_ref
  18.9 5.8 %collective-permute-done.got_ref = f32[264,256]{1,0:T(8,128)S(1)} collective-permute-done((f32[264,256]{1,0:T(8,128)S(1)}, f32[264,256]{1,0:T(8,128)S(1)}, u32[]{:S(2)}, u32[]{:S(2)}) %collective-permute-start) | collective-permute-done | bytes 270368 | tf_op jit(solution)/shard_map/ppermute | solution.py:91
  24.7 0.7 copy-done.8
  25.4 0.6 broadcast_in_dim.5.sv_ref
  26.0 2.5 %shard_map.67 = (f32[264,256]{1,0:T(8,128)}, f32[256,256]{1,0:T(8,128)}, f32[8,256]{1,0:T(8,128)}) custom-call(f32[264,256]{1,0:T(8,128)} %copy-done.4, f32[264,256]{1,0:T(8,128)} %copy-done.8, f32[256,256]{1,0:T(8,128)} %fusion.18.sq_ref, f32[8,256]{1,0:T(8,128)} %broadcast_in_dim.5.sv_ref), custom_call_target="tpu_custom_call" | custom-call | tf_op jit(solution)/shard_map/pallas_call | solution.py:73
  28.5 0.0 collective-permute-start.1
  28.5 1.8 %collective-permute-done.1.got_ref = f32[264,256]{1,0:T(8,128)S(1)} collective-permute-done((f32[264,256]{1,0:T(8,128)}, f32[264,256]{1,0:T(8,128)S(1)}, u32[]{:S(2)}, u32[]{:S(2)}) %collective-permute-start.1) | collective-permute-done | bytes 270368 | tf_op jit(solution)/shard_map/ppermute | solution.py:91
  30.3 0.7 copy-done.6
  31.0 2.5 %shard_map.68 = (f32[264,256]{1,0:T(8,128)}, f32[256,256]{1,0:T(8,128)}, f32[8,256]{1,0:T(8,128)}) custom-call(f32[264,256]{1,0:T(8,128)} %get-tuple-element.27.own_ref, f32[264,256]{1,0:T(8,128)} %copy-done.6, f32[256,256]{1,0:T(8,128)} %get-tuple-element.28.sq_ref, f32[8,256]{1,0:T(8,128)} %get-tuple-element.29.sv_ref), custom_call_target="tpu_custom_call" | custom-call | tf_op jit(solution)/shard_map/pallas_call | solution.py:73
  33.5 1.7 %collective-permute-start.2 = (f32[264,256]{1,0:T(8,128)}, f32[264,256]{1,0:T(8,128)S(1)}, u32[]{:S(2)}, u32[]{:S(2)}) collective-permute-start(f32[264,256]{1,0:T(8,128)} %get-tuple-element.30.own_ref), channel_id=1, source_target_pairs={{0,2},{16,18},{1,3},{17,19},{2,0},{18,16},{3,1},{19,17},{4,6},{20,... | collective-permute-start | bytes 811016 | tf_op jit(solution)/shard_map/ppermute | solution.py:91
  35.2 7.0 %collective-permute-done.2.got_ref = f32[264,256]{1,0:T(8,128)S(1)} collective-permute-done((f32[264,256]{1,0:T(8,128)}, f32[264,256]{1,0:T(8,128)S(1)}, u32[]{:S(2)}, u32[]{:S(2)}) %collective-permute-start.2) | collective-permute-done | bytes 270368 | tf_op jit(solution)/shard_map/ppermute | solution.py:91
  42.3 0.7 copy-done.7
  42.9 2.5 %shard_map.69 = (f32[264,256]{1,0:T(8,128)}, f32[256,256]{1,0:T(8,128)}, f32[8,256]{1,0:T(8,128)}) custom-call(f32[264,256]{1,0:T(8,128)} %get-tuple-element.30.own_ref, f32[264,256]{1,0:T(8,128)} %copy-done.7, f32[256,256]{1,0:T(8,128)} %get-tuple-element.31.sq_ref, f32[8,256]{1,0:T(8,128)} %get-tuple-element.32.sv_ref), custom_call_target="tpu_custom_call" | custom-call | tf_op jit(solution)/shard_map/pallas_call | solution.py:73
  45.5 1.8 %collective-permute-start.3 = (f32[264,256]{1,0:T(8,128)}, f32[264,256]{1,0:T(8,128)S(1)}, u32[]{:S(2)}, u32[]{:S(2)}) collective-permute-start(f32[264,256]{1,0:T(8,128)} %get-tuple-element.33.own_ref), channel_id=1, source_target_pairs={{0,4},{16,20},{1,5},{17,21},{2,6},{18,22},{3,7},{19,23},{4,0},{20,... | collective-permute-start | bytes 811016 | tf_op jit(solution)/shard_map/ppermute | solution.py:91
  47.3 6.1 %collective-permute-done.3.got_ref = f32[264,256]{1,0:T(8,128)S(1)} collective-permute-done((f32[264,256]{1,0:T(8,128)}, f32[264,256]{1,0:T(8,128)S(1)}, u32[]{:S(2)}, u32[]{:S(2)}) %collective-permute-start.3) | collective-permute-done | bytes 270368 | tf_op jit(solution)/shard_map/ppermute | solution.py:91
  53.4 0.7 copy-done.5
  54.2 2.5 %shard_map.70 = (f32[264,256]{1,0:T(8,128)}, f32[256,256]{1,0:T(8,128)}, f32[8,256]{1,0:T(8,128)}) custom-call(f32[264,256]{1,0:T(8,128)} %get-tuple-element.33.own_ref, f32[264,256]{1,0:T(8,128)} %copy-done.5, f32[256,256]{1,0:T(8,128)} %get-tuple-element.34.sq_ref, f32[8,256]{1,0:T(8,128)} %get-tuple-element.35.sv_ref), custom_call_target="tpu_custom_call" | custom-call | tf_op jit(solution)/shard_map/pallas_call | solution.py:73
  56.7 0.7 slice.133
  57.4 2.8 %collective-permute-start.4 = (f32[256]{0:T(256)S(1)}, f32[256]{0:T(256)S(1)}, u32[]{:S(2)}, u32[]{:S(2)}) collective-permute-start(f32[256]{0:T(256)S(1)} %bitcast.90), channel_id=1, source_target_pairs={{0,8},{16,24},{1,9},{17,25},{2,10},{18,26},{3,11},{19,27},{4,12},{... | collective-permute-start | bytes 3080 | tf_op jit(solution)/shard_map/ppermute | solution.py:91
  60.1 0.6 compare_reduce_fusion
  60.8 1.1 %collective-permute-done.4 = f32[256]{0:T(256)S(1)} collective-permute-done((f32[256]{0:T(256)S(1)}, f32[256]{0:T(256)S(1)}, u32[]{:S(2)}, u32[]{:S(2)}) %collective-permute-start.4) | collective-permute-done | bytes 1056 | tf_op jit(solution)/shard_map/ppermute | solution.py:91
  61.8 1.1 %multiply_reduce_fusion.4 = f32[256]{0:T(256)S(1)} fusion(f32[256,256]{1,0:T(8,128)} %get-tuple-element.37, f32[256]{0:T(256)S(1)} %collective-permute-done.4), kind=kLoop, calls=%fused_computation.28 | loop fusion | flops 130816 | bytes 264192 | tf_op jit(solution)/shard_map/reduce_sum | solution.py:118
  62.9 0.7 broadcast_select_fusion
  63.6 1.1 %convolution_add_fusion.2 = f32[1,256]{1,0:T(1,128)S(1)} fusion(f32[3,256,256]{2,1,0:T(8,128)} %copy-done.3, f32[1,256]{1,0:T(1,128)S(1)} %broadcast_select_fusion, f32[3,256]{1,0:T(4,128)S(1)} %add.78), kind=kOutput, calls=%fused_computation.16 | convolution fusion | flops 786688 | bytes 265216 | tf_op jit(solution)/shard_map/nj,njk->nk/dot_general | solution.py:16
  64.8 1.2 %fusion.10 = f32[1,1,256]{2,1,0:T(1,128)S(1)} fusion(f32[3,256,256]{2,1,0:T(8,128)} %copy-done.3, f32[1,256]{1,0:T(1,128)S(1)} %convolution_add_fusion.2, f32[3,256]{1,0:T(4,128)S(1)} %add.78), kind=kOutput, calls=%fused_computation.15 | convolution fusion | flops 786688 | bytes 265216 | tf_op jit(solution)/shard_map/nj,njk->nk/dot_general | solution.py:16
  66.0 1.6 %fusion.13 = f32[3,1,256]{2,1,0:T(1,128)S(1)} fusion(f32[6,256,256]{2,1,0:T(8,128)} %fusion, f32[3,256,1]{1,0,2:T(4,128)S(1)} %get-tuple-element.45), kind=kOutput, calls=%fused_computation.20 | convolution fusion | flops 2359296 | bytes 792576 | tf_op jit(solution)/shard_map/nj,njk->nk/dot_general | solution.py:16
  67.7 0.0 copy-start.9
  67.7 0.0 copy-start.11
  67.7 2.3 %fusion.2 = f32[6,1,256]{2,1,0:T(1,128)S(1)} fusion(f32[6,256,1]{1,2,0:T(1,128)S(1)} %reshape.131, f32[12,256,256]{2,1,0:T(8,128)} %fusion.5), kind=kOutput, calls=%fused_computation.5 | convolution fusion | flops 4718592 | bytes 1585152 | tf_op jit(solution)/shard_map/nj,njk->nk/dot_general | solution.py:16
  70.1 0.7 fusion.7
  70.9 0.0 copy-done.9
  70.9 0.0 copy-done.11
  70.9 0.6 fusion.21
  72.1 0.3 fusion.24
  72.4 0.3 convolution_add_fusion
  73.4 1.8 %collective-permute-start.5 = (f32[129,128]{1,0:T(8,128)S(1)}, f32[129,128]{1,0:T(8,128)S(1)}, u32[]{:S(2)}, u32[]{:S(2)}) collective-permute-start(f32[129,128]{1,0:T(8,128)S(1)} %select_maximum_fusion), channel_id=1, source_target_pairs={{0,16},{16,0},{1,17},{17,1},{2,18},{18,2},{3,19},{19,3},{4,20},{20... | collective-permute-start | bytes 198152 | tf_op jit(solution)/shard_map/ppermute | solution.py:91
  75.1 2.6 %collective-permute-done.5 = f32[129,128]{1,0:T(8,128)S(1)} collective-permute-done((f32[129,128]{1,0:T(8,128)S(1)}, f32[129,128]{1,0:T(8,128)S(1)}, u32[]{:S(2)}, u32[]{:S(2)}) %collective-permute-start.5) | collective-permute-done | bytes 66080 | tf_op jit(solution)/shard_map/ppermute | solution.py:91
  77.8 0.1 collective-permute-start.6
  77.9 1.2 %collective-permute-done.6 = f32[129,128]{1,0:T(8,128)S(1)} collective-permute-done((f32[129,128]{1,0:T(8,128)S(1)}, f32[129,128]{1,0:T(8,128)S(1)}, u32[]{:S(2)}, u32[]{:S(2)}) %collective-permute-start.6) | collective-permute-done | bytes 66080 | tf_op jit(solution)/shard_map/ppermute | solution.py:91
  79.1 1.7 %collective-permute-start.7 = (f32[129,128]{1,0:T(8,128)S(1)}, f32[129,128]{1,0:T(8,128)S(1)}, u32[]{:S(2)}, u32[]{:S(2)}) collective-permute-start(f32[129,128]{1,0:T(8,128)S(1)} %add.91), channel_id=1, source_target_pairs={{0,2},{16,18},{1,3},{17,19},{2,0},{18,16},{3,1},{19,17},{4,6},{20,... | collective-permute-start | bytes 198152 | tf_op jit(solution)/shard_map/ppermute | solution.py:91
  80.8 2.7 %collective-permute-done.7 = f32[129,128]{1,0:T(8,128)S(1)} collective-permute-done((f32[129,128]{1,0:T(8,128)S(1)}, f32[129,128]{1,0:T(8,128)S(1)}, u32[]{:S(2)}, u32[]{:S(2)}) %collective-permute-start.7) | collective-permute-done | bytes 66080 | tf_op jit(solution)/shard_map/ppermute | solution.py:91
  83.5 1.8 %collective-permute-start.8 = (f32[129,128]{1,0:T(8,128)S(1)}, f32[129,128]{1,0:T(8,128)S(1)}, u32[]{:S(2)}, u32[]{:S(2)}) collective-permute-start(f32[129,128]{1,0:T(8,128)S(1)} %add.92), channel_id=1, source_target_pairs={{0,4},{16,20},{1,5},{17,21},{2,6},{18,22},{3,7},{19,23},{4,0},{20,... | collective-permute-start | bytes 198152 | tf_op jit(solution)/shard_map/ppermute | solution.py:91
  85.3 2.6 %collective-permute-done.8 = f32[129,128]{1,0:T(8,128)S(1)} collective-permute-done((f32[129,128]{1,0:T(8,128)S(1)}, f32[129,128]{1,0:T(8,128)S(1)}, u32[]{:S(2)}, u32[]{:S(2)}) %collective-permute-start.8) | collective-permute-done | bytes 66080 | tf_op jit(solution)/shard_map/ppermute | solution.py:91
  87.9 2.8 %collective-permute-start.9 = (f32[129,128]{1,0:T(8,128)S(1)}, f32[129,128]{1,0:T(8,128)S(1)}, u32[]{:S(2)}, u32[]{:S(2)}) collective-permute-start(f32[129,128]{1,0:T(8,128)S(1)} %add.93), channel_id=1, source_target_pairs={{0,8},{16,24},{1,9},{17,25},{2,10},{18,26},{3,11},{19,27},{4,12},{... | collective-permute-start | bytes 198152 | tf_op jit(solution)/shard_map/ppermute | solution.py:91
  90.7 0.6 add.87
  91.4 1.8 %collective-permute-done.9 = f32[129,128]{1,0:T(8,128)S(1)} collective-permute-done((f32[129,128]{1,0:T(8,128)S(1)}, f32[129,128]{1,0:T(8,128)S(1)}, u32[]{:S(2)}, u32[]{:S(2)}) %collective-permute-start.9) | collective-permute-done | bytes 66080 | tf_op jit(solution)/shard_map/ppermute | solution.py:91
  93.2 0.6 slice.151
  93.8 0.5 slice.152
  (49 shorter events, 0.5 us)
Async XLA Ops:
  0.6 2.9 %copy-start = (bf16[1,24,256,256]{3,2,1,0:T(8,128)(2,1)S(1)}, bf16[1,24,256,256]{3,2,1,0:T(8,128)(2,1)}, u32[]{:S(2)}) copy-start(bf16[1,24,256,256]{3,2,1,0:T(8,128)(2,1)} %param.6) | copy-start | bytes 9437188
  6.3 4.8 %copy-start.1 = (f32[12,256,256]{2,1,0:T(8,128)S(1)}, f32[12,256,256]{2,1,0:T(8,128)}, u32[]{:S(2)}) copy-start(f32[12,256,256]{2,1,0:T(8,128)} %fusion.5) | copy-start | bytes 9437188
  11.4 2.4 %copy-start.2 = (f32[6,256,256]{2,1,0:T(8,128)S(1)}, f32[6,256,256]{2,1,0:T(8,128)}, u32[]{:S(2)}) copy-start(f32[6,256,256]{2,1,0:T(8,128)} %fusion) | copy-start | bytes 4718596
  13.8 1.3 %copy-start.3 = (f32[3,256,256]{2,1,0:T(8,128)}, f32[3,256,256]{2,1,0:T(8,128)S(1)}, u32[]{:S(2)}) copy-start(f32[3,256,256]{2,1,0:T(8,128)S(1)} %fusion.11) | copy-start | bytes 2359300
  15.0 32.2 %copy-start.10 = (f32[1,24,2,128]{3,2,1,0:T(2,128)S(1)}, f32[1,24,2,128]{3,2,1,0:T(2,128)}, u32[]{:S(2)}) copy-start(f32[1,24,2,128]{3,2,1,0:T(2,128)} %param.8) | copy-start | bytes 73732
  15.2 10.8 %copy-start.4 = (f32[264,256]{1,0:T(8,128)}, f32[264,256]{1,0:T(8,128)S(1)}, u32[]{:S(2)}) copy-start(f32[264,256]{1,0:T(8,128)S(1)} %maximum_maximum_fusion.own_ref) | copy-start | bytes 811012
  15.2 9.5 %collective-permute-start = (f32[264,256]{1,0:T(8,128)S(1)}, f32[264,256]{1,0:T(8,128)S(1)}, u32[]{:S(2)}, u32[]{:S(2)}) collective-permute-start(f32[264,256]{1,0:T(8,128)S(1)} %maximum_maximum_fusion.own_ref), channel_id=1, source_target_pairs={{0,16},{16,0},{1,17},{17,1},{2,18},{18,2},{3,19},{19,3},{4,20},{20... | collective-permute-start | bytes 811016 | tf_op jit(solution)/shard_map/ppermute | solution.py:91
  24.7 0.7 copy-start.8
  28.5 1.8 %collective-permute-start.1 = (f32[264,256]{1,0:T(8,128)}, f32[264,256]{1,0:T(8,128)S(1)}, u32[]{:S(2)}, u32[]{:S(2)}) collective-permute-start(f32[264,256]{1,0:T(8,128)} %get-tuple-element.27.own_ref), channel_id=1, source_target_pairs={{0,1},{16,17},{1,0},{17,16},{2,3},{18,19},{3,2},{19,18},{4,5},{20,... | collective-permute-start | bytes 811016 | tf_op jit(solution)/shard_map/ppermute | solution.py:91
  30.3 0.7 copy-start.6
  33.5 8.7 %collective-permute-start.2 = (f32[264,256]{1,0:T(8,128)}, f32[264,256]{1,0:T(8,128)S(1)}, u32[]{:S(2)}, u32[]{:S(2)}) collective-permute-start(f32[264,256]{1,0:T(8,128)} %get-tuple-element.30.own_ref), channel_id=1, source_target_pairs={{0,2},{16,18},{1,3},{17,19},{2,0},{18,16},{3,1},{19,17},{4,6},{20,... | collective-permute-start | bytes 811016 | tf_op jit(solution)/shard_map/ppermute | solution.py:91
  42.3 0.7 copy-start.7
  45.5 8.0 %collective-permute-start.3 = (f32[264,256]{1,0:T(8,128)}, f32[264,256]{1,0:T(8,128)S(1)}, u32[]{:S(2)}, u32[]{:S(2)}) collective-permute-start(f32[264,256]{1,0:T(8,128)} %get-tuple-element.33.own_ref), channel_id=1, source_target_pairs={{0,4},{16,20},{1,5},{17,21},{2,6},{18,22},{3,7},{19,23},{4,0},{20,... | collective-permute-start | bytes 811016 | tf_op jit(solution)/shard_map/ppermute | solution.py:91
  53.4 0.7 copy-start.5
  57.4 4.5 %collective-permute-start.4 = (f32[256]{0:T(256)S(1)}, f32[256]{0:T(256)S(1)}, u32[]{:S(2)}, u32[]{:S(2)}) collective-permute-start(f32[256]{0:T(256)S(1)} %bitcast.90), channel_id=1, source_target_pairs={{0,8},{16,24},{1,9},{17,25},{2,10},{18,26},{3,11},{19,27},{4,12},{... | collective-permute-start | bytes 3080 | tf_op jit(solution)/shard_map/ppermute | solution.py:91
  67.7 3.2 %copy-start.9 = (f32[1,24,256]{2,1,0:T(8,128)S(1)}, f32[1,24,256]{2,1,0:T(8,128)}, u32[]{:S(2)}) copy-start(f32[1,24,256]{2,1,0:T(8,128)} %param.7) | copy-start | bytes 73732
  67.7 3.2 %copy-start.11 = (f32[1,24,256]{2,1,0:T(8,128)S(1)}, f32[1,24,256]{2,1,0:T(8,128)}, u32[]{:S(2)}) copy-start(f32[1,24,256]{2,1,0:T(8,128)} %param.9) | copy-start | bytes 73732
  73.4 4.4 %collective-permute-start.5 = (f32[129,128]{1,0:T(8,128)S(1)}, f32[129,128]{1,0:T(8,128)S(1)}, u32[]{:S(2)}, u32[]{:S(2)}) collective-permute-start(f32[129,128]{1,0:T(8,128)S(1)} %select_maximum_fusion), channel_id=1, source_target_pairs={{0,16},{16,0},{1,17},{17,1},{2,18},{18,2},{3,19},{19,3},{4,20},{20... | collective-permute-start | bytes 198152 | tf_op jit(solution)/shard_map/ppermute | solution.py:91
  77.8 1.3 %collective-permute-start.6 = (f32[129,128]{1,0:T(8,128)S(1)}, f32[129,128]{1,0:T(8,128)S(1)}, u32[]{:S(2)}, u32[]{:S(2)}) collective-permute-start(f32[129,128]{1,0:T(8,128)S(1)} %fusion.34), channel_id=1, source_target_pairs={{0,1},{16,17},{1,0},{17,16},{2,3},{18,19},{3,2},{19,18},{4,5},{20,... | collective-permute-start | bytes 198152 | tf_op jit(solution)/shard_map/ppermute | solution.py:91
  79.1 4.4 %collective-permute-start.7 = (f32[129,128]{1,0:T(8,128)S(1)}, f32[129,128]{1,0:T(8,128)S(1)}, u32[]{:S(2)}, u32[]{:S(2)}) collective-permute-start(f32[129,128]{1,0:T(8,128)S(1)} %add.91), channel_id=1, source_target_pairs={{0,2},{16,18},{1,3},{17,19},{2,0},{18,16},{3,1},{19,17},{4,6},{20,... | collective-permute-start | bytes 198152 | tf_op jit(solution)/shard_map/ppermute | solution.py:91
  83.5 4.4 %collective-permute-start.8 = (f32[129,128]{1,0:T(8,128)S(1)}, f32[129,128]{1,0:T(8,128)S(1)}, u32[]{:S(2)}, u32[]{:S(2)}) collective-permute-start(f32[129,128]{1,0:T(8,128)S(1)} %add.92), channel_id=1, source_target_pairs={{0,4},{16,20},{1,5},{17,21},{2,6},{18,22},{3,7},{19,23},{4,0},{20,... | collective-permute-start | bytes 198152 | tf_op jit(solution)/shard_map/ppermute | solution.py:91
  87.9 5.3 %collective-permute-start.9 = (f32[129,128]{1,0:T(8,128)S(1)}, f32[129,128]{1,0:T(8,128)S(1)}, u32[]{:S(2)}, u32[]{:S(2)}) collective-permute-start(f32[129,128]{1,0:T(8,128)S(1)} %add.93), channel_id=1, source_target_pairs={{0,8},{16,24},{1,9},{17,25},{2,10},{18,26},{3,11},{19,27},{4,12},{... | collective-permute-start | bytes 198152 | tf_op jit(solution)/shard_map/ppermute | solution.py:91

commit v8 on v7

--- a/solution.py
+++ b/solution.py
@@ -82,6 +82,53 @@
     return run
 
 
+def column(row):
+    return jnp.broadcast_to(row, (8, row.shape[1])).T[:, 0:1]
+
+
+def row_times(row, q):
+    return jnp.sum(column(row) * q.astype(jnp.float32), axis=0, keepdims=True)
+
+
+def finish(d, sizes, width):
+    depth = len(sizes) - 1
+
+    def kernel(*refs):
+        rv_ref, sq_ref, sv_ref, grads_ref = refs[:4]
+        tree = refs[4 : 4 + 2 * depth]
+        out_ref = refs[4 + 2 * depth]
+        me = lax.axis_index("outer") * lax.axis_size("inner") + lax.axis_index("inner")
+        lower = (me // d) % 2 == 0
+        sv = sv_ref[0:1, :]
+        entering = jnp.where(lower, row_times(rv_ref[0:1, :], sq_ref[...]) + sv, sv)
+        rows = [entering]
+        for level in reversed(range(depth)):
+            q_ref, v_ref = tree[2 * level], tree[2 * level + 1]
+            n = sizes[level]
+            new = []
+            for j in range(n // 2):
+                upper = rows[j]
+                new.append(row_times(upper, q_ref[j]) + v_ref[j : j + 1, :])
+                new.append(upper)
+            if n % 2:
+                new.append(rows[-1])
+            rows = new
+        for t, row in enumerate(rows):
+            out_ref[t : t + 1, :] = grads_ref[t : t + 1, :] + row
+
+    def run(rv, sq, sv, grads, levels):
+        args = [rv, sq, sv, grads]
+        for level in range(depth):
+            q, v = levels[level]
+            half = sizes[level] // 2
+            args += [q[1 : 2 * half : 2], v[1 : 2 * half : 2]]
+        return pl.pallas_call(
+            kernel, out_shape=jax.ShapeDtypeStruct(grads.shape, jnp.float32)
+        )(*args)
+
+    return run
+
+
 def place(b):
     inner = lax.axis_size("inner")
     return (b % inner) * lax.axis_size("outer") + b // inner
@@ -113,12 +160,9 @@
         got = exchange(packed, d, count)
         packed, sq, sv = scan_round(d, width)(packed, got, sq, sv)
         d *= 2
-    lower = (me // d) % 2 == 0
-    rv = exchange(packed[width], d, count)
-    incoming = jnp.where(lower, jnp.sum(rv[:, None] * sq, axis=0) + sv[0], sv[0])
-
-    after = downsweep(levels, incoming[None, :])
-    length_rates = grads + after
+    rv = exchange(packed[width:], d, count)
+    sizes = [level[0].shape[0] for level in levels]
+    length_rates = finish(d, sizes, width)(rv, sq, sv, grads, levels)
     argument_values = station_loadings[0]
     local_kernel = jnp.dot(
         length_rates[:, :stations].T, argument_values[:, 0, :], precision=EXACT

time: 94.8 us -> 96.5 us (1.018)
  matrix products: 17.6 us -> 12.1 us
  Pallas kernels: 10.2 us -> 15 us
  local copies, waits for them, and re-layouts: 5.82 us -> 7.61 us
  other arithmetic: 8.3 us -> 9.41 us
    dot_general x5 -> x0, matrix products: 6.89 us -> none  [vecmat_mxu(): return jnp.einsum('nj,njk->nk', v, q.astype(jnp.float32), precision=EXACT)]
    pallas_call x0 -> x1, Pallas kernels: none -> 4.71 us  [run(): pl.pallas_call(kernel, out_shape=jax.ShapeDtypeStruct(grads.shape, jnp.fl...]
    slice x0 -> x3, other arithmetic: none -> 3.44 us  [the longest x2 2.62 us: upsweep(): qa, qb = (q[0:2 * half:2], q[1:2 * half:2])]
    slice x2 -> x3, local copies, waits for them, and re-layouts: 0.72 us -> 1.98 us  [the longest x1 1.26 us: upsweep(): qa, qb = (q[0:2 * half:2], q[1:2 * half:2])]
    reduce_sum x1 -> x0, other arithmetic: 1.06 us -> none  [body(): jnp.sum(rv[:, None] * sq, axis=0) + sv[0]]
    unnamed x24 -> x32, local copies, waits for them, and re-layouts: 3.03 us -> 3.7 us
    reduce_sum x5 -> x2, other arithmetic: 3.66 us -> 3.08 us  [vecmat(): return jnp.sum(v[:, :, None] * q.astype(jnp.float32), axis=1)]
  transfers between devices with their start and end apart: 10 -> 10, of which waited for: 10 -> 9; matrix products, arithmetic and copies ran while one was open for 2% -> 3% of each run, Pallas kernels for 0% -> 0%
where the time goes in v8:
time: 96.5 us; the launch traced here: 96.1 us
  waiting for transfers between devices  32.8 us (34%)
  starting transfers between devices  16.9 us (18%)
  Pallas kernels  15 us (16%)
  matrix products  12.1 us (13%)
  other arithmetic  9.41 us (10%)
  local copies, waits for them, and re-layouts  7.61 us (8%)
  between operations  2.16 us (2%)
    ppermute x10, waiting for transfers between devices, exchange(): lax.ppermute(x, AXES, [(place(j), place(j ^ mask)) for j in range(count)])  32.8 us
    ppermute x10, starting transfers between devices, exchange(): lax.ppermute(x, AXES, [(place(j), place(j ^ mask)) for j in range(count)])  16.9 us
    pallas_call x4, Pallas kernels, run(): pl.pallas_call(kernel, out_shape=(jax.ShapeDtypeStruct(own.shape, jnp.flo...  10.3 us
    dot_general x4, matrix products, matmat(): jnp.einsum('nij,njk->nik', later.astype(jnp.float32), earlier.astype(jnp....  7.94 us
    pallas_call x1, Pallas kernels, run(): pl.pallas_call(kernel, out_shape=jax.ShapeDtypeStruct(grads.shape, jnp.fl...  4.71 us
    unnamed x32, local copies, waits for them, and re-layouts  3.7 us
    reduce_sum x2, other arithmetic, vecmat(): return jnp.sum(v[:, :, None] * q.astype(jnp.float32), axis=1)  3.08 us
    slice x2, other arithmetic, upsweep(): qa, qb = (q[0:2 * half:2], q[1:2 * half:2])  2.62 us
  transfers between devices with their start and end apart: 10, of which 9 were waited for; matrix products, arithmetic and copies ran while one was open for 3% of the time, Pallas kernels for 0%

profile of v8, /device:TPU:0, one launch (start us, length us, event | category | flops | bytes accessed | tf_op | source)
XLA Modules:
  0.0 96.1 jit_solution(8149236377350820896)
XLA Ops:
  0.6 0.0 copy-start
  0.6 2.6 %multiply_reduce_fusion = f32[24,256]{1,0:T(8,128)S(1)} fusion(f32[24,256]{1,0:T(8,128)} %bitcast.37, bf16[1,24,256,256]{3,2,1,0:T(8,128)(2,1)} %param.6), kind=kLoop, calls=%fused_computation | loop fusion | flops 4712448 | bytes 3194880 | tf_op jit(solution)/shard_map/reduce_sum | solution.py:12
  3.3 0.0 copy-start.8
  3.3 0.2 copy-done
  3.5 2.2 %fusion.2 = f32[12,256,256]{2,1,0:T(8,128)} fusion(bf16[24,256,256]{2,1,0:T(8,128)(2,1)S(1)} %bitcast.33), kind=kOutput, calls=%fused_computation.5 | convolution fusion | flops 402653184 | bytes 6291456 | tf_op jit(solution)/shard_map/nij,njk->nik/dot_general | solution.py:21
  5.7 0.0 copy-done.8
  5.7 0.5 multiply_reduce_fusion.1
  6.3 4.8 %fusion = f32[6,256,256]{2,1,0:T(8,128)} fusion(f32[12,256,256]{2,1,0:T(8,128)} %fusion.2), kind=kOutput, calls=%fused_computation.3 | convolution fusion | flops 1207959552 | bytes 4718592 | tf_op jit(solution)/shard_map/nij,njk->nik/dot_general | solution.py:22
  11.1 0.0 copy-done.9
  11.1 0.0 copy-done.1
  11.1 1.6 %fusion.24 = (f32[6,256,256]{2,1,0:T(8,128)}, f32[6,256]{1,0:T(8,128)S(1)}) fusion(f32[12,256,256]{2,1,0:T(8,128)S(1)} %copy-done.1, f32[6,256]{1,0:T(8,128)S(1)} %slice.118.refs_7_), kind=kLoop, calls=%fused_computation.38 | loop fusion | flops 784896 | bytes 4730880 | tf_op jit(solution)/shard_map/slice | solution.py:32
  12.7 2.4 %fusion.4 = f32[3,256,256]{2,1,0:T(8,128)S(1)} fusion(f32[6,256,256]{2,1,0:T(8,128)} %fusion), kind=kOutput, calls=%fused_computation.9 | convolution fusion | flops 603979776 | bytes 2359296 | tf_op jit(solution)/shard_map/nij,njk->nik/dot_general | solution.py:22
  15.1 0.0 copy-done.2
  15.1 1.1 %fusion.25 = (f32[3,256,256]{2,1,0:T(8,128)}, f32[3,256]{1,0:T(4,128)S(1)}) fusion(f32[6,256,256]{2,1,0:T(8,128)S(1)} %copy-done.2, f32[3,256]{1,0:T(4,128)S(1)} %slice.120.refs_9_), kind=kLoop, calls=%fused_computation.39 | loop fusion | flops 392448 | bytes 2365440 | tf_op jit(solution)/shard_map/slice | solution.py:32
  16.1 0.0 copy-done.10
  16.2 0.0 copy-start.14
  16.2 0.8 fusion.26
  17.0 0.4 multiply_reduce_fusion.5
  17.4 0.4 fusion.9
  17.8 0.1 pad.10.clone
  17.9 0.1 maximum_maximum_fusion.own_ref
  18.0 0.0 copy-done.13
  18.0 0.0 copy-done.14
  18.0 3.0 %collective-permute-start = (f32[264,256]{1,0:T(8,128)S(1)}, f32[264,256]{1,0:T(8,128)S(1)}, u32[]{:S(2)}, u32[]{:S(2)}) collective-permute-start(f32[264,256]{1,0:T(8,128)S(1)} %maximum_maximum_fusion.own_ref), channel_id=1, source_target_pairs={{0,16},{16,0},{1,17},{17,1},{2,18},{18,2},{3,19},{19,3},{4,20},{20... | collective-permute-start | bytes 811016 | tf_op jit(solution)/shard_map/ppermute | solution.py:138
  21.0 0.7 fusion.11.sq_ref
  21.8 5.8 %collective-permute-done.got_ref = f32[264,256]{1,0:T(8,128)S(1)} collective-permute-done((f32[264,256]{1,0:T(8,128)S(1)}, f32[264,256]{1,0:T(8,128)S(1)}, u32[]{:S(2)}, u32[]{:S(2)}) %collective-permute-start) | collective-permute-done | bytes 270368 | tf_op jit(solution)/shard_map/ppermute | solution.py:138
  27.5 0.7 copy-done.7
  28.2 0.6 broadcast_in_dim.7.sv_ref
  28.8 2.6 %shard_map.67 = (f32[264,256]{1,0:T(8,128)}, f32[256,256]{1,0:T(8,128)}, f32[8,256]{1,0:T(8,128)}) custom-call(f32[264,256]{1,0:T(8,128)} %copy-done.3, f32[264,256]{1,0:T(8,128)} %copy-done.7, f32[256,256]{1,0:T(8,128)} %fusion.11.sq_ref, f32[8,256]{1,0:T(8,128)} %broadcast_in_dim.7.sv_ref), custom_call_target="tpu_custom_call" | custom-call | tf_op jit(solution)/shard_map/pallas_call | solution.py:73
  31.5 0.0 collective-permute-start.1
  31.5 1.8 %collective-permute-done.1.got_ref = f32[264,256]{1,0:T(8,128)S(1)} collective-permute-done((f32[264,256]{1,0:T(8,128)}, f32[264,256]{1,0:T(8,128)S(1)}, u32[]{:S(2)}, u32[]{:S(2)}) %collective-permute-start.1) | collective-permute-done | bytes 270368 | tf_op jit(solution)/shard_map/ppermute | solution.py:138
  33.2 0.7 copy-done.4
  33.9 2.5 %shard_map.68 = (f32[264,256]{1,0:T(8,128)}, f32[256,256]{1,0:T(8,128)}, f32[8,256]{1,0:T(8,128)}) custom-call(f32[264,256]{1,0:T(8,128)} %get-tuple-element.27.own_ref, f32[264,256]{1,0:T(8,128)} %copy-done.4, f32[256,256]{1,0:T(8,128)} %get-tuple-element.28.sq_ref, f32[8,256]{1,0:T(8,128)} %get-tuple-element.29.sv_ref), custom_call_target="tpu_custom_call" | custom-call | tf_op jit(solution)/shard_map/pallas_call | solution.py:73
  36.5 1.7 %collective-permute-start.2 = (f32[264,256]{1,0:T(8,128)}, f32[264,256]{1,0:T(8,128)S(1)}, u32[]{:S(2)}, u32[]{:S(2)}) collective-permute-start(f32[264,256]{1,0:T(8,128)} %get-tuple-element.30.own_ref), channel_id=1, source_target_pairs={{0,2},{16,18},{1,3},{17,19},{2,0},{18,16},{3,1},{19,17},{4,6},{20,... | collective-permute-start | bytes 811016 | tf_op jit(solution)/shard_map/ppermute | solution.py:138
  38.2 7.0 %collective-permute-done.2.got_ref = f32[264,256]{1,0:T(8,128)S(1)} collective-permute-done((f32[264,256]{1,0:T(8,128)}, f32[264,256]{1,0:T(8,128)S(1)}, u32[]{:S(2)}, u32[]{:S(2)}) %collective-permute-start.2) | collective-permute-done | bytes 270368 | tf_op jit(solution)/shard_map/ppermute | solution.py:138
  45.2 0.7 copy-done.5
  45.9 2.6 %shard_map.69 = (f32[264,256]{1,0:T(8,128)}, f32[256,256]{1,0:T(8,128)}, f32[8,256]{1,0:T(8,128)}) custom-call(f32[264,256]{1,0:T(8,128)} %get-tuple-element.30.own_ref, f32[264,256]{1,0:T(8,128)} %copy-done.5, f32[256,256]{1,0:T(8,128)} %get-tuple-element.31.sq_ref, f32[8,256]{1,0:T(8,128)} %get-tuple-element.32.sv_ref), custom_call_target="tpu_custom_call" | custom-call | tf_op jit(solution)/shard_map/pallas_call | solution.py:73
  48.5 1.8 %collective-permute-start.3 = (f32[264,256]{1,0:T(8,128)}, f32[264,256]{1,0:T(8,128)S(1)}, u32[]{:S(2)}, u32[]{:S(2)}) collective-permute-start(f32[264,256]{1,0:T(8,128)} %get-tuple-element.33.own_ref), channel_id=1, source_target_pairs={{0,4},{16,20},{1,5},{17,21},{2,6},{18,22},{3,7},{19,23},{4,0},{20,... | collective-permute-start | bytes 811016 | tf_op jit(solution)/shard_map/ppermute | solution.py:138
  50.3 6.2 %collective-permute-done.3.got_ref = f32[264,256]{1,0:T(8,128)S(1)} collective-permute-done((f32[264,256]{1,0:T(8,128)}, f32[264,256]{1,0:T(8,128)S(1)}, u32[]{:S(2)}, u32[]{:S(2)}) %collective-permute-start.3) | collective-permute-done | bytes 270368 | tf_op jit(solution)/shard_map/ppermute | solution.py:138
  56.5 0.7 copy-done.6
  57.2 2.6 %shard_map.70 = (f32[264,256]{1,0:T(8,128)}, f32[256,256]{1,0:T(8,128)}, f32[8,256]{1,0:T(8,128)}) custom-call(f32[264,256]{1,0:T(8,128)} %get-tuple-element.33.own_ref, f32[264,256]{1,0:T(8,128)} %copy-done.6, f32[256,256]{1,0:T(8,128)} %get-tuple-element.34.sq_ref, f32[8,256]{1,0:T(8,128)} %get-tuple-element.35.sv_ref), custom_call_target="tpu_custom_call" | custom-call | tf_op jit(solution)/shard_map/pallas_call | solution.py:73
  59.7 0.7 slice.125
  60.4 2.8 %collective-permute-start.4 = (f32[8,256]{1,0:T(8,128)S(1)}, f32[8,256]{1,0:T(8,128)S(1)}, u32[]{:S(2)}, u32[]{:S(2)}) collective-permute-start(f32[8,256]{1,0:T(8,128)S(1)} %slice.125), channel_id=1, source_target_pairs={{0,8},{16,24},{1,9},{17,25},{2,10},{18,26},{3,11},{19,27},{4,12},{... | collective-permute-start | bytes 24584 | tf_op jit(solution)/shard_map/ppermute | solution.py:138
  63.2 1.3 %slice.107.refs_4_ = bf16[12,256,256]{2,1,0:T(8,128)(2,1)} slice(bf16[24,256,256]{2,1,0:T(8,128)(2,1)S(1)} %bitcast.35), slice={[1:24:2], [0:256:1], [0:256:1]} | slice | bytes 3145728 | tf_op jit(solution)/shard_map/slice | solution.py:32
  64.5 0.6 compare_reduce_fusion
  65.1 0.0 collective-permute-done.4.refs_0_
  65.1 0.6 copy-done.15
  65.7 4.7 %shard_map.71 = f32[24,256]{1,0:T(8,128)} custom-call(f32[8,256]{1,0:T(8,128)} %copy-done.15, f32[256,256]{1,0:T(8,128)} %get-tuple-element.37.refs_1_, f32[8,256]{1,0:T(8,128)} %get-tuple-element.38.refs_2_, f32[24,256]{1,0:T(8,128)} %bitcast.38, bf16[12,256,256]{2,1,0:T(8,128)(2,1)} %slice.107.refs_4_, f32[12,256]{1,0:T(8,128)} %copy-done.8, ...), custom_call_target="tpu_custom_call" | custom-call | tf_op jit(solution)/shard_map/pallas_call | solution.py:125
  70.4 1.0 %fusion.14 = f32[128,128]{1,0:T(8,128)S(1)} fusion(f32[24,128]{1,0:T(8,128)S(1)} %bitcast.40, f32[24,256]{1,0:T(8,128)} %shard_map.71), kind=kOutput, calls=%fused_computation.26 | convolution fusion | flops 4718592 | bytes 90112 | tf_op jit(solution)/shard_map/dot_general | solution.py:170
  71.4 0.0 copy-done.12
  71.5 1.4 %fusion.13 = f32[]{:T(128)} fusion(f32[24,256]{1,0:T(8,128)} %shard_map.71, f32[1,24,256]{2,1,0:T(8,128)S(1)} %copy-done.12), kind=kLoop, calls=%fused_computation.25 | loop fusion | flops 12287 | bytes 49156 | tf_op jit(solution)/shard_map/reduce_sum | solution.py:173
  73.5 1.0 %convolution_add_fusion = f32[128,128]{1,0:T(8,128)S(1)} fusion(f32[128,128]{1,0:T(8,128)S(1)} %fusion.14, f32[24,128]{1,0:T(8,128)S(1)} %bitcast.39, f32[24,256]{1,0:T(8,128)} %shard_map.71), kind=kOutput, calls=%fused_computation.7 | convolution fusion | flops 4734976 | bytes 155648 | tf_op jit(solution)/shard_map/dot_general | solution.py:167
  75.1 1.6 %collective-permute-start.5 = (f32[129,128]{1,0:T(8,128)S(1)}, f32[129,128]{1,0:T(8,128)S(1)}, u32[]{:S(2)}, u32[]{:S(2)}) collective-permute-start(f32[129,128]{1,0:T(8,128)S(1)} %select_maximum_fusion), channel_id=1, source_target_pairs={{0,16},{16,0},{1,17},{17,1},{2,18},{18,2},{3,19},{19,3},{4,20},{20... | collective-permute-start | bytes 198152 | tf_op jit(solution)/shard_map/ppermute | solution.py:138
  76.7 2.8 %collective-permute-done.5 = f32[129,128]{1,0:T(8,128)S(1)} collective-permute-done((f32[129,128]{1,0:T(8,128)S(1)}, f32[129,128]{1,0:T(8,128)S(1)}, u32[]{:S(2)}, u32[]{:S(2)}) %collective-permute-start.5) | collective-permute-done | bytes 66080 | tf_op jit(solution)/shard_map/ppermute | solution.py:138
  79.5 0.1 collective-permute-start.6
  79.6 1.2 %collective-permute-done.6 = f32[129,128]{1,0:T(8,128)S(1)} collective-permute-done((f32[129,128]{1,0:T(8,128)S(1)}, f32[129,128]{1,0:T(8,128)S(1)}, u32[]{:S(2)}, u32[]{:S(2)}) %collective-permute-start.6) | collective-permute-done | bytes 66080 | tf_op jit(solution)/shard_map/ppermute | solution.py:138
  80.9 1.6 %collective-permute-start.7 = (f32[129,128]{1,0:T(8,128)S(1)}, f32[129,128]{1,0:T(8,128)S(1)}, u32[]{:S(2)}, u32[]{:S(2)}) collective-permute-start(f32[129,128]{1,0:T(8,128)S(1)} %add.44), channel_id=1, source_target_pairs={{0,2},{16,18},{1,3},{17,19},{2,0},{18,16},{3,1},{19,17},{4,6},{20,... | collective-permute-start | bytes 198152 | tf_op jit(solution)/shard_map/ppermute | solution.py:138
  82.4 2.8 %collective-permute-done.7 = f32[129,128]{1,0:T(8,128)S(1)} collective-permute-done((f32[129,128]{1,0:T(8,128)S(1)}, f32[129,128]{1,0:T(8,128)S(1)}, u32[]{:S(2)}, u32[]{:S(2)}) %collective-permute-start.7) | collective-permute-done | bytes 66080 | tf_op jit(solution)/shard_map/ppermute | solution.py:138
  85.2 1.7 %collective-permute-start.8 = (f32[129,128]{1,0:T(8,128)S(1)}, f32[129,128]{1,0:T(8,128)S(1)}, u32[]{:S(2)}, u32[]{:S(2)}) collective-permute-start(f32[129,128]{1,0:T(8,128)S(1)} %add.45), channel_id=1, source_target_pairs={{0,4},{16,20},{1,5},{17,21},{2,6},{18,22},{3,7},{19,23},{4,0},{20,... | collective-permute-start | bytes 198152 | tf_op jit(solution)/shard_map/ppermute | solution.py:138
  86.9 2.7 %collective-permute-done.8 = f32[129,128]{1,0:T(8,128)S(1)} collective-permute-done((f32[129,128]{1,0:T(8,128)S(1)}, f32[129,128]{1,0:T(8,128)S(1)}, u32[]{:S(2)}, u32[]{:S(2)}) %collective-permute-start.8) | collective-permute-done | bytes 66080 | tf_op jit(solution)/shard_map/ppermute | solution.py:138
  89.6 2.7 %collective-permute-start.9 = (f32[129,128]{1,0:T(8,128)S(1)}, f32[129,128]{1,0:T(8,128)S(1)}, u32[]{:S(2)}, u32[]{:S(2)}) collective-permute-start(f32[129,128]{1,0:T(8,128)S(1)} %add.46), channel_id=1, source_target_pairs={{0,8},{16,24},{1,9},{17,25},{2,10},{18,26},{3,11},{19,27},{4,12},{... | collective-permute-start | bytes 198152 | tf_op jit(solution)/shard_map/ppermute | solution.py:138
  92.3 2.6 %collective-permute-done.9 = f32[129,128]{1,0:T(8,128)S(1)} collective-permute-done((f32[129,128]{1,0:T(8,128)S(1)}, f32[129,128]{1,0:T(8,128)S(1)}, u32[]{:S(2)}, u32[]{:S(2)}) %collective-permute-start.9) | collective-permute-done | bytes 66080 | tf_op jit(solution)/shard_map/ppermute | solution.py:138
  94.9 0.6 slice.142
  95.6 0.5 slice.143
  (34 shorter events, 0.2 us)
Async XLA Ops:
  0.6 2.9 %copy-start = (bf16[1,24,256,256]{3,2,1,0:T(8,128)(2,1)S(1)}, bf16[1,24,256,256]{3,2,1,0:T(8,128)(2,1)}, u32[]{:S(2)}) copy-start(bf16[1,24,256,256]{3,2,1,0:T(8,128)(2,1)} %param.6) | copy-start | bytes 9437188
  3.3 2.5 %copy-start.8 = (f32[12,256]{1,0:T(8,128)}, f32[12,256]{1,0:T(8,128)S(1)}, u32[]{:S(2)}) copy-start(f32[12,256]{1,0:T(8,128)S(1)} %slice.116.refs_5_) | copy-start | bytes 36868
  6.2 4.8 %copy-start.9 = (f32[6,256]{1,0:T(8,128)}, f32[6,256]{1,0:T(8,128)S(1)}, u32[]{:S(2)}) copy-start(f32[6,256]{1,0:T(8,128)S(1)} %slice.118.refs_7_) | copy-start | bytes 18436
  6.3 4.8 %copy-start.1 = (f32[12,256,256]{2,1,0:T(8,128)S(1)}, f32[12,256,256]{2,1,0:T(8,128)}, u32[]{:S(2)}) copy-start(f32[12,256,256]{2,1,0:T(8,128)} %fusion.2) | copy-start | bytes 9437188
  12.7 3.5 %copy-start.10 = (f32[3,256]{1,0:T(4,128)}, f32[3,256]{1,0:T(4,128)S(1)}, u32[]{:S(2)}) copy-start(f32[3,256]{1,0:T(4,128)S(1)} %slice.120.refs_9_) | copy-start | bytes 9220
  12.7 2.4 %copy-start.2 = (f32[6,256,256]{2,1,0:T(8,128)S(1)}, f32[6,256,256]{2,1,0:T(8,128)}, u32[]{:S(2)}) copy-start(f32[6,256,256]{2,1,0:T(8,128)} %fusion) | copy-start | bytes 4718596
  16.2 1.8 %copy-start.13 = (f32[1,256]{1,0:T(1,128)}, f32[1,256]{1,0:T(1,128)S(1)}, u32[]{:S(2)}) copy-start(f32[1,256]{1,0:T(1,128)S(1)} %get-tuple-element.48.refs_11_) | copy-start | bytes 3076
  16.2 1.8 %copy-start.14 = (f32[1,256]{1,0:T(1,128)}, f32[1,256]{1,0:T(1,128)S(1)}, u32[]{:S(2)}) copy-start(f32[1,256]{1,0:T(1,128)S(1)} %get-tuple-element.49.refs_13_) | copy-start | bytes 3076
  18.0 10.8 %copy-start.3 = (f32[264,256]{1,0:T(8,128)}, f32[264,256]{1,0:T(8,128)S(1)}, u32[]{:S(2)}) copy-start(f32[264,256]{1,0:T(8,128)S(1)} %maximum_maximum_fusion.own_ref) | copy-start | bytes 811012
  18.0 9.5 %collective-permute-start = (f32[264,256]{1,0:T(8,128)S(1)}, f32[264,256]{1,0:T(8,128)S(1)}, u32[]{:S(2)}, u32[]{:S(2)}) collective-permute-start(f32[264,256]{1,0:T(8,128)S(1)} %maximum_maximum_fusion.own_ref), channel_id=1, source_target_pairs={{0,16},{16,0},{1,17},{17,1},{2,18},{18,2},{3,19},{19,3},{4,20},{20... | collective-permute-start | bytes 811016 | tf_op jit(solution)/shard_map/ppermute | solution.py:138
  27.5 0.7 copy-start.7
  28.8 34.4 %copy-start.11 = (f32[1,24,2,128]{3,2,1,0:T(2,128)S(1)}, f32[1,24,2,128]{3,2,1,0:T(2,128)}, u32[]{:S(2)}) copy-start(f32[1,24,2,128]{3,2,1,0:T(2,128)} %param.8) | copy-start | bytes 73732
  31.5 1.8 %collective-permute-start.1 = (f32[264,256]{1,0:T(8,128)}, f32[264,256]{1,0:T(8,128)S(1)}, u32[]{:S(2)}, u32[]{:S(2)}) collective-permute-start(f32[264,256]{1,0:T(8,128)} %get-tuple-element.27.own_ref), channel_id=1, source_target_pairs={{0,1},{16,17},{1,0},{17,16},{2,3},{18,19},{3,2},{19,18},{4,5},{20,... | collective-permute-start | bytes 811016 | tf_op jit(solution)/shard_map/ppermute | solution.py:138
  33.2 0.7 copy-start.4
  36.5 8.7 %collective-permute-start.2 = (f32[264,256]{1,0:T(8,128)}, f32[264,256]{1,0:T(8,128)S(1)}, u32[]{:S(2)}, u32[]{:S(2)}) collective-permute-start(f32[264,256]{1,0:T(8,128)} %get-tuple-element.30.own_ref), channel_id=1, source_target_pairs={{0,2},{16,18},{1,3},{17,19},{2,0},{18,16},{3,1},{19,17},{4,6},{20,... | collective-permute-start | bytes 811016 | tf_op jit(solution)/shard_map/ppermute | solution.py:138
  45.2 0.7 copy-start.5
  48.5 8.0 %collective-permute-start.3 = (f32[264,256]{1,0:T(8,128)}, f32[264,256]{1,0:T(8,128)S(1)}, u32[]{:S(2)}, u32[]{:S(2)}) collective-permute-start(f32[264,256]{1,0:T(8,128)} %get-tuple-element.33.own_ref), channel_id=1, source_target_pairs={{0,4},{16,20},{1,5},{17,21},{2,6},{18,22},{3,7},{19,23},{4,0},{20,... | collective-permute-start | bytes 811016 | tf_op jit(solution)/shard_map/ppermute | solution.py:138
  56.5 0.7 copy-start.6
  60.4 4.7 %collective-permute-start.4 = (f32[8,256]{1,0:T(8,128)S(1)}, f32[8,256]{1,0:T(8,128)S(1)}, u32[]{:S(2)}, u32[]{:S(2)}) collective-permute-start(f32[8,256]{1,0:T(8,128)S(1)} %slice.125), channel_id=1, source_target_pairs={{0,8},{16,24},{1,9},{17,25},{2,10},{18,26},{3,11},{19,27},{4,12},{... | collective-permute-start | bytes 24584 | tf_op jit(solution)/shard_map/ppermute | solution.py:138
  65.1 0.6 copy-start.15
  65.7 5.7 %copy-start.12 = (f32[1,24,256]{2,1,0:T(8,128)S(1)}, f32[1,24,256]{2,1,0:T(8,128)}, u32[]{:S(2)}) copy-start(f32[1,24,256]{2,1,0:T(8,128)} %param.9) | copy-start | bytes 73732
  75.1 4.4 %collective-permute-start.5 = (f32[129,128]{1,0:T(8,128)S(1)}, f32[129,128]{1,0:T(8,128)S(1)}, u32[]{:S(2)}, u32[]{:S(2)}) collective-permute-start(f32[129,128]{1,0:T(8,128)S(1)} %select_maximum_fusion), channel_id=1, source_target_pairs={{0,16},{16,0},{1,17},{17,1},{2,18},{18,2},{3,19},{19,3},{4,20},{20... | collective-permute-start | bytes 198152 | tf_op jit(solution)/shard_map/ppermute | solution.py:138
  79.5 1.3 %collective-permute-start.6 = (f32[129,128]{1,0:T(8,128)S(1)}, f32[129,128]{1,0:T(8,128)S(1)}, u32[]{:S(2)}, u32[]{:S(2)}) collective-permute-start(f32[129,128]{1,0:T(8,128)S(1)} %fusion.20), channel_id=1, source_target_pairs={{0,1},{16,17},{1,0},{17,16},{2,3},{18,19},{3,2},{19,18},{4,5},{20,... | collective-permute-start | bytes 198152 | tf_op jit(solution)/shard_map/ppermute | solution.py:138
  80.9 4.4 %collective-permute-start.7 = (f32[129,128]{1,0:T(8,128)S(1)}, f32[129,128]{1,0:T(8,128)S(1)}, u32[]{:S(2)}, u32[]{:S(2)}) collective-permute-start(f32[129,128]{1,0:T(8,128)S(1)} %add.44), channel_id=1, source_target_pairs={{0,2},{16,18},{1,3},{17,19},{2,0},{18,16},{3,1},{19,17},{4,6},{20,... | collective-permute-start | bytes 198152 | tf_op jit(solution)/shard_map/ppermute | solution.py:138
  85.2 4.4 %collective-permute-start.8 = (f32[129,128]{1,0:T(8,128)S(1)}, f32[129,128]{1,0:T(8,128)S(1)}, u32[]{:S(2)}, u32[]{:S(2)}) collective-permute-start(f32[129,128]{1,0:T(8,128)S(1)} %add.45), channel_id=1, source_target_pairs={{0,4},{16,20},{1,5},{17,21},{2,6},{18,22},{3,7},{19,23},{4,0},{20,... | collective-permute-start | bytes 198152 | tf_op jit(solution)/shard_map/ppermute | solution.py:138
  89.6 5.3 %collective-permute-start.9 = (f32[129,128]{1,0:T(8,128)S(1)}, f32[129,128]{1,0:T(8,128)S(1)}, u32[]{:S(2)}, u32[]{:S(2)}) collective-permute-start(f32[129,128]{1,0:T(8,128)S(1)} %add.46), channel_id=1, source_target_pairs={{0,8},{16,24},{1,9},{17,25},{2,10},{18,26},{3,11},{19,27},{4,12},{... | collective-permute-start | bytes 198152 | tf_op jit(solution)/shard_map/ppermute | solution.py:138

commit v9 on v8

--- a/solution.py
+++ b/solution.py
@@ -90,13 +90,13 @@
     return jnp.sum(column(row) * q.astype(jnp.float32), axis=0, keepdims=True)
 
 
-def finish(d, sizes, width):
+def finish(d, sizes, width, stations):
     depth = len(sizes) - 1
 
     def kernel(*refs):
-        rv_ref, sq_ref, sv_ref, grads_ref = refs[:4]
-        tree = refs[4 : 4 + 2 * depth]
-        out_ref = refs[4 + 2 * depth]
+        rv_ref, sq_ref, sv_ref, grads_ref, load_ref, resp_ref = refs[:6]
+        tree = refs[6 : 6 + 2 * depth]
+        out_ref = refs[6 + 2 * depth]
         me = lax.axis_index("outer") * lax.axis_size("inner") + lax.axis_index("inner")
         lower = (me // d) % 2 == 0
         sv = sv_ref[0:1, :]
@@ -108,7 +108,7 @@
             new = []
             for j in range(n // 2):
                 upper = rows[j]
-                new.append(row_times(upper, q_ref[j]) + v_ref[j : j + 1, :])
+                new.append(row_times(upper, q_ref[2 * j + 1]) + v_ref[2 * j + 1 : 2 * j + 2, :])
                 new.append(upper)
             if n % 2:
                 new.append(rows[-1])
@@ -116,14 +116,13 @@
         for t, row in enumerate(rows):
             out_ref[t : t + 1, :] = grads_ref[t : t + 1, :] + row
 
-    def run(rv, sq, sv, grads, levels):
-        args = [rv, sq, sv, grads]
+    def run(rv, sq, sv, grads, loads, resp, levels):
+        args = [rv, sq, sv, grads, loads, resp]
         for level in range(depth):
-            q, v = levels[level]
-            half = sizes[level] // 2
-            args += [q[1 : 2 * half : 2], v[1 : 2 * half : 2]]
+            args += list(levels[level])
         return pl.pallas_call(
-            kernel, out_shape=jax.ShapeDtypeStruct(grads.shape, jnp.float32)
+            kernel,
+            out_shape=jax.ShapeDtypeStruct(grads.shape, jnp.float32),
         )(*args)
 
     return run
@@ -162,7 +161,9 @@
         d *= 2
     rv = exchange(packed[width:], d, count)
     sizes = [level[0].shape[0] for level in levels]
-    length_rates = finish(d, sizes, width)(rv, sq, sv, grads, levels)
+    length_rates = finish(d, sizes, width, stations)(
+        rv, sq, sv, grads, station_loadings[0], offset_response[0], levels
+    )
     argument_values = station_loadings[0]
     local_kernel = jnp.dot(
         length_rates[:, :stations].T, argument_values[:, 0, :], precision=EXACT

time: 96.5 us -> 95.6 us (level)
  local copies, waits for them, and re-layouts: 7.61 us -> 5.71 us
  Pallas kernels: 15 us -> 16.3 us
    slice x2 -> x0, other arithmetic: 2.62 us -> none  [upsweep(): qa, qb = (q[0:2 * half:2], q[1:2 * half:2])]
    reduce_sum x2 -> x4, other arithmetic: 3.08 us -> 4.97 us  [vecmat(): return jnp.sum(v[:, :, None] * q.astype(jnp.float32), axis=1)]
    concatenate x0 -> x2, other arithmetic: none -> 1.44 us  [the longest x1 0.85 us: upsweep(): nq = jnp.concatenate([nq, q[-1:].astype(jnp.float32)], axis=0)]
    pallas_call x1, Pallas kernels: 4.71 us -> 6.09 us  [run(): pl.pallas_call(kernel, out_shape=jax.ShapeDtypeStruct(grads.shape, jnp.fl...]
    slice x1 -> x0, local copies, waits for them, and re-layouts: 1.26 us -> none  [upsweep(): qa, qb = (q[0:2 * half:2], q[1:2 * half:2])]
    unnamed x32 -> x30, local copies, waits for them, and re-layouts: 3.7 us -> 3.04 us
  transfers between devices with their start and end apart: 10 -> 10, of which waited for: 9 -> 10; matrix products, arithmetic and copies ran while one was open for 3% -> 3% of each run, Pallas kernels for 0% -> 0%
where the time goes in v9:
time: 95.6 us; the launch traced here: 95.1 us
  waiting for transfers between devices  31.9 us (33%)
  starting transfers between devices  17.5 us (18%)
  Pallas kernels  16.3 us (17%)
  matrix products  12 us (13%)
  other arithmetic  9.4 us (10%)
  local copies, waits for them, and re-layouts  5.71 us (6%)
  between operations  2.18 us (2%)
    ppermute x10, waiting for transfers between devices, exchange(): lax.ppermute(x, AXES, [(place(j), place(j ^ mask)) for j in range(count)])  31.9 us
    ppermute x10, starting transfers between devices, exchange(): lax.ppermute(x, AXES, [(place(j), place(j ^ mask)) for j in range(count)])  17.5 us
    pallas_call x4, Pallas kernels, run(): pl.pallas_call(kernel, out_shape=(jax.ShapeDtypeStruct(own.shape, jnp.flo...  10.2 us
    dot_general x4, matrix products, matmat(): jnp.einsum('nij,njk->nik', later.astype(jnp.float32), earlier.astype(jnp....  7.83 us
    pallas_call x1, Pallas kernels, run(): pl.pallas_call(kernel, out_shape=jax.ShapeDtypeStruct(grads.shape, jnp.fl...  6.09 us
    reduce_sum x4, other arithmetic, vecmat(): return jnp.sum(v[:, :, None] * q.astype(jnp.float32), axis=1)  4.97 us
    unnamed x30, local copies, waits for them, and re-layouts  3.04 us
    dot_general x1, matrix products, matmat(): jnp.einsum('nij,njk->nik', later, earlier, preferred_element_type=jnp.flo...  2.22 us
  transfers between devices with their start and end apart: 10, of which 10 were waited for; matrix products, arithmetic and copies ran while one was open for 3% of the time, Pallas kernels for 0%

profile of v9, /device:TPU:0, one launch (start us, length us, event | category | flops | bytes accessed | tf_op | source)
XLA Modules:
  0.0 95.1 jit_solution(11392848785053453619)
XLA Ops:
  0.6 0.0 copy-start
  0.6 2.6 %multiply_reduce_fusion.refs_7_ = f32[24,256]{1,0:T(8,128)S(1)} fusion(f32[24,256]{1,0:T(8,128)} %bitcast.37, bf16[1,24,256,256]{3,2,1,0:T(8,128)(2,1)} %param.6), kind=kLoop, calls=%fused_computation | loop fusion | flops 4712448 | bytes 3194880 | tf_op jit(solution)/shard_map/reduce_sum | solution.py:12
  3.2 0.0 copy-start.4
  3.3 0.2 copy-done
  3.5 2.2 %fusion.2.refs_8_ = f32[12,256,256]{2,1,0:T(8,128)} fusion(bf16[24,256,256]{2,1,0:T(8,128)(2,1)S(1)} %bitcast.33), kind=kOutput, calls=%fused_computation.5 | convolution fusion | flops 402653184 | bytes 6291456 | tf_op jit(solution)/shard_map/nij,njk->nik/dot_general | solution.py:21
  5.7 0.0 copy-done.4
  5.7 0.5 multiply_reduce_fusion.1
  6.2 0.0 copy-start.1
  6.2 0.0 copy-start.9
  6.3 4.8 %fusion.refs_10_ = f32[6,256,256]{2,1,0:T(8,128)} fusion(f32[12,256,256]{2,1,0:T(8,128)} %fusion.2.refs_8_), kind=kOutput, calls=%fused_computation.3 | convolution fusion | flops 1207959552 | bytes 4718592 | tf_op jit(solution)/shard_map/nij,njk->nik/dot_general | solution.py:22
  11.1 0.0 copy-done.1
  11.1 0.3 multiply_reduce_fusion.2
  11.4 0.0 copy-done.9
  11.5 2.3 %fusion.6.refs_12_ = f32[3,256,256]{2,1,0:T(8,128)S(1)} fusion(f32[6,256,256]{2,1,0:T(8,128)} %fusion.refs_10_), kind=kOutput, calls=%fused_computation.11 | convolution fusion | flops 603979776 | bytes 2359296 | tf_op jit(solution)/shard_map/nij,njk->nik/dot_general | solution.py:22
  13.7 0.0 copy-start.2
  13.7 1.6 %multiply_reduce_fusion.3 = f32[3,256]{1,0:T(4,128)S(1)} fusion(f32[6,256,256]{2,1,0:T(8,128)} %fusion.refs_10_, f32[3,256]{1,0:T(4,128)S(1)} %slice.112), kind=kLoop, calls=%fused_computation.10 | loop fusion | flops 392448 | bytes 792576 | tf_op jit(solution)/shard_map/reduce_sum | solution.py:12
  15.4 0.4 multiply_reduce_fusion.5
  15.8 0.0 copy-start.10
  15.8 0.1 fusion.21
  15.9 0.4 fusion.11
  16.3 0.1 pad.14.clone
  16.4 0.1 maximum_maximum_fusion.own_ref
  16.5 3.0 %collective-permute-start = (f32[264,256]{1,0:T(8,128)S(1)}, f32[264,256]{1,0:T(8,128)S(1)}, u32[]{:S(2)}, u32[]{:S(2)}) collective-permute-start(f32[264,256]{1,0:T(8,128)S(1)} %maximum_maximum_fusion.own_ref), channel_id=1, source_target_pairs={{0,16},{16,0},{1,17},{17,1},{2,18},{18,2},{3,19},{19,3},{4,20},{20... | collective-permute-start | bytes 811016 | tf_op jit(solution)/shard_map/ppermute | solution.py:137
  19.5 0.7 fusion.13.sq_ref
  20.2 5.8 %collective-permute-done.got_ref = f32[264,256]{1,0:T(8,128)S(1)} collective-permute-done((f32[264,256]{1,0:T(8,128)S(1)}, f32[264,256]{1,0:T(8,128)S(1)}, u32[]{:S(2)}, u32[]{:S(2)}) %collective-permute-start) | collective-permute-done | bytes 270368 | tf_op jit(solution)/shard_map/ppermute | solution.py:137
  26.0 0.6 broadcast_in_dim.7.sv_ref
  26.6 0.1 copy-done.8
  26.7 2.6 %shard_map.67 = (f32[264,256]{1,0:T(8,128)}, f32[256,256]{1,0:T(8,128)}, f32[8,256]{1,0:T(8,128)}) custom-call(f32[264,256]{1,0:T(8,128)} %copy-done.3, f32[264,256]{1,0:T(8,128)} %copy-done.8, f32[256,256]{1,0:T(8,128)} %fusion.13.sq_ref, f32[8,256]{1,0:T(8,128)} %broadcast_in_dim.7.sv_ref), custom_call_target="tpu_custom_call" | custom-call | tf_op jit(solution)/shard_map/pallas_call | solution.py:73
  29.3 0.0 collective-permute-start.1
  29.3 1.8 %collective-permute-done.1.got_ref = f32[264,256]{1,0:T(8,128)S(1)} collective-permute-done((f32[264,256]{1,0:T(8,128)}, f32[264,256]{1,0:T(8,128)S(1)}, u32[]{:S(2)}, u32[]{:S(2)}) %collective-permute-start.1) | collective-permute-done | bytes 270368 | tf_op jit(solution)/shard_map/ppermute | solution.py:137
  31.0 0.7 copy-done.6
  31.7 2.6 %shard_map.68 = (f32[264,256]{1,0:T(8,128)}, f32[256,256]{1,0:T(8,128)}, f32[8,256]{1,0:T(8,128)}) custom-call(f32[264,256]{1,0:T(8,128)} %get-tuple-element.27.own_ref, f32[264,256]{1,0:T(8,128)} %copy-done.6, f32[256,256]{1,0:T(8,128)} %get-tuple-element.28.sq_ref, f32[8,256]{1,0:T(8,128)} %get-tuple-element.29.sv_ref), custom_call_target="tpu_custom_call" | custom-call | tf_op jit(solution)/shard_map/pallas_call | solution.py:73
  34.3 1.7 %collective-permute-start.2 = (f32[264,256]{1,0:T(8,128)}, f32[264,256]{1,0:T(8,128)S(1)}, u32[]{:S(2)}, u32[]{:S(2)}) collective-permute-start(f32[264,256]{1,0:T(8,128)} %get-tuple-element.30.own_ref), channel_id=1, source_target_pairs={{0,2},{16,18},{1,3},{17,19},{2,0},{18,16},{3,1},{19,17},{4,6},{20,... | collective-permute-start | bytes 811016 | tf_op jit(solution)/shard_map/ppermute | solution.py:137
  36.0 7.0 %collective-permute-done.2.got_ref = f32[264,256]{1,0:T(8,128)S(1)} collective-permute-done((f32[264,256]{1,0:T(8,128)}, f32[264,256]{1,0:T(8,128)S(1)}, u32[]{:S(2)}, u32[]{:S(2)}) %collective-permute-start.2) | collective-permute-done | bytes 270368 | tf_op jit(solution)/shard_map/ppermute | solution.py:137
  43.0 0.7 copy-done.7
  43.7 2.5 %shard_map.69 = (f32[264,256]{1,0:T(8,128)}, f32[256,256]{1,0:T(8,128)}, f32[8,256]{1,0:T(8,128)}) custom-call(f32[264,256]{1,0:T(8,128)} %get-tuple-element.30.own_ref, f32[264,256]{1,0:T(8,128)} %copy-done.7, f32[256,256]{1,0:T(8,128)} %get-tuple-element.31.sq_ref, f32[8,256]{1,0:T(8,128)} %get-tuple-element.32.sv_ref), custom_call_target="tpu_custom_call" | custom-call | tf_op jit(solution)/shard_map/pallas_call | solution.py:73
  46.3 1.8 %collective-permute-start.3 = (f32[264,256]{1,0:T(8,128)}, f32[264,256]{1,0:T(8,128)S(1)}, u32[]{:S(2)}, u32[]{:S(2)}) collective-permute-start(f32[264,256]{1,0:T(8,128)} %get-tuple-element.33.own_ref), channel_id=1, source_target_pairs={{0,4},{16,20},{1,5},{17,21},{2,6},{18,22},{3,7},{19,23},{4,0},{20,... | collective-permute-start | bytes 811016 | tf_op jit(solution)/shard_map/ppermute | solution.py:137
  48.1 0.9 pad_maximum_fusion.refs_14_
  48.9 0.0 copy-done.10
  49.0 5.3 %collective-permute-done.3.got_ref = f32[264,256]{1,0:T(8,128)S(1)} collective-permute-done((f32[264,256]{1,0:T(8,128)}, f32[264,256]{1,0:T(8,128)S(1)}, u32[]{:S(2)}, u32[]{:S(2)}) %collective-permute-start.3) | collective-permute-done | bytes 270368 | tf_op jit(solution)/shard_map/ppermute | solution.py:137
  54.3 0.7 copy-done.5
  55.0 2.6 %shard_map.70 = (f32[264,256]{1,0:T(8,128)}, f32[256,256]{1,0:T(8,128)}, f32[8,256]{1,0:T(8,128)}) custom-call(f32[264,256]{1,0:T(8,128)} %get-tuple-element.33.own_ref, f32[264,256]{1,0:T(8,128)} %copy-done.5, f32[256,256]{1,0:T(8,128)} %get-tuple-element.34.sq_ref, f32[8,256]{1,0:T(8,128)} %get-tuple-element.35.sv_ref), custom_call_target="tpu_custom_call" | custom-call | tf_op jit(solution)/shard_map/pallas_call | solution.py:73
  57.5 0.7 slice.117
  58.2 2.8 %collective-permute-start.4 = (f32[8,256]{1,0:T(8,128)S(1)}, f32[8,256]{1,0:T(8,128)S(1)}, u32[]{:S(2)}, u32[]{:S(2)}) collective-permute-start(f32[8,256]{1,0:T(8,128)S(1)} %slice.117), channel_id=1, source_target_pairs={{0,8},{16,24},{1,9},{17,25},{2,10},{18,26},{3,11},{19,27},{4,12},{... | collective-permute-start | bytes 24584 | tf_op jit(solution)/shard_map/ppermute | solution.py:137
  61.0 0.6 pad_maximum_fusion.1.refs_15_
  61.6 0.6 compare_reduce_fusion
  62.2 0.6 collective-permute-done.4.refs_0_
  62.8 0.6 copy-done.14
  63.4 6.1 %shard_map.71 = f32[24,256]{1,0:T(8,128)} custom-call(f32[8,256]{1,0:T(8,128)} %copy-done.14, f32[256,256]{1,0:T(8,128)} %get-tuple-element.37.refs_1_, f32[8,256]{1,0:T(8,128)} %get-tuple-element.38.refs_2_, f32[24,256]{1,0:T(8,128)} %bitcast.38, f32[24,2,128]{2,1,0:T(2,128)} %bitcast.39, f32[24,256]{1,0:T(8,128)} %bitcast.41, ...), custom_call_target="tpu_custom_call" | custom-call | tf_op jit(solution)/shard_map/pallas_call | solution.py:123
  69.5 1.3 %multiply_reduce_fusion.6 = f32[]{:T(128)} fusion(f32[24,256]{1,0:T(8,128)} %shard_map.71, f32[1,24,256]{2,1,0:T(8,128)S(1)} %copy-done.11), kind=kLoop, calls=%fused_computation.28 | loop fusion | flops 12287 | bytes 49156 | tf_op jit(solution)/shard_map/reduce_sum | solution.py:174
  70.8 1.0 %fusion.15 = f32[128,128]{1,0:T(8,128)S(1)} fusion(f32[24,128]{1,0:T(8,128)S(1)} %bitcast.43, f32[24,256]{1,0:T(8,128)} %shard_map.71), kind=kOutput, calls=%fused_computation.29 | convolution fusion | flops 4718592 | bytes 90112 | tf_op jit(solution)/shard_map/dot_general | solution.py:171
  72.5 1.0 %convolution_add_fusion = f32[128,128]{1,0:T(8,128)S(1)} fusion(f32[128,128]{1,0:T(8,128)S(1)} %fusion.15, f32[24,128]{1,0:T(8,128)S(1)} %bitcast.42, f32[24,256]{1,0:T(8,128)} %shard_map.71), kind=kOutput, calls=%fused_computation.9 | convolution fusion | flops 4734976 | bytes 155648 | tf_op jit(solution)/shard_map/dot_general | solution.py:168
  74.1 1.7 %collective-permute-start.5 = (f32[129,128]{1,0:T(8,128)S(1)}, f32[129,128]{1,0:T(8,128)S(1)}, u32[]{:S(2)}, u32[]{:S(2)}) collective-permute-start(f32[129,128]{1,0:T(8,128)S(1)} %select_maximum_fusion), channel_id=1, source_target_pairs={{0,16},{16,0},{1,17},{17,1},{2,18},{18,2},{3,19},{19,3},{4,20},{20... | collective-permute-start | bytes 198152 | tf_op jit(solution)/shard_map/ppermute | solution.py:137
  75.9 2.6 %collective-permute-done.5 = f32[129,128]{1,0:T(8,128)S(1)} collective-permute-done((f32[129,128]{1,0:T(8,128)S(1)}, f32[129,128]{1,0:T(8,128)S(1)}, u32[]{:S(2)}, u32[]{:S(2)}) %collective-permute-start.5) | collective-permute-done | bytes 66080 | tf_op jit(solution)/shard_map/ppermute | solution.py:137
  78.5 0.1 collective-permute-start.6
  78.6 1.2 %collective-permute-done.6 = f32[129,128]{1,0:T(8,128)S(1)} collective-permute-done((f32[129,128]{1,0:T(8,128)S(1)}, f32[129,128]{1,0:T(8,128)S(1)}, u32[]{:S(2)}, u32[]{:S(2)}) %collective-permute-start.6) | collective-permute-done | bytes 66080 | tf_op jit(solution)/shard_map/ppermute | solution.py:137
  79.9 1.7 %collective-permute-start.7 = (f32[129,128]{1,0:T(8,128)S(1)}, f32[129,128]{1,0:T(8,128)S(1)}, u32[]{:S(2)}, u32[]{:S(2)}) collective-permute-start(f32[129,128]{1,0:T(8,128)S(1)} %add.44), channel_id=1, source_target_pairs={{0,2},{16,18},{1,3},{17,19},{2,0},{18,16},{3,1},{19,17},{4,6},{20,... | collective-permute-start | bytes 198152 | tf_op jit(solution)/shard_map/ppermute | solution.py:137
  81.6 2.7 %collective-permute-done.7 = f32[129,128]{1,0:T(8,128)S(1)} collective-permute-done((f32[129,128]{1,0:T(8,128)S(1)}, f32[129,128]{1,0:T(8,128)S(1)}, u32[]{:S(2)}, u32[]{:S(2)}) %collective-permute-start.7) | collective-permute-done | bytes 66080 | tf_op jit(solution)/shard_map/ppermute | solution.py:137
  84.2 1.8 %collective-permute-start.8 = (f32[129,128]{1,0:T(8,128)S(1)}, f32[129,128]{1,0:T(8,128)S(1)}, u32[]{:S(2)}, u32[]{:S(2)}) collective-permute-start(f32[129,128]{1,0:T(8,128)S(1)} %add.45), channel_id=1, source_target_pairs={{0,4},{16,20},{1,5},{17,21},{2,6},{18,22},{3,7},{19,23},{4,0},{20,... | collective-permute-start | bytes 198152 | tf_op jit(solution)/shard_map/ppermute | solution.py:137
  86.1 2.6 %collective-permute-done.8 = f32[129,128]{1,0:T(8,128)S(1)} collective-permute-done((f32[129,128]{1,0:T(8,128)S(1)}, f32[129,128]{1,0:T(8,128)S(1)}, u32[]{:S(2)}, u32[]{:S(2)}) %collective-permute-start.8) | collective-permute-done | bytes 66080 | tf_op jit(solution)/shard_map/ppermute | solution.py:137
  88.6 2.8 %collective-permute-start.9 = (f32[129,128]{1,0:T(8,128)S(1)}, f32[129,128]{1,0:T(8,128)S(1)}, u32[]{:S(2)}, u32[]{:S(2)}) collective-permute-start(f32[129,128]{1,0:T(8,128)S(1)} %add.46), channel_id=1, source_target_pairs={{0,8},{16,24},{1,9},{17,25},{2,10},{18,26},{3,11},{19,27},{4,12},{... | collective-permute-start | bytes 198152 | tf_op jit(solution)/shard_map/ppermute | solution.py:137
  91.5 2.5 %collective-permute-done.9 = f32[129,128]{1,0:T(8,128)S(1)} collective-permute-done((f32[129,128]{1,0:T(8,128)S(1)}, f32[129,128]{1,0:T(8,128)S(1)}, u32[]{:S(2)}, u32[]{:S(2)}) %collective-permute-start.9) | collective-permute-done | bytes 66080 | tf_op jit(solution)/shard_map/ppermute | solution.py:137
  93.9 0.6 slice.134
  94.6 0.5 slice.135
  (33 shorter events, 0.2 us)
Async XLA Ops:
  0.6 2.9 %copy-start = (bf16[1,24,256,256]{3,2,1,0:T(8,128)(2,1)S(1)}, bf16[1,24,256,256]{3,2,1,0:T(8,128)(2,1)}, u32[]{:S(2)}) copy-start(bf16[1,24,256,256]{3,2,1,0:T(8,128)(2,1)} %param.6) | copy-start | bytes 9437188
  3.2 2.5 %copy-start.4 = (f32[24,256]{1,0:T(8,128)}, f32[24,256]{1,0:T(8,128)S(1)}, u32[]{:S(2)}) copy-start(f32[24,256]{1,0:T(8,128)S(1)} %multiply_reduce_fusion.refs_7_) | copy-start | bytes 73732
  6.2 4.9 %copy-start.1 = (f32[12,256,256]{2,1,0:T(8,128)S(1)}, f32[12,256,256]{2,1,0:T(8,128)}, u32[]{:S(2)}) copy-start(f32[12,256,256]{2,1,0:T(8,128)} %fusion.2.refs_8_) | copy-start | bytes 9437188
  6.2 5.1 %copy-start.9 = (f32[12,256]{1,0:T(8,128)}, f32[12,256]{1,0:T(8,128)S(1)}, u32[]{:S(2)}) copy-start(f32[12,256]{1,0:T(8,128)S(1)} %add.37.refs_9_) | copy-start | bytes 36868
  11.4 8.8 %copy-start.12 = (f32[6,256]{1,0:T(8,128)}, f32[6,256]{1,0:T(8,128)S(1)}, u32[]{:S(2)}) copy-start(f32[6,256]{1,0:T(8,128)S(1)} %add.38.refs_11_) | copy-start | bytes 18436
  13.7 32.6 %copy-start.2 = (f32[3,256,256]{2,1,0:T(8,128)}, f32[3,256,256]{2,1,0:T(8,128)S(1)}, u32[]{:S(2)}) copy-start(f32[3,256,256]{2,1,0:T(8,128)S(1)} %fusion.6.refs_12_) | copy-start | bytes 2359300
  15.3 33.6 %copy-start.13 = (f32[3,256]{1,0:T(4,128)}, f32[3,256]{1,0:T(4,128)S(1)}, u32[]{:S(2)}) copy-start(f32[3,256]{1,0:T(4,128)S(1)} %add.39.refs_13_) | copy-start | bytes 9220
  15.8 33.2 %copy-start.10 = (f32[1,24,2,128]{3,2,1,0:T(2,128)S(1)}, f32[1,24,2,128]{3,2,1,0:T(2,128)}, u32[]{:S(2)}) copy-start(f32[1,24,2,128]{3,2,1,0:T(2,128)} %param.8) | copy-start | bytes 73732
  16.5 10.2 %copy-start.3 = (f32[264,256]{1,0:T(8,128)}, f32[264,256]{1,0:T(8,128)S(1)}, u32[]{:S(2)}) copy-start(f32[264,256]{1,0:T(8,128)S(1)} %maximum_maximum_fusion.own_ref) | copy-start | bytes 811012
  16.5 9.5 %collective-permute-start = (f32[264,256]{1,0:T(8,128)S(1)}, f32[264,256]{1,0:T(8,128)S(1)}, u32[]{:S(2)}, u32[]{:S(2)}) collective-permute-start(f32[264,256]{1,0:T(8,128)S(1)} %maximum_maximum_fusion.own_ref), channel_id=1, source_target_pairs={{0,16},{16,0},{1,17},{17,1},{2,18},{18,2},{3,19},{19,3},{4,20},{20... | collective-permute-start | bytes 811016 | tf_op jit(solution)/shard_map/ppermute | solution.py:137
  26.0 0.7 copy-start.8
  29.3 1.8 %collective-permute-start.1 = (f32[264,256]{1,0:T(8,128)}, f32[264,256]{1,0:T(8,128)S(1)}, u32[]{:S(2)}, u32[]{:S(2)}) collective-permute-start(f32[264,256]{1,0:T(8,128)} %get-tuple-element.27.own_ref), channel_id=1, source_target_pairs={{0,1},{16,17},{1,0},{17,16},{2,3},{18,19},{3,2},{19,18},{4,5},{20,... | collective-permute-start | bytes 811016 | tf_op jit(solution)/shard_map/ppermute | solution.py:137
  31.0 0.7 copy-start.6
  34.3 8.7 %collective-permute-start.2 = (f32[264,256]{1,0:T(8,128)}, f32[264,256]{1,0:T(8,128)S(1)}, u32[]{:S(2)}, u32[]{:S(2)}) collective-permute-start(f32[264,256]{1,0:T(8,128)} %get-tuple-element.30.own_ref), channel_id=1, source_target_pairs={{0,2},{16,18},{1,3},{17,19},{2,0},{18,16},{3,1},{19,17},{4,6},{20,... | collective-permute-start | bytes 811016 | tf_op jit(solution)/shard_map/ppermute | solution.py:137
  43.0 0.7 copy-start.7
  46.3 8.0 %collective-permute-start.3 = (f32[264,256]{1,0:T(8,128)}, f32[264,256]{1,0:T(8,128)S(1)}, u32[]{:S(2)}, u32[]{:S(2)}) collective-permute-start(f32[264,256]{1,0:T(8,128)} %get-tuple-element.33.own_ref), channel_id=1, source_target_pairs={{0,4},{16,20},{1,5},{17,21},{2,6},{18,22},{3,7},{19,23},{4,0},{20,... | collective-permute-start | bytes 811016 | tf_op jit(solution)/shard_map/ppermute | solution.py:137
  54.2 0.7 copy-start.5
  58.2 4.5 %collective-permute-start.4 = (f32[8,256]{1,0:T(8,128)S(1)}, f32[8,256]{1,0:T(8,128)S(1)}, u32[]{:S(2)}, u32[]{:S(2)}) collective-permute-start(f32[8,256]{1,0:T(8,128)S(1)} %slice.117), channel_id=1, source_target_pairs={{0,8},{16,24},{1,9},{17,25},{2,10},{18,26},{3,11},{19,27},{4,12},{... | collective-permute-start | bytes 24584 | tf_op jit(solution)/shard_map/ppermute | solution.py:137
  62.8 0.6 copy-start.14
  63.4 6.1 %copy-start.11 = (f32[1,24,256]{2,1,0:T(8,128)S(1)}, f32[1,24,256]{2,1,0:T(8,128)}, u32[]{:S(2)}) copy-start(f32[1,24,256]{2,1,0:T(8,128)} %param.9) | copy-start | bytes 73732
  74.1 4.4 %collective-permute-start.5 = (f32[129,128]{1,0:T(8,128)S(1)}, f32[129,128]{1,0:T(8,128)S(1)}, u32[]{:S(2)}, u32[]{:S(2)}) collective-permute-start(f32[129,128]{1,0:T(8,128)S(1)} %select_maximum_fusion), channel_id=1, source_target_pairs={{0,16},{16,0},{1,17},{17,1},{2,18},{18,2},{3,19},{19,3},{4,20},{20... | collective-permute-start | bytes 198152 | tf_op jit(solution)/shard_map/ppermute | solution.py:137
  78.5 1.3 %collective-permute-start.6 = (f32[129,128]{1,0:T(8,128)S(1)}, f32[129,128]{1,0:T(8,128)S(1)}, u32[]{:S(2)}, u32[]{:S(2)}) collective-permute-start(f32[129,128]{1,0:T(8,128)S(1)} %fusion.19), channel_id=1, source_target_pairs={{0,1},{16,17},{1,0},{17,16},{2,3},{18,19},{3,2},{19,18},{4,5},{20,... | collective-permute-start | bytes 198152 | tf_op jit(solution)/shard_map/ppermute | solution.py:137
  79.9 4.4 %collective-permute-start.7 = (f32[129,128]{1,0:T(8,128)S(1)}, f32[129,128]{1,0:T(8,128)S(1)}, u32[]{:S(2)}, u32[]{:S(2)}) collective-permute-start(f32[129,128]{1,0:T(8,128)S(1)} %add.44), channel_id=1, source_target_pairs={{0,2},{16,18},{1,3},{17,19},{2,0},{18,16},{3,1},{19,17},{4,6},{20,... | collective-permute-start | bytes 198152 | tf_op jit(solution)/shard_map/ppermute | solution.py:137
  84.2 4.4 %collective-permute-start.8 = (f32[129,128]{1,0:T(8,128)S(1)}, f32[129,128]{1,0:T(8,128)S(1)}, u32[]{:S(2)}, u32[]{:S(2)}) collective-permute-start(f32[129,128]{1,0:T(8,128)S(1)} %add.45), channel_id=1, source_target_pairs={{0,4},{16,20},{1,5},{17,21},{2,6},{18,22},{3,7},{19,23},{4,0},{20,... | collective-permute-start | bytes 198152 | tf_op jit(solution)/shard_map/ppermute | solution.py:137
  88.6 5.3 %collective-permute-start.9 = (f32[129,128]{1,0:T(8,128)S(1)}, f32[129,128]{1,0:T(8,128)S(1)}, u32[]{:S(2)}, u32[]{:S(2)}) collective-permute-start(f32[129,128]{1,0:T(8,128)S(1)} %add.46), channel_id=1, source_target_pairs={{0,8},{16,24},{1,9},{17,25},{2,10},{18,26},{3,11},{19,27},{4,12},{... | collective-permute-start | bytes 198152 | tf_op jit(solution)/shard_map/ppermute | solution.py:137

commit v10 on v9

--- a/solution.py
+++ b/solution.py
@@ -56,28 +56,35 @@
 
 
 def scan_round(d, width):
-    def kernel(own_ref, got_ref, sq_ref, sv_ref, own_out, sq_out, sv_out):
+    def lower_half():
         me = lax.axis_index("outer") * lax.axis_size("inner") + lax.axis_index("inner")
-        lower = (me // d) % 2 == 0
+        return (me // d) % 2 == 0
+
+    def group_kernel(own_ref, got_ref, own_out):
+        lower = lower_half()
         later = jnp.where(lower, got_ref[...], own_ref[...])
         early_q = jnp.where(lower, own_ref[0:width, :], got_ref[0:width, :])
         early_v = jnp.where(lower, own_ref[width:, :], got_ref[width:, :])
         new_q = jnp.dot(later, early_q, precision=EXACT, preferred_element_type=jnp.float32)
-        new_s = jnp.dot(later, sq_ref[...], precision=EXACT, preferred_element_type=jnp.float32)
         own_out[0:width, :] = new_q[0:width]
         own_out[width:, :] = new_q[width:] + early_v
+
+    def suffix_kernel(got_ref, sq_ref, sv_ref, sq_out, sv_out):
+        lower = lower_half()
+        new_s = jnp.dot(got_ref[...], sq_ref[...], precision=EXACT, preferred_element_type=jnp.float32)
         sq_out[...] = jnp.where(lower, new_s[0:width], sq_ref[...])
         sv_out[...] = jnp.where(lower, new_s[width:] + sv_ref[...], sv_ref[...])
 
     def run(own, got, sq, sv):
-        return pl.pallas_call(
-            kernel,
+        new = pl.pallas_call(group_kernel, out_shape=jax.ShapeDtypeStruct(own.shape, jnp.float32))(own, got)
+        sq, sv = pl.pallas_call(
+            suffix_kernel,
             out_shape=(
-                jax.ShapeDtypeStruct(own.shape, jnp.float32),
                 jax.ShapeDtypeStruct(sq.shape, jnp.float32),
                 jax.ShapeDtypeStruct(sv.shape, jnp.float32),
             ),
-        )(own, got, sq, sv)
+        )(got, sq, sv)
+        return new, sq, sv
 
     return run
 

time: 95.6 us -> 98.4 us (1.029)
  Pallas kernels: 16.3 us -> 23.2 us
  matrix products: 12 us -> 7.73 us
  starting transfers between devices: 17.5 us -> 14.4 us
  waiting for transfers between devices: 31.9 us -> 34.5 us
  local copies, waits for them, and re-layouts: 5.71 us -> 7.95 us
  other arithmetic: 9.4 us -> 7.96 us
    pallas_call x4 -> x8, Pallas kernels: 10.2 us -> 17.1 us  [the longest x4 8.57 us: run(): pl.pallas_call(group_kernel, out_shape=jax.ShapeDtypeStruct(own.shape, jn...]
    ppermute x10, starting transfers between devices: 17.5 us -> 14.4 us  [exchange(): lax.ppermute(x, AXES, [(place(j), place(j ^ mask)) for j in range(count)])]
    dot_general x4, matrix products: 7.83 us -> 5.17 us  [matmat(): jnp.einsum('nij,njk->nik', later.astype(jnp.float32), earlier.astype(jnp....]
    ppermute x10, waiting for transfers between devices: 31.9 us -> 34.5 us  [exchange(): lax.ppermute(x, AXES, [(place(j), place(j ^ mask)) for j in range(count)])]
    unnamed x30 -> x32, local copies, waits for them, and re-layouts: 3.04 us -> 5.3 us
    dot_general x1, matrix products: 2.22 us -> 0.57 us  [matmat(): jnp.einsum('nij,njk->nik', later, earlier, preferred_element_type=jnp.flo...]
    reduce_sum x4, other arithmetic: 4.97 us -> 3.55 us  [vecmat(): return jnp.sum(v[:, :, None] * q.astype(jnp.float32), axis=1)]
  transfers between devices with their start and end apart: 10 -> 10, of which waited for: 10 -> 9; matrix products, arithmetic and copies ran while one was open for 3% -> 3% of each run, Pallas kernels for 0% -> 9%
where the time goes in v10:
time: 98.4 us; the launch traced here: 97.9 us
  waiting for transfers between devices  34.5 us (35%)
  Pallas kernels  23.2 us (24%)
  starting transfers between devices  14.4 us (15%)
  other arithmetic  7.96 us (8%)
  local copies, waits for them, and re-layouts  7.95 us (8%)
  matrix products  7.73 us (8%)
  between operations  2.21 us (2%)
    ppermute x10, waiting for transfers between devices, exchange(): lax.ppermute(x, AXES, [(place(j), place(j ^ mask)) for j in range(count)])  34.5 us
    ppermute x10, starting transfers between devices, exchange(): lax.ppermute(x, AXES, [(place(j), place(j ^ mask)) for j in range(count)])  14.4 us
    pallas_call x4, Pallas kernels, run(): pl.pallas_call(group_kernel, out_shape=jax.ShapeDtypeStruct(own.shape, jn...  8.57 us
    pallas_call x4, Pallas kernels, run(): pl.pallas_call(suffix_kernel, out_shape=(jax.ShapeDtypeStruct(sq.shape, j...  8.5 us
    pallas_call x1, Pallas kernels, run(): pl.pallas_call(kernel, out_shape=jax.ShapeDtypeStruct(grads.shape, jnp.fl...  6.09 us
    unnamed x32, local copies, waits for them, and re-layouts  5.3 us
    dot_general x4, matrix products, matmat(): jnp.einsum('nij,njk->nik', later.astype(jnp.float32), earlier.astype(jnp....  5.17 us
    reduce_sum x4, other arithmetic, vecmat(): return jnp.sum(v[:, :, None] * q.astype(jnp.float32), axis=1)  3.55 us
  transfers between devices with their start and end apart: 10, of which 9 were waited for; matrix products, arithmetic and copies ran while one was open for 3% of the time, Pallas kernels for 9%

profile of v10, /device:TPU:0, one launch (start us, length us, event | category | flops | bytes accessed | tf_op | source)
XLA Modules:
  0.0 97.9 jit_solution(15245939255481238004)
XLA Ops:
  0.6 0.0 copy-start
  0.6 2.6 %multiply_reduce_fusion.refs_7_ = f32[24,256]{1,0:T(8,128)S(1)} fusion(f32[24,256]{1,0:T(8,128)} %bitcast.37, bf16[1,24,256,256]{3,2,1,0:T(8,128)(2,1)} %param.6), kind=kLoop, calls=%fused_computation | loop fusion | flops 4712448 | bytes 3194880 | tf_op jit(solution)/shard_map/reduce_sum | solution.py:12
  3.2 0.0 copy-start.9
  3.3 0.2 copy-done
  3.5 0.5 multiply_reduce_fusion.1
  4.0 0.6 fusion.2.refs_8_
  4.7 1.6 %copy-done.1 = f32[12,256,256]{2,1,0:T(8,128)} copy-done((f32[12,256,256]{2,1,0:T(8,128)}, f32[12,256,256]{2,1,0:T(8,128)S(1)}, u32[]{:S(2)}) %copy-start.1) | copy-done | bytes 3145752
  6.3 0.3 multiply_reduce_fusion.2
  6.6 3.5 %fusion.refs_10_ = f32[6,256,256]{2,1,0:T(8,128)S(1)} fusion(f32[12,256,256]{2,1,0:T(8,128)} %copy-done.1), kind=kOutput, calls=%fused_computation.3 | convolution fusion | flops 1207959552 | bytes 4718592 | tf_op jit(solution)/shard_map/nij,njk->nik/dot_general | solution.py:22
  10.1 0.0 copy-start.2
  10.1 0.9 fusion.6.refs_12_
  11.0 0.0 copy-done.13
  11.1 0.2 multiply_reduce_fusion.3
  11.3 0.0 copy-start.11
  11.3 0.1 fusion.21
  11.4 0.4 multiply_reduce_fusion.5
  11.8 0.4 fusion.11
  12.2 0.1 pad.14.clone
  12.3 0.1 maximum_maximum_fusion.own_ref
  12.4 3.0 %collective-permute-start = (f32[264,256]{1,0:T(8,128)S(1)}, f32[264,256]{1,0:T(8,128)S(1)}, u32[]{:S(2)}, u32[]{:S(2)}) collective-permute-start(f32[264,256]{1,0:T(8,128)S(1)} %maximum_maximum_fusion.own_ref), channel_id=1, source_target_pairs={{0,16},{16,0},{1,17},{17,1},{2,18},{18,2},{3,19},{19,3},{4,20},{20... | collective-permute-start | bytes 811016 | tf_op jit(solution)/shard_map/ppermute | solution.py:144
  15.4 6.5 %collective-permute-done.got_ref = f32[264,256]{1,0:T(8,128)S(1)} collective-permute-done((f32[264,256]{1,0:T(8,128)S(1)}, f32[264,256]{1,0:T(8,128)S(1)}, u32[]{:S(2)}, u32[]{:S(2)}) %collective-permute-start) | collective-permute-done | bytes 270368 | tf_op jit(solution)/shard_map/ppermute | solution.py:144
  21.9 0.7 copy-done.4
  22.6 2.2 %shard_map.67.own_ref = f32[264,256]{1,0:T(8,128)} custom-call(f32[264,256]{1,0:T(8,128)} %copy-done.8, f32[264,256]{1,0:T(8,128)} %copy-done.4), custom_call_target="tpu_custom_call" | custom-call | tf_op jit(solution)/shard_map/pallas_call | solution.py:79
  24.8 0.0 collective-permute-start.1
  24.8 1.8 %collective-permute-done.1.got_ref = f32[264,256]{1,0:T(8,128)S(1)} collective-permute-done((f32[264,256]{1,0:T(8,128)}, f32[264,256]{1,0:T(8,128)S(1)}, u32[]{:S(2)}, u32[]{:S(2)}) %collective-permute-start.1) | collective-permute-done | bytes 270368 | tf_op jit(solution)/shard_map/ppermute | solution.py:144
  26.6 0.7 copy-done.5
  27.3 2.1 %shard_map.68.own_ref = f32[264,256]{1,0:T(8,128)} custom-call(f32[264,256]{1,0:T(8,128)} %shard_map.67.own_ref, f32[264,256]{1,0:T(8,128)} %copy-done.5), custom_call_target="tpu_custom_call" | custom-call | tf_op jit(solution)/shard_map/pallas_call | solution.py:79
  29.4 1.7 %collective-permute-start.2 = (f32[264,256]{1,0:T(8,128)}, f32[264,256]{1,0:T(8,128)S(1)}, u32[]{:S(2)}, u32[]{:S(2)}) collective-permute-start(f32[264,256]{1,0:T(8,128)} %shard_map.68.own_ref), channel_id=1, source_target_pairs={{0,2},{16,18},{1,3},{17,19},{2,0},{18,16},{3,1},{19,17},{4,6},{20,... | collective-permute-start | bytes 811016 | tf_op jit(solution)/shard_map/ppermute | solution.py:144
  31.1 0.8 pad_maximum_fusion.refs_14_
  32.0 6.2 %collective-permute-done.2.got_ref = f32[264,256]{1,0:T(8,128)S(1)} collective-permute-done((f32[264,256]{1,0:T(8,128)}, f32[264,256]{1,0:T(8,128)S(1)}, u32[]{:S(2)}, u32[]{:S(2)}) %collective-permute-start.2) | collective-permute-done | bytes 270368 | tf_op jit(solution)/shard_map/ppermute | solution.py:144
  38.2 0.7 copy-done.6
  38.8 2.1 %shard_map.69.own_ref = f32[264,256]{1,0:T(8,128)} custom-call(f32[264,256]{1,0:T(8,128)} %shard_map.68.own_ref, f32[264,256]{1,0:T(8,128)} %copy-done.6), custom_call_target="tpu_custom_call" | custom-call | tf_op jit(solution)/shard_map/pallas_call | solution.py:79
  41.0 1.8 %collective-permute-start.3 = (f32[264,256]{1,0:T(8,128)}, f32[264,256]{1,0:T(8,128)S(1)}, u32[]{:S(2)}, u32[]{:S(2)}) collective-permute-start(f32[264,256]{1,0:T(8,128)} %shard_map.69.own_ref), channel_id=1, source_target_pairs={{0,4},{16,20},{1,5},{17,21},{2,6},{18,22},{3,7},{19,23},{4,0},{20,... | collective-permute-start | bytes 811016 | tf_op jit(solution)/shard_map/ppermute | solution.py:144
  42.8 0.7 fusion.13.sq_ref
  43.5 5.4 %collective-permute-done.3.got_ref = f32[264,256]{1,0:T(8,128)S(1)} collective-permute-done((f32[264,256]{1,0:T(8,128)}, f32[264,256]{1,0:T(8,128)S(1)}, u32[]{:S(2)}, u32[]{:S(2)}) %collective-permute-start.3) | collective-permute-done | bytes 270368 | tf_op jit(solution)/shard_map/ppermute | solution.py:144
  48.9 0.7 copy-done.7
  49.6 2.1 %shard_map.70 = f32[264,256]{1,0:T(8,128)} custom-call(f32[264,256]{1,0:T(8,128)} %shard_map.69.own_ref, f32[264,256]{1,0:T(8,128)} %copy-done.7), custom_call_target="tpu_custom_call" | custom-call | tf_op jit(solution)/shard_map/pallas_call | solution.py:79
  51.8 0.7 slice.130
  52.5 2.8 %collective-permute-start.4 = (f32[8,256]{1,0:T(8,128)S(1)}, f32[8,256]{1,0:T(8,128)S(1)}, u32[]{:S(2)}, u32[]{:S(2)}) collective-permute-start(f32[8,256]{1,0:T(8,128)S(1)} %slice.130), channel_id=1, source_target_pairs={{0,8},{16,24},{1,9},{17,25},{2,10},{18,26},{3,11},{19,27},{4,12},{... | collective-permute-start | bytes 24584 | tf_op jit(solution)/shard_map/ppermute | solution.py:144
  55.2 0.6 pad_maximum_fusion.1.refs_15_
  55.8 0.6 compare_reduce_fusion
  56.5 0.6 broadcast_in_dim.7.sv_ref
  57.1 2.1 %shard_map.71 = (f32[256,256]{1,0:T(8,128)}, f32[8,256]{1,0:T(8,128)}) custom-call(f32[264,256]{1,0:T(8,128)} %copy-done.4, f32[256,256]{1,0:T(8,128)} %fusion.13.sq_ref, f32[8,256]{1,0:T(8,128)} %broadcast_in_dim.7.sv_ref), custom_call_target="tpu_custom_call" | custom-call | tf_op jit(solution)/shard_map/pallas_call | solution.py:80
  59.2 2.1 %shard_map.72 = (f32[256,256]{1,0:T(8,128)}, f32[8,256]{1,0:T(8,128)}) custom-call(f32[264,256]{1,0:T(8,128)} %copy-done.5, f32[256,256]{1,0:T(8,128)} %get-tuple-element.23.sq_ref, f32[8,256]{1,0:T(8,128)} %get-tuple-element.24.sv_ref), custom_call_target="tpu_custom_call" | custom-call | tf_op jit(solution)/shard_map/pallas_call | solution.py:80
  61.3 2.1 %shard_map.73 = (f32[256,256]{1,0:T(8,128)}, f32[8,256]{1,0:T(8,128)}) custom-call(f32[264,256]{1,0:T(8,128)} %copy-done.6, f32[256,256]{1,0:T(8,128)} %get-tuple-element.25.sq_ref, f32[8,256]{1,0:T(8,128)} %get-tuple-element.26.sv_ref), custom_call_target="tpu_custom_call" | custom-call | tf_op jit(solution)/shard_map/pallas_call | solution.py:80
  63.4 2.1 %shard_map.74 = (f32[256,256]{1,0:T(8,128)}, f32[8,256]{1,0:T(8,128)}) custom-call(f32[264,256]{1,0:T(8,128)} %copy-done.7, f32[256,256]{1,0:T(8,128)} %get-tuple-element.27.sq_ref, f32[8,256]{1,0:T(8,128)} %get-tuple-element.28.sv_ref), custom_call_target="tpu_custom_call" | custom-call | tf_op jit(solution)/shard_map/pallas_call | solution.py:80
  65.6 0.0 collective-permute-done.4.refs_0_
  65.6 0.6 copy-done.15
  66.2 6.1 %shard_map.75 = f32[24,256]{1,0:T(8,128)} custom-call(f32[8,256]{1,0:T(8,128)} %copy-done.15, f32[256,256]{1,0:T(8,128)} %get-tuple-element.29.refs_1_, f32[8,256]{1,0:T(8,128)} %get-tuple-element.30.refs_2_, f32[24,256]{1,0:T(8,128)} %bitcast.38, f32[24,2,128]{2,1,0:T(2,128)} %bitcast.39, f32[24,256]{1,0:T(8,128)} %bitcast.41, ...), custom_call_target="tpu_custom_call" | custom-call | tf_op jit(solution)/shard_map/pallas_call | solution.py:130
  72.3 1.3 %multiply_reduce_fusion.6 = f32[]{:T(128)} fusion(f32[24,256]{1,0:T(8,128)} %shard_map.75, f32[1,24,256]{2,1,0:T(8,128)S(1)} %copy-done.12), kind=kLoop, calls=%fused_computation.28 | loop fusion | flops 12287 | bytes 49156 | tf_op jit(solution)/shard_map/reduce_sum | solution.py:181
  74.3 1.0 %fusion.15 = f32[128,128]{1,0:T(8,128)S(1)} fusion(f32[24,128]{1,0:T(8,128)S(1)} %bitcast.43, f32[24,256]{1,0:T(8,128)} %shard_map.75), kind=kOutput, calls=%fused_computation.29 | convolution fusion | flops 4718592 | bytes 90112 | tf_op jit(solution)/shard_map/dot_general | solution.py:178
  75.9 1.0 %convolution_add_fusion = f32[128,128]{1,0:T(8,128)S(1)} fusion(f32[128,128]{1,0:T(8,128)S(1)} %fusion.15, f32[24,128]{1,0:T(8,128)S(1)} %bitcast.42, f32[24,256]{1,0:T(8,128)} %shard_map.75), kind=kOutput, calls=%fused_computation.9 | convolution fusion | flops 4734976 | bytes 155648 | tf_op jit(solution)/shard_map/dot_general | solution.py:175
  76.9 1.6 %collective-permute-start.5 = (f32[129,128]{1,0:T(8,128)S(1)}, f32[129,128]{1,0:T(8,128)S(1)}, u32[]{:S(2)}, u32[]{:S(2)}) collective-permute-start(f32[129,128]{1,0:T(8,128)S(1)} %select_maximum_fusion), channel_id=1, source_target_pairs={{0,16},{16,0},{1,17},{17,1},{2,18},{18,2},{3,19},{19,3},{4,20},{20... | collective-permute-start | bytes 198152 | tf_op jit(solution)/shard_map/ppermute | solution.py:144
  78.5 2.8 %collective-permute-done.5 = f32[129,128]{1,0:T(8,128)S(1)} collective-permute-done((f32[129,128]{1,0:T(8,128)S(1)}, f32[129,128]{1,0:T(8,128)S(1)}, u32[]{:S(2)}, u32[]{:S(2)}) %collective-permute-start.5) | collective-permute-done | bytes 66080 | tf_op jit(solution)/shard_map/ppermute | solution.py:144
  81.3 0.1 collective-permute-start.6
  81.4 1.2 %collective-permute-done.6 = f32[129,128]{1,0:T(8,128)S(1)} collective-permute-done((f32[129,128]{1,0:T(8,128)S(1)}, f32[129,128]{1,0:T(8,128)S(1)}, u32[]{:S(2)}, u32[]{:S(2)}) %collective-permute-start.6) | collective-permute-done | bytes 66080 | tf_op jit(solution)/shard_map/ppermute | solution.py:144
  82.7 1.5 %collective-permute-start.7 = (f32[129,128]{1,0:T(8,128)S(1)}, f32[129,128]{1,0:T(8,128)S(1)}, u32[]{:S(2)}, u32[]{:S(2)}) collective-permute-start(f32[129,128]{1,0:T(8,128)S(1)} %add.44), channel_id=1, source_target_pairs={{0,2},{16,18},{1,3},{17,19},{2,0},{18,16},{3,1},{19,17},{4,6},{20,... | collective-permute-start | bytes 198152 | tf_op jit(solution)/shard_map/ppermute | solution.py:144
  84.2 2.8 %collective-permute-done.7 = f32[129,128]{1,0:T(8,128)S(1)} collective-permute-done((f32[129,128]{1,0:T(8,128)S(1)}, f32[129,128]{1,0:T(8,128)S(1)}, u32[]{:S(2)}, u32[]{:S(2)}) %collective-permute-start.7) | collective-permute-done | bytes 66080 | tf_op jit(solution)/shard_map/ppermute | solution.py:144
  87.0 1.6 %collective-permute-start.8 = (f32[129,128]{1,0:T(8,128)S(1)}, f32[129,128]{1,0:T(8,128)S(1)}, u32[]{:S(2)}, u32[]{:S(2)}) collective-permute-start(f32[129,128]{1,0:T(8,128)S(1)} %add.45), channel_id=1, source_target_pairs={{0,4},{16,20},{1,5},{17,21},{2,6},{18,22},{3,7},{19,23},{4,0},{20,... | collective-permute-start | bytes 198152 | tf_op jit(solution)/shard_map/ppermute | solution.py:144
  88.7 2.7 %collective-permute-done.8 = f32[129,128]{1,0:T(8,128)S(1)} collective-permute-done((f32[129,128]{1,0:T(8,128)S(1)}, f32[129,128]{1,0:T(8,128)S(1)}, u32[]{:S(2)}, u32[]{:S(2)}) %collective-permute-start.8) | collective-permute-done | bytes 66080 | tf_op jit(solution)/shard_map/ppermute | solution.py:144
  91.4 0.2 collective-permute-start.9
  91.7 5.0 %collective-permute-done.9 = f32[129,128]{1,0:T(8,128)S(1)} collective-permute-done((f32[129,128]{1,0:T(8,128)S(1)}, f32[129,128]{1,0:T(8,128)S(1)}, u32[]{:S(2)}, u32[]{:S(2)}) %collective-permute-start.9) | collective-permute-done | bytes 66080 | tf_op jit(solution)/shard_map/ppermute | solution.py:144
  96.7 0.5 slice.136
  97.2 0.6 slice.135
  (39 shorter events, 0.2 us)
Async XLA Ops:
  0.6 2.9 %copy-start = (bf16[1,24,256,256]{3,2,1,0:T(8,128)(2,1)S(1)}, bf16[1,24,256,256]{3,2,1,0:T(8,128)(2,1)}, u32[]{:S(2)}) copy-start(bf16[1,24,256,256]{3,2,1,0:T(8,128)(2,1)} %param.6) | copy-start | bytes 9437188
  3.2 1.4 %copy-start.9 = (f32[24,256]{1,0:T(8,128)}, f32[24,256]{1,0:T(8,128)S(1)}, u32[]{:S(2)}) copy-start(f32[24,256]{1,0:T(8,128)S(1)} %multiply_reduce_fusion.refs_7_) | copy-start | bytes 73732
  4.0 0.6 copy-start.10
  4.6 1.6 %copy-start.1 = (f32[12,256,256]{2,1,0:T(8,128)}, f32[12,256,256]{2,1,0:T(8,128)S(1)}, u32[]{:S(2)}) copy-start(f32[12,256,256]{2,1,0:T(8,128)S(1)} %fusion.2.refs_8_) | copy-start | bytes 9437188
  6.6 4.5 %copy-start.13 = (f32[6,256]{1,0:T(8,128)}, f32[6,256]{1,0:T(8,128)S(1)}, u32[]{:S(2)}) copy-start(f32[6,256]{1,0:T(8,128)S(1)} %add.38.refs_11_) | copy-start | bytes 18436
  10.1 14.7 %copy-start.2 = (f32[6,256,256]{2,1,0:T(8,128)}, f32[6,256,256]{2,1,0:T(8,128)S(1)}, u32[]{:S(2)}) copy-start(f32[6,256,256]{2,1,0:T(8,128)S(1)} %fusion.refs_10_) | copy-start | bytes 4718596
  11.1 20.9 %copy-start.3 = (f32[3,256,256]{2,1,0:T(8,128)}, f32[3,256,256]{2,1,0:T(8,128)S(1)}, u32[]{:S(2)}) copy-start(f32[3,256,256]{2,1,0:T(8,128)S(1)} %fusion.6.refs_12_) | copy-start | bytes 2359300
  11.3 29.7 %copy-start.14 = (f32[3,256]{1,0:T(4,128)}, f32[3,256]{1,0:T(4,128)S(1)}, u32[]{:S(2)}) copy-start(f32[3,256]{1,0:T(4,128)S(1)} %add.39.refs_13_) | copy-start | bytes 9220
  11.3 32.2 %copy-start.11 = (f32[1,24,2,128]{3,2,1,0:T(2,128)S(1)}, f32[1,24,2,128]{3,2,1,0:T(2,128)}, u32[]{:S(2)}) copy-start(f32[1,24,2,128]{3,2,1,0:T(2,128)} %param.8) | copy-start | bytes 73732
  12.4 9.5 %copy-start.8 = (f32[264,256]{1,0:T(8,128)}, f32[264,256]{1,0:T(8,128)S(1)}, u32[]{:S(2)}) copy-start(f32[264,256]{1,0:T(8,128)S(1)} %maximum_maximum_fusion.own_ref) | copy-start | bytes 811012
  12.4 9.5 %collective-permute-start = (f32[264,256]{1,0:T(8,128)S(1)}, f32[264,256]{1,0:T(8,128)S(1)}, u32[]{:S(2)}, u32[]{:S(2)}) collective-permute-start(f32[264,256]{1,0:T(8,128)S(1)} %maximum_maximum_fusion.own_ref), channel_id=1, source_target_pairs={{0,16},{16,0},{1,17},{17,1},{2,18},{18,2},{3,19},{19,3},{4,20},{20... | collective-permute-start | bytes 811016 | tf_op jit(solution)/shard_map/ppermute | solution.py:144
  21.9 0.7 copy-start.4
  24.8 1.8 %collective-permute-start.1 = (f32[264,256]{1,0:T(8,128)}, f32[264,256]{1,0:T(8,128)S(1)}, u32[]{:S(2)}, u32[]{:S(2)}) collective-permute-start(f32[264,256]{1,0:T(8,128)} %shard_map.67.own_ref), channel_id=1, source_target_pairs={{0,1},{16,17},{1,0},{17,16},{2,3},{18,19},{3,2},{19,18},{4,5},{20,... | collective-permute-start | bytes 811016 | tf_op jit(solution)/shard_map/ppermute | solution.py:144
  26.6 0.7 copy-start.5
  29.4 8.7 %collective-permute-start.2 = (f32[264,256]{1,0:T(8,128)}, f32[264,256]{1,0:T(8,128)S(1)}, u32[]{:S(2)}, u32[]{:S(2)}) collective-permute-start(f32[264,256]{1,0:T(8,128)} %shard_map.68.own_ref), channel_id=1, source_target_pairs={{0,2},{16,18},{1,3},{17,19},{2,0},{18,16},{3,1},{19,17},{4,6},{20,... | collective-permute-start | bytes 811016 | tf_op jit(solution)/shard_map/ppermute | solution.py:144
  38.1 0.7 copy-start.6
  41.0 8.0 %collective-permute-start.3 = (f32[264,256]{1,0:T(8,128)}, f32[264,256]{1,0:T(8,128)S(1)}, u32[]{:S(2)}, u32[]{:S(2)}) collective-permute-start(f32[264,256]{1,0:T(8,128)} %shard_map.69.own_ref), channel_id=1, source_target_pairs={{0,4},{16,20},{1,5},{17,21},{2,6},{18,22},{3,7},{19,23},{4,0},{20,... | collective-permute-start | bytes 811016 | tf_op jit(solution)/shard_map/ppermute | solution.py:144
  48.9 0.7 copy-start.7
  52.5 13.1 %collective-permute-start.4 = (f32[8,256]{1,0:T(8,128)S(1)}, f32[8,256]{1,0:T(8,128)S(1)}, u32[]{:S(2)}, u32[]{:S(2)}) collective-permute-start(f32[8,256]{1,0:T(8,128)S(1)} %slice.130), channel_id=1, source_target_pairs={{0,8},{16,24},{1,9},{17,25},{2,10},{18,26},{3,11},{19,27},{4,12},{... | collective-permute-start | bytes 24584 | tf_op jit(solution)/shard_map/ppermute | solution.py:144
  65.6 0.6 copy-start.15
  66.2 6.1 %copy-start.12 = (f32[1,24,256]{2,1,0:T(8,128)S(1)}, f32[1,24,256]{2,1,0:T(8,128)}, u32[]{:S(2)}) copy-start(f32[1,24,256]{2,1,0:T(8,128)} %param.9) | copy-start | bytes 73732
  76.9 4.4 %collective-permute-start.5 = (f32[129,128]{1,0:T(8,128)S(1)}, f32[129,128]{1,0:T(8,128)S(1)}, u32[]{:S(2)}, u32[]{:S(2)}) collective-permute-start(f32[129,128]{1,0:T(8,128)S(1)} %select_maximum_fusion), channel_id=1, source_target_pairs={{0,16},{16,0},{1,17},{17,1},{2,18},{18,2},{3,19},{19,3},{4,20},{20... | collective-permute-start | bytes 198152 | tf_op jit(solution)/shard_map/ppermute | solution.py:144
  81.3 1.3 %collective-permute-start.6 = (f32[129,128]{1,0:T(8,128)S(1)}, f32[129,128]{1,0:T(8,128)S(1)}, u32[]{:S(2)}, u32[]{:S(2)}) collective-permute-start(f32[129,128]{1,0:T(8,128)S(1)} %fusion.19), channel_id=1, source_target_pairs={{0,1},{16,17},{1,0},{17,16},{2,3},{18,19},{3,2},{19,18},{4,5},{20,... | collective-permute-start | bytes 198152 | tf_op jit(solution)/shard_map/ppermute | solution.py:144
  82.7 4.4 %collective-permute-start.7 = (f32[129,128]{1,0:T(8,128)S(1)}, f32[129,128]{1,0:T(8,128)S(1)}, u32[]{:S(2)}, u32[]{:S(2)}) collective-permute-start(f32[129,128]{1,0:T(8,128)S(1)} %add.44), channel_id=1, source_target_pairs={{0,2},{16,18},{1,3},{17,19},{2,0},{18,16},{3,1},{19,17},{4,6},{20,... | collective-permute-start | bytes 198152 | tf_op jit(solution)/shard_map/ppermute | solution.py:144
  87.0 4.4 %collective-permute-start.8 = (f32[129,128]{1,0:T(8,128)S(1)}, f32[129,128]{1,0:T(8,128)S(1)}, u32[]{:S(2)}, u32[]{:S(2)}) collective-permute-start(f32[129,128]{1,0:T(8,128)S(1)} %add.45), channel_id=1, source_target_pairs={{0,4},{16,20},{1,5},{17,21},{2,6},{18,22},{3,7},{19,23},{4,0},{20,... | collective-permute-start | bytes 198152 | tf_op jit(solution)/shard_map/ppermute | solution.py:144
  91.4 5.3 %collective-permute-start.9 = (f32[129,128]{1,0:T(8,128)S(1)}, f32[129,128]{1,0:T(8,128)S(1)}, u32[]{:S(2)}, u32[]{:S(2)}) collective-permute-start(f32[129,128]{1,0:T(8,128)S(1)} %add.46), channel_id=1, source_target_pairs={{0,8},{16,24},{1,9},{17,25},{2,10},{18,26},{3,11},{19,27},{4,12},{... | collective-permute-start | bytes 198152 | tf_op jit(solution)/shard_map/ppermute | solution.py:144

commit v11 on v9

--- a/solution.py
+++ b/solution.py
@@ -96,7 +96,7 @@
     def kernel(*refs):
         rv_ref, sq_ref, sv_ref, grads_ref, load_ref, resp_ref = refs[:6]
         tree = refs[6 : 6 + 2 * depth]
-        out_ref = refs[6 + 2 * depth]
+        out_ref, grad_ref = refs[6 + 2 * depth :]
         me = lax.axis_index("outer") * lax.axis_size("inner") + lax.axis_index("inner")
         lower = (me // d) % 2 == 0
         sv = sv_ref[0:1, :]
@@ -113,8 +113,15 @@
             if n % 2:
                 new.append(rows[-1])
             rows = new
+        kernel_grad = jnp.zeros((stations, stations), jnp.float32)
         for t, row in enumerate(rows):
-            out_ref[t : t + 1, :] = grads_ref[t : t + 1, :] + row
+            rate = grads_ref[t : t + 1, :] + row
+            out_ref[t : t + 1, :] = rate
+            col = column(rate)
+            kernel_grad = kernel_grad + col[:stations] * load_ref[t, 0:1, :]
+            kernel_grad = kernel_grad + col[stations:] * load_ref[t, 1:2, :]
+        grad_ref[0:stations, :] = kernel_grad
+        grad_ref[stations:, :] = jnp.zeros((8, stations), jnp.float32)
 
     def run(rv, sq, sv, grads, loads, resp, levels):
         args = [rv, sq, sv, grads, loads, resp]
@@ -122,7 +129,10 @@
             args += list(levels[level])
         return pl.pallas_call(
             kernel,
-            out_shape=jax.ShapeDtypeStruct(grads.shape, jnp.float32),
+            out_shape=(
+                jax.ShapeDtypeStruct(grads.shape, jnp.float32),
+                jax.ShapeDtypeStruct((stations + 8, stations), jnp.float32),
+            ),
         )(*args)
 
     return run
@@ -161,19 +171,11 @@
         d *= 2
     rv = exchange(packed[width:], d, count)
     sizes = [level[0].shape[0] for level in levels]
-    length_rates = finish(d, sizes, width, stations)(
+    length_rates, packed = finish(d, sizes, width, stations)(
         rv, sq, sv, grads, station_loadings[0], offset_response[0], levels
     )
-    argument_values = station_loadings[0]
-    local_kernel = jnp.dot(
-        length_rates[:, :stations].T, argument_values[:, 0, :], precision=EXACT
-    )
-    local_kernel = local_kernel + jnp.dot(
-        length_rates[:, stations:].T, argument_values[:, 1, :], precision=EXACT
-    )
     local_noise = -jnp.sum(length_rates * offset_response[0])
-    noise_row = jnp.zeros((1, local_kernel.shape[1]), jnp.float32).at[0, 0].set(local_noise)
-    packed = jnp.concatenate([local_kernel, noise_row], axis=0)
+    packed = packed.at[stations, 0].set(local_noise)
     d = 1
     while d < count:
         packed = packed + exchange(packed, d, count)

time: 95.6 us -> 92.8 us (0.971)
  matrix products: 12 us -> 5.79 us
  local copies, waits for them, and re-layouts: 5.71 us -> 8.65 us
  Pallas kernels: 16.3 us -> 18 us
  other arithmetic: 9.4 us -> 8.19 us
    dot_general x4, matrix products: 7.83 us -> 5.22 us  [matmat(): jnp.einsum('nij,njk->nik', later.astype(jnp.float32), earlier.astype(jnp....]
    dot_general x2 -> x0, matrix products: 1.99 us -> none  [the longest x1 1 us: body(): jnp.dot(length_rates[:, :stations].T, argument_values[:, 0, :], precision...]
    pallas_call x1, Pallas kernels: 6.09 us -> 7.74 us  [run(): pl.pallas_call(kernel, out_shape=(jax.ShapeDtypeStruct(grads.shape, jnp.f...]
    unnamed x30, local copies, waits for them, and re-layouts: 3.04 us -> 4.69 us
    dot_general x1, matrix products: 2.22 us -> 0.57 us  [matmat(): jnp.einsum('nij,njk->nik', later, earlier, preferred_element_type=jnp.flo...]
    reduce_sum x4, other arithmetic: 4.97 us -> 3.55 us  [vecmat(): return jnp.sum(v[:, :, None] * q.astype(jnp.float32), axis=1)]
    scatter x0 -> x1, local copies, waits for them, and re-layouts: none -> 1.29 us  [body(): packed = packed.at[stations, 0].set(local_noise)]
  transfers between devices with their start and end apart: 10 -> 10, of which waited for: 10 -> 10; matrix products, arithmetic and copies ran while one was open for 3% -> 2% of each run, Pallas kernels for 0% -> 0%
where the time goes in v11:
time: 92.8 us; the launch traced here: 92.4 us
  waiting for transfers between devices  32.8 us (35%)
  Pallas kernels  18 us (19%)
  starting transfers between devices  17.4 us (19%)
  local copies, waits for them, and re-layouts  8.65 us (9%)
  other arithmetic  8.19 us (9%)
  matrix products  5.79 us (6%)
  between operations  1.52 us (2%)
    ppermute x10, waiting for transfers between devices, exchange(): lax.ppermute(x, AXES, [(place(j), place(j ^ mask)) for j in range(count)])  32.8 us
    ppermute x10, starting transfers between devices, exchange(): lax.ppermute(x, AXES, [(place(j), place(j ^ mask)) for j in range(count)])  17.4 us
    pallas_call x4, Pallas kernels, run(): pl.pallas_call(kernel, out_shape=(jax.ShapeDtypeStruct(own.shape, jnp.flo...  10.3 us
    pallas_call x1, Pallas kernels, run(): pl.pallas_call(kernel, out_shape=(jax.ShapeDtypeStruct(grads.shape, jnp.f...  7.74 us
    dot_general x4, matrix products, matmat(): jnp.einsum('nij,njk->nik', later.astype(jnp.float32), earlier.astype(jnp....  5.22 us
    unnamed x30, local copies, waits for them, and re-layouts  4.69 us
    reduce_sum x4, other arithmetic, vecmat(): return jnp.sum(v[:, :, None] * q.astype(jnp.float32), axis=1)  3.55 us
  transfers between devices with their start and end apart: 10, of which 10 were waited for; matrix products, arithmetic and copies ran while one was open for 2% of the time, Pallas kernels for 0%

profile of v11, /device:TPU:0, one launch (start us, length us, event | category | flops | bytes accessed | tf_op | source)
XLA Modules:
  0.0 92.4 jit_solution(16544503418424108587)
XLA Ops:
  0.6 0.0 copy-start
  0.6 2.6 %multiply_reduce_fusion.refs_7_ = f32[24,256]{1,0:T(8,128)S(1)} fusion(f32[24,256]{1,0:T(8,128)} %bitcast.32, bf16[1,24,256,256]{3,2,1,0:T(8,128)(2,1)} %param.6), kind=kLoop, calls=%fused_computation | loop fusion | flops 4712448 | bytes 3194880 | tf_op jit(solution)/shard_map/reduce_sum | solution.py:12
  3.2 0.0 copy-start.5
  3.3 0.2 copy-done
  3.5 0.5 multiply_reduce_fusion.1
  4.1 0.6 fusion.2.refs_8_
  4.6 0.0 copy-done.5
  4.6 0.0 copy-done.10
  4.6 0.0 copy-start.1
  4.7 1.6 %copy-done.1 = f32[12,256,256]{2,1,0:T(8,128)} copy-done((f32[12,256,256]{2,1,0:T(8,128)}, f32[12,256,256]{2,1,0:T(8,128)S(1)}, u32[]{:S(2)}) %copy-start.1) | copy-done | bytes 3145752
  6.3 0.3 multiply_reduce_fusion.2
  6.6 0.0 copy-start.12
  6.6 3.5 %fusion.refs_10_ = f32[6,256,256]{2,1,0:T(8,128)S(1)} fusion(f32[12,256,256]{2,1,0:T(8,128)} %copy-done.1), kind=kOutput, calls=%fused_computation.3 | convolution fusion | flops 1207959552 | bytes 4718592 | tf_op jit(solution)/shard_map/nij,njk->nik/dot_general | solution.py:22
  10.2 0.9 fusion.6.refs_12_
  11.1 0.0 copy-done.12
  11.1 0.0 copy-start.3
  11.1 0.2 multiply_reduce_fusion.3
  11.3 0.1 fusion.17
  11.5 0.4 multiply_reduce_fusion.5
  11.9 0.4 fusion.11
  12.3 0.1 pad.10.clone
  12.3 0.1 maximum_maximum_fusion.own_ref
  12.4 0.0 copy-start.4
  12.4 3.0 %collective-permute-start = (f32[264,256]{1,0:T(8,128)S(1)}, f32[264,256]{1,0:T(8,128)S(1)}, u32[]{:S(2)}, u32[]{:S(2)}) collective-permute-start(f32[264,256]{1,0:T(8,128)S(1)} %maximum_maximum_fusion.own_ref), channel_id=1, source_target_pairs={{0,16},{16,0},{1,17},{17,1},{2,18},{18,2},{3,19},{19,3},{4,20},{20... | collective-permute-start | bytes 811016 | tf_op jit(solution)/shard_map/ppermute | solution.py:147
  15.5 0.7 fusion.13.sq_ref
  16.2 5.8 %collective-permute-done.got_ref = f32[264,256]{1,0:T(8,128)S(1)} collective-permute-done((f32[264,256]{1,0:T(8,128)S(1)}, f32[264,256]{1,0:T(8,128)S(1)}, u32[]{:S(2)}, u32[]{:S(2)}) %collective-permute-start) | collective-permute-done | bytes 270368 | tf_op jit(solution)/shard_map/ppermute | solution.py:147
  22.0 0.6 broadcast_in_dim.7.sv_ref
  22.6 0.1 copy-done.7
  22.7 2.6 %shard_map.67 = (f32[264,256]{1,0:T(8,128)}, f32[256,256]{1,0:T(8,128)}, f32[8,256]{1,0:T(8,128)}) custom-call(f32[264,256]{1,0:T(8,128)} %copy-done.4, f32[264,256]{1,0:T(8,128)} %copy-done.7, f32[256,256]{1,0:T(8,128)} %fusion.13.sq_ref, f32[8,256]{1,0:T(8,128)} %broadcast_in_dim.7.sv_ref), custom_call_target="tpu_custom_call" | custom-call | tf_op jit(solution)/shard_map/pallas_call | solution.py:73
  25.3 0.0 collective-permute-start.1
  25.3 1.8 %collective-permute-done.1.got_ref = f32[264,256]{1,0:T(8,128)S(1)} collective-permute-done((f32[264,256]{1,0:T(8,128)}, f32[264,256]{1,0:T(8,128)S(1)}, u32[]{:S(2)}, u32[]{:S(2)}) %collective-permute-start.1) | collective-permute-done | bytes 270368 | tf_op jit(solution)/shard_map/ppermute | solution.py:147
  27.0 0.7 copy-done.8
  27.7 2.6 %shard_map.68 = (f32[264,256]{1,0:T(8,128)}, f32[256,256]{1,0:T(8,128)}, f32[8,256]{1,0:T(8,128)}) custom-call(f32[264,256]{1,0:T(8,128)} %get-tuple-element.29.own_ref, f32[264,256]{1,0:T(8,128)} %copy-done.8, f32[256,256]{1,0:T(8,128)} %get-tuple-element.30.sq_ref, f32[8,256]{1,0:T(8,128)} %get-tuple-element.31.sv_ref), custom_call_target="tpu_custom_call" | custom-call | tf_op jit(solution)/shard_map/pallas_call | solution.py:73
  30.3 1.7 %collective-permute-start.2 = (f32[264,256]{1,0:T(8,128)}, f32[264,256]{1,0:T(8,128)S(1)}, u32[]{:S(2)}, u32[]{:S(2)}) collective-permute-start(f32[264,256]{1,0:T(8,128)} %get-tuple-element.32.own_ref), channel_id=1, source_target_pairs={{0,2},{16,18},{1,3},{17,19},{2,0},{18,16},{3,1},{19,17},{4,6},{20,... | collective-permute-start | bytes 811016 | tf_op jit(solution)/shard_map/ppermute | solution.py:147
  32.0 7.0 %collective-permute-done.2.got_ref = f32[264,256]{1,0:T(8,128)S(1)} collective-permute-done((f32[264,256]{1,0:T(8,128)}, f32[264,256]{1,0:T(8,128)S(1)}, u32[]{:S(2)}, u32[]{:S(2)}) %collective-permute-start.2) | collective-permute-done | bytes 270368 | tf_op jit(solution)/shard_map/ppermute | solution.py:147
  39.0 0.7 copy-done.9
  39.7 2.6 %shard_map.69 = (f32[264,256]{1,0:T(8,128)}, f32[256,256]{1,0:T(8,128)}, f32[8,256]{1,0:T(8,128)}) custom-call(f32[264,256]{1,0:T(8,128)} %get-tuple-element.32.own_ref, f32[264,256]{1,0:T(8,128)} %copy-done.9, f32[256,256]{1,0:T(8,128)} %get-tuple-element.33.sq_ref, f32[8,256]{1,0:T(8,128)} %get-tuple-element.34.sv_ref), custom_call_target="tpu_custom_call" | custom-call | tf_op jit(solution)/shard_map/pallas_call | solution.py:73
  42.3 1.8 %collective-permute-start.3 = (f32[264,256]{1,0:T(8,128)}, f32[264,256]{1,0:T(8,128)S(1)}, u32[]{:S(2)}, u32[]{:S(2)}) collective-permute-start(f32[264,256]{1,0:T(8,128)} %get-tuple-element.35.own_ref), channel_id=1, source_target_pairs={{0,4},{16,20},{1,5},{17,21},{2,6},{18,22},{3,7},{19,23},{4,0},{20,... | collective-permute-start | bytes 811016 | tf_op jit(solution)/shard_map/ppermute | solution.py:147
  44.1 0.8 pad_maximum_fusion.refs_14_
  44.9 5.3 %collective-permute-done.3.got_ref = f32[264,256]{1,0:T(8,128)S(1)} collective-permute-done((f32[264,256]{1,0:T(8,128)}, f32[264,256]{1,0:T(8,128)S(1)}, u32[]{:S(2)}, u32[]{:S(2)}) %collective-permute-start.3) | collective-permute-done | bytes 270368 | tf_op jit(solution)/shard_map/ppermute | solution.py:147
  50.2 0.7 copy-done.6
  51.0 2.6 %shard_map.70 = (f32[264,256]{1,0:T(8,128)}, f32[256,256]{1,0:T(8,128)}, f32[8,256]{1,0:T(8,128)}) custom-call(f32[264,256]{1,0:T(8,128)} %get-tuple-element.35.own_ref, f32[264,256]{1,0:T(8,128)} %copy-done.6, f32[256,256]{1,0:T(8,128)} %get-tuple-element.36.sq_ref, f32[8,256]{1,0:T(8,128)} %get-tuple-element.37.sv_ref), custom_call_target="tpu_custom_call" | custom-call | tf_op jit(solution)/shard_map/pallas_call | solution.py:73
  53.5 0.7 slice.108
  54.2 2.8 %collective-permute-start.4 = (f32[8,256]{1,0:T(8,128)S(1)}, f32[8,256]{1,0:T(8,128)S(1)}, u32[]{:S(2)}, u32[]{:S(2)}) collective-permute-start(f32[8,256]{1,0:T(8,128)S(1)} %slice.108), channel_id=1, source_target_pairs={{0,8},{16,24},{1,9},{17,25},{2,10},{18,26},{3,11},{19,27},{4,12},{... | collective-permute-start | bytes 24584 | tf_op jit(solution)/shard_map/ppermute | solution.py:147
  57.0 0.6 pad_maximum_fusion.1.refs_15_
  57.6 1.2 %collective-permute-done.4.refs_0_ = f32[8,256]{1,0:T(8,128)S(1)} collective-permute-done((f32[8,256]{1,0:T(8,128)S(1)}, f32[8,256]{1,0:T(8,128)S(1)}, u32[]{:S(2)}, u32[]{:S(2)}) %collective-permute-start.4) | collective-permute-done | bytes 8224 | tf_op jit(solution)/shard_map/ppermute | solution.py:147
  58.8 0.6 copy-done.14
  59.4 7.7 %shard_map.71 = (f32[24,256]{1,0:T(8,128)}, f32[136,128]{1,0:T(8,128)}) custom-call(f32[8,256]{1,0:T(8,128)} %copy-done.14, f32[256,256]{1,0:T(8,128)} %get-tuple-element.39.refs_1_, f32[8,256]{1,0:T(8,128)} %get-tuple-element.40.refs_2_, f32[24,256]{1,0:T(8,128)} %bitcast.33, f32[24,2,128]{2,1,0:T(2,128)} %bitcast.36, f32[24,256]{1,0:T(8,128)} %bitcast.34, ...), custom_call_target="tpu_custom_call" | custom-call | tf_op jit(solution)/shard_map/pallas_call | solution.py:130
  67.1 0.0 copy-done.11
  67.1 1.3 %multiply_reduce_fusion.6 = f32[]{:T(128)} fusion(f32[24,256]{1,0:T(8,128)} %get-tuple-element.41, f32[1,24,256]{2,1,0:T(8,128)S(1)} %copy-done.11), kind=kLoop, calls=%fused_computation.25 | loop fusion | flops 12287 | bytes 49156 | tf_op jit(solution)/shard_map/reduce_sum | solution.py:177
  69.1 1.3 %scatter.4 = f32[136,128]{1,0:T(8,128)} dynamic-update-slice(f32[136,128]{1,0:T(8,128)} %get-tuple-element.42, f32[1,1]{1,0:T(1,128)} %bitcast.13, s32[]{:T(128)} %constant.32.clone.1, s32[]{:T(128)} %constant.33.clone.1) | dynamic-update-slice | bytes 12 | tf_op jit(solution)/shard_map/scatter | solution.py:178
  70.4 1.7 %collective-permute-start.5 = (f32[136,128]{1,0:T(8,128)}, f32[136,128]{1,0:T(8,128)S(1)}, u32[]{:S(2)}, u32[]{:S(2)}) collective-permute-start(f32[136,128]{1,0:T(8,128)} %scatter.4), channel_id=1, source_target_pairs={{0,16},{16,0},{1,17},{17,1},{2,18},{18,2},{3,19},{19,3},{4,20},{20... | collective-permute-start | bytes 208904 | tf_op jit(solution)/shard_map/ppermute | solution.py:147
  72.1 2.8 %collective-permute-done.5 = f32[136,128]{1,0:T(8,128)S(1)} collective-permute-done((f32[136,128]{1,0:T(8,128)}, f32[136,128]{1,0:T(8,128)S(1)}, u32[]{:S(2)}, u32[]{:S(2)}) %collective-permute-start.5) | collective-permute-done | bytes 69664 | tf_op jit(solution)/shard_map/ppermute | solution.py:147
  74.9 0.9 add.37
  75.8 0.1 collective-permute-start.6
  75.9 1.2 %collective-permute-done.6 = f32[136,128]{1,0:T(8,128)S(1)} collective-permute-done((f32[136,128]{1,0:T(8,128)S(1)}, f32[136,128]{1,0:T(8,128)S(1)}, u32[]{:S(2)}, u32[]{:S(2)}) %collective-permute-start.6) | collective-permute-done | bytes 69664 | tf_op jit(solution)/shard_map/ppermute | solution.py:147
  77.2 1.7 %collective-permute-start.7 = (f32[136,128]{1,0:T(8,128)S(1)}, f32[136,128]{1,0:T(8,128)S(1)}, u32[]{:S(2)}, u32[]{:S(2)}) collective-permute-start(f32[136,128]{1,0:T(8,128)S(1)} %add.38), channel_id=1, source_target_pairs={{0,2},{16,18},{1,3},{17,19},{2,0},{18,16},{3,1},{19,17},{4,6},{20,... | collective-permute-start | bytes 208904 | tf_op jit(solution)/shard_map/ppermute | solution.py:147
  78.9 2.6 %collective-permute-done.7 = f32[136,128]{1,0:T(8,128)S(1)} collective-permute-done((f32[136,128]{1,0:T(8,128)S(1)}, f32[136,128]{1,0:T(8,128)S(1)}, u32[]{:S(2)}, u32[]{:S(2)}) %collective-permute-start.7) | collective-permute-done | bytes 69664 | tf_op jit(solution)/shard_map/ppermute | solution.py:147
  81.6 1.8 %collective-permute-start.8 = (f32[136,128]{1,0:T(8,128)S(1)}, f32[136,128]{1,0:T(8,128)S(1)}, u32[]{:S(2)}, u32[]{:S(2)}) collective-permute-start(f32[136,128]{1,0:T(8,128)S(1)} %add.39), channel_id=1, source_target_pairs={{0,4},{16,20},{1,5},{17,21},{2,6},{18,22},{3,7},{19,23},{4,0},{20,... | collective-permute-start | bytes 208904 | tf_op jit(solution)/shard_map/ppermute | solution.py:147
  83.4 2.6 %collective-permute-done.8 = f32[136,128]{1,0:T(8,128)S(1)} collective-permute-done((f32[136,128]{1,0:T(8,128)S(1)}, f32[136,128]{1,0:T(8,128)S(1)}, u32[]{:S(2)}, u32[]{:S(2)}) %collective-permute-start.8) | collective-permute-done | bytes 69664 | tf_op jit(solution)/shard_map/ppermute | solution.py:147
  85.9 2.8 %collective-permute-start.9 = (f32[136,128]{1,0:T(8,128)S(1)}, f32[136,128]{1,0:T(8,128)S(1)}, u32[]{:S(2)}, u32[]{:S(2)}) collective-permute-start(f32[136,128]{1,0:T(8,128)S(1)} %add.40), channel_id=1, source_target_pairs={{0,8},{16,24},{1,9},{17,25},{2,10},{18,26},{3,11},{19,27},{4,12},{... | collective-permute-start | bytes 208904 | tf_op jit(solution)/shard_map/ppermute | solution.py:147
  88.8 2.4 %collective-permute-done.9 = f32[136,128]{1,0:T(8,128)S(1)} collective-permute-done((f32[136,128]{1,0:T(8,128)S(1)}, f32[136,128]{1,0:T(8,128)S(1)}, u32[]{:S(2)}, u32[]{:S(2)}) %collective-permute-start.9) | collective-permute-done | bytes 69664 | tf_op jit(solution)/shard_map/ppermute | solution.py:147
  91.2 0.5 slice.118
  91.8 0.6 slice.117
  (29 shorter events, 0.2 us)
Async XLA Ops:
  0.6 2.9 %copy-start = (bf16[1,24,256,256]{3,2,1,0:T(8,128)(2,1)S(1)}, bf16[1,24,256,256]{3,2,1,0:T(8,128)(2,1)}, u32[]{:S(2)}) copy-start(bf16[1,24,256,256]{3,2,1,0:T(8,128)(2,1)} %param.6) | copy-start | bytes 9437188
  3.2 1.4 %copy-start.5 = (f32[24,256]{1,0:T(8,128)}, f32[24,256]{1,0:T(8,128)S(1)}, u32[]{:S(2)}) copy-start(f32[24,256]{1,0:T(8,128)S(1)} %multiply_reduce_fusion.refs_7_) | copy-start | bytes 73732
  4.0 0.6 copy-start.10
  4.6 1.6 %copy-start.1 = (f32[12,256,256]{2,1,0:T(8,128)}, f32[12,256,256]{2,1,0:T(8,128)S(1)}, u32[]{:S(2)}) copy-start(f32[12,256,256]{2,1,0:T(8,128)S(1)} %fusion.2.refs_8_) | copy-start | bytes 9437188
  6.6 4.5 %copy-start.12 = (f32[6,256]{1,0:T(8,128)}, f32[6,256]{1,0:T(8,128)S(1)}, u32[]{:S(2)}) copy-start(f32[6,256]{1,0:T(8,128)S(1)} %add.33.refs_11_) | copy-start | bytes 18436
  10.2 6.0 %copy-start.2 = (f32[6,256,256]{2,1,0:T(8,128)}, f32[6,256,256]{2,1,0:T(8,128)S(1)}, u32[]{:S(2)}) copy-start(f32[6,256,256]{2,1,0:T(8,128)S(1)} %fusion.refs_10_) | copy-start | bytes 4718596
  11.1 31.2 %copy-start.3 = (f32[3,256,256]{2,1,0:T(8,128)}, f32[3,256,256]{2,1,0:T(8,128)S(1)}, u32[]{:S(2)}) copy-start(f32[3,256,256]{2,1,0:T(8,128)S(1)} %fusion.6.refs_12_) | copy-start | bytes 2359300
  11.3 33.6 %copy-start.13 = (f32[3,256]{1,0:T(4,128)}, f32[3,256]{1,0:T(4,128)S(1)}, u32[]{:S(2)}) copy-start(f32[3,256]{1,0:T(4,128)S(1)} %add.34.refs_13_) | copy-start | bytes 9220
  12.4 10.2 %copy-start.4 = (f32[264,256]{1,0:T(8,128)}, f32[264,256]{1,0:T(8,128)S(1)}, u32[]{:S(2)}) copy-start(f32[264,256]{1,0:T(8,128)S(1)} %maximum_maximum_fusion.own_ref) | copy-start | bytes 811012
  12.4 9.5 %collective-permute-start = (f32[264,256]{1,0:T(8,128)S(1)}, f32[264,256]{1,0:T(8,128)S(1)}, u32[]{:S(2)}, u32[]{:S(2)}) collective-permute-start(f32[264,256]{1,0:T(8,128)S(1)} %maximum_maximum_fusion.own_ref), channel_id=1, source_target_pairs={{0,16},{16,0},{1,17},{17,1},{2,18},{18,2},{3,19},{19,3},{4,20},{20... | collective-permute-start | bytes 811016 | tf_op jit(solution)/shard_map/ppermute | solution.py:147
  22.0 0.7 copy-start.7
  25.3 1.8 %collective-permute-start.1 = (f32[264,256]{1,0:T(8,128)}, f32[264,256]{1,0:T(8,128)S(1)}, u32[]{:S(2)}, u32[]{:S(2)}) collective-permute-start(f32[264,256]{1,0:T(8,128)} %get-tuple-element.29.own_ref), channel_id=1, source_target_pairs={{0,1},{16,17},{1,0},{17,16},{2,3},{18,19},{3,2},{19,18},{4,5},{20,... | collective-permute-start | bytes 811016 | tf_op jit(solution)/shard_map/ppermute | solution.py:147
  27.0 0.7 copy-start.8
  30.3 8.7 %collective-permute-start.2 = (f32[264,256]{1,0:T(8,128)}, f32[264,256]{1,0:T(8,128)S(1)}, u32[]{:S(2)}, u32[]{:S(2)}) collective-permute-start(f32[264,256]{1,0:T(8,128)} %get-tuple-element.32.own_ref), channel_id=1, source_target_pairs={{0,2},{16,18},{1,3},{17,19},{2,0},{18,16},{3,1},{19,17},{4,6},{20,... | collective-permute-start | bytes 811016 | tf_op jit(solution)/shard_map/ppermute | solution.py:147
  39.0 0.7 copy-start.9
  42.3 7.9 %collective-permute-start.3 = (f32[264,256]{1,0:T(8,128)}, f32[264,256]{1,0:T(8,128)S(1)}, u32[]{:S(2)}, u32[]{:S(2)}) collective-permute-start(f32[264,256]{1,0:T(8,128)} %get-tuple-element.35.own_ref), channel_id=1, source_target_pairs={{0,4},{16,20},{1,5},{17,21},{2,6},{18,22},{3,7},{19,23},{4,0},{20,... | collective-permute-start | bytes 811016 | tf_op jit(solution)/shard_map/ppermute | solution.py:147
  50.2 0.7 copy-start.6
  54.2 4.5 %collective-permute-start.4 = (f32[8,256]{1,0:T(8,128)S(1)}, f32[8,256]{1,0:T(8,128)S(1)}, u32[]{:S(2)}, u32[]{:S(2)}) collective-permute-start(f32[8,256]{1,0:T(8,128)S(1)} %slice.108), channel_id=1, source_target_pairs={{0,8},{16,24},{1,9},{17,25},{2,10},{18,26},{3,11},{19,27},{4,12},{... | collective-permute-start | bytes 24584 | tf_op jit(solution)/shard_map/ppermute | solution.py:147
  58.8 0.6 copy-start.14
  59.4 7.7 %copy-start.11 = (f32[1,24,256]{2,1,0:T(8,128)S(1)}, f32[1,24,256]{2,1,0:T(8,128)}, u32[]{:S(2)}) copy-start(f32[1,24,256]{2,1,0:T(8,128)} %param.9) | copy-start | bytes 73732
  70.4 4.5 %collective-permute-start.5 = (f32[136,128]{1,0:T(8,128)}, f32[136,128]{1,0:T(8,128)S(1)}, u32[]{:S(2)}, u32[]{:S(2)}) collective-permute-start(f32[136,128]{1,0:T(8,128)} %scatter.4), channel_id=1, source_target_pairs={{0,16},{16,0},{1,17},{17,1},{2,18},{18,2},{3,19},{19,3},{4,20},{20... | collective-permute-start | bytes 208904 | tf_op jit(solution)/shard_map/ppermute | solution.py:147
  75.8 1.3 %collective-permute-start.6 = (f32[136,128]{1,0:T(8,128)S(1)}, f32[136,128]{1,0:T(8,128)S(1)}, u32[]{:S(2)}, u32[]{:S(2)}) collective-permute-start(f32[136,128]{1,0:T(8,128)S(1)} %add.37), channel_id=1, source_target_pairs={{0,1},{16,17},{1,0},{17,16},{2,3},{18,19},{3,2},{19,18},{4,5},{20,... | collective-permute-start | bytes 208904 | tf_op jit(solution)/shard_map/ppermute | solution.py:147
  77.2 4.4 %collective-permute-start.7 = (f32[136,128]{1,0:T(8,128)S(1)}, f32[136,128]{1,0:T(8,128)S(1)}, u32[]{:S(2)}, u32[]{:S(2)}) collective-permute-start(f32[136,128]{1,0:T(8,128)S(1)} %add.38), channel_id=1, source_target_pairs={{0,2},{16,18},{1,3},{17,19},{2,0},{18,16},{3,1},{19,17},{4,6},{20,... | collective-permute-start | bytes 208904 | tf_op jit(solution)/shard_map/ppermute | solution.py:147
  81.6 4.4 %collective-permute-start.8 = (f32[136,128]{1,0:T(8,128)S(1)}, f32[136,128]{1,0:T(8,128)S(1)}, u32[]{:S(2)}, u32[]{:S(2)}) collective-permute-start(f32[136,128]{1,0:T(8,128)S(1)} %add.39), channel_id=1, source_target_pairs={{0,4},{16,20},{1,5},{17,21},{2,6},{18,22},{3,7},{19,23},{4,0},{20,... | collective-permute-start | bytes 208904 | tf_op jit(solution)/shard_map/ppermute | solution.py:147
  85.9 5.3 %collective-permute-start.9 = (f32[136,128]{1,0:T(8,128)S(1)}, f32[136,128]{1,0:T(8,128)S(1)}, u32[]{:S(2)}, u32[]{:S(2)}) collective-permute-start(f32[136,128]{1,0:T(8,128)S(1)} %add.40), channel_id=1, source_target_pairs={{0,8},{16,24},{1,9},{17,25},{2,10},{18,26},{3,11},{19,27},{4,12},{... | collective-permute-start | bytes 208904 | tf_op jit(solution)/shard_map/ppermute | solution.py:147

commit v12 on v11

--- a/solution.py
+++ b/solution.py
@@ -2,6 +2,7 @@
 import jax.numpy as jnp
 from jax import lax
 from jax.experimental import pallas as pl
+from jax.experimental.pallas import tpu as pltpu
 from jax.sharding import PartitionSpec as P
 
 EXACT = lax.Precision.HIGHEST
@@ -90,25 +91,38 @@
     return jnp.sum(column(row) * q.astype(jnp.float32), axis=0, keepdims=True)
 
 
-def finish(d, sizes, width, stations):
+def finish(d, sizes, width, stations, dtypes):
     depth = len(sizes) - 1
+    halves = [sizes[level] // 2 for level in range(depth)]
 
     def kernel(*refs):
-        rv_ref, sq_ref, sv_ref, grads_ref, load_ref, resp_ref = refs[:6]
-        tree = refs[6 : 6 + 2 * depth]
-        out_ref, grad_ref = refs[6 + 2 * depth :]
+        rv_ref, sq_ref, sv_ref, grads_ref, load_ref = refs[:5]
+        q_hbm = refs[5 : 5 + depth]
+        v_refs = refs[5 + depth : 5 + 2 * depth]
+        out_ref, grad_ref = refs[5 + 2 * depth : 7 + 2 * depth]
+        bufs = refs[7 + 2 * depth : 7 + 3 * depth]
+        sems = refs[7 + 3 * depth]
+        copies = {}
+        k = 0
+        for level in reversed(range(depth)):
+            for j in range(halves[level]):
+                copy = pltpu.make_async_copy(q_hbm[level].at[2 * j + 1], bufs[level].at[j], sems.at[k])
+                copy.start()
+                copies[level, j] = copy
+                k += 1
         me = lax.axis_index("outer") * lax.axis_size("inner") + lax.axis_index("inner")
         lower = (me // d) % 2 == 0
         sv = sv_ref[0:1, :]
         entering = jnp.where(lower, row_times(rv_ref[0:1, :], sq_ref[...]) + sv, sv)
         rows = [entering]
         for level in reversed(range(depth)):
-            q_ref, v_ref = tree[2 * level], tree[2 * level + 1]
+            v_ref = v_refs[level]
             n = sizes[level]
             new = []
             for j in range(n // 2):
                 upper = rows[j]
-                new.append(row_times(upper, q_ref[2 * j + 1]) + v_ref[2 * j + 1 : 2 * j + 2, :])
+                copies[level, j].wait()
+                new.append(row_times(upper, bufs[level][j]) + v_ref[2 * j + 1 : 2 * j + 2, :])
                 new.append(upper)
             if n % 2:
                 new.append(rows[-1])
@@ -123,17 +137,21 @@
         grad_ref[0:stations, :] = kernel_grad
         grad_ref[stations:, :] = jnp.zeros((8, stations), jnp.float32)
 
-    def run(rv, sq, sv, grads, loads, resp, levels):
-        args = [rv, sq, sv, grads, loads, resp]
-        for level in range(depth):
-            args += list(levels[level])
+    def run(rv, sq, sv, grads, loads, levels):
+        qs = [levels[level][0] for level in range(depth)]
+        vs = [levels[level][1] for level in range(depth)]
+        vmem = pl.BlockSpec(memory_space=pltpu.VMEM)
         return pl.pallas_call(
             kernel,
             out_shape=(
                 jax.ShapeDtypeStruct(grads.shape, jnp.float32),
                 jax.ShapeDtypeStruct((stations + 8, stations), jnp.float32),
             ),
-        )(*args)
+            in_specs=[vmem] * 5 + [pl.BlockSpec(memory_space=pl.ANY)] * depth + [vmem] * depth,
+            out_specs=(vmem, vmem),
+            scratch_shapes=[pltpu.VMEM((max(halves[level], 1), width, width), dtypes[level]) for level in range(depth)]
+            + [pltpu.SemaphoreType.DMA((max(sum(halves), 1),))],
+        )(rv, sq, sv, grads, loads, *qs, *vs)
 
     return run
 
@@ -171,11 +189,15 @@
         d *= 2
     rv = exchange(packed[width:], d, count)
     sizes = [level[0].shape[0] for level in levels]
-    length_rates, packed = finish(d, sizes, width, stations)(
-        rv, sq, sv, grads, station_loadings[0], offset_response[0], levels
+    dtypes = [level[0].dtype for level in levels]
+    length_rates, packed = finish(d, sizes, width, stations, dtypes)(
+        rv, sq, sv, grads, station_loadings[0], levels
     )
     local_noise = -jnp.sum(length_rates * offset_response[0])
-    packed = packed.at[stations, 0].set(local_noise)
+    spot = (lax.broadcasted_iota(jnp.int32, packed.shape, 0) == stations) & (
+        lax.broadcasted_iota(jnp.int32, packed.shape, 1) == 0
+    )
+    packed = jnp.where(spot, local_noise, packed)
     d = 1
     while d < count:
         packed = packed + exchange(packed, d, count)

time: 92.8 us -> 96.9 us (1.044)
  matrix products: 5.79 us -> 10 us
  local copies, waits for them, and re-layouts: 8.65 us -> 5.71 us
  other arithmetic: 8.19 us -> 10.7 us
    dot_general x4, matrix products: 5.22 us -> 7.83 us  [matmat(): jnp.einsum('nij,njk->nik', later.astype(jnp.float32), earlier.astype(jnp....]
    dot_general x1, matrix products: 0.57 us -> 2.21 us  [matmat(): jnp.einsum('nij,njk->nik', later, earlier, preferred_element_type=jnp.flo...]
    unnamed x30 -> x28, local copies, waits for them, and re-layouts: 4.69 us -> 3.06 us
    reduce_sum x4, other arithmetic: 3.55 us -> 4.97 us  [vecmat(): return jnp.sum(v[:, :, None] * q.astype(jnp.float32), axis=1)]
    scatter x1 -> x0, local copies, waits for them, and re-layouts: 1.29 us -> none  [body(): packed = packed.at[stations, 0].set(local_noise)]
where the time goes in v12:
time: 96.9 us; the launch traced here: 96.4 us
  waiting for transfers between devices  32.6 us (34%)
  Pallas kernels  18.3 us (19%)
  starting transfers between devices  17.5 us (18%)
  other arithmetic  10.7 us (11%)
  matrix products  10 us (10%)
  local copies, waits for them, and re-layouts  5.71 us (6%)
  between operations  1.53 us (2%)
    ppermute x10, waiting for transfers between devices, exchange(): lax.ppermute(x, AXES, [(place(j), place(j ^ mask)) for j in range(count)])  32.6 us
    ppermute x10, starting transfers between devices, exchange(): lax.ppermute(x, AXES, [(place(j), place(j ^ mask)) for j in range(count)])  17.5 us
    pallas_call x4, Pallas kernels, run(): pl.pallas_call(kernel, out_shape=(jax.ShapeDtypeStruct(own.shape, jnp.flo...  10.2 us
    pallas_call x1, Pallas kernels, run(): pl.pallas_call(kernel, out_shape=(jax.ShapeDtypeStruct(grads.shape, jnp.f...  8.09 us
    dot_general x4, matrix products, matmat(): jnp.einsum('nij,njk->nik', later.astype(jnp.float32), earlier.astype(jnp....  7.83 us
    reduce_sum x4, other arithmetic, vecmat(): return jnp.sum(v[:, :, None] * q.astype(jnp.float32), axis=1)  4.97 us
    unnamed x28, local copies, waits for them, and re-layouts  3.06 us
    dot_general x1, matrix products, matmat(): jnp.einsum('nij,njk->nik', later, earlier, preferred_element_type=jnp.flo...  2.21 us
  transfers between devices with their start and end apart: 10, of which 10 were waited for; matrix products, arithmetic and copies ran while one was open for 2% of the time, Pallas kernels for 0%

profile of v12, /device:TPU:0, one launch (start us, length us, event | category | flops | bytes accessed | tf_op | source)
XLA Modules:
  0.0 96.4 jit_solution(4624341933437969639)
XLA Ops:
  0.6 0.0 copy-start
  0.6 2.6 %multiply_reduce_fusion.refs_10_ = f32[24,256]{1,0:T(8,128)S(1)} fusion(f32[24,256]{1,0:T(8,128)} %bitcast.33, bf16[1,24,256,256]{3,2,1,0:T(8,128)(2,1)} %param.4), kind=kLoop, calls=%fused_computation | loop fusion | flops 4712448 | bytes 3194880 | tf_op jit(solution)/shard_map/reduce_sum | solution.py:13
  3.2 0.0 copy-start.4
  3.3 0.2 copy-done
  3.5 2.2 %fusion.2.refs_6_ = f32[12,256,256]{2,1,0:T(8,128)} fusion(bf16[24,256,256]{2,1,0:T(8,128)(2,1)S(1)} %bitcast.30), kind=kOutput, calls=%fused_computation.5 | convolution fusion | flops 402653184 | bytes 6291456 | tf_op jit(solution)/shard_map/nij,njk->nik/dot_general | solution.py:22
  5.7 0.0 copy-done.4
  5.7 0.5 multiply_reduce_fusion.1
  6.2 0.0 copy-start.1
  6.2 0.0 copy-start.9
  6.3 4.8 %fusion.refs_7_ = f32[6,256,256]{2,1,0:T(8,128)} fusion(f32[12,256,256]{2,1,0:T(8,128)} %fusion.2.refs_6_), kind=kOutput, calls=%fused_computation.3 | convolution fusion | flops 1207959552 | bytes 4718592 | tf_op jit(solution)/shard_map/nij,njk->nik/dot_general | solution.py:23
  11.1 0.0 copy-done.1
  11.1 0.3 multiply_reduce_fusion.2
  11.4 0.0 copy-done.9
  11.4 0.0 copy-start.10
  11.4 2.3 %fusion.6.refs_8_ = f32[3,256,256]{2,1,0:T(8,128)S(1)} fusion(f32[6,256,256]{2,1,0:T(8,128)} %fusion.refs_7_), kind=kOutput, calls=%fused_computation.10 | convolution fusion | flops 603979776 | bytes 2359296 | tf_op jit(solution)/shard_map/nij,njk->nik/dot_general | solution.py:23
  13.7 0.0 copy-start.2
  13.7 1.6 %multiply_reduce_fusion.3 = f32[3,256]{1,0:T(4,128)S(1)} fusion(f32[6,256,256]{2,1,0:T(8,128)} %fusion.refs_7_, f32[3,256]{1,0:T(4,128)S(1)} %slice.84), kind=kLoop, calls=%fused_computation.9 | loop fusion | flops 392448 | bytes 792576 | tf_op jit(solution)/shard_map/reduce_sum | solution.py:13
  15.4 0.4 multiply_reduce_fusion.5
  15.8 0.1 fusion.18
  15.9 0.4 fusion.11
  16.3 0.1 pad.6.clone
  16.4 0.1 maximum_maximum_fusion.own_ref
  16.5 0.0 copy-start.3
  16.5 3.0 %collective-permute-start = (f32[264,256]{1,0:T(8,128)S(1)}, f32[264,256]{1,0:T(8,128)S(1)}, u32[]{:S(2)}, u32[]{:S(2)}) collective-permute-start(f32[264,256]{1,0:T(8,128)S(1)} %maximum_maximum_fusion.own_ref), channel_id=1, source_target_pairs={{0,16},{16,0},{1,17},{17,1},{2,18},{18,2},{3,19},{19,3},{4,20},{20... | collective-permute-start | bytes 811016 | tf_op jit(solution)/shard_map/ppermute | solution.py:165
  19.5 0.7 fusion.13.sq_ref
  20.2 5.8 %collective-permute-done.got_ref = f32[264,256]{1,0:T(8,128)S(1)} collective-permute-done((f32[264,256]{1,0:T(8,128)S(1)}, f32[264,256]{1,0:T(8,128)S(1)}, u32[]{:S(2)}, u32[]{:S(2)}) %collective-permute-start) | collective-permute-done | bytes 270368 | tf_op jit(solution)/shard_map/ppermute | solution.py:165
  26.0 0.6 broadcast_in_dim.19.sv_ref
  26.6 0.1 copy-done.6
  26.7 2.6 %shard_map.67 = (f32[264,256]{1,0:T(8,128)}, f32[256,256]{1,0:T(8,128)}, f32[8,256]{1,0:T(8,128)}) custom-call(f32[264,256]{1,0:T(8,128)} %copy-done.3, f32[264,256]{1,0:T(8,128)} %copy-done.6, f32[256,256]{1,0:T(8,128)} %fusion.13.sq_ref, f32[8,256]{1,0:T(8,128)} %broadcast_in_dim.19.sv_ref), custom_call_target="tpu_custom_call" | custom-call | tf_op jit(solution)/shard_map/pallas_call | solution.py:74
  29.3 0.0 collective-permute-start.1
  29.3 1.8 %collective-permute-done.1.got_ref = f32[264,256]{1,0:T(8,128)S(1)} collective-permute-done((f32[264,256]{1,0:T(8,128)}, f32[264,256]{1,0:T(8,128)S(1)}, u32[]{:S(2)}, u32[]{:S(2)}) %collective-permute-start.1) | collective-permute-done | bytes 270368 | tf_op jit(solution)/shard_map/ppermute | solution.py:165
  31.0 0.7 copy-done.7
  31.8 2.6 %shard_map.68 = (f32[264,256]{1,0:T(8,128)}, f32[256,256]{1,0:T(8,128)}, f32[8,256]{1,0:T(8,128)}) custom-call(f32[264,256]{1,0:T(8,128)} %get-tuple-element.17.own_ref, f32[264,256]{1,0:T(8,128)} %copy-done.7, f32[256,256]{1,0:T(8,128)} %get-tuple-element.18.sq_ref, f32[8,256]{1,0:T(8,128)} %get-tuple-element.19.sv_ref), custom_call_target="tpu_custom_call" | custom-call | tf_op jit(solution)/shard_map/pallas_call | solution.py:74
  34.3 1.7 %collective-permute-start.2 = (f32[264,256]{1,0:T(8,128)}, f32[264,256]{1,0:T(8,128)S(1)}, u32[]{:S(2)}, u32[]{:S(2)}) collective-permute-start(f32[264,256]{1,0:T(8,128)} %get-tuple-element.20.own_ref), channel_id=1, source_target_pairs={{0,2},{16,18},{1,3},{17,19},{2,0},{18,16},{3,1},{19,17},{4,6},{20,... | collective-permute-start | bytes 811016 | tf_op jit(solution)/shard_map/ppermute | solution.py:165
  36.0 7.0 %collective-permute-done.2.got_ref = f32[264,256]{1,0:T(8,128)S(1)} collective-permute-done((f32[264,256]{1,0:T(8,128)}, f32[264,256]{1,0:T(8,128)S(1)}, u32[]{:S(2)}, u32[]{:S(2)}) %collective-permute-start.2) | collective-permute-done | bytes 270368 | tf_op jit(solution)/shard_map/ppermute | solution.py:165
  43.1 0.7 copy-done.8
  43.8 2.5 %shard_map.69 = (f32[264,256]{1,0:T(8,128)}, f32[256,256]{1,0:T(8,128)}, f32[8,256]{1,0:T(8,128)}) custom-call(f32[264,256]{1,0:T(8,128)} %get-tuple-element.20.own_ref, f32[264,256]{1,0:T(8,128)} %copy-done.8, f32[256,256]{1,0:T(8,128)} %get-tuple-element.21.sq_ref, f32[8,256]{1,0:T(8,128)} %get-tuple-element.22.sv_ref), custom_call_target="tpu_custom_call" | custom-call | tf_op jit(solution)/shard_map/pallas_call | solution.py:74
  46.3 1.8 %collective-permute-start.3 = (f32[264,256]{1,0:T(8,128)}, f32[264,256]{1,0:T(8,128)S(1)}, u32[]{:S(2)}, u32[]{:S(2)}) collective-permute-start(f32[264,256]{1,0:T(8,128)} %get-tuple-element.23.own_ref), channel_id=1, source_target_pairs={{0,4},{16,20},{1,5},{17,21},{2,6},{18,22},{3,7},{19,23},{4,0},{20,... | collective-permute-start | bytes 811016 | tf_op jit(solution)/shard_map/ppermute | solution.py:165
  48.1 0.6 pad_maximum_fusion.1.refs_14_
  48.7 0.9 pad_maximum_fusion.refs_9_
  49.6 4.7 %collective-permute-done.3.got_ref = f32[264,256]{1,0:T(8,128)S(1)} collective-permute-done((f32[264,256]{1,0:T(8,128)}, f32[264,256]{1,0:T(8,128)S(1)}, u32[]{:S(2)}, u32[]{:S(2)}) %collective-permute-start.3) | collective-permute-done | bytes 270368 | tf_op jit(solution)/shard_map/ppermute | solution.py:165
  54.3 0.7 copy-done.5
  55.0 2.6 %shard_map.70 = (f32[264,256]{1,0:T(8,128)}, f32[256,256]{1,0:T(8,128)}, f32[8,256]{1,0:T(8,128)}) custom-call(f32[264,256]{1,0:T(8,128)} %get-tuple-element.23.own_ref, f32[264,256]{1,0:T(8,128)} %copy-done.5, f32[256,256]{1,0:T(8,128)} %get-tuple-element.24.sq_ref, f32[8,256]{1,0:T(8,128)} %get-tuple-element.25.sv_ref), custom_call_target="tpu_custom_call" | custom-call | tf_op jit(solution)/shard_map/pallas_call | solution.py:74
  57.5 0.7 slice.89
  58.2 2.8 %collective-permute-start.4 = (f32[8,256]{1,0:T(8,128)S(1)}, f32[8,256]{1,0:T(8,128)S(1)}, u32[]{:S(2)}, u32[]{:S(2)}) collective-permute-start(f32[8,256]{1,0:T(8,128)S(1)} %slice.89), channel_id=1, source_target_pairs={{0,8},{16,24},{1,9},{17,25},{2,10},{18,26},{3,11},{19,27},{4,12},{... | collective-permute-start | bytes 24584 | tf_op jit(solution)/shard_map/ppermute | solution.py:165
  61.0 1.8 %collective-permute-done.4.refs_0_ = f32[8,256]{1,0:T(8,128)S(1)} collective-permute-done((f32[8,256]{1,0:T(8,128)S(1)}, f32[8,256]{1,0:T(8,128)S(1)}, u32[]{:S(2)}, u32[]{:S(2)}) %collective-permute-start.4) | collective-permute-done | bytes 8224 | tf_op jit(solution)/shard_map/ppermute | solution.py:165
  62.8 0.6 copy-done.13
  63.4 8.1 %shard_map.71 = (f32[24,256]{1,0:T(8,128)}, f32[136,128]{1,0:T(8,128)}) custom-call(f32[8,256]{1,0:T(8,128)} %copy-done.13, f32[256,256]{1,0:T(8,128)} %get-tuple-element.27.refs_1_, f32[8,256]{1,0:T(8,128)} %get-tuple-element.28.refs_2_, f32[24,256]{1,0:T(8,128)} %bitcast.34, f32[24,2,128]{2,1,0:T(2,128)} %bitcast.35, bf16[24,256,256]{2,1,0:T(8,128)(2,1)} %bitcast.29, ...), custom_call_target="tpu_custom_call" | custom-call | tf_op jit(solution)/shard_map/pallas_call | solution.py:144
  71.5 0.0 copy-done.12
  71.5 1.4 %fusion.15 = f32[]{:T(128)} fusion(f32[24,256]{1,0:T(8,128)} %get-tuple-element.29, f32[1,24,256]{2,1,0:T(8,128)S(1)} %copy-done.12), kind=kLoop, calls=%fused_computation.27 | loop fusion | flops 12287 | bytes 49156 | tf_op jit(solution)/shard_map/reduce_sum | solution.py:196
  73.5 1.0 %and_select_fusion = f32[136,128]{1,0:T(8,128)S(1)} fusion(f32[136,128]{1,0:T(8,128)} %get-tuple-element.30, f32[]{:T(128)S(6)} %neg.3, pred[128]{0:T(512)(128)(4,1)S(1)} %iota_compare_fusion.2, pred[136]{0:T(512)(128)(4,1)S(1)} %iota_compare_fusion.1), kind=kLoop, calls=%fused_computation.25 | loop fusion | flops 34816 | bytes 139532 | tf_op jit(solution)/shard_map/jit(_where)/select_n | solution.py:200
  74.5 1.7 %collective-permute-start.5 = (f32[136,128]{1,0:T(8,128)S(1)}, f32[136,128]{1,0:T(8,128)S(1)}, u32[]{:S(2)}, u32[]{:S(2)}) collective-permute-start(f32[136,128]{1,0:T(8,128)S(1)} %and_select_fusion), channel_id=1, source_target_pairs={{0,16},{16,0},{1,17},{17,1},{2,18},{18,2},{3,19},{19,3},{4,20},{20... | collective-permute-start | bytes 208904 | tf_op jit(solution)/shard_map/ppermute | solution.py:165
  76.2 2.6 %collective-permute-done.5 = f32[136,128]{1,0:T(8,128)S(1)} collective-permute-done((f32[136,128]{1,0:T(8,128)S(1)}, f32[136,128]{1,0:T(8,128)S(1)}, u32[]{:S(2)}, u32[]{:S(2)}) %collective-permute-start.5) | collective-permute-done | bytes 69664 | tf_op jit(solution)/shard_map/ppermute | solution.py:165
  78.9 1.0 %fusion.21 = f32[136,128]{1,0:T(8,128)S(1)} fusion(f32[136,128]{1,0:T(8,128)S(1)} %collective-permute-done.5, f32[136,128]{1,0:T(8,128)} %get-tuple-element.30, f32[]{:T(128)S(6)} %neg.3, pred[128]{0:T(512)(128)(4,1)S(1)} %iota_compare_fusion.2, pred[136]{0:T(512)(128)(4,1)S(1)} %iota_compare_fusion.1), kind=kLoop, calls=%fused_computation.36 | loop fusion | flops 52224 | bytes 209164 | tf_op jit(solution)/shard_map/add | solution.py:203
  79.8 0.1 collective-permute-start.6
  79.9 1.2 %collective-permute-done.6 = f32[136,128]{1,0:T(8,128)S(1)} collective-permute-done((f32[136,128]{1,0:T(8,128)S(1)}, f32[136,128]{1,0:T(8,128)S(1)}, u32[]{:S(2)}, u32[]{:S(2)}) %collective-permute-start.6) | collective-permute-done | bytes 69664 | tf_op jit(solution)/shard_map/ppermute | solution.py:165
  81.2 1.7 %collective-permute-start.7 = (f32[136,128]{1,0:T(8,128)S(1)}, f32[136,128]{1,0:T(8,128)S(1)}, u32[]{:S(2)}, u32[]{:S(2)}) collective-permute-start(f32[136,128]{1,0:T(8,128)S(1)} %add.36), channel_id=1, source_target_pairs={{0,2},{16,18},{1,3},{17,19},{2,0},{18,16},{3,1},{19,17},{4,6},{20,... | collective-permute-start | bytes 208904 | tf_op jit(solution)/shard_map/ppermute | solution.py:165
  82.9 2.7 %collective-permute-done.7 = f32[136,128]{1,0:T(8,128)S(1)} collective-permute-done((f32[136,128]{1,0:T(8,128)S(1)}, f32[136,128]{1,0:T(8,128)S(1)}, u32[]{:S(2)}, u32[]{:S(2)}) %collective-permute-start.7) | collective-permute-done | bytes 69664 | tf_op jit(solution)/shard_map/ppermute | solution.py:165
  85.6 1.8 %collective-permute-start.8 = (f32[136,128]{1,0:T(8,128)S(1)}, f32[136,128]{1,0:T(8,128)S(1)}, u32[]{:S(2)}, u32[]{:S(2)}) collective-permute-start(f32[136,128]{1,0:T(8,128)S(1)} %add.37), channel_id=1, source_target_pairs={{0,4},{16,20},{1,5},{17,21},{2,6},{18,22},{3,7},{19,23},{4,0},{20,... | collective-permute-start | bytes 208904 | tf_op jit(solution)/shard_map/ppermute | solution.py:165
  87.4 2.6 %collective-permute-done.8 = f32[136,128]{1,0:T(8,128)S(1)} collective-permute-done((f32[136,128]{1,0:T(8,128)S(1)}, f32[136,128]{1,0:T(8,128)S(1)}, u32[]{:S(2)}, u32[]{:S(2)}) %collective-permute-start.8) | collective-permute-done | bytes 69664 | tf_op jit(solution)/shard_map/ppermute | solution.py:165
  89.9 2.8 %collective-permute-start.9 = (f32[136,128]{1,0:T(8,128)S(1)}, f32[136,128]{1,0:T(8,128)S(1)}, u32[]{:S(2)}, u32[]{:S(2)}) collective-permute-start(f32[136,128]{1,0:T(8,128)S(1)} %add.38), channel_id=1, source_target_pairs={{0,8},{16,24},{1,9},{17,25},{2,10},{18,26},{3,11},{19,27},{4,12},{... | collective-permute-start | bytes 208904 | tf_op jit(solution)/shard_map/ppermute | solution.py:165
  92.8 2.5 %collective-permute-done.9 = f32[136,128]{1,0:T(8,128)S(1)} collective-permute-done((f32[136,128]{1,0:T(8,128)S(1)}, f32[136,128]{1,0:T(8,128)S(1)}, u32[]{:S(2)}, u32[]{:S(2)}) %collective-permute-start.9) | collective-permute-done | bytes 69664 | tf_op jit(solution)/shard_map/ppermute | solution.py:165
  95.2 0.6 slice.98
  95.9 0.5 slice.99
  (29 shorter events, 0.2 us)
Async XLA Ops:
  0.6 2.9 %copy-start = (bf16[1,24,256,256]{3,2,1,0:T(8,128)(2,1)S(1)}, bf16[1,24,256,256]{3,2,1,0:T(8,128)(2,1)}, u32[]{:S(2)}) copy-start(bf16[1,24,256,256]{3,2,1,0:T(8,128)(2,1)} %param.4) | copy-start | bytes 9437188
  3.2 2.5 %copy-start.4 = (f32[24,256]{1,0:T(8,128)}, f32[24,256]{1,0:T(8,128)S(1)}, u32[]{:S(2)}) copy-start(f32[24,256]{1,0:T(8,128)S(1)} %multiply_reduce_fusion.refs_10_) | copy-start | bytes 73732
  6.2 4.9 %copy-start.1 = (f32[12,256,256]{2,1,0:T(8,128)S(1)}, f32[12,256,256]{2,1,0:T(8,128)}, u32[]{:S(2)}) copy-start(f32[12,256,256]{2,1,0:T(8,128)} %fusion.2.refs_6_) | copy-start | bytes 9437188
  6.2 5.1 %copy-start.9 = (f32[12,256]{1,0:T(8,128)}, f32[12,256]{1,0:T(8,128)S(1)}, u32[]{:S(2)}) copy-start(f32[12,256]{1,0:T(8,128)S(1)} %add.30.refs_11_) | copy-start | bytes 36868
  11.4 8.8 %copy-start.10 = (f32[6,256]{1,0:T(8,128)}, f32[6,256]{1,0:T(8,128)S(1)}, u32[]{:S(2)}) copy-start(f32[6,256]{1,0:T(8,128)S(1)} %add.31.refs_12_) | copy-start | bytes 18436
  13.7 32.6 %copy-start.2 = (f32[3,256,256]{2,1,0:T(8,128)}, f32[3,256,256]{2,1,0:T(8,128)S(1)}, u32[]{:S(2)}) copy-start(f32[3,256,256]{2,1,0:T(8,128)S(1)} %fusion.6.refs_8_) | copy-start | bytes 2359300
  15.3 34.2 %copy-start.11 = (f32[3,256]{1,0:T(4,128)}, f32[3,256]{1,0:T(4,128)S(1)}, u32[]{:S(2)}) copy-start(f32[3,256]{1,0:T(4,128)S(1)} %add.32.refs_13_) | copy-start | bytes 9220
  16.5 10.2 %copy-start.3 = (f32[264,256]{1,0:T(8,128)}, f32[264,256]{1,0:T(8,128)S(1)}, u32[]{:S(2)}) copy-start(f32[264,256]{1,0:T(8,128)S(1)} %maximum_maximum_fusion.own_ref) | copy-start | bytes 811012
  16.5 9.5 %collective-permute-start = (f32[264,256]{1,0:T(8,128)S(1)}, f32[264,256]{1,0:T(8,128)S(1)}, u32[]{:S(2)}, u32[]{:S(2)}) collective-permute-start(f32[264,256]{1,0:T(8,128)S(1)} %maximum_maximum_fusion.own_ref), channel_id=1, source_target_pairs={{0,16},{16,0},{1,17},{17,1},{2,18},{18,2},{3,19},{19,3},{4,20},{20... | collective-permute-start | bytes 811016 | tf_op jit(solution)/shard_map/ppermute | solution.py:165
  26.0 0.7 copy-start.6
  29.3 1.8 %collective-permute-start.1 = (f32[264,256]{1,0:T(8,128)}, f32[264,256]{1,0:T(8,128)S(1)}, u32[]{:S(2)}, u32[]{:S(2)}) collective-permute-start(f32[264,256]{1,0:T(8,128)} %get-tuple-element.17.own_ref), channel_id=1, source_target_pairs={{0,1},{16,17},{1,0},{17,16},{2,3},{18,19},{3,2},{19,18},{4,5},{20,... | collective-permute-start | bytes 811016 | tf_op jit(solution)/shard_map/ppermute | solution.py:165
  31.0 0.7 copy-start.7
  34.3 8.7 %collective-permute-start.2 = (f32[264,256]{1,0:T(8,128)}, f32[264,256]{1,0:T(8,128)S(1)}, u32[]{:S(2)}, u32[]{:S(2)}) collective-permute-start(f32[264,256]{1,0:T(8,128)} %get-tuple-element.20.own_ref), channel_id=1, source_target_pairs={{0,2},{16,18},{1,3},{17,19},{2,0},{18,16},{3,1},{19,17},{4,6},{20,... | collective-permute-start | bytes 811016 | tf_op jit(solution)/shard_map/ppermute | solution.py:165
  43.1 0.7 copy-start.8
  46.3 8.0 %collective-permute-start.3 = (f32[264,256]{1,0:T(8,128)}, f32[264,256]{1,0:T(8,128)S(1)}, u32[]{:S(2)}, u32[]{:S(2)}) collective-permute-start(f32[264,256]{1,0:T(8,128)} %get-tuple-element.23.own_ref), channel_id=1, source_target_pairs={{0,4},{16,20},{1,5},{17,21},{2,6},{18,22},{3,7},{19,23},{4,0},{20,... | collective-permute-start | bytes 811016 | tf_op jit(solution)/shard_map/ppermute | solution.py:165
  54.3 0.7 copy-start.5
  58.2 4.5 %collective-permute-start.4 = (f32[8,256]{1,0:T(8,128)S(1)}, f32[8,256]{1,0:T(8,128)S(1)}, u32[]{:S(2)}, u32[]{:S(2)}) collective-permute-start(f32[8,256]{1,0:T(8,128)S(1)} %slice.89), channel_id=1, source_target_pairs={{0,8},{16,24},{1,9},{17,25},{2,10},{18,26},{3,11},{19,27},{4,12},{... | collective-permute-start | bytes 24584 | tf_op jit(solution)/shard_map/ppermute | solution.py:165
  62.8 0.6 copy-start.13
  63.4 8.1 %copy-start.12 = (f32[1,24,256]{2,1,0:T(8,128)S(1)}, f32[1,24,256]{2,1,0:T(8,128)}, u32[]{:S(2)}) copy-start(f32[1,24,256]{2,1,0:T(8,128)} %param.7) | copy-start | bytes 73732
  74.5 4.4 %collective-permute-start.5 = (f32[136,128]{1,0:T(8,128)S(1)}, f32[136,128]{1,0:T(8,128)S(1)}, u32[]{:S(2)}, u32[]{:S(2)}) collective-permute-start(f32[136,128]{1,0:T(8,128)S(1)} %and_select_fusion), channel_id=1, source_target_pairs={{0,16},{16,0},{1,17},{17,1},{2,18},{18,2},{3,19},{19,3},{4,20},{20... | collective-permute-start | bytes 208904 | tf_op jit(solution)/shard_map/ppermute | solution.py:165
  79.8 1.3 %collective-permute-start.6 = (f32[136,128]{1,0:T(8,128)S(1)}, f32[136,128]{1,0:T(8,128)S(1)}, u32[]{:S(2)}, u32[]{:S(2)}) collective-permute-start(f32[136,128]{1,0:T(8,128)S(1)} %fusion.21), channel_id=1, source_target_pairs={{0,1},{16,17},{1,0},{17,16},{2,3},{18,19},{3,2},{19,18},{4,5},{20,... | collective-permute-start | bytes 208904 | tf_op jit(solution)/shard_map/ppermute | solution.py:165
  81.2 4.4 %collective-permute-start.7 = (f32[136,128]{1,0:T(8,128)S(1)}, f32[136,128]{1,0:T(8,128)S(1)}, u32[]{:S(2)}, u32[]{:S(2)}) collective-permute-start(f32[136,128]{1,0:T(8,128)S(1)} %add.36), channel_id=1, source_target_pairs={{0,2},{16,18},{1,3},{17,19},{2,0},{18,16},{3,1},{19,17},{4,6},{20,... | collective-permute-start | bytes 208904 | tf_op jit(solution)/shard_map/ppermute | solution.py:165
  85.6 4.4 %collective-permute-start.8 = (f32[136,128]{1,0:T(8,128)S(1)}, f32[136,128]{1,0:T(8,128)S(1)}, u32[]{:S(2)}, u32[]{:S(2)}) collective-permute-start(f32[136,128]{1,0:T(8,128)S(1)} %add.37), channel_id=1, source_target_pairs={{0,4},{16,20},{1,5},{17,21},{2,6},{18,22},{3,7},{19,23},{4,0},{20,... | collective-permute-start | bytes 208904 | tf_op jit(solution)/shard_map/ppermute | solution.py:165
  89.9 5.3 %collective-permute-start.9 = (f32[136,128]{1,0:T(8,128)S(1)}, f32[136,128]{1,0:T(8,128)S(1)}, u32[]{:S(2)}, u32[]{:S(2)}) collective-permute-start(f32[136,128]{1,0:T(8,128)S(1)} %add.38), channel_id=1, source_target_pairs={{0,8},{16,24},{1,9},{17,25},{2,10},{18,26},{3,11},{19,27},{4,12},{... | collective-permute-start | bytes 208904 | tf_op jit(solution)/shard_map/ppermute | solution.py:165

commit v13 on v11

--- a/solution.py
+++ b/solution.py
@@ -113,13 +113,13 @@
             if n % 2:
                 new.append(rows[-1])
             rows = new
-        kernel_grad = jnp.zeros((stations, stations), jnp.float32)
         for t, row in enumerate(rows):
-            rate = grads_ref[t : t + 1, :] + row
-            out_ref[t : t + 1, :] = rate
-            col = column(rate)
-            kernel_grad = kernel_grad + col[:stations] * load_ref[t, 0:1, :]
-            kernel_grad = kernel_grad + col[stations:] * load_ref[t, 1:2, :]
+            out_ref[t : t + 1, :] = grads_ref[t : t + 1, :] + row
+        rates = out_ref[...].T
+        kernel_grad = jnp.dot(rates[:stations], load_ref[0], precision=EXACT, preferred_element_type=jnp.float32)
+        kernel_grad = kernel_grad + jnp.dot(
+            rates[stations:], load_ref[1], precision=EXACT, preferred_element_type=jnp.float32
+        )
         grad_ref[0:stations, :] = kernel_grad
         grad_ref[stations:, :] = jnp.zeros((8, stations), jnp.float32)
 
@@ -172,7 +172,7 @@
     rv = exchange(packed[width:], d, count)
     sizes = [level[0].shape[0] for level in levels]
     length_rates, packed = finish(d, sizes, width, stations)(
-        rv, sq, sv, grads, station_loadings[0], offset_response[0], levels
+        rv, sq, sv, grads, jnp.transpose(station_loadings[0], (1, 0, 2)), offset_response[0], levels
     )
     local_noise = -jnp.sum(length_rates * offset_response[0])
     packed = packed.at[stations, 0].set(local_noise)

time: 92.8 us -> 95.6 us (1.030)
  matrix products: 5.79 us -> 10.1 us
  other arithmetic: 8.19 us -> 9.64 us
  Pallas kernels: 18 us -> 16.7 us
  local copies, waits for them, and re-layouts: 8.65 us -> 7.63 us
    dot_general x4, matrix products: 5.22 us -> 7.84 us  [matmat(): jnp.einsum('nij,njk->nik', later.astype(jnp.float32), earlier.astype(jnp....]
    dot_general x1, matrix products: 0.57 us -> 2.22 us  [matmat(): jnp.einsum('nij,njk->nik', later, earlier, preferred_element_type=jnp.flo...]
    reduce_sum x4, other arithmetic: 3.55 us -> 4.97 us  [vecmat(): return jnp.sum(v[:, :, None] * q.astype(jnp.float32), axis=1)]
    pallas_call x1, Pallas kernels: 7.74 us -> 6.44 us  [run(): pl.pallas_call(kernel, out_shape=(jax.ShapeDtypeStruct(grads.shape, jnp.f...]
    unnamed x30 -> x31, local copies, waits for them, and re-layouts: 4.69 us -> 3.68 us
  transfers between devices with their start and end apart: 10 -> 10, of which waited for: 10 -> 10; matrix products, arithmetic and copies ran while one was open for 2% -> 3% of each run, Pallas kernels for 0% -> 0%
where the time goes in v13:
time: 95.6 us; the launch traced here: 95.1 us
  waiting for transfers between devices  32.2 us (34%)
  starting transfers between devices  17.4 us (18%)
  Pallas kernels  16.7 us (17%)
  matrix products  10.1 us (11%)
  other arithmetic  9.64 us (10%)
  local copies, waits for them, and re-layouts  7.63 us (8%)
  between operations  1.51 us (2%)
    ppermute x10, waiting for transfers between devices, exchange(): lax.ppermute(x, AXES, [(place(j), place(j ^ mask)) for j in range(count)])  32.2 us
    ppermute x10, starting transfers between devices, exchange(): lax.ppermute(x, AXES, [(place(j), place(j ^ mask)) for j in range(count)])  17.4 us
    pallas_call x4, Pallas kernels, run(): pl.pallas_call(kernel, out_shape=(jax.ShapeDtypeStruct(own.shape, jnp.flo...  10.2 us
    dot_general x4, matrix products, matmat(): jnp.einsum('nij,njk->nik', later.astype(jnp.float32), earlier.astype(jnp....  7.84 us
    pallas_call x1, Pallas kernels, run(): pl.pallas_call(kernel, out_shape=(jax.ShapeDtypeStruct(grads.shape, jnp.f...  6.44 us
    reduce_sum x4, other arithmetic, vecmat(): return jnp.sum(v[:, :, None] * q.astype(jnp.float32), axis=1)  4.97 us
    unnamed x31, local copies, waits for them, and re-layouts  3.68 us
    dot_general x1, matrix products, matmat(): jnp.einsum('nij,njk->nik', later, earlier, preferred_element_type=jnp.flo...  2.22 us
  transfers between devices with their start and end apart: 10, of which 10 were waited for; matrix products, arithmetic and copies ran while one was open for 3% of the time, Pallas kernels for 0%

profile of v13, /device:TPU:0, one launch (start us, length us, event | category | flops | bytes accessed | tf_op | source)
XLA Modules:
  0.0 95.1 jit_solution(11465707472885915551)
XLA Ops:
  0.6 0.0 copy-start
  0.6 2.6 %multiply_reduce_fusion.refs_7_ = f32[24,256]{1,0:T(8,128)S(1)} fusion(f32[24,256]{1,0:T(8,128)} %bitcast.36, bf16[1,24,256,256]{3,2,1,0:T(8,128)(2,1)} %param.6), kind=kLoop, calls=%fused_computation | loop fusion | flops 4712448 | bytes 3194880 | tf_op jit(solution)/shard_map/reduce_sum | solution.py:12
  3.2 0.0 copy-start.4
  3.3 0.2 copy-done
  3.5 2.2 %fusion.2.refs_8_ = f32[12,256,256]{2,1,0:T(8,128)} fusion(bf16[24,256,256]{2,1,0:T(8,128)(2,1)S(1)} %bitcast.33), kind=kOutput, calls=%fused_computation.5 | convolution fusion | flops 402653184 | bytes 6291456 | tf_op jit(solution)/shard_map/nij,njk->nik/dot_general | solution.py:21
  5.7 0.0 copy-done.4
  5.7 0.5 multiply_reduce_fusion.1
  6.2 0.0 copy-start.1
  6.2 0.0 copy-start.9
  6.3 4.8 %fusion.refs_10_ = f32[6,256,256]{2,1,0:T(8,128)} fusion(f32[12,256,256]{2,1,0:T(8,128)} %fusion.2.refs_8_), kind=kOutput, calls=%fused_computation.3 | convolution fusion | flops 1207959552 | bytes 4718592 | tf_op jit(solution)/shard_map/nij,njk->nik/dot_general | solution.py:22
  11.1 0.0 copy-done.1
  11.1 0.3 multiply_reduce_fusion.2
  11.4 0.0 copy-done.9
  11.4 0.0 copy-start.11
  11.5 2.3 %fusion.6.refs_12_ = f32[3,256,256]{2,1,0:T(8,128)S(1)} fusion(f32[6,256,256]{2,1,0:T(8,128)} %fusion.refs_10_), kind=kOutput, calls=%fused_computation.10 | convolution fusion | flops 603979776 | bytes 2359296 | tf_op jit(solution)/shard_map/nij,njk->nik/dot_general | solution.py:22
  13.7 1.6 %multiply_reduce_fusion.3 = f32[3,256]{1,0:T(4,128)S(1)} fusion(f32[6,256,256]{2,1,0:T(8,128)} %fusion.refs_10_, f32[3,256]{1,0:T(4,128)S(1)} %slice.103), kind=kLoop, calls=%fused_computation.9 | loop fusion | flops 392448 | bytes 792576 | tf_op jit(solution)/shard_map/reduce_sum | solution.py:12
  15.4 0.4 multiply_reduce_fusion.5
  15.8 0.1 fusion.17
  15.9 0.4 fusion.11
  16.3 0.1 pad.10.clone
  16.4 0.1 maximum_maximum_fusion.own_ref
  16.5 3.0 %collective-permute-start = (f32[264,256]{1,0:T(8,128)S(1)}, f32[264,256]{1,0:T(8,128)S(1)}, u32[]{:S(2)}, u32[]{:S(2)}) collective-permute-start(f32[264,256]{1,0:T(8,128)S(1)} %maximum_maximum_fusion.own_ref), channel_id=1, source_target_pairs={{0,16},{16,0},{1,17},{17,1},{2,18},{18,2},{3,19},{19,3},{4,20},{20... | collective-permute-start | bytes 811016 | tf_op jit(solution)/shard_map/ppermute | solution.py:147
  19.5 0.7 fusion.13.sq_ref
  20.3 5.7 %collective-permute-done.got_ref = f32[264,256]{1,0:T(8,128)S(1)} collective-permute-done((f32[264,256]{1,0:T(8,128)S(1)}, f32[264,256]{1,0:T(8,128)S(1)}, u32[]{:S(2)}, u32[]{:S(2)}) %collective-permute-start) | collective-permute-done | bytes 270368 | tf_op jit(solution)/shard_map/ppermute | solution.py:147
  26.0 0.6 broadcast_in_dim.7.sv_ref
  26.7 0.1 copy-done.6
  26.7 2.6 %shard_map.67 = (f32[264,256]{1,0:T(8,128)}, f32[256,256]{1,0:T(8,128)}, f32[8,256]{1,0:T(8,128)}) custom-call(f32[264,256]{1,0:T(8,128)} %copy-done.3, f32[264,256]{1,0:T(8,128)} %copy-done.6, f32[256,256]{1,0:T(8,128)} %fusion.13.sq_ref, f32[8,256]{1,0:T(8,128)} %broadcast_in_dim.7.sv_ref), custom_call_target="tpu_custom_call" | custom-call | tf_op jit(solution)/shard_map/pallas_call | solution.py:73
  29.3 0.0 collective-permute-start.1
  29.3 1.8 %collective-permute-done.1.got_ref = f32[264,256]{1,0:T(8,128)S(1)} collective-permute-done((f32[264,256]{1,0:T(8,128)}, f32[264,256]{1,0:T(8,128)S(1)}, u32[]{:S(2)}, u32[]{:S(2)}) %collective-permute-start.1) | collective-permute-done | bytes 270368 | tf_op jit(solution)/shard_map/ppermute | solution.py:147
  31.1 0.7 copy-done.7
  31.8 2.5 %shard_map.68 = (f32[264,256]{1,0:T(8,128)}, f32[256,256]{1,0:T(8,128)}, f32[8,256]{1,0:T(8,128)}) custom-call(f32[264,256]{1,0:T(8,128)} %get-tuple-element.29.own_ref, f32[264,256]{1,0:T(8,128)} %copy-done.7, f32[256,256]{1,0:T(8,128)} %get-tuple-element.30.sq_ref, f32[8,256]{1,0:T(8,128)} %get-tuple-element.31.sv_ref), custom_call_target="tpu_custom_call" | custom-call | tf_op jit(solution)/shard_map/pallas_call | solution.py:73
  34.3 1.7 %collective-permute-start.2 = (f32[264,256]{1,0:T(8,128)}, f32[264,256]{1,0:T(8,128)S(1)}, u32[]{:S(2)}, u32[]{:S(2)}) collective-permute-start(f32[264,256]{1,0:T(8,128)} %get-tuple-element.32.own_ref), channel_id=1, source_target_pairs={{0,2},{16,18},{1,3},{17,19},{2,0},{18,16},{3,1},{19,17},{4,6},{20,... | collective-permute-start | bytes 811016 | tf_op jit(solution)/shard_map/ppermute | solution.py:147
  36.0 7.0 %collective-permute-done.2.got_ref = f32[264,256]{1,0:T(8,128)S(1)} collective-permute-done((f32[264,256]{1,0:T(8,128)}, f32[264,256]{1,0:T(8,128)S(1)}, u32[]{:S(2)}, u32[]{:S(2)}) %collective-permute-start.2) | collective-permute-done | bytes 270368 | tf_op jit(solution)/shard_map/ppermute | solution.py:147
  43.1 0.7 copy-done.8
  43.8 2.6 %shard_map.69 = (f32[264,256]{1,0:T(8,128)}, f32[256,256]{1,0:T(8,128)}, f32[8,256]{1,0:T(8,128)}) custom-call(f32[264,256]{1,0:T(8,128)} %get-tuple-element.32.own_ref, f32[264,256]{1,0:T(8,128)} %copy-done.8, f32[256,256]{1,0:T(8,128)} %get-tuple-element.33.sq_ref, f32[8,256]{1,0:T(8,128)} %get-tuple-element.34.sv_ref), custom_call_target="tpu_custom_call" | custom-call | tf_op jit(solution)/shard_map/pallas_call | solution.py:73
  46.3 1.8 %collective-permute-start.3 = (f32[264,256]{1,0:T(8,128)}, f32[264,256]{1,0:T(8,128)S(1)}, u32[]{:S(2)}, u32[]{:S(2)}) collective-permute-start(f32[264,256]{1,0:T(8,128)} %get-tuple-element.35.own_ref), channel_id=1, source_target_pairs={{0,4},{16,20},{1,5},{17,21},{2,6},{18,22},{3,7},{19,23},{4,0},{20,... | collective-permute-start | bytes 811016 | tf_op jit(solution)/shard_map/ppermute | solution.py:147
  48.1 0.8 pad_maximum_fusion.refs_14_
  49.0 0.0 copy-done.12
  49.0 5.3 %collective-permute-done.3.got_ref = f32[264,256]{1,0:T(8,128)S(1)} collective-permute-done((f32[264,256]{1,0:T(8,128)}, f32[264,256]{1,0:T(8,128)S(1)}, u32[]{:S(2)}, u32[]{:S(2)}) %collective-permute-start.3) | collective-permute-done | bytes 270368 | tf_op jit(solution)/shard_map/ppermute | solution.py:147
  54.3 0.7 copy-done.5
  55.0 2.6 %shard_map.70 = (f32[264,256]{1,0:T(8,128)}, f32[256,256]{1,0:T(8,128)}, f32[8,256]{1,0:T(8,128)}) custom-call(f32[264,256]{1,0:T(8,128)} %get-tuple-element.35.own_ref, f32[264,256]{1,0:T(8,128)} %copy-done.5, f32[256,256]{1,0:T(8,128)} %get-tuple-element.36.sq_ref, f32[8,256]{1,0:T(8,128)} %get-tuple-element.37.sv_ref), custom_call_target="tpu_custom_call" | custom-call | tf_op jit(solution)/shard_map/pallas_call | solution.py:73
  57.6 0.7 slice.108
  58.3 2.8 %collective-permute-start.4 = (f32[8,256]{1,0:T(8,128)S(1)}, f32[8,256]{1,0:T(8,128)S(1)}, u32[]{:S(2)}, u32[]{:S(2)}) collective-permute-start(f32[8,256]{1,0:T(8,128)S(1)} %slice.108), channel_id=1, source_target_pairs={{0,8},{16,24},{1,9},{17,25},{2,10},{18,26},{3,11},{19,27},{4,12},{... | collective-permute-start | bytes 24584 | tf_op jit(solution)/shard_map/ppermute | solution.py:147
  61.0 0.6 pad_maximum_fusion.1.refs_15_
  61.6 0.0 copy-done.13
  61.6 0.6 copy.9
  62.2 0.6 collective-permute-done.4.refs_0_
  62.8 0.6 copy-done.14
  63.4 6.4 %shard_map.71 = (f32[24,256]{1,0:T(8,128)}, f32[136,128]{1,0:T(8,128)}) custom-call(f32[8,256]{1,0:T(8,128)} %copy-done.14, f32[256,256]{1,0:T(8,128)} %get-tuple-element.39.refs_1_, f32[8,256]{1,0:T(8,128)} %get-tuple-element.40.refs_2_, f32[24,256]{1,0:T(8,128)} %bitcast.37, f32[2,24,128]{2,1,0:T(8,128)} %bitcast.39, f32[24,256]{1,0:T(8,128)} %bitcast.38, ...), custom_call_target="tpu_custom_call" | custom-call | tf_op jit(solution)/shard_map/pallas_call | solution.py:130
  69.9 1.3 %multiply_reduce_fusion.6 = f32[]{:T(128)} fusion(f32[24,256]{1,0:T(8,128)} %get-tuple-element.41, f32[1,24,256]{2,1,0:T(8,128)S(1)} %copy-done.10), kind=kLoop, calls=%fused_computation.26 | loop fusion | flops 12287 | bytes 49156 | tf_op jit(solution)/shard_map/reduce_sum | solution.py:177
  71.9 1.3 %scatter.4 = f32[136,128]{1,0:T(8,128)} dynamic-update-slice(f32[136,128]{1,0:T(8,128)} %get-tuple-element.42, f32[1,1]{1,0:T(1,128)} %bitcast.14, s32[]{:T(128)} %constant.32.clone.1, s32[]{:T(128)} %constant.33.clone.1) | dynamic-update-slice | bytes 12 | tf_op jit(solution)/shard_map/scatter | solution.py:178
  73.1 1.7 %collective-permute-start.5 = (f32[136,128]{1,0:T(8,128)}, f32[136,128]{1,0:T(8,128)S(1)}, u32[]{:S(2)}, u32[]{:S(2)}) collective-permute-start(f32[136,128]{1,0:T(8,128)} %scatter.4), channel_id=1, source_target_pairs={{0,16},{16,0},{1,17},{17,1},{2,18},{18,2},{3,19},{19,3},{4,20},{20... | collective-permute-start | bytes 208904 | tf_op jit(solution)/shard_map/ppermute | solution.py:147
  74.8 2.8 %collective-permute-done.5 = f32[136,128]{1,0:T(8,128)S(1)} collective-permute-done((f32[136,128]{1,0:T(8,128)}, f32[136,128]{1,0:T(8,128)S(1)}, u32[]{:S(2)}, u32[]{:S(2)}) %collective-permute-start.5) | collective-permute-done | bytes 69664 | tf_op jit(solution)/shard_map/ppermute | solution.py:147
  77.7 0.9 add.37
  78.6 0.1 collective-permute-start.6
  78.6 1.2 %collective-permute-done.6 = f32[136,128]{1,0:T(8,128)S(1)} collective-permute-done((f32[136,128]{1,0:T(8,128)S(1)}, f32[136,128]{1,0:T(8,128)S(1)}, u32[]{:S(2)}, u32[]{:S(2)}) %collective-permute-start.6) | collective-permute-done | bytes 69664 | tf_op jit(solution)/shard_map/ppermute | solution.py:147
  79.9 1.7 %collective-permute-start.7 = (f32[136,128]{1,0:T(8,128)S(1)}, f32[136,128]{1,0:T(8,128)S(1)}, u32[]{:S(2)}, u32[]{:S(2)}) collective-permute-start(f32[136,128]{1,0:T(8,128)S(1)} %add.38), channel_id=1, source_target_pairs={{0,2},{16,18},{1,3},{17,19},{2,0},{18,16},{3,1},{19,17},{4,6},{20,... | collective-permute-start | bytes 208904 | tf_op jit(solution)/shard_map/ppermute | solution.py:147
  81.6 2.6 %collective-permute-done.7 = f32[136,128]{1,0:T(8,128)S(1)} collective-permute-done((f32[136,128]{1,0:T(8,128)S(1)}, f32[136,128]{1,0:T(8,128)S(1)}, u32[]{:S(2)}, u32[]{:S(2)}) %collective-permute-start.7) | collective-permute-done | bytes 69664 | tf_op jit(solution)/shard_map/ppermute | solution.py:147
  84.3 1.8 %collective-permute-start.8 = (f32[136,128]{1,0:T(8,128)S(1)}, f32[136,128]{1,0:T(8,128)S(1)}, u32[]{:S(2)}, u32[]{:S(2)}) collective-permute-start(f32[136,128]{1,0:T(8,128)S(1)} %add.39), channel_id=1, source_target_pairs={{0,4},{16,20},{1,5},{17,21},{2,6},{18,22},{3,7},{19,23},{4,0},{20,... | collective-permute-start | bytes 208904 | tf_op jit(solution)/shard_map/ppermute | solution.py:147
  86.1 2.6 %collective-permute-done.8 = f32[136,128]{1,0:T(8,128)S(1)} collective-permute-done((f32[136,128]{1,0:T(8,128)S(1)}, f32[136,128]{1,0:T(8,128)S(1)}, u32[]{:S(2)}, u32[]{:S(2)}) %collective-permute-start.8) | collective-permute-done | bytes 69664 | tf_op jit(solution)/shard_map/ppermute | solution.py:147
  88.7 2.8 %collective-permute-start.9 = (f32[136,128]{1,0:T(8,128)S(1)}, f32[136,128]{1,0:T(8,128)S(1)}, u32[]{:S(2)}, u32[]{:S(2)}) collective-permute-start(f32[136,128]{1,0:T(8,128)S(1)} %add.40), channel_id=1, source_target_pairs={{0,8},{16,24},{1,9},{17,25},{2,10},{18,26},{3,11},{19,27},{4,12},{... | collective-permute-start | bytes 208904 | tf_op jit(solution)/shard_map/ppermute | solution.py:147
  91.5 2.5 %collective-permute-done.9 = f32[136,128]{1,0:T(8,128)S(1)} collective-permute-done((f32[136,128]{1,0:T(8,128)S(1)}, f32[136,128]{1,0:T(8,128)S(1)}, u32[]{:S(2)}, u32[]{:S(2)}) %collective-permute-start.9) | collective-permute-done | bytes 69664 | tf_op jit(solution)/shard_map/ppermute | solution.py:147
  94.0 0.6 slice.117
  94.6 0.5 slice.118
  (30 shorter events, 0.2 us)
Async XLA Ops:
  0.6 2.9 %copy-start = (bf16[1,24,256,256]{3,2,1,0:T(8,128)(2,1)S(1)}, bf16[1,24,256,256]{3,2,1,0:T(8,128)(2,1)}, u32[]{:S(2)}) copy-start(bf16[1,24,256,256]{3,2,1,0:T(8,128)(2,1)} %param.6) | copy-start | bytes 9437188
  3.2 2.5 %copy-start.4 = (f32[24,256]{1,0:T(8,128)}, f32[24,256]{1,0:T(8,128)S(1)}, u32[]{:S(2)}) copy-start(f32[24,256]{1,0:T(8,128)S(1)} %multiply_reduce_fusion.refs_7_) | copy-start | bytes 73732
  6.2 4.9 %copy-start.1 = (f32[12,256,256]{2,1,0:T(8,128)S(1)}, f32[12,256,256]{2,1,0:T(8,128)}, u32[]{:S(2)}) copy-start(f32[12,256,256]{2,1,0:T(8,128)} %fusion.2.refs_8_) | copy-start | bytes 9437188
  6.2 5.1 %copy-start.9 = (f32[12,256]{1,0:T(8,128)}, f32[12,256]{1,0:T(8,128)S(1)}, u32[]{:S(2)}) copy-start(f32[12,256]{1,0:T(8,128)S(1)} %add.32.refs_9_) | copy-start | bytes 36868
  11.4 8.9 %copy-start.11 = (f32[6,256]{1,0:T(8,128)}, f32[6,256]{1,0:T(8,128)S(1)}, u32[]{:S(2)}) copy-start(f32[6,256]{1,0:T(8,128)S(1)} %add.33.refs_11_) | copy-start | bytes 18436
  13.7 32.6 %copy-start.2 = (f32[3,256,256]{2,1,0:T(8,128)}, f32[3,256,256]{2,1,0:T(8,128)S(1)}, u32[]{:S(2)}) copy-start(f32[3,256,256]{2,1,0:T(8,128)S(1)} %fusion.6.refs_12_) | copy-start | bytes 2359300
  15.4 33.6 %copy-start.12 = (f32[3,256]{1,0:T(4,128)}, f32[3,256]{1,0:T(4,128)S(1)}, u32[]{:S(2)}) copy-start(f32[3,256]{1,0:T(4,128)S(1)} %add.34.refs_13_) | copy-start | bytes 9220
  15.9 45.7 %copy-start.13 = (f32[1,24,2,128]{3,2,1,0:T(2,128)S(1)}, f32[1,24,2,128]{3,2,1,0:T(2,128)}, u32[]{:S(2)}) copy-start(f32[1,24,2,128]{3,2,1,0:T(2,128)} %param.8) | copy-start | bytes 73732
  16.5 10.2 %copy-start.3 = (f32[264,256]{1,0:T(8,128)}, f32[264,256]{1,0:T(8,128)S(1)}, u32[]{:S(2)}) copy-start(f32[264,256]{1,0:T(8,128)S(1)} %maximum_maximum_fusion.own_ref) | copy-start | bytes 811012
  16.5 9.5 %collective-permute-start = (f32[264,256]{1,0:T(8,128)S(1)}, f32[264,256]{1,0:T(8,128)S(1)}, u32[]{:S(2)}, u32[]{:S(2)}) collective-permute-start(f32[264,256]{1,0:T(8,128)S(1)} %maximum_maximum_fusion.own_ref), channel_id=1, source_target_pairs={{0,16},{16,0},{1,17},{17,1},{2,18},{18,2},{3,19},{19,3},{4,20},{20... | collective-permute-start | bytes 811016 | tf_op jit(solution)/shard_map/ppermute | solution.py:147
  26.0 0.7 copy-start.6
  29.3 1.8 %collective-permute-start.1 = (f32[264,256]{1,0:T(8,128)}, f32[264,256]{1,0:T(8,128)S(1)}, u32[]{:S(2)}, u32[]{:S(2)}) collective-permute-start(f32[264,256]{1,0:T(8,128)} %get-tuple-element.29.own_ref), channel_id=1, source_target_pairs={{0,1},{16,17},{1,0},{17,16},{2,3},{18,19},{3,2},{19,18},{4,5},{20,... | collective-permute-start | bytes 811016 | tf_op jit(solution)/shard_map/ppermute | solution.py:147
  31.1 0.7 copy-start.7
  34.3 8.7 %collective-permute-start.2 = (f32[264,256]{1,0:T(8,128)}, f32[264,256]{1,0:T(8,128)S(1)}, u32[]{:S(2)}, u32[]{:S(2)}) collective-permute-start(f32[264,256]{1,0:T(8,128)} %get-tuple-element.32.own_ref), channel_id=1, source_target_pairs={{0,2},{16,18},{1,3},{17,19},{2,0},{18,16},{3,1},{19,17},{4,6},{20,... | collective-permute-start | bytes 811016 | tf_op jit(solution)/shard_map/ppermute | solution.py:147
  43.0 0.7 copy-start.8
  46.3 8.0 %collective-permute-start.3 = (f32[264,256]{1,0:T(8,128)}, f32[264,256]{1,0:T(8,128)S(1)}, u32[]{:S(2)}, u32[]{:S(2)}) collective-permute-start(f32[264,256]{1,0:T(8,128)} %get-tuple-element.35.own_ref), channel_id=1, source_target_pairs={{0,4},{16,20},{1,5},{17,21},{2,6},{18,22},{3,7},{19,23},{4,0},{20,... | collective-permute-start | bytes 811016 | tf_op jit(solution)/shard_map/ppermute | solution.py:147
  54.3 0.7 copy-start.5
  58.3 4.5 %collective-permute-start.4 = (f32[8,256]{1,0:T(8,128)S(1)}, f32[8,256]{1,0:T(8,128)S(1)}, u32[]{:S(2)}, u32[]{:S(2)}) collective-permute-start(f32[8,256]{1,0:T(8,128)S(1)} %slice.108), channel_id=1, source_target_pairs={{0,8},{16,24},{1,9},{17,25},{2,10},{18,26},{3,11},{19,27},{4,12},{... | collective-permute-start | bytes 24584 | tf_op jit(solution)/shard_map/ppermute | solution.py:147
  62.8 0.6 copy-start.14
  63.4 6.4 %copy-start.10 = (f32[1,24,256]{2,1,0:T(8,128)S(1)}, f32[1,24,256]{2,1,0:T(8,128)}, u32[]{:S(2)}) copy-start(f32[1,24,256]{2,1,0:T(8,128)} %param.9) | copy-start | bytes 73732
  73.1 4.5 %collective-permute-start.5 = (f32[136,128]{1,0:T(8,128)}, f32[136,128]{1,0:T(8,128)S(1)}, u32[]{:S(2)}, u32[]{:S(2)}) collective-permute-start(f32[136,128]{1,0:T(8,128)} %scatter.4), channel_id=1, source_target_pairs={{0,16},{16,0},{1,17},{17,1},{2,18},{18,2},{3,19},{19,3},{4,20},{20... | collective-permute-start | bytes 208904 | tf_op jit(solution)/shard_map/ppermute | solution.py:147
  78.6 1.3 %collective-permute-start.6 = (f32[136,128]{1,0:T(8,128)S(1)}, f32[136,128]{1,0:T(8,128)S(1)}, u32[]{:S(2)}, u32[]{:S(2)}) collective-permute-start(f32[136,128]{1,0:T(8,128)S(1)} %add.37), channel_id=1, source_target_pairs={{0,1},{16,17},{1,0},{17,16},{2,3},{18,19},{3,2},{19,18},{4,5},{20,... | collective-permute-start | bytes 208904 | tf_op jit(solution)/shard_map/ppermute | solution.py:147
  79.9 4.4 %collective-permute-start.7 = (f32[136,128]{1,0:T(8,128)S(1)}, f32[136,128]{1,0:T(8,128)S(1)}, u32[]{:S(2)}, u32[]{:S(2)}) collective-permute-start(f32[136,128]{1,0:T(8,128)S(1)} %add.38), channel_id=1, source_target_pairs={{0,2},{16,18},{1,3},{17,19},{2,0},{18,16},{3,1},{19,17},{4,6},{20,... | collective-permute-start | bytes 208904 | tf_op jit(solution)/shard_map/ppermute | solution.py:147
  84.3 4.4 %collective-permute-start.8 = (f32[136,128]{1,0:T(8,128)S(1)}, f32[136,128]{1,0:T(8,128)S(1)}, u32[]{:S(2)}, u32[]{:S(2)}) collective-permute-start(f32[136,128]{1,0:T(8,128)S(1)} %add.39), channel_id=1, source_target_pairs={{0,4},{16,20},{1,5},{17,21},{2,6},{18,22},{3,7},{19,23},{4,0},{20,... | collective-permute-start | bytes 208904 | tf_op jit(solution)/shard_map/ppermute | solution.py:147
  88.7 5.3 %collective-permute-start.9 = (f32[136,128]{1,0:T(8,128)S(1)}, f32[136,128]{1,0:T(8,128)S(1)}, u32[]{:S(2)}, u32[]{:S(2)}) collective-permute-start(f32[136,128]{1,0:T(8,128)S(1)} %add.40), channel_id=1, source_target_pairs={{0,8},{16,24},{1,9},{17,25},{2,10},{18,26},{3,11},{19,27},{4,12},{... | collective-permute-start | bytes 208904 | tf_op jit(solution)/shard_map/ppermute | solution.py:147

commit v14 on v11

--- a/solution.py
+++ b/solution.py
@@ -10,6 +10,18 @@
 
 def vecmat(v, q):
     return jnp.sum(v[:, :, None] * q.astype(jnp.float32), axis=1)
+
+
+def split_rows(v):
+    first = lax.reduce_precision(v, exponent_bits=8, mantissa_bits=7)
+    rest = v - first
+    second = lax.reduce_precision(rest, exponent_bits=8, mantissa_bits=7)
+    return jnp.stack([first, second, rest - second], axis=1).astype(jnp.bfloat16)
+
+
+def vecmat_bf16(v, q):
+    parts = jnp.einsum("npj,njk->npk", split_rows(v), q, preferred_element_type=jnp.float32)
+    return (parts[:, 0] + parts[:, 1]) + parts[:, 2]
 
 
 def vecmat_mxu(v, q):
@@ -155,7 +167,7 @@
     count = lax.axis_size("outer") * lax.axis_size("inner")
     me = lax.axis_index("outer") * lax.axis_size("inner") + lax.axis_index("inner")
 
-    leaf_v = vecmat(grads, blocks)
+    leaf_v = vecmat_bf16(grads, blocks)
     levels = upsweep(blocks, leaf_v)
     tq, tv = levels[-1]
     tq, tv = tq[0].astype(jnp.float32), tv[0]

time: 92.8 us -> 93.6 us (level)
  matrix products: 5.79 us -> 8.34 us
  other arithmetic: 8.19 us -> 6.37 us
    reduce_sum x4 -> x3, other arithmetic: 3.55 us -> 0.95 us  [vecmat(): return jnp.sum(v[:, :, None] * q.astype(jnp.float32), axis=1)]
    dot_general x0 -> x1, matrix products: none -> 2.55 us  [vecmat_bf16(): jnp.einsum('npj,njk->npk', split_rows(v), q, preferred_element_type=jnp.f...]
where the time goes in v14:
time: 93.6 us; the launch traced here: 93.2 us
  waiting for transfers between devices  32.8 us (35%)
  Pallas kernels  18 us (19%)
  starting transfers between devices  17.4 us (19%)
  local copies, waits for them, and re-layouts  8.69 us (9%)
  matrix products  8.34 us (9%)
  other arithmetic  6.37 us (7%)
  between operations  1.52 us (2%)
    ppermute x10, waiting for transfers between devices, exchange(): lax.ppermute(x, AXES, [(place(j), place(j ^ mask)) for j in range(count)])  32.8 us
    ppermute x10, starting transfers between devices, exchange(): lax.ppermute(x, AXES, [(place(j), place(j ^ mask)) for j in range(count)])  17.4 us
    pallas_call x4, Pallas kernels, run(): pl.pallas_call(kernel, out_shape=(jax.ShapeDtypeStruct(own.shape, jnp.flo...  10.3 us
    pallas_call x1, Pallas kernels, run(): pl.pallas_call(kernel, out_shape=(jax.ShapeDtypeStruct(grads.shape, jnp.f...  7.74 us
    dot_general x4, matrix products, matmat(): jnp.einsum('nij,njk->nik', later.astype(jnp.float32), earlier.astype(jnp....  5.22 us
    unnamed x30, local copies, waits for them, and re-layouts  4.72 us
    dot_general x1, matrix products, vecmat_bf16(): jnp.einsum('npj,njk->npk', split_rows(v), q, preferred_element_type=jnp.f...  2.55 us
  transfers between devices with their start and end apart: 10, of which 10 were waited for; matrix products, arithmetic and copies ran while one was open for 2% of the time, Pallas kernels for 0%

profile of v14, /device:TPU:0, one launch (start us, length us, event | category | flops | bytes accessed | tf_op | source)
XLA Modules:
  0.0 93.2 jit_solution(14272026159723298940)
XLA Ops:
  0.6 0.7 reduce-precision_convert_fusion.1
  1.4 0.0 copy-start
  1.4 2.6 %fusion.15 = f32[24,3,256]{2,1,0:T(4,128)S(1)} fusion(bf16[24,3,256]{2,0,1:T(8,128)(2,1)S(1)} %pad_maximum_fusion.1, bf16[1,24,256,256]{3,2,1,0:T(8,128)(2,1)} %param.6), kind=kOutput, calls=%fused_computation.24 | convolution fusion | flops 9437184 | bytes 3256320 | tf_op jit(solution)/shard_map/npj,njk->npk/dot_general | solution.py:23
  4.0 0.1 fusion.23
  4.0 0.0 copy-start.5
  4.1 0.2 copy-done
  4.2 0.5 multiply_reduce_fusion
  4.7 0.0 copy-start.10
  4.8 0.6 fusion.2.refs_8_
  5.4 0.0 copy-done.5
  5.4 0.0 copy-done.10
  5.4 1.6 %copy-done.1 = f32[12,256,256]{2,1,0:T(8,128)} copy-done((f32[12,256,256]{2,1,0:T(8,128)}, f32[12,256,256]{2,1,0:T(8,128)S(1)}, u32[]{:S(2)}) %copy-start.1) | copy-done | bytes 3145752
  7.0 0.3 multiply_reduce_fusion.1
  7.3 0.0 copy-start.12
  7.4 3.5 %fusion.refs_10_ = f32[6,256,256]{2,1,0:T(8,128)S(1)} fusion(f32[12,256,256]{2,1,0:T(8,128)} %copy-done.1), kind=kOutput, calls=%fused_computation.2 | convolution fusion | flops 1207959552 | bytes 4718592 | tf_op jit(solution)/shard_map/nij,njk->nik/dot_general | solution.py:34
  10.9 0.9 fusion.6.refs_12_
  11.9 0.2 multiply_reduce_fusion.2
  12.0 0.0 copy-done.2
  12.1 0.1 fusion.22
  12.2 0.4 multiply_reduce_fusion.4
  12.6 0.4 fusion.11
  13.0 0.1 pad.10.clone
  13.1 0.1 maximum_maximum_fusion.own_ref
  13.2 3.0 %collective-permute-start = (f32[264,256]{1,0:T(8,128)S(1)}, f32[264,256]{1,0:T(8,128)S(1)}, u32[]{:S(2)}, u32[]{:S(2)}) collective-permute-start(f32[264,256]{1,0:T(8,128)S(1)} %maximum_maximum_fusion.own_ref), channel_id=1, source_target_pairs={{0,16},{16,0},{1,17},{17,1},{2,18},{18,2},{3,19},{19,3},{4,20},{20... | collective-permute-start | bytes 811016 | tf_op jit(solution)/shard_map/ppermute | solution.py:159
  16.2 0.7 fusion.13.sq_ref
  17.0 5.8 %collective-permute-done.got_ref = f32[264,256]{1,0:T(8,128)S(1)} collective-permute-done((f32[264,256]{1,0:T(8,128)S(1)}, f32[264,256]{1,0:T(8,128)S(1)}, u32[]{:S(2)}, u32[]{:S(2)}) %collective-permute-start) | collective-permute-done | bytes 270368 | tf_op jit(solution)/shard_map/ppermute | solution.py:159
  22.7 0.6 broadcast_in_dim.7.sv_ref
  23.4 0.1 copy-done.7
  23.4 2.6 %shard_map.67 = (f32[264,256]{1,0:T(8,128)}, f32[256,256]{1,0:T(8,128)}, f32[8,256]{1,0:T(8,128)}) custom-call(f32[264,256]{1,0:T(8,128)} %copy-done.4, f32[264,256]{1,0:T(8,128)} %copy-done.7, f32[256,256]{1,0:T(8,128)} %fusion.13.sq_ref, f32[8,256]{1,0:T(8,128)} %broadcast_in_dim.7.sv_ref), custom_call_target="tpu_custom_call" | custom-call | tf_op jit(solution)/shard_map/pallas_call | solution.py:85
  26.0 0.0 collective-permute-start.1
  26.0 1.8 %collective-permute-done.1.got_ref = f32[264,256]{1,0:T(8,128)S(1)} collective-permute-done((f32[264,256]{1,0:T(8,128)}, f32[264,256]{1,0:T(8,128)S(1)}, u32[]{:S(2)}, u32[]{:S(2)}) %collective-permute-start.1) | collective-permute-done | bytes 270368 | tf_op jit(solution)/shard_map/ppermute | solution.py:159
  27.8 0.7 copy-done.8
  28.5 2.5 %shard_map.68 = (f32[264,256]{1,0:T(8,128)}, f32[256,256]{1,0:T(8,128)}, f32[8,256]{1,0:T(8,128)}) custom-call(f32[264,256]{1,0:T(8,128)} %get-tuple-element.29.own_ref, f32[264,256]{1,0:T(8,128)} %copy-done.8, f32[256,256]{1,0:T(8,128)} %get-tuple-element.30.sq_ref, f32[8,256]{1,0:T(8,128)} %get-tuple-element.31.sv_ref), custom_call_target="tpu_custom_call" | custom-call | tf_op jit(solution)/shard_map/pallas_call | solution.py:85
  31.1 1.7 %collective-permute-start.2 = (f32[264,256]{1,0:T(8,128)}, f32[264,256]{1,0:T(8,128)S(1)}, u32[]{:S(2)}, u32[]{:S(2)}) collective-permute-start(f32[264,256]{1,0:T(8,128)} %get-tuple-element.32.own_ref), channel_id=1, source_target_pairs={{0,2},{16,18},{1,3},{17,19},{2,0},{18,16},{3,1},{19,17},{4,6},{20,... | collective-permute-start | bytes 811016 | tf_op jit(solution)/shard_map/ppermute | solution.py:159
  32.8 7.0 %collective-permute-done.2.got_ref = f32[264,256]{1,0:T(8,128)S(1)} collective-permute-done((f32[264,256]{1,0:T(8,128)}, f32[264,256]{1,0:T(8,128)S(1)}, u32[]{:S(2)}, u32[]{:S(2)}) %collective-permute-start.2) | collective-permute-done | bytes 270368 | tf_op jit(solution)/shard_map/ppermute | solution.py:159
  39.8 0.7 copy-done.9
  40.5 2.6 %shard_map.69 = (f32[264,256]{1,0:T(8,128)}, f32[256,256]{1,0:T(8,128)}, f32[8,256]{1,0:T(8,128)}) custom-call(f32[264,256]{1,0:T(8,128)} %get-tuple-element.32.own_ref, f32[264,256]{1,0:T(8,128)} %copy-done.9, f32[256,256]{1,0:T(8,128)} %get-tuple-element.33.sq_ref, f32[8,256]{1,0:T(8,128)} %get-tuple-element.34.sv_ref), custom_call_target="tpu_custom_call" | custom-call | tf_op jit(solution)/shard_map/pallas_call | solution.py:85
  43.1 1.8 %collective-permute-start.3 = (f32[264,256]{1,0:T(8,128)}, f32[264,256]{1,0:T(8,128)S(1)}, u32[]{:S(2)}, u32[]{:S(2)}) collective-permute-start(f32[264,256]{1,0:T(8,128)} %get-tuple-element.35.own_ref), channel_id=1, source_target_pairs={{0,4},{16,20},{1,5},{17,21},{2,6},{18,22},{3,7},{19,23},{4,0},{20,... | collective-permute-start | bytes 811016 | tf_op jit(solution)/shard_map/ppermute | solution.py:159
  44.9 0.8 pad_maximum_fusion.refs_14_
  45.7 5.3 %collective-permute-done.3.got_ref = f32[264,256]{1,0:T(8,128)S(1)} collective-permute-done((f32[264,256]{1,0:T(8,128)}, f32[264,256]{1,0:T(8,128)S(1)}, u32[]{:S(2)}, u32[]{:S(2)}) %collective-permute-start.3) | collective-permute-done | bytes 270368 | tf_op jit(solution)/shard_map/ppermute | solution.py:159
  51.1 0.7 copy-done.6
  51.8 2.6 %shard_map.70 = (f32[264,256]{1,0:T(8,128)}, f32[256,256]{1,0:T(8,128)}, f32[8,256]{1,0:T(8,128)}) custom-call(f32[264,256]{1,0:T(8,128)} %get-tuple-element.35.own_ref, f32[264,256]{1,0:T(8,128)} %copy-done.6, f32[256,256]{1,0:T(8,128)} %get-tuple-element.36.sq_ref, f32[8,256]{1,0:T(8,128)} %get-tuple-element.37.sv_ref), custom_call_target="tpu_custom_call" | custom-call | tf_op jit(solution)/shard_map/pallas_call | solution.py:85
  54.4 0.7 slice.120
  55.0 2.8 %collective-permute-start.4 = (f32[8,256]{1,0:T(8,128)S(1)}, f32[8,256]{1,0:T(8,128)S(1)}, u32[]{:S(2)}, u32[]{:S(2)}) collective-permute-start(f32[8,256]{1,0:T(8,128)S(1)} %slice.120), channel_id=1, source_target_pairs={{0,8},{16,24},{1,9},{17,25},{2,10},{18,26},{3,11},{19,27},{4,12},{... | collective-permute-start | bytes 24584 | tf_op jit(solution)/shard_map/ppermute | solution.py:159
  57.8 0.6 pad_maximum_fusion.2.refs_15_
  58.4 1.2 %collective-permute-done.4.refs_0_ = f32[8,256]{1,0:T(8,128)S(1)} collective-permute-done((f32[8,256]{1,0:T(8,128)S(1)}, f32[8,256]{1,0:T(8,128)S(1)}, u32[]{:S(2)}, u32[]{:S(2)}) %collective-permute-start.4) | collective-permute-done | bytes 8224 | tf_op jit(solution)/shard_map/ppermute | solution.py:159
  59.6 0.6 copy-done.14
  60.2 7.7 %shard_map.71 = (f32[24,256]{1,0:T(8,128)}, f32[136,128]{1,0:T(8,128)}) custom-call(f32[8,256]{1,0:T(8,128)} %copy-done.14, f32[256,256]{1,0:T(8,128)} %get-tuple-element.39.refs_1_, f32[8,256]{1,0:T(8,128)} %get-tuple-element.40.refs_2_, f32[24,256]{1,0:T(8,128)} %bitcast.43, f32[24,2,128]{2,1,0:T(2,128)} %bitcast.45, f32[24,256]{1,0:T(8,128)} %bitcast.42, ...), custom_call_target="tpu_custom_call" | custom-call | tf_op jit(solution)/shard_map/pallas_call | solution.py:142
  68.0 0.0 copy-done.11
  68.0 1.3 %multiply_reduce_fusion.5 = f32[]{:T(128)} fusion(f32[24,256]{1,0:T(8,128)} %get-tuple-element.41, f32[1,24,256]{2,1,0:T(8,128)S(1)} %copy-done.11), kind=kLoop, calls=%fused_computation.35 | loop fusion | flops 12287 | bytes 49156 | tf_op jit(solution)/shard_map/reduce_sum | solution.py:189
  70.0 1.3 %scatter.4 = f32[136,128]{1,0:T(8,128)} dynamic-update-slice(f32[136,128]{1,0:T(8,128)} %get-tuple-element.42, f32[1,1]{1,0:T(1,128)} %bitcast.15, s32[]{:T(128)} %constant.32.clone.1, s32[]{:T(128)} %constant.33.clone.1) | dynamic-update-slice | bytes 12 | tf_op jit(solution)/shard_map/scatter | solution.py:190
  71.2 1.7 %collective-permute-start.5 = (f32[136,128]{1,0:T(8,128)}, f32[136,128]{1,0:T(8,128)S(1)}, u32[]{:S(2)}, u32[]{:S(2)}) collective-permute-start(f32[136,128]{1,0:T(8,128)} %scatter.4), channel_id=1, source_target_pairs={{0,16},{16,0},{1,17},{17,1},{2,18},{18,2},{3,19},{19,3},{4,20},{20... | collective-permute-start | bytes 208904 | tf_op jit(solution)/shard_map/ppermute | solution.py:159
  72.9 2.8 %collective-permute-done.5 = f32[136,128]{1,0:T(8,128)S(1)} collective-permute-done((f32[136,128]{1,0:T(8,128)}, f32[136,128]{1,0:T(8,128)S(1)}, u32[]{:S(2)}, u32[]{:S(2)}) %collective-permute-start.5) | collective-permute-done | bytes 69664 | tf_op jit(solution)/shard_map/ppermute | solution.py:159
  75.7 0.9 add.49
  76.6 0.1 collective-permute-start.6
  76.7 1.2 %collective-permute-done.6 = f32[136,128]{1,0:T(8,128)S(1)} collective-permute-done((f32[136,128]{1,0:T(8,128)S(1)}, f32[136,128]{1,0:T(8,128)S(1)}, u32[]{:S(2)}, u32[]{:S(2)}) %collective-permute-start.6) | collective-permute-done | bytes 69664 | tf_op jit(solution)/shard_map/ppermute | solution.py:159
  78.0 1.7 %collective-permute-start.7 = (f32[136,128]{1,0:T(8,128)S(1)}, f32[136,128]{1,0:T(8,128)S(1)}, u32[]{:S(2)}, u32[]{:S(2)}) collective-permute-start(f32[136,128]{1,0:T(8,128)S(1)} %add.50), channel_id=1, source_target_pairs={{0,2},{16,18},{1,3},{17,19},{2,0},{18,16},{3,1},{19,17},{4,6},{20,... | collective-permute-start | bytes 208904 | tf_op jit(solution)/shard_map/ppermute | solution.py:159
  79.7 2.7 %collective-permute-done.7 = f32[136,128]{1,0:T(8,128)S(1)} collective-permute-done((f32[136,128]{1,0:T(8,128)S(1)}, f32[136,128]{1,0:T(8,128)S(1)}, u32[]{:S(2)}, u32[]{:S(2)}) %collective-permute-start.7) | collective-permute-done | bytes 69664 | tf_op jit(solution)/shard_map/ppermute | solution.py:159
  82.4 1.8 %collective-permute-start.8 = (f32[136,128]{1,0:T(8,128)S(1)}, f32[136,128]{1,0:T(8,128)S(1)}, u32[]{:S(2)}, u32[]{:S(2)}) collective-permute-start(f32[136,128]{1,0:T(8,128)S(1)} %add.51), channel_id=1, source_target_pairs={{0,4},{16,20},{1,5},{17,21},{2,6},{18,22},{3,7},{19,23},{4,0},{20,... | collective-permute-start | bytes 208904 | tf_op jit(solution)/shard_map/ppermute | solution.py:159
  84.2 2.6 %collective-permute-done.8 = f32[136,128]{1,0:T(8,128)S(1)} collective-permute-done((f32[136,128]{1,0:T(8,128)S(1)}, f32[136,128]{1,0:T(8,128)S(1)}, u32[]{:S(2)}, u32[]{:S(2)}) %collective-permute-start.8) | collective-permute-done | bytes 69664 | tf_op jit(solution)/shard_map/ppermute | solution.py:159
  86.7 2.8 %collective-permute-start.9 = (f32[136,128]{1,0:T(8,128)S(1)}, f32[136,128]{1,0:T(8,128)S(1)}, u32[]{:S(2)}, u32[]{:S(2)}) collective-permute-start(f32[136,128]{1,0:T(8,128)S(1)} %add.52), channel_id=1, source_target_pairs={{0,8},{16,24},{1,9},{17,25},{2,10},{18,26},{3,11},{19,27},{4,12},{... | collective-permute-start | bytes 208904 | tf_op jit(solution)/shard_map/ppermute | solution.py:159
  89.6 2.5 %collective-permute-done.9 = f32[136,128]{1,0:T(8,128)S(1)} collective-permute-done((f32[136,128]{1,0:T(8,128)S(1)}, f32[136,128]{1,0:T(8,128)S(1)}, u32[]{:S(2)}, u32[]{:S(2)}) %collective-permute-start.9) | collective-permute-done | bytes 69664 | tf_op jit(solution)/shard_map/ppermute | solution.py:159
  92.0 0.5 slice.133
  92.5 0.6 slice.132
  (33 shorter events, 0.2 us)
Async XLA Ops:
  1.4 2.8 %copy-start = (bf16[1,24,256,256]{3,2,1,0:T(8,128)(2,1)S(1)}, bf16[1,24,256,256]{3,2,1,0:T(8,128)(2,1)}, u32[]{:S(2)}) copy-start(bf16[1,24,256,256]{3,2,1,0:T(8,128)(2,1)} %param.6) | copy-start | bytes 9437188
  4.0 1.3 %copy-start.5 = (f32[24,256]{1,0:T(8,128)}, f32[24,256]{1,0:T(8,128)S(1)}, u32[]{:S(2)}) copy-start(f32[24,256]{1,0:T(8,128)S(1)} %fusion.18.refs_7_) | copy-start | bytes 73732
  4.7 0.6 copy-start.10
  5.4 1.6 %copy-start.1 = (f32[12,256,256]{2,1,0:T(8,128)}, f32[12,256,256]{2,1,0:T(8,128)S(1)}, u32[]{:S(2)}) copy-start(f32[12,256,256]{2,1,0:T(8,128)S(1)} %fusion.2.refs_8_) | copy-start | bytes 9437188
  7.3 3.6 %copy-start.12 = (f32[6,256]{1,0:T(8,128)}, f32[6,256]{1,0:T(8,128)S(1)}, u32[]{:S(2)}) copy-start(f32[6,256]{1,0:T(8,128)S(1)} %add.45.refs_11_) | copy-start | bytes 18436
  10.9 1.2 %copy-start.2 = (f32[6,256,256]{2,1,0:T(8,128)}, f32[6,256,256]{2,1,0:T(8,128)S(1)}, u32[]{:S(2)}) copy-start(f32[6,256,256]{2,1,0:T(8,128)S(1)} %fusion.refs_10_) | copy-start | bytes 4718596
  11.8 1.1 %copy-start.3 = (f32[3,256,256]{2,1,0:T(8,128)}, f32[3,256,256]{2,1,0:T(8,128)S(1)}, u32[]{:S(2)}) copy-start(f32[3,256,256]{2,1,0:T(8,128)S(1)} %fusion.6.refs_12_) | copy-start | bytes 2359300
  12.1 4.9 %copy-start.13 = (f32[3,256]{1,0:T(4,128)}, f32[3,256]{1,0:T(4,128)S(1)}, u32[]{:S(2)}) copy-start(f32[3,256]{1,0:T(4,128)S(1)} %add.46.refs_13_) | copy-start | bytes 9220
  13.2 10.2 %copy-start.4 = (f32[264,256]{1,0:T(8,128)}, f32[264,256]{1,0:T(8,128)S(1)}, u32[]{:S(2)}) copy-start(f32[264,256]{1,0:T(8,128)S(1)} %maximum_maximum_fusion.own_ref) | copy-start | bytes 811012
  13.2 9.5 %collective-permute-start = (f32[264,256]{1,0:T(8,128)S(1)}, f32[264,256]{1,0:T(8,128)S(1)}, u32[]{:S(2)}, u32[]{:S(2)}) collective-permute-start(f32[264,256]{1,0:T(8,128)S(1)} %maximum_maximum_fusion.own_ref), channel_id=1, source_target_pairs={{0,16},{16,0},{1,17},{17,1},{2,18},{18,2},{3,19},{19,3},{4,20},{20... | collective-permute-start | bytes 811016 | tf_op jit(solution)/shard_map/ppermute | solution.py:159
  22.7 0.7 copy-start.7
  26.0 1.8 %collective-permute-start.1 = (f32[264,256]{1,0:T(8,128)}, f32[264,256]{1,0:T(8,128)S(1)}, u32[]{:S(2)}, u32[]{:S(2)}) collective-permute-start(f32[264,256]{1,0:T(8,128)} %get-tuple-element.29.own_ref), channel_id=1, source_target_pairs={{0,1},{16,17},{1,0},{17,16},{2,3},{18,19},{3,2},{19,18},{4,5},{20,... | collective-permute-start | bytes 811016 | tf_op jit(solution)/shard_map/ppermute | solution.py:159
  27.8 0.7 copy-start.8
  31.1 8.7 %collective-permute-start.2 = (f32[264,256]{1,0:T(8,128)}, f32[264,256]{1,0:T(8,128)S(1)}, u32[]{:S(2)}, u32[]{:S(2)}) collective-permute-start(f32[264,256]{1,0:T(8,128)} %get-tuple-element.32.own_ref), channel_id=1, source_target_pairs={{0,2},{16,18},{1,3},{17,19},{2,0},{18,16},{3,1},{19,17},{4,6},{20,... | collective-permute-start | bytes 811016 | tf_op jit(solution)/shard_map/ppermute | solution.py:159
  39.8 0.7 copy-start.9
  43.1 8.0 %collective-permute-start.3 = (f32[264,256]{1,0:T(8,128)}, f32[264,256]{1,0:T(8,128)S(1)}, u32[]{:S(2)}, u32[]{:S(2)}) collective-permute-start(f32[264,256]{1,0:T(8,128)} %get-tuple-element.35.own_ref), channel_id=1, source_target_pairs={{0,4},{16,20},{1,5},{17,21},{2,6},{18,22},{3,7},{19,23},{4,0},{20,... | collective-permute-start | bytes 811016 | tf_op jit(solution)/shard_map/ppermute | solution.py:159
  51.1 0.7 copy-start.6
  55.0 4.5 %collective-permute-start.4 = (f32[8,256]{1,0:T(8,128)S(1)}, f32[8,256]{1,0:T(8,128)S(1)}, u32[]{:S(2)}, u32[]{:S(2)}) collective-permute-start(f32[8,256]{1,0:T(8,128)S(1)} %slice.120), channel_id=1, source_target_pairs={{0,8},{16,24},{1,9},{17,25},{2,10},{18,26},{3,11},{19,27},{4,12},{... | collective-permute-start | bytes 24584 | tf_op jit(solution)/shard_map/ppermute | solution.py:159
  59.6 0.6 copy-start.14
  60.2 7.7 %copy-start.11 = (f32[1,24,256]{2,1,0:T(8,128)S(1)}, f32[1,24,256]{2,1,0:T(8,128)}, u32[]{:S(2)}) copy-start(f32[1,24,256]{2,1,0:T(8,128)} %param.9) | copy-start | bytes 73732
  71.2 4.5 %collective-permute-start.5 = (f32[136,128]{1,0:T(8,128)}, f32[136,128]{1,0:T(8,128)S(1)}, u32[]{:S(2)}, u32[]{:S(2)}) collective-permute-start(f32[136,128]{1,0:T(8,128)} %scatter.4), channel_id=1, source_target_pairs={{0,16},{16,0},{1,17},{17,1},{2,18},{18,2},{3,19},{19,3},{4,20},{20... | collective-permute-start | bytes 208904 | tf_op jit(solution)/shard_map/ppermute | solution.py:159
  76.6 1.3 %collective-permute-start.6 = (f32[136,128]{1,0:T(8,128)S(1)}, f32[136,128]{1,0:T(8,128)S(1)}, u32[]{:S(2)}, u32[]{:S(2)}) collective-permute-start(f32[136,128]{1,0:T(8,128)S(1)} %add.49), channel_id=1, source_target_pairs={{0,1},{16,17},{1,0},{17,16},{2,3},{18,19},{3,2},{19,18},{4,5},{20,... | collective-permute-start | bytes 208904 | tf_op jit(solution)/shard_map/ppermute | solution.py:159
  78.0 4.4 %collective-permute-start.7 = (f32[136,128]{1,0:T(8,128)S(1)}, f32[136,128]{1,0:T(8,128)S(1)}, u32[]{:S(2)}, u32[]{:S(2)}) collective-permute-start(f32[136,128]{1,0:T(8,128)S(1)} %add.50), channel_id=1, source_target_pairs={{0,2},{16,18},{1,3},{17,19},{2,0},{18,16},{3,1},{19,17},{4,6},{20,... | collective-permute-start | bytes 208904 | tf_op jit(solution)/shard_map/ppermute | solution.py:159
  82.4 4.4 %collective-permute-start.8 = (f32[136,128]{1,0:T(8,128)S(1)}, f32[136,128]{1,0:T(8,128)S(1)}, u32[]{:S(2)}, u32[]{:S(2)}) collective-permute-start(f32[136,128]{1,0:T(8,128)S(1)} %add.51), channel_id=1, source_target_pairs={{0,4},{16,20},{1,5},{17,21},{2,6},{18,22},{3,7},{19,23},{4,0},{20,... | collective-permute-start | bytes 208904 | tf_op jit(solution)/shard_map/ppermute | solution.py:159
  86.7 5.3 %collective-permute-start.9 = (f32[136,128]{1,0:T(8,128)S(1)}, f32[136,128]{1,0:T(8,128)S(1)}, u32[]{:S(2)}, u32[]{:S(2)}) collective-permute-start(f32[136,128]{1,0:T(8,128)S(1)} %add.52), channel_id=1, source_target_pairs={{0,8},{16,24},{1,9},{17,25},{2,10},{18,26},{3,11},{19,27},{4,12},{... | collective-permute-start | bytes 208904 | tf_op jit(solution)/shard_map/ppermute | solution.py:159

commit v15 on v11

--- a/solution.py
+++ b/solution.py
@@ -62,12 +62,12 @@
         later = jnp.where(lower, got_ref[...], own_ref[...])
         early_q = jnp.where(lower, own_ref[0:width, :], got_ref[0:width, :])
         early_v = jnp.where(lower, own_ref[width:, :], got_ref[width:, :])
-        new_q = jnp.dot(later, early_q, precision=EXACT, preferred_element_type=jnp.float32)
-        new_s = jnp.dot(later, sq_ref[...], precision=EXACT, preferred_element_type=jnp.float32)
-        own_out[0:width, :] = new_q[0:width]
-        own_out[width:, :] = new_q[width:] + early_v
-        sq_out[...] = jnp.where(lower, new_s[0:width], sq_ref[...])
-        sv_out[...] = jnp.where(lower, new_s[width:] + sv_ref[...], sv_ref[...])
+        right = jnp.concatenate([early_q, sq_ref[...]], axis=1)
+        both = jnp.dot(later, right, precision=EXACT, preferred_element_type=jnp.float32)
+        own_out[0:width, :] = both[0:width, 0:width]
+        own_out[width:, :] = both[width:, 0:width] + early_v
+        sq_out[...] = jnp.where(lower, both[0:width, width:], sq_ref[...])
+        sv_out[...] = jnp.where(lower, both[width:, width:] + sv_ref[...], sv_ref[...])
 
     def run(own, got, sq, sv):
         return pl.pallas_call(
@@ -175,7 +175,10 @@
         rv, sq, sv, grads, station_loadings[0], offset_response[0], levels
     )
     local_noise = -jnp.sum(length_rates * offset_response[0])
-    packed = packed.at[stations, 0].set(local_noise)
+    spot = (lax.broadcasted_iota(jnp.int32, packed.shape, 0) == stations) & (
+        lax.broadcasted_iota(jnp.int32, packed.shape, 1) == 0
+    )
+    packed = jnp.where(spot, local_noise, packed)
     d = 1
     while d < count:
         packed = packed + exchange(packed, d, count)

time: 92.8 us -> 96.5 us (1.040)
  matrix products: 5.79 us -> 10 us
  local copies, waits for them, and re-layouts: 8.65 us -> 5.71 us
  other arithmetic: 8.19 us -> 10.7 us
    dot_general x4, matrix products: 5.22 us -> 7.83 us  [matmat(): jnp.einsum('nij,njk->nik', later.astype(jnp.float32), earlier.astype(jnp....]
    dot_general x1, matrix products: 0.57 us -> 2.21 us  [matmat(): jnp.einsum('nij,njk->nik', later, earlier, preferred_element_type=jnp.flo...]
    unnamed x30 -> x28, local copies, waits for them, and re-layouts: 4.69 us -> 3.06 us
    reduce_sum x4, other arithmetic: 3.55 us -> 4.97 us  [vecmat(): return jnp.sum(v[:, :, None] * q.astype(jnp.float32), axis=1)]
    scatter x1 -> x0, local copies, waits for them, and re-layouts: 1.29 us -> none  [body(): packed = packed.at[stations, 0].set(local_noise)]
    select_n x0 -> x1, other arithmetic: none -> 0.97 us  [body(): packed = jnp.where(spot, local_noise, packed)]
where the time goes in v15:
time: 96.5 us; the launch traced here: 96 us
  waiting for transfers between devices  32.6 us (34%)
  Pallas kernels  18 us (19%)
  starting transfers between devices  17.5 us (18%)
  other arithmetic  10.7 us (11%)
  matrix products  10 us (10%)
  local copies, waits for them, and re-layouts  5.71 us (6%)
  between operations  1.51 us (2%)
    ppermute x10, waiting for transfers between devices, exchange(): lax.ppermute(x, AXES, [(place(j), place(j ^ mask)) for j in range(count)])  32.6 us
    ppermute x10, starting transfers between devices, exchange(): lax.ppermute(x, AXES, [(place(j), place(j ^ mask)) for j in range(count)])  17.5 us
    pallas_call x4, Pallas kernels, run(): pl.pallas_call(kernel, out_shape=(jax.ShapeDtypeStruct(own.shape, jnp.flo...  10.2 us
    dot_general x4, matrix products, matmat(): jnp.einsum('nij,njk->nik', later.astype(jnp.float32), earlier.astype(jnp....  7.83 us
    pallas_call x1, Pallas kernels, run(): pl.pallas_call(kernel, out_shape=(jax.ShapeDtypeStruct(grads.shape, jnp.f...  7.76 us
    reduce_sum x4, other arithmetic, vecmat(): return jnp.sum(v[:, :, None] * q.astype(jnp.float32), axis=1)  4.97 us
    unnamed x28, local copies, waits for them, and re-layouts  3.06 us
    dot_general x1, matrix products, matmat(): jnp.einsum('nij,njk->nik', later, earlier, preferred_element_type=jnp.flo...  2.21 us
  transfers between devices with their start and end apart: 10, of which 10 were waited for; matrix products, arithmetic and copies ran while one was open for 2% of the time, Pallas kernels for 0%

profile of v15, /device:TPU:0, one launch (start us, length us, event | category | flops | bytes accessed | tf_op | source)
XLA Modules:
  0.0 96.0 jit_solution(10897953292481485082)
XLA Ops:
  0.6 0.0 copy-start
  0.6 2.6 %multiply_reduce_fusion.refs_7_ = f32[24,256]{1,0:T(8,128)S(1)} fusion(f32[24,256]{1,0:T(8,128)} %bitcast.31, bf16[1,24,256,256]{3,2,1,0:T(8,128)(2,1)} %param.4), kind=kLoop, calls=%fused_computation | loop fusion | flops 4712448 | bytes 3194880 | tf_op jit(solution)/shard_map/reduce_sum | solution.py:12
  3.2 0.0 copy-start.4
  3.3 0.2 copy-done
  3.5 2.2 %fusion.2.refs_8_ = f32[12,256,256]{2,1,0:T(8,128)} fusion(bf16[24,256,256]{2,1,0:T(8,128)(2,1)S(1)} %bitcast.28), kind=kOutput, calls=%fused_computation.5 | convolution fusion | flops 402653184 | bytes 6291456 | tf_op jit(solution)/shard_map/nij,njk->nik/dot_general | solution.py:21
  5.7 0.0 copy-done.4
  5.7 0.5 multiply_reduce_fusion.1
  6.2 0.0 copy-start.1
  6.2 0.0 copy-start.9
  6.3 4.8 %fusion.refs_10_ = f32[6,256,256]{2,1,0:T(8,128)} fusion(f32[12,256,256]{2,1,0:T(8,128)} %fusion.2.refs_8_), kind=kOutput, calls=%fused_computation.3 | convolution fusion | flops 1207959552 | bytes 4718592 | tf_op jit(solution)/shard_map/nij,njk->nik/dot_general | solution.py:22
  11.1 0.0 copy-done.1
  11.1 0.3 multiply_reduce_fusion.2
  11.4 0.0 copy-done.9
  11.4 0.0 copy-start.11
  11.4 2.3 %fusion.6.refs_12_ = f32[3,256,256]{2,1,0:T(8,128)S(1)} fusion(f32[6,256,256]{2,1,0:T(8,128)} %fusion.refs_10_), kind=kOutput, calls=%fused_computation.10 | convolution fusion | flops 603979776 | bytes 2359296 | tf_op jit(solution)/shard_map/nij,njk->nik/dot_general | solution.py:22
  13.7 0.0 copy-start.2
  13.7 1.6 %multiply_reduce_fusion.3 = f32[3,256]{1,0:T(4,128)S(1)} fusion(f32[6,256,256]{2,1,0:T(8,128)} %fusion.refs_10_, f32[3,256]{1,0:T(4,128)S(1)} %slice.84), kind=kLoop, calls=%fused_computation.9 | loop fusion | flops 392448 | bytes 792576 | tf_op jit(solution)/shard_map/reduce_sum | solution.py:12
  15.4 0.4 multiply_reduce_fusion.5
  15.8 0.1 fusion.17
  15.9 0.4 fusion.11
  16.3 0.1 pad.6.clone
  16.4 0.1 maximum_maximum_fusion.own_ref
  16.5 0.0 copy-start.3
  16.5 3.0 %collective-permute-start = (f32[264,256]{1,0:T(8,128)S(1)}, f32[264,256]{1,0:T(8,128)S(1)}, u32[]{:S(2)}, u32[]{:S(2)}) collective-permute-start(f32[264,256]{1,0:T(8,128)S(1)} %maximum_maximum_fusion.own_ref), channel_id=1, source_target_pairs={{0,16},{16,0},{1,17},{17,1},{2,18},{18,2},{3,19},{19,3},{4,20},{20... | collective-permute-start | bytes 811016 | tf_op jit(solution)/shard_map/ppermute | solution.py:147
  19.5 0.7 fusion.13.sq_ref
  20.2 5.8 %collective-permute-done.got_ref = f32[264,256]{1,0:T(8,128)S(1)} collective-permute-done((f32[264,256]{1,0:T(8,128)S(1)}, f32[264,256]{1,0:T(8,128)S(1)}, u32[]{:S(2)}, u32[]{:S(2)}) %collective-permute-start) | collective-permute-done | bytes 270368 | tf_op jit(solution)/shard_map/ppermute | solution.py:147
  26.0 0.6 broadcast_in_dim.19.sv_ref
  26.6 0.1 copy-done.6
  26.7 2.6 %shard_map.67 = (f32[264,256]{1,0:T(8,128)}, f32[256,256]{1,0:T(8,128)}, f32[8,256]{1,0:T(8,128)}) custom-call(f32[264,256]{1,0:T(8,128)} %copy-done.3, f32[264,256]{1,0:T(8,128)} %copy-done.6, f32[256,256]{1,0:T(8,128)} %fusion.13.sq_ref, f32[8,256]{1,0:T(8,128)} %broadcast_in_dim.19.sv_ref), custom_call_target="tpu_custom_call" | custom-call | tf_op jit(solution)/shard_map/pallas_call | solution.py:73
  29.3 0.0 collective-permute-start.1
  29.3 1.8 %collective-permute-done.1.got_ref = f32[264,256]{1,0:T(8,128)S(1)} collective-permute-done((f32[264,256]{1,0:T(8,128)}, f32[264,256]{1,0:T(8,128)S(1)}, u32[]{:S(2)}, u32[]{:S(2)}) %collective-permute-start.1) | collective-permute-done | bytes 270368 | tf_op jit(solution)/shard_map/ppermute | solution.py:147
  31.0 0.7 copy-done.7
  31.8 2.6 %shard_map.68 = (f32[264,256]{1,0:T(8,128)}, f32[256,256]{1,0:T(8,128)}, f32[8,256]{1,0:T(8,128)}) custom-call(f32[264,256]{1,0:T(8,128)} %get-tuple-element.17.own_ref, f32[264,256]{1,0:T(8,128)} %copy-done.7, f32[256,256]{1,0:T(8,128)} %get-tuple-element.18.sq_ref, f32[8,256]{1,0:T(8,128)} %get-tuple-element.19.sv_ref), custom_call_target="tpu_custom_call" | custom-call | tf_op jit(solution)/shard_map/pallas_call | solution.py:73
  34.3 1.7 %collective-permute-start.2 = (f32[264,256]{1,0:T(8,128)}, f32[264,256]{1,0:T(8,128)S(1)}, u32[]{:S(2)}, u32[]{:S(2)}) collective-permute-start(f32[264,256]{1,0:T(8,128)} %get-tuple-element.20.own_ref), channel_id=1, source_target_pairs={{0,2},{16,18},{1,3},{17,19},{2,0},{18,16},{3,1},{19,17},{4,6},{20,... | collective-permute-start | bytes 811016 | tf_op jit(solution)/shard_map/ppermute | solution.py:147
  36.0 7.0 %collective-permute-done.2.got_ref = f32[264,256]{1,0:T(8,128)S(1)} collective-permute-done((f32[264,256]{1,0:T(8,128)}, f32[264,256]{1,0:T(8,128)S(1)}, u32[]{:S(2)}, u32[]{:S(2)}) %collective-permute-start.2) | collective-permute-done | bytes 270368 | tf_op jit(solution)/shard_map/ppermute | solution.py:147
  43.1 0.7 copy-done.8
  43.8 2.5 %shard_map.69 = (f32[264,256]{1,0:T(8,128)}, f32[256,256]{1,0:T(8,128)}, f32[8,256]{1,0:T(8,128)}) custom-call(f32[264,256]{1,0:T(8,128)} %get-tuple-element.20.own_ref, f32[264,256]{1,0:T(8,128)} %copy-done.8, f32[256,256]{1,0:T(8,128)} %get-tuple-element.21.sq_ref, f32[8,256]{1,0:T(8,128)} %get-tuple-element.22.sv_ref), custom_call_target="tpu_custom_call" | custom-call | tf_op jit(solution)/shard_map/pallas_call | solution.py:73
  46.3 1.8 %collective-permute-start.3 = (f32[264,256]{1,0:T(8,128)}, f32[264,256]{1,0:T(8,128)S(1)}, u32[]{:S(2)}, u32[]{:S(2)}) collective-permute-start(f32[264,256]{1,0:T(8,128)} %get-tuple-element.23.own_ref), channel_id=1, source_target_pairs={{0,4},{16,20},{1,5},{17,21},{2,6},{18,22},{3,7},{19,23},{4,0},{20,... | collective-permute-start | bytes 811016 | tf_op jit(solution)/shard_map/ppermute | solution.py:147
  48.1 0.6 pad_maximum_fusion.1.refs_15_
  48.7 0.9 pad_maximum_fusion.refs_14_
  49.6 4.7 %collective-permute-done.3.got_ref = f32[264,256]{1,0:T(8,128)S(1)} collective-permute-done((f32[264,256]{1,0:T(8,128)}, f32[264,256]{1,0:T(8,128)S(1)}, u32[]{:S(2)}, u32[]{:S(2)}) %collective-permute-start.3) | collective-permute-done | bytes 270368 | tf_op jit(solution)/shard_map/ppermute | solution.py:147
  54.3 0.7 copy-done.5
  55.0 2.6 %shard_map.70 = (f32[264,256]{1,0:T(8,128)}, f32[256,256]{1,0:T(8,128)}, f32[8,256]{1,0:T(8,128)}) custom-call(f32[264,256]{1,0:T(8,128)} %get-tuple-element.23.own_ref, f32[264,256]{1,0:T(8,128)} %copy-done.5, f32[256,256]{1,0:T(8,128)} %get-tuple-element.24.sq_ref, f32[8,256]{1,0:T(8,128)} %get-tuple-element.25.sv_ref), custom_call_target="tpu_custom_call" | custom-call | tf_op jit(solution)/shard_map/pallas_call | solution.py:73
  57.5 0.7 slice.89
  58.2 2.8 %collective-permute-start.4 = (f32[8,256]{1,0:T(8,128)S(1)}, f32[8,256]{1,0:T(8,128)S(1)}, u32[]{:S(2)}, u32[]{:S(2)}) collective-permute-start(f32[8,256]{1,0:T(8,128)S(1)} %slice.89), channel_id=1, source_target_pairs={{0,8},{16,24},{1,9},{17,25},{2,10},{18,26},{3,11},{19,27},{4,12},{... | collective-permute-start | bytes 24584 | tf_op jit(solution)/shard_map/ppermute | solution.py:147
  61.0 1.8 %collective-permute-done.4.refs_0_ = f32[8,256]{1,0:T(8,128)S(1)} collective-permute-done((f32[8,256]{1,0:T(8,128)S(1)}, f32[8,256]{1,0:T(8,128)S(1)}, u32[]{:S(2)}, u32[]{:S(2)}) %collective-permute-start.4) | collective-permute-done | bytes 8224 | tf_op jit(solution)/shard_map/ppermute | solution.py:147
  62.8 0.6 copy-done.13
  63.4 7.8 %shard_map.71 = (f32[24,256]{1,0:T(8,128)}, f32[136,128]{1,0:T(8,128)}) custom-call(f32[8,256]{1,0:T(8,128)} %copy-done.13, f32[256,256]{1,0:T(8,128)} %get-tuple-element.27.refs_1_, f32[8,256]{1,0:T(8,128)} %get-tuple-element.28.refs_2_, f32[24,256]{1,0:T(8,128)} %bitcast.32, f32[24,2,128]{2,1,0:T(2,128)} %bitcast.35, f32[24,256]{1,0:T(8,128)} %bitcast.33, ...), custom_call_target="tpu_custom_call" | custom-call | tf_op jit(solution)/shard_map/pallas_call | solution.py:130
  71.1 0.0 copy-done.10
  71.2 1.3 %multiply_reduce_fusion.6 = f32[]{:T(128)} fusion(f32[24,256]{1,0:T(8,128)} %get-tuple-element.29, f32[1,24,256]{2,1,0:T(8,128)S(1)} %copy-done.10), kind=kLoop, calls=%fused_computation.26 | loop fusion | flops 12287 | bytes 49156 | tf_op jit(solution)/shard_map/reduce_sum | solution.py:177
  73.2 1.0 %and_select_fusion = f32[136,128]{1,0:T(8,128)S(1)} fusion(f32[136,128]{1,0:T(8,128)} %get-tuple-element.30, f32[]{:T(128)S(6)} %neg.3, pred[128]{0:T(512)(128)(4,1)S(1)} %iota_compare_fusion.2, pred[136]{0:T(512)(128)(4,1)S(1)} %iota_compare_fusion.1), kind=kLoop, calls=%fused_computation.25 | loop fusion | flops 34816 | bytes 139532 | tf_op jit(solution)/shard_map/jit(_where)/select_n | solution.py:181
  74.1 1.7 %collective-permute-start.5 = (f32[136,128]{1,0:T(8,128)S(1)}, f32[136,128]{1,0:T(8,128)S(1)}, u32[]{:S(2)}, u32[]{:S(2)}) collective-permute-start(f32[136,128]{1,0:T(8,128)S(1)} %and_select_fusion), channel_id=1, source_target_pairs={{0,16},{16,0},{1,17},{17,1},{2,18},{18,2},{3,19},{19,3},{4,20},{20... | collective-permute-start | bytes 208904 | tf_op jit(solution)/shard_map/ppermute | solution.py:147
  75.9 2.6 %collective-permute-done.5 = f32[136,128]{1,0:T(8,128)S(1)} collective-permute-done((f32[136,128]{1,0:T(8,128)S(1)}, f32[136,128]{1,0:T(8,128)S(1)}, u32[]{:S(2)}, u32[]{:S(2)}) %collective-permute-start.5) | collective-permute-done | bytes 69664 | tf_op jit(solution)/shard_map/ppermute | solution.py:147
  78.5 1.0 %fusion.20 = f32[136,128]{1,0:T(8,128)S(1)} fusion(f32[136,128]{1,0:T(8,128)S(1)} %collective-permute-done.5, f32[136,128]{1,0:T(8,128)} %get-tuple-element.30, f32[]{:T(128)S(6)} %neg.3, pred[128]{0:T(512)(128)(4,1)S(1)} %iota_compare_fusion.2, pred[136]{0:T(512)(128)(4,1)S(1)} %iota_compare_fusion.1), kind=kLoop, calls=%fused_computation.35 | loop fusion | flops 52224 | bytes 209164 | tf_op jit(solution)/shard_map/add | solution.py:184
  79.5 0.1 collective-permute-start.6
  79.6 1.2 %collective-permute-done.6 = f32[136,128]{1,0:T(8,128)S(1)} collective-permute-done((f32[136,128]{1,0:T(8,128)S(1)}, f32[136,128]{1,0:T(8,128)S(1)}, u32[]{:S(2)}, u32[]{:S(2)}) %collective-permute-start.6) | collective-permute-done | bytes 69664 | tf_op jit(solution)/shard_map/ppermute | solution.py:147
  80.8 1.7 %collective-permute-start.7 = (f32[136,128]{1,0:T(8,128)S(1)}, f32[136,128]{1,0:T(8,128)S(1)}, u32[]{:S(2)}, u32[]{:S(2)}) collective-permute-start(f32[136,128]{1,0:T(8,128)S(1)} %add.36), channel_id=1, source_target_pairs={{0,2},{16,18},{1,3},{17,19},{2,0},{18,16},{3,1},{19,17},{4,6},{20,... | collective-permute-start | bytes 208904 | tf_op jit(solution)/shard_map/ppermute | solution.py:147
  82.5 2.7 %collective-permute-done.7 = f32[136,128]{1,0:T(8,128)S(1)} collective-permute-done((f32[136,128]{1,0:T(8,128)S(1)}, f32[136,128]{1,0:T(8,128)S(1)}, u32[]{:S(2)}, u32[]{:S(2)}) %collective-permute-start.7) | collective-permute-done | bytes 69664 | tf_op jit(solution)/shard_map/ppermute | solution.py:147
  85.2 1.8 %collective-permute-start.8 = (f32[136,128]{1,0:T(8,128)S(1)}, f32[136,128]{1,0:T(8,128)S(1)}, u32[]{:S(2)}, u32[]{:S(2)}) collective-permute-start(f32[136,128]{1,0:T(8,128)S(1)} %add.37), channel_id=1, source_target_pairs={{0,4},{16,20},{1,5},{17,21},{2,6},{18,22},{3,7},{19,23},{4,0},{20,... | collective-permute-start | bytes 208904 | tf_op jit(solution)/shard_map/ppermute | solution.py:147
  87.0 2.6 %collective-permute-done.8 = f32[136,128]{1,0:T(8,128)S(1)} collective-permute-done((f32[136,128]{1,0:T(8,128)S(1)}, f32[136,128]{1,0:T(8,128)S(1)}, u32[]{:S(2)}, u32[]{:S(2)}) %collective-permute-start.8) | collective-permute-done | bytes 69664 | tf_op jit(solution)/shard_map/ppermute | solution.py:147
  89.6 2.8 %collective-permute-start.9 = (f32[136,128]{1,0:T(8,128)S(1)}, f32[136,128]{1,0:T(8,128)S(1)}, u32[]{:S(2)}, u32[]{:S(2)}) collective-permute-start(f32[136,128]{1,0:T(8,128)S(1)} %add.38), channel_id=1, source_target_pairs={{0,8},{16,24},{1,9},{17,25},{2,10},{18,26},{3,11},{19,27},{4,12},{... | collective-permute-start | bytes 208904 | tf_op jit(solution)/shard_map/ppermute | solution.py:147
  92.4 2.5 %collective-permute-done.9 = f32[136,128]{1,0:T(8,128)S(1)} collective-permute-done((f32[136,128]{1,0:T(8,128)S(1)}, f32[136,128]{1,0:T(8,128)S(1)}, u32[]{:S(2)}, u32[]{:S(2)}) %collective-permute-start.9) | collective-permute-done | bytes 69664 | tf_op jit(solution)/shard_map/ppermute | solution.py:147
  94.9 0.6 slice.98
  95.5 0.5 slice.99
  (29 shorter events, 0.2 us)
Async XLA Ops:
  0.6 2.9 %copy-start = (bf16[1,24,256,256]{3,2,1,0:T(8,128)(2,1)S(1)}, bf16[1,24,256,256]{3,2,1,0:T(8,128)(2,1)}, u32[]{:S(2)}) copy-start(bf16[1,24,256,256]{3,2,1,0:T(8,128)(2,1)} %param.4) | copy-start | bytes 9437188
  3.2 2.5 %copy-start.4 = (f32[24,256]{1,0:T(8,128)}, f32[24,256]{1,0:T(8,128)S(1)}, u32[]{:S(2)}) copy-start(f32[24,256]{1,0:T(8,128)S(1)} %multiply_reduce_fusion.refs_7_) | copy-start | bytes 73732
  6.2 4.9 %copy-start.1 = (f32[12,256,256]{2,1,0:T(8,128)S(1)}, f32[12,256,256]{2,1,0:T(8,128)}, u32[]{:S(2)}) copy-start(f32[12,256,256]{2,1,0:T(8,128)} %fusion.2.refs_8_) | copy-start | bytes 9437188
  6.2 5.1 %copy-start.9 = (f32[12,256]{1,0:T(8,128)}, f32[12,256]{1,0:T(8,128)S(1)}, u32[]{:S(2)}) copy-start(f32[12,256]{1,0:T(8,128)S(1)} %add.30.refs_9_) | copy-start | bytes 36868
  11.4 8.8 %copy-start.11 = (f32[6,256]{1,0:T(8,128)}, f32[6,256]{1,0:T(8,128)S(1)}, u32[]{:S(2)}) copy-start(f32[6,256]{1,0:T(8,128)S(1)} %add.31.refs_11_) | copy-start | bytes 18436
  13.7 32.6 %copy-start.2 = (f32[3,256,256]{2,1,0:T(8,128)}, f32[3,256,256]{2,1,0:T(8,128)S(1)}, u32[]{:S(2)}) copy-start(f32[3,256,256]{2,1,0:T(8,128)S(1)} %fusion.6.refs_12_) | copy-start | bytes 2359300
  15.3 34.2 %copy-start.12 = (f32[3,256]{1,0:T(4,128)}, f32[3,256]{1,0:T(4,128)S(1)}, u32[]{:S(2)}) copy-start(f32[3,256]{1,0:T(4,128)S(1)} %add.32.refs_13_) | copy-start | bytes 9220
  16.5 10.2 %copy-start.3 = (f32[264,256]{1,0:T(8,128)}, f32[264,256]{1,0:T(8,128)S(1)}, u32[]{:S(2)}) copy-start(f32[264,256]{1,0:T(8,128)S(1)} %maximum_maximum_fusion.own_ref) | copy-start | bytes 811012
  16.5 9.5 %collective-permute-start = (f32[264,256]{1,0:T(8,128)S(1)}, f32[264,256]{1,0:T(8,128)S(1)}, u32[]{:S(2)}, u32[]{:S(2)}) collective-permute-start(f32[264,256]{1,0:T(8,128)S(1)} %maximum_maximum_fusion.own_ref), channel_id=1, source_target_pairs={{0,16},{16,0},{1,17},{17,1},{2,18},{18,2},{3,19},{19,3},{4,20},{20... | collective-permute-start | bytes 811016 | tf_op jit(solution)/shard_map/ppermute | solution.py:147
  26.0 0.7 copy-start.6
  29.3 1.8 %collective-permute-start.1 = (f32[264,256]{1,0:T(8,128)}, f32[264,256]{1,0:T(8,128)S(1)}, u32[]{:S(2)}, u32[]{:S(2)}) collective-permute-start(f32[264,256]{1,0:T(8,128)} %get-tuple-element.17.own_ref), channel_id=1, source_target_pairs={{0,1},{16,17},{1,0},{17,16},{2,3},{18,19},{3,2},{19,18},{4,5},{20,... | collective-permute-start | bytes 811016 | tf_op jit(solution)/shard_map/ppermute | solution.py:147
  31.0 0.7 copy-start.7
  34.3 8.7 %collective-permute-start.2 = (f32[264,256]{1,0:T(8,128)}, f32[264,256]{1,0:T(8,128)S(1)}, u32[]{:S(2)}, u32[]{:S(2)}) collective-permute-start(f32[264,256]{1,0:T(8,128)} %get-tuple-element.20.own_ref), channel_id=1, source_target_pairs={{0,2},{16,18},{1,3},{17,19},{2,0},{18,16},{3,1},{19,17},{4,6},{20,... | collective-permute-start | bytes 811016 | tf_op jit(solution)/shard_map/ppermute | solution.py:147
  43.1 0.7 copy-start.8
  46.3 8.0 %collective-permute-start.3 = (f32[264,256]{1,0:T(8,128)}, f32[264,256]{1,0:T(8,128)S(1)}, u32[]{:S(2)}, u32[]{:S(2)}) collective-permute-start(f32[264,256]{1,0:T(8,128)} %get-tuple-element.23.own_ref), channel_id=1, source_target_pairs={{0,4},{16,20},{1,5},{17,21},{2,6},{18,22},{3,7},{19,23},{4,0},{20,... | collective-permute-start | bytes 811016 | tf_op jit(solution)/shard_map/ppermute | solution.py:147
  54.3 0.7 copy-start.5
  58.2 4.5 %collective-permute-start.4 = (f32[8,256]{1,0:T(8,128)S(1)}, f32[8,256]{1,0:T(8,128)S(1)}, u32[]{:S(2)}, u32[]{:S(2)}) collective-permute-start(f32[8,256]{1,0:T(8,128)S(1)} %slice.89), channel_id=1, source_target_pairs={{0,8},{16,24},{1,9},{17,25},{2,10},{18,26},{3,11},{19,27},{4,12},{... | collective-permute-start | bytes 24584 | tf_op jit(solution)/shard_map/ppermute | solution.py:147
  62.8 0.6 copy-start.13
  63.4 7.8 %copy-start.10 = (f32[1,24,256]{2,1,0:T(8,128)S(1)}, f32[1,24,256]{2,1,0:T(8,128)}, u32[]{:S(2)}) copy-start(f32[1,24,256]{2,1,0:T(8,128)} %param.7) | copy-start | bytes 73732
  74.1 4.4 %collective-permute-start.5 = (f32[136,128]{1,0:T(8,128)S(1)}, f32[136,128]{1,0:T(8,128)S(1)}, u32[]{:S(2)}, u32[]{:S(2)}) collective-permute-start(f32[136,128]{1,0:T(8,128)S(1)} %and_select_fusion), channel_id=1, source_target_pairs={{0,16},{16,0},{1,17},{17,1},{2,18},{18,2},{3,19},{19,3},{4,20},{20... | collective-permute-start | bytes 208904 | tf_op jit(solution)/shard_map/ppermute | solution.py:147
  79.5 1.3 %collective-permute-start.6 = (f32[136,128]{1,0:T(8,128)S(1)}, f32[136,128]{1,0:T(8,128)S(1)}, u32[]{:S(2)}, u32[]{:S(2)}) collective-permute-start(f32[136,128]{1,0:T(8,128)S(1)} %fusion.20), channel_id=1, source_target_pairs={{0,1},{16,17},{1,0},{17,16},{2,3},{18,19},{3,2},{19,18},{4,5},{20,... | collective-permute-start | bytes 208904 | tf_op jit(solution)/shard_map/ppermute | solution.py:147
  80.8 4.4 %collective-permute-start.7 = (f32[136,128]{1,0:T(8,128)S(1)}, f32[136,128]{1,0:T(8,128)S(1)}, u32[]{:S(2)}, u32[]{:S(2)}) collective-permute-start(f32[136,128]{1,0:T(8,128)S(1)} %add.36), channel_id=1, source_target_pairs={{0,2},{16,18},{1,3},{17,19},{2,0},{18,16},{3,1},{19,17},{4,6},{20,... | collective-permute-start | bytes 208904 | tf_op jit(solution)/shard_map/ppermute | solution.py:147
  85.2 4.4 %collective-permute-start.8 = (f32[136,128]{1,0:T(8,128)S(1)}, f32[136,128]{1,0:T(8,128)S(1)}, u32[]{:S(2)}, u32[]{:S(2)}) collective-permute-start(f32[136,128]{1,0:T(8,128)S(1)} %add.37), channel_id=1, source_target_pairs={{0,4},{16,20},{1,5},{17,21},{2,6},{18,22},{3,7},{19,23},{4,0},{20,... | collective-permute-start | bytes 208904 | tf_op jit(solution)/shard_map/ppermute | solution.py:147
  89.6 5.3 %collective-permute-start.9 = (f32[136,128]{1,0:T(8,128)S(1)}, f32[136,128]{1,0:T(8,128)S(1)}, u32[]{:S(2)}, u32[]{:S(2)}) collective-permute-start(f32[136,128]{1,0:T(8,128)S(1)} %add.38), channel_id=1, source_target_pairs={{0,8},{16,24},{1,9},{17,25},{2,10},{18,26},{3,11},{19,27},{4,12},{... | collective-permute-start | bytes 208904 | tf_op jit(solution)/shard_map/ppermute | solution.py:147

commit v16 on v11

--- a/solution.py
+++ b/solution.py
@@ -94,9 +94,9 @@
     depth = len(sizes) - 1
 
     def kernel(*refs):
-        rv_ref, sq_ref, sv_ref, grads_ref, load_ref, resp_ref = refs[:6]
-        tree = refs[6 : 6 + 2 * depth]
-        out_ref, grad_ref = refs[6 + 2 * depth :]
+        rv_ref, sq_ref, sv_ref, grads_ref, load_ref = refs[:5]
+        tree = refs[5 : 5 + 2 * depth]
+        out_ref, grad_ref = refs[5 + 2 * depth :]
         me = lax.axis_index("outer") * lax.axis_size("inner") + lax.axis_index("inner")
         lower = (me // d) % 2 == 0
         sv = sv_ref[0:1, :]
@@ -108,7 +108,8 @@
             new = []
             for j in range(n // 2):
                 upper = rows[j]
-                new.append(row_times(upper, q_ref[2 * j + 1]) + v_ref[2 * j + 1 : 2 * j + 2, :])
+                q = q_ref[j, 0] if n % 2 == 0 else q_ref[2 * j + 1]
+                new.append(row_times(upper, q) + v_ref[2 * j + 1 : 2 * j + 2, :])
                 new.append(upper)
             if n % 2:
                 new.append(rows[-1])
@@ -123,16 +124,33 @@
         grad_ref[0:stations, :] = kernel_grad
         grad_ref[stations:, :] = jnp.zeros((8, stations), jnp.float32)
 
-    def run(rv, sq, sv, grads, loads, resp, levels):
-        args = [rv, sq, sv, grads, loads, resp]
+    def whole(x):
+        return pl.BlockSpec(x.shape, lambda i, nd=x.ndim: (0,) * nd)
+
+    def run(rv, sq, sv, grads, loads, levels):
+        args = [rv, sq, sv, grads, loads]
+        specs = [whole(x) for x in args]
         for level in range(depth):
-            args += list(levels[level])
+            q, v = levels[level]
+            n = sizes[level]
+            if n % 2 == 0:
+                q = q.reshape((n // 2, 2) + q.shape[1:])
+                specs.append(pl.BlockSpec((n // 2, 1) + q.shape[2:], lambda i: (0, 1, 0, 0)))
+            else:
+                specs.append(whole(q))
+            args.append(q)
+            specs.append(whole(v))
+            args.append(v)
+        out_shape = (
+            jax.ShapeDtypeStruct(grads.shape, jnp.float32),
+            jax.ShapeDtypeStruct((stations + 8, stations), jnp.float32),
+        )
         return pl.pallas_call(
             kernel,
-            out_shape=(
-                jax.ShapeDtypeStruct(grads.shape, jnp.float32),
-                jax.ShapeDtypeStruct((stations + 8, stations), jnp.float32),
-            ),
+            out_shape=out_shape,
+            grid=(1,),
+            in_specs=specs,
+            out_specs=tuple(whole(o) for o in out_shape),
         )(*args)
 
     return run
@@ -172,7 +190,7 @@
     rv = exchange(packed[width:], d, count)
     sizes = [level[0].shape[0] for level in levels]
     length_rates, packed = finish(d, sizes, width, stations)(
-        rv, sq, sv, grads, station_loadings[0], offset_response[0], levels
+        rv, sq, sv, grads, station_loadings[0], levels
     )
     local_noise = -jnp.sum(length_rates * offset_response[0])
     packed = packed.at[stations, 0].set(local_noise)

time: 92.8 us -> 91.6 us (0.987)
  Pallas kernels: 18 us -> 16.8 us
    pallas_call x1, Pallas kernels: 7.74 us -> 6.54 us  [run(): pl.pallas_call(kernel, out_shape=out_shape, grid=(1,), in_specs=specs, ou...]
where the time goes in v16:
time: 91.6 us; the launch traced here: 91.2 us
  waiting for transfers between devices  32.8 us (36%)
  starting transfers between devices  17.4 us (19%)
  Pallas kernels  16.8 us (18%)
  local copies, waits for them, and re-layouts  8.65 us (9%)
  other arithmetic  8.19 us (9%)
  matrix products  5.79 us (6%)
  between operations  1.52 us (2%)
    ppermute x10, waiting for transfers between devices, exchange(): lax.ppermute(x, AXES, [(place(j), place(j ^ mask)) for j in range(count)])  32.8 us
    ppermute x10, starting transfers between devices, exchange(): lax.ppermute(x, AXES, [(place(j), place(j ^ mask)) for j in range(count)])  17.4 us
    pallas_call x4, Pallas kernels, run(): pl.pallas_call(kernel, out_shape=(jax.ShapeDtypeStruct(own.shape, jnp.flo...  10.3 us
    pallas_call x1, Pallas kernels, run(): pl.pallas_call(kernel, out_shape=out_shape, grid=(1,), in_specs=specs, ou...  6.54 us
    dot_general x4, matrix products, matmat(): jnp.einsum('nij,njk->nik', later.astype(jnp.float32), earlier.astype(jnp....  5.22 us
    unnamed x30, local copies, waits for them, and re-layouts  4.69 us
    reduce_sum x4, other arithmetic, vecmat(): return jnp.sum(v[:, :, None] * q.astype(jnp.float32), axis=1)  3.55 us
  transfers between devices with their start and end apart: 10, of which 10 were waited for; matrix products, arithmetic and copies ran while one was open for 2% of the time, Pallas kernels for 0%

profile of v16, /device:TPU:0, one launch (start us, length us, event | category | flops | bytes accessed | tf_op | source)
XLA Modules:
  0.0 91.2 jit_solution(3071323817188273991)
XLA Ops:
  0.6 0.0 copy-start
  0.6 2.6 %multiply_reduce_fusion.refs_6_ = f32[24,256]{1,0:T(8,128)S(1)} fusion(f32[24,256]{1,0:T(8,128)} %bitcast.41, bf16[1,24,256,256]{3,2,1,0:T(8,128)(2,1)} %param.6), kind=kLoop, calls=%fused_computation | loop fusion | flops 4712448 | bytes 3194880 | tf_op jit(solution)/shard_map/reduce_sum | solution.py:12
  3.2 0.0 copy-start.5
  3.3 0.2 copy-done
  3.5 0.5 multiply_reduce_fusion.1
  4.0 0.0 copy-start.10
  4.1 0.6 fusion.2
  4.6 0.0 copy-done.5
  4.6 0.0 copy-done.10
  4.6 0.0 copy-start.1
  4.7 1.6 %copy-done.1 = f32[12,256,256]{2,1,0:T(8,128)} copy-done((f32[12,256,256]{2,1,0:T(8,128)}, f32[12,256,256]{2,1,0:T(8,128)S(1)}, u32[]{:S(2)}) %copy-start.1) | copy-done | bytes 3145752
  6.3 0.3 multiply_reduce_fusion.2
  6.6 0.0 copy-start.11
  6.6 3.5 %fusion = f32[6,256,256]{2,1,0:T(8,128)S(1)} fusion(f32[12,256,256]{2,1,0:T(8,128)} %copy-done.1), kind=kOutput, calls=%fused_computation.3 | convolution fusion | flops 1207959552 | bytes 4718592 | tf_op jit(solution)/shard_map/nij,njk->nik/dot_general | solution.py:22
  10.2 0.9 %fusion.6.refs_11_ = f32[3,256,256]{2,1,0:T(8,128)S(1)} fusion(f32[6,256,256]{2,1,0:T(8,128)S(1)} %fusion), kind=kOutput, calls=%fused_computation.10 | convolution fusion | flops 603979776 | bytes 2359296 | tf_op jit(solution)/shard_map/nij,njk->nik/dot_general | solution.py:22
  11.1 0.0 copy-done.11
  11.1 0.0 copy-start.3
  11.1 0.2 multiply_reduce_fusion.3
  11.3 0.1 fusion.18
  11.5 0.4 multiply_reduce_fusion.5
  11.9 0.4 fusion.11
  12.3 0.1 pad.10.clone
  12.3 0.1 maximum_maximum_fusion.own_ref
  12.4 0.0 copy-start.4
  12.4 3.0 %collective-permute-start = (f32[264,256]{1,0:T(8,128)S(1)}, f32[264,256]{1,0:T(8,128)S(1)}, u32[]{:S(2)}, u32[]{:S(2)}) collective-permute-start(f32[264,256]{1,0:T(8,128)S(1)} %maximum_maximum_fusion.own_ref), channel_id=1, source_target_pairs={{0,16},{16,0},{1,17},{17,1},{2,18},{18,2},{3,19},{19,3},{4,20},{20... | collective-permute-start | bytes 811016 | tf_op jit(solution)/shard_map/ppermute | solution.py:165
  15.5 0.7 fusion.13.sq_ref
  16.2 5.8 %collective-permute-done.got_ref = f32[264,256]{1,0:T(8,128)S(1)} collective-permute-done((f32[264,256]{1,0:T(8,128)S(1)}, f32[264,256]{1,0:T(8,128)S(1)}, u32[]{:S(2)}, u32[]{:S(2)}) %collective-permute-start) | collective-permute-done | bytes 270368 | tf_op jit(solution)/shard_map/ppermute | solution.py:165
  22.0 0.6 broadcast_in_dim.7.sv_ref
  22.6 0.1 copy-done.7
  22.7 2.6 %shard_map.67 = (f32[264,256]{1,0:T(8,128)}, f32[256,256]{1,0:T(8,128)}, f32[8,256]{1,0:T(8,128)}) custom-call(f32[264,256]{1,0:T(8,128)} %copy-done.4, f32[264,256]{1,0:T(8,128)} %copy-done.7, f32[256,256]{1,0:T(8,128)} %fusion.13.sq_ref, f32[8,256]{1,0:T(8,128)} %broadcast_in_dim.7.sv_ref), custom_call_target="tpu_custom_call" | custom-call | tf_op jit(solution)/shard_map/pallas_call | solution.py:73
  25.3 0.0 collective-permute-start.1
  25.3 1.8 %collective-permute-done.1.got_ref = f32[264,256]{1,0:T(8,128)S(1)} collective-permute-done((f32[264,256]{1,0:T(8,128)}, f32[264,256]{1,0:T(8,128)S(1)}, u32[]{:S(2)}, u32[]{:S(2)}) %collective-permute-start.1) | collective-permute-done | bytes 270368 | tf_op jit(solution)/shard_map/ppermute | solution.py:165
  27.0 0.7 copy-done.8
  27.7 2.6 %shard_map.68 = (f32[264,256]{1,0:T(8,128)}, f32[256,256]{1,0:T(8,128)}, f32[8,256]{1,0:T(8,128)}) custom-call(f32[264,256]{1,0:T(8,128)} %get-tuple-element.29.own_ref, f32[264,256]{1,0:T(8,128)} %copy-done.8, f32[256,256]{1,0:T(8,128)} %get-tuple-element.30.sq_ref, f32[8,256]{1,0:T(8,128)} %get-tuple-element.31.sv_ref), custom_call_target="tpu_custom_call" | custom-call | tf_op jit(solution)/shard_map/pallas_call | solution.py:73
  30.3 1.7 %collective-permute-start.2 = (f32[264,256]{1,0:T(8,128)}, f32[264,256]{1,0:T(8,128)S(1)}, u32[]{:S(2)}, u32[]{:S(2)}) collective-permute-start(f32[264,256]{1,0:T(8,128)} %get-tuple-element.32.own_ref), channel_id=1, source_target_pairs={{0,2},{16,18},{1,3},{17,19},{2,0},{18,16},{3,1},{19,17},{4,6},{20,... | collective-permute-start | bytes 811016 | tf_op jit(solution)/shard_map/ppermute | solution.py:165
  32.0 7.0 %collective-permute-done.2.got_ref = f32[264,256]{1,0:T(8,128)S(1)} collective-permute-done((f32[264,256]{1,0:T(8,128)}, f32[264,256]{1,0:T(8,128)S(1)}, u32[]{:S(2)}, u32[]{:S(2)}) %collective-permute-start.2) | collective-permute-done | bytes 270368 | tf_op jit(solution)/shard_map/ppermute | solution.py:165
  39.0 0.7 copy-done.9
  39.7 2.6 %shard_map.69 = (f32[264,256]{1,0:T(8,128)}, f32[256,256]{1,0:T(8,128)}, f32[8,256]{1,0:T(8,128)}) custom-call(f32[264,256]{1,0:T(8,128)} %get-tuple-element.32.own_ref, f32[264,256]{1,0:T(8,128)} %copy-done.9, f32[256,256]{1,0:T(8,128)} %get-tuple-element.33.sq_ref, f32[8,256]{1,0:T(8,128)} %get-tuple-element.34.sv_ref), custom_call_target="tpu_custom_call" | custom-call | tf_op jit(solution)/shard_map/pallas_call | solution.py:73
  42.3 1.8 %collective-permute-start.3 = (f32[264,256]{1,0:T(8,128)}, f32[264,256]{1,0:T(8,128)S(1)}, u32[]{:S(2)}, u32[]{:S(2)}) collective-permute-start(f32[264,256]{1,0:T(8,128)} %get-tuple-element.35.own_ref), channel_id=1, source_target_pairs={{0,4},{16,20},{1,5},{17,21},{2,6},{18,22},{3,7},{19,23},{4,0},{20,... | collective-permute-start | bytes 811016 | tf_op jit(solution)/shard_map/ppermute | solution.py:165
  44.1 0.8 maximum_bitcast_fusion.refs_13_
  44.9 5.3 %collective-permute-done.3.got_ref = f32[264,256]{1,0:T(8,128)S(1)} collective-permute-done((f32[264,256]{1,0:T(8,128)}, f32[264,256]{1,0:T(8,128)S(1)}, u32[]{:S(2)}, u32[]{:S(2)}) %collective-permute-start.3) | collective-permute-done | bytes 270368 | tf_op jit(solution)/shard_map/ppermute | solution.py:165
  50.2 0.7 copy-done.6
  51.0 2.6 %shard_map.70 = (f32[264,256]{1,0:T(8,128)}, f32[256,256]{1,0:T(8,128)}, f32[8,256]{1,0:T(8,128)}) custom-call(f32[264,256]{1,0:T(8,128)} %get-tuple-element.35.own_ref, f32[264,256]{1,0:T(8,128)} %copy-done.6, f32[256,256]{1,0:T(8,128)} %get-tuple-element.36.sq_ref, f32[8,256]{1,0:T(8,128)} %get-tuple-element.37.sv_ref), custom_call_target="tpu_custom_call" | custom-call | tf_op jit(solution)/shard_map/pallas_call | solution.py:73
  53.5 0.7 slice.108
  54.2 2.8 %collective-permute-start.4 = (f32[8,256]{1,0:T(8,128)S(1)}, f32[8,256]{1,0:T(8,128)S(1)}, u32[]{:S(2)}, u32[]{:S(2)}) collective-permute-start(f32[8,256]{1,0:T(8,128)S(1)} %slice.108), channel_id=1, source_target_pairs={{0,8},{16,24},{1,9},{17,25},{2,10},{18,26},{3,11},{19,27},{4,12},{... | collective-permute-start | bytes 24584 | tf_op jit(solution)/shard_map/ppermute | solution.py:165
  57.0 0.6 pad_maximum_fusion.refs_14_
  57.6 1.2 %collective-permute-done.4.refs_0_ = f32[8,256]{1,0:T(8,128)S(1)} collective-permute-done((f32[8,256]{1,0:T(8,128)S(1)}, f32[8,256]{1,0:T(8,128)S(1)}, u32[]{:S(2)}, u32[]{:S(2)}) %collective-permute-start.4) | collective-permute-done | bytes 8224 | tf_op jit(solution)/shard_map/ppermute | solution.py:165
  58.8 0.6 copy-done.14
  59.4 6.5 %shard_map.71 = (f32[24,256]{1,0:T(8,128)}, f32[136,128]{1,0:T(8,128)}) custom-call(f32[8,256]{1,0:T(8,128)} %copy-done.14, f32[256,256]{1,0:T(8,128)} %get-tuple-element.39.refs_1_, f32[8,256]{1,0:T(8,128)} %get-tuple-element.40.refs_2_, f32[24,256]{1,0:T(8,128)} %bitcast.42, f32[24,2,128]{2,1,0:T(2,128)} %bitcast.43, bf16[12,2,256,256]{3,2,1,0:T(8,128)(2,1)} %bitcast.35, ...), custom_call_target="tpu_custom_call" | custom-call | tf_op jit(solution)/shard_map/pallas_call | solution.py:148
  65.9 1.3 %fusion.15 = f32[]{:T(128)} fusion(f32[24,256]{1,0:T(8,128)} %get-tuple-element.41, f32[1,24,256]{2,1,0:T(8,128)S(1)} %copy-done.13), kind=kLoop, calls=%fused_computation.26 | loop fusion | flops 12287 | bytes 49156 | tf_op jit(solution)/shard_map/reduce_sum | solution.py:195
  67.9 1.3 %scatter.4 = f32[136,128]{1,0:T(8,128)} dynamic-update-slice(f32[136,128]{1,0:T(8,128)} %get-tuple-element.42, f32[1,1]{1,0:T(1,128)} %bitcast.17, s32[]{:T(128)} %constant.32.clone.1, s32[]{:T(128)} %constant.33.clone.1) | dynamic-update-slice | bytes 12 | tf_op jit(solution)/shard_map/scatter | solution.py:196
  69.2 1.7 %collective-permute-start.5 = (f32[136,128]{1,0:T(8,128)}, f32[136,128]{1,0:T(8,128)S(1)}, u32[]{:S(2)}, u32[]{:S(2)}) collective-permute-start(f32[136,128]{1,0:T(8,128)} %scatter.4), channel_id=1, source_target_pairs={{0,16},{16,0},{1,17},{17,1},{2,18},{18,2},{3,19},{19,3},{4,20},{20... | collective-permute-start | bytes 208904 | tf_op jit(solution)/shard_map/ppermute | solution.py:165
  70.9 2.8 %collective-permute-done.5 = f32[136,128]{1,0:T(8,128)S(1)} collective-permute-done((f32[136,128]{1,0:T(8,128)}, f32[136,128]{1,0:T(8,128)S(1)}, u32[]{:S(2)}, u32[]{:S(2)}) %collective-permute-start.5) | collective-permute-done | bytes 69664 | tf_op jit(solution)/shard_map/ppermute | solution.py:165
  73.7 0.9 add.37
  74.6 0.1 collective-permute-start.6
  74.7 1.2 %collective-permute-done.6 = f32[136,128]{1,0:T(8,128)S(1)} collective-permute-done((f32[136,128]{1,0:T(8,128)S(1)}, f32[136,128]{1,0:T(8,128)S(1)}, u32[]{:S(2)}, u32[]{:S(2)}) %collective-permute-start.6) | collective-permute-done | bytes 69664 | tf_op jit(solution)/shard_map/ppermute | solution.py:165
  76.0 1.7 %collective-permute-start.7 = (f32[136,128]{1,0:T(8,128)S(1)}, f32[136,128]{1,0:T(8,128)S(1)}, u32[]{:S(2)}, u32[]{:S(2)}) collective-permute-start(f32[136,128]{1,0:T(8,128)S(1)} %add.38), channel_id=1, source_target_pairs={{0,2},{16,18},{1,3},{17,19},{2,0},{18,16},{3,1},{19,17},{4,6},{20,... | collective-permute-start | bytes 208904 | tf_op jit(solution)/shard_map/ppermute | solution.py:165
  77.7 2.6 %collective-permute-done.7 = f32[136,128]{1,0:T(8,128)S(1)} collective-permute-done((f32[136,128]{1,0:T(8,128)S(1)}, f32[136,128]{1,0:T(8,128)S(1)}, u32[]{:S(2)}, u32[]{:S(2)}) %collective-permute-start.7) | collective-permute-done | bytes 69664 | tf_op jit(solution)/shard_map/ppermute | solution.py:165
  80.4 1.8 %collective-permute-start.8 = (f32[136,128]{1,0:T(8,128)S(1)}, f32[136,128]{1,0:T(8,128)S(1)}, u32[]{:S(2)}, u32[]{:S(2)}) collective-permute-start(f32[136,128]{1,0:T(8,128)S(1)} %add.39), channel_id=1, source_target_pairs={{0,4},{16,20},{1,5},{17,21},{2,6},{18,22},{3,7},{19,23},{4,0},{20,... | collective-permute-start | bytes 208904 | tf_op jit(solution)/shard_map/ppermute | solution.py:165
  82.2 2.6 %collective-permute-done.8 = f32[136,128]{1,0:T(8,128)S(1)} collective-permute-done((f32[136,128]{1,0:T(8,128)S(1)}, f32[136,128]{1,0:T(8,128)S(1)}, u32[]{:S(2)}, u32[]{:S(2)}) %collective-permute-start.8) | collective-permute-done | bytes 69664 | tf_op jit(solution)/shard_map/ppermute | solution.py:165
  84.7 2.8 %collective-permute-start.9 = (f32[136,128]{1,0:T(8,128)S(1)}, f32[136,128]{1,0:T(8,128)S(1)}, u32[]{:S(2)}, u32[]{:S(2)}) collective-permute-start(f32[136,128]{1,0:T(8,128)S(1)} %add.40), channel_id=1, source_target_pairs={{0,8},{16,24},{1,9},{17,25},{2,10},{18,26},{3,11},{19,27},{4,12},{... | collective-permute-start | bytes 208904 | tf_op jit(solution)/shard_map/ppermute | solution.py:165
  87.6 2.4 %collective-permute-done.9 = f32[136,128]{1,0:T(8,128)S(1)} collective-permute-done((f32[136,128]{1,0:T(8,128)S(1)}, f32[136,128]{1,0:T(8,128)S(1)}, u32[]{:S(2)}, u32[]{:S(2)}) %collective-permute-start.9) | collective-permute-done | bytes 69664 | tf_op jit(solution)/shard_map/ppermute | solution.py:165
  90.0 0.5 slice.118
  90.5 0.6 slice.117
  (29 shorter events, 0.2 us)
Async XLA Ops:
  0.6 2.9 %copy-start = (bf16[1,24,256,256]{3,2,1,0:T(8,128)(2,1)S(1)}, bf16[1,24,256,256]{3,2,1,0:T(8,128)(2,1)}, u32[]{:S(2)}) copy-start(bf16[1,24,256,256]{3,2,1,0:T(8,128)(2,1)} %param.6) | copy-start | bytes 9437188
  3.2 1.4 %copy-start.5 = (f32[24,256]{1,0:T(8,128)}, f32[24,256]{1,0:T(8,128)S(1)}, u32[]{:S(2)}) copy-start(f32[24,256]{1,0:T(8,128)S(1)} %multiply_reduce_fusion.refs_6_) | copy-start | bytes 73732
  4.0 0.6 copy-start.10
  4.6 1.6 %copy-start.1 = (f32[12,256,256]{2,1,0:T(8,128)}, f32[12,256,256]{2,1,0:T(8,128)S(1)}, u32[]{:S(2)}) copy-start(f32[12,256,256]{2,1,0:T(8,128)S(1)} %fusion.2) | copy-start | bytes 9437188
  6.6 4.5 %copy-start.11 = (f32[6,256]{1,0:T(8,128)}, f32[6,256]{1,0:T(8,128)S(1)}, u32[]{:S(2)}) copy-start(f32[6,256]{1,0:T(8,128)S(1)} %add.33.refs_10_) | copy-start | bytes 18436
  10.2 6.0 %copy-start.2 = (f32[6,256,256]{2,1,0:T(8,128)}, f32[6,256,256]{2,1,0:T(8,128)S(1)}, u32[]{:S(2)}) copy-start(f32[6,256,256]{2,1,0:T(8,128)S(1)} %fusion) | copy-start | bytes 4718596
  11.1 31.2 %copy-start.3 = (f32[3,256,256]{2,1,0:T(8,128)}, f32[3,256,256]{2,1,0:T(8,128)S(1)}, u32[]{:S(2)}) copy-start(f32[3,256,256]{2,1,0:T(8,128)S(1)} %fusion.6.refs_11_) | copy-start | bytes 2359300
  11.3 33.6 %copy-start.12 = (f32[3,256]{1,0:T(4,128)}, f32[3,256]{1,0:T(4,128)S(1)}, u32[]{:S(2)}) copy-start(f32[3,256]{1,0:T(4,128)S(1)} %add.34.refs_12_) | copy-start | bytes 9220
  12.4 10.2 %copy-start.4 = (f32[264,256]{1,0:T(8,128)}, f32[264,256]{1,0:T(8,128)S(1)}, u32[]{:S(2)}) copy-start(f32[264,256]{1,0:T(8,128)S(1)} %maximum_maximum_fusion.own_ref) | copy-start | bytes 811012
  12.4 9.5 %collective-permute-start = (f32[264,256]{1,0:T(8,128)S(1)}, f32[264,256]{1,0:T(8,128)S(1)}, u32[]{:S(2)}, u32[]{:S(2)}) collective-permute-start(f32[264,256]{1,0:T(8,128)S(1)} %maximum_maximum_fusion.own_ref), channel_id=1, source_target_pairs={{0,16},{16,0},{1,17},{17,1},{2,18},{18,2},{3,19},{19,3},{4,20},{20... | collective-permute-start | bytes 811016 | tf_op jit(solution)/shard_map/ppermute | solution.py:165
  22.0 0.7 copy-start.7
  25.3 1.8 %collective-permute-start.1 = (f32[264,256]{1,0:T(8,128)}, f32[264,256]{1,0:T(8,128)S(1)}, u32[]{:S(2)}, u32[]{:S(2)}) collective-permute-start(f32[264,256]{1,0:T(8,128)} %get-tuple-element.29.own_ref), channel_id=1, source_target_pairs={{0,1},{16,17},{1,0},{17,16},{2,3},{18,19},{3,2},{19,18},{4,5},{20,... | collective-permute-start | bytes 811016 | tf_op jit(solution)/shard_map/ppermute | solution.py:165
  27.0 0.7 copy-start.8
  30.3 8.7 %collective-permute-start.2 = (f32[264,256]{1,0:T(8,128)}, f32[264,256]{1,0:T(8,128)S(1)}, u32[]{:S(2)}, u32[]{:S(2)}) collective-permute-start(f32[264,256]{1,0:T(8,128)} %get-tuple-element.32.own_ref), channel_id=1, source_target_pairs={{0,2},{16,18},{1,3},{17,19},{2,0},{18,16},{3,1},{19,17},{4,6},{20,... | collective-permute-start | bytes 811016 | tf_op jit(solution)/shard_map/ppermute | solution.py:165
  39.0 0.7 copy-start.9
  42.3 7.9 %collective-permute-start.3 = (f32[264,256]{1,0:T(8,128)}, f32[264,256]{1,0:T(8,128)S(1)}, u32[]{:S(2)}, u32[]{:S(2)}) collective-permute-start(f32[264,256]{1,0:T(8,128)} %get-tuple-element.35.own_ref), channel_id=1, source_target_pairs={{0,4},{16,20},{1,5},{17,21},{2,6},{18,22},{3,7},{19,23},{4,0},{20,... | collective-permute-start | bytes 811016 | tf_op jit(solution)/shard_map/ppermute | solution.py:165
  50.2 0.7 copy-start.6
  54.2 4.5 %collective-permute-start.4 = (f32[8,256]{1,0:T(8,128)S(1)}, f32[8,256]{1,0:T(8,128)S(1)}, u32[]{:S(2)}, u32[]{:S(2)}) collective-permute-start(f32[8,256]{1,0:T(8,128)S(1)} %slice.108), channel_id=1, source_target_pairs={{0,8},{16,24},{1,9},{17,25},{2,10},{18,26},{3,11},{19,27},{4,12},{... | collective-permute-start | bytes 24584 | tf_op jit(solution)/shard_map/ppermute | solution.py:165
  58.8 0.6 copy-start.14
  59.4 6.5 %copy-start.13 = (f32[1,24,256]{2,1,0:T(8,128)S(1)}, f32[1,24,256]{2,1,0:T(8,128)}, u32[]{:S(2)}) copy-start(f32[1,24,256]{2,1,0:T(8,128)} %param.9) | copy-start | bytes 73732
  69.2 4.5 %collective-permute-start.5 = (f32[136,128]{1,0:T(8,128)}, f32[136,128]{1,0:T(8,128)S(1)}, u32[]{:S(2)}, u32[]{:S(2)}) collective-permute-start(f32[136,128]{1,0:T(8,128)} %scatter.4), channel_id=1, source_target_pairs={{0,16},{16,0},{1,17},{17,1},{2,18},{18,2},{3,19},{19,3},{4,20},{20... | collective-permute-start | bytes 208904 | tf_op jit(solution)/shard_map/ppermute | solution.py:165
  74.6 1.3 %collective-permute-start.6 = (f32[136,128]{1,0:T(8,128)S(1)}, f32[136,128]{1,0:T(8,128)S(1)}, u32[]{:S(2)}, u32[]{:S(2)}) collective-permute-start(f32[136,128]{1,0:T(8,128)S(1)} %add.37), channel_id=1, source_target_pairs={{0,1},{16,17},{1,0},{17,16},{2,3},{18,19},{3,2},{19,18},{4,5},{20,... | collective-permute-start | bytes 208904 | tf_op jit(solution)/shard_map/ppermute | solution.py:165
  76.0 4.4 %collective-permute-start.7 = (f32[136,128]{1,0:T(8,128)S(1)}, f32[136,128]{1,0:T(8,128)S(1)}, u32[]{:S(2)}, u32[]{:S(2)}) collective-permute-start(f32[136,128]{1,0:T(8,128)S(1)} %add.38), channel_id=1, source_target_pairs={{0,2},{16,18},{1,3},{17,19},{2,0},{18,16},{3,1},{19,17},{4,6},{20,... | collective-permute-start | bytes 208904 | tf_op jit(solution)/shard_map/ppermute | solution.py:165
  80.4 4.4 %collective-permute-start.8 = (f32[136,128]{1,0:T(8,128)S(1)}, f32[136,128]{1,0:T(8,128)S(1)}, u32[]{:S(2)}, u32[]{:S(2)}) collective-permute-start(f32[136,128]{1,0:T(8,128)S(1)} %add.39), channel_id=1, source_target_pairs={{0,4},{16,20},{1,5},{17,21},{2,6},{18,22},{3,7},{19,23},{4,0},{20,... | collective-permute-start | bytes 208904 | tf_op jit(solution)/shard_map/ppermute | solution.py:165
  84.7 5.3 %collective-permute-start.9 = (f32[136,128]{1,0:T(8,128)S(1)}, f32[136,128]{1,0:T(8,128)S(1)}, u32[]{:S(2)}, u32[]{:S(2)}) collective-permute-start(f32[136,128]{1,0:T(8,128)S(1)} %add.40), channel_id=1, source_target_pairs={{0,8},{16,24},{1,9},{17,25},{2,10},{18,26},{3,11},{19,27},{4,12},{... | collective-permute-start | bytes 208904 | tf_op jit(solution)/shard_map/ppermute | solution.py:165

commit v17 on v16

--- a/solution.py
+++ b/solution.py
@@ -193,7 +193,10 @@
         rv, sq, sv, grads, station_loadings[0], levels
     )
     local_noise = -jnp.sum(length_rates * offset_response[0])
-    packed = packed.at[stations, 0].set(local_noise)
+    spot = (lax.broadcasted_iota(jnp.int32, packed.shape, 0) == stations) & (
+        lax.broadcasted_iota(jnp.int32, packed.shape, 1) == 0
+    )
+    packed = jnp.where(spot, local_noise, packed)
     d = 1
     while d < count:
         packed = packed + exchange(packed, d, count)

time: 91.6 us -> 95.3 us (1.040)
  matrix products: 5.79 us -> 10 us
  local copies, waits for them, and re-layouts: 8.65 us -> 5.71 us
  other arithmetic: 8.19 us -> 10.7 us
    dot_general x4, matrix products: 5.22 us -> 7.83 us  [matmat(): jnp.einsum('nij,njk->nik', later.astype(jnp.float32), earlier.astype(jnp....]
    dot_general x1, matrix products: 0.57 us -> 2.21 us  [matmat(): jnp.einsum('nij,njk->nik', later, earlier, preferred_element_type=jnp.flo...]
    unnamed x30 -> x28, local copies, waits for them, and re-layouts: 4.69 us -> 3.06 us
    reduce_sum x4, other arithmetic: 3.55 us -> 4.97 us  [vecmat(): return jnp.sum(v[:, :, None] * q.astype(jnp.float32), axis=1)]
    scatter x1 -> x0, local copies, waits for them, and re-layouts: 1.29 us -> none  [body(): packed = packed.at[stations, 0].set(local_noise)]
    select_n x0 -> x1, other arithmetic: none -> 0.97 us  [body(): packed = jnp.where(spot, local_noise, packed)]
where the time goes in v17:
time: 95.3 us; the launch traced here: 94.8 us
  waiting for transfers between devices  32.6 us (34%)
  starting transfers between devices  17.5 us (18%)
  Pallas kernels  16.8 us (18%)
  other arithmetic  10.7 us (11%)
  matrix products  10 us (10%)
  local copies, waits for them, and re-layouts  5.71 us (6%)
  between operations  1.51 us (2%)
    ppermute x10, waiting for transfers between devices, exchange(): lax.ppermute(x, AXES, [(place(j), place(j ^ mask)) for j in range(count)])  32.6 us
    ppermute x10, starting transfers between devices, exchange(): lax.ppermute(x, AXES, [(place(j), place(j ^ mask)) for j in range(count)])  17.5 us
    pallas_call x4, Pallas kernels, run(): pl.pallas_call(kernel, out_shape=(jax.ShapeDtypeStruct(own.shape, jnp.flo...  10.2 us
    dot_general x4, matrix products, matmat(): jnp.einsum('nij,njk->nik', later.astype(jnp.float32), earlier.astype(jnp....  7.83 us
    pallas_call x1, Pallas kernels, run(): pl.pallas_call(kernel, out_shape=out_shape, grid=(1,), in_specs=specs, ou...  6.55 us
    reduce_sum x4, other arithmetic, vecmat(): return jnp.sum(v[:, :, None] * q.astype(jnp.float32), axis=1)  4.97 us
    unnamed x28, local copies, waits for them, and re-layouts  3.06 us
    dot_general x1, matrix products, matmat(): jnp.einsum('nij,njk->nik', later, earlier, preferred_element_type=jnp.flo...  2.21 us
  transfers between devices with their start and end apart: 10, of which 10 were waited for; matrix products, arithmetic and copies ran while one was open for 2% of the time, Pallas kernels for 0%

profile of v17, /device:TPU:0, one launch (start us, length us, event | category | flops | bytes accessed | tf_op | source)
XLA Modules:
  0.0 94.8 jit_solution(2426463302079369183)
XLA Ops:
  0.6 0.0 copy-start
  0.6 2.6 %multiply_reduce_fusion.refs_6_ = f32[24,256]{1,0:T(8,128)S(1)} fusion(f32[24,256]{1,0:T(8,128)} %bitcast.40, bf16[1,24,256,256]{3,2,1,0:T(8,128)(2,1)} %param.4), kind=kLoop, calls=%fused_computation | loop fusion | flops 4712448 | bytes 3194880 | tf_op jit(solution)/shard_map/reduce_sum | solution.py:12
  3.2 0.0 copy-start.4
  3.3 0.2 copy-done
  3.5 2.2 %fusion.2 = f32[12,256,256]{2,1,0:T(8,128)} fusion(bf16[24,256,256]{2,1,0:T(8,128)(2,1)S(1)} %bitcast.35), kind=kOutput, calls=%fused_computation.5 | convolution fusion | flops 402653184 | bytes 6291456 | tf_op jit(solution)/shard_map/nij,njk->nik/dot_general | solution.py:21
  5.7 0.0 copy-done.4
  5.7 0.5 multiply_reduce_fusion.1
  6.2 0.0 copy-start.1
  6.2 0.0 copy-start.9
  6.3 4.8 %fusion = f32[6,256,256]{2,1,0:T(8,128)} fusion(f32[12,256,256]{2,1,0:T(8,128)} %fusion.2), kind=kOutput, calls=%fused_computation.3 | convolution fusion | flops 1207959552 | bytes 4718592 | tf_op jit(solution)/shard_map/nij,njk->nik/dot_general | solution.py:22
  11.1 0.0 copy-done.1
  11.1 0.3 multiply_reduce_fusion.2
  11.4 0.0 copy-done.9
  11.4 0.0 copy-start.10
  11.4 2.3 %fusion.6.refs_11_ = f32[3,256,256]{2,1,0:T(8,128)S(1)} fusion(f32[6,256,256]{2,1,0:T(8,128)} %fusion), kind=kOutput, calls=%fused_computation.10 | convolution fusion | flops 603979776 | bytes 2359296 | tf_op jit(solution)/shard_map/nij,njk->nik/dot_general | solution.py:22
  13.7 0.0 copy-start.2
  13.7 1.6 %multiply_reduce_fusion.3 = f32[3,256]{1,0:T(4,128)S(1)} fusion(f32[6,256,256]{2,1,0:T(8,128)} %fusion, f32[3,256]{1,0:T(4,128)S(1)} %slice.84), kind=kLoop, calls=%fused_computation.9 | loop fusion | flops 392448 | bytes 792576 | tf_op jit(solution)/shard_map/reduce_sum | solution.py:12
  15.4 0.4 multiply_reduce_fusion.5
  15.8 0.1 fusion.18
  15.9 0.4 fusion.11
  16.3 0.1 pad.6.clone
  16.4 0.1 maximum_maximum_fusion.own_ref
  16.5 0.0 copy-start.3
  16.5 3.0 %collective-permute-start = (f32[264,256]{1,0:T(8,128)S(1)}, f32[264,256]{1,0:T(8,128)S(1)}, u32[]{:S(2)}, u32[]{:S(2)}) collective-permute-start(f32[264,256]{1,0:T(8,128)S(1)} %maximum_maximum_fusion.own_ref), channel_id=1, source_target_pairs={{0,16},{16,0},{1,17},{17,1},{2,18},{18,2},{3,19},{19,3},{4,20},{20... | collective-permute-start | bytes 811016 | tf_op jit(solution)/shard_map/ppermute | solution.py:165
  19.5 0.7 fusion.13.sq_ref
  20.2 5.8 %collective-permute-done.got_ref = f32[264,256]{1,0:T(8,128)S(1)} collective-permute-done((f32[264,256]{1,0:T(8,128)S(1)}, f32[264,256]{1,0:T(8,128)S(1)}, u32[]{:S(2)}, u32[]{:S(2)}) %collective-permute-start) | collective-permute-done | bytes 270368 | tf_op jit(solution)/shard_map/ppermute | solution.py:165
  26.0 0.6 broadcast_in_dim.19.sv_ref
  26.6 0.1 copy-done.6
  26.7 2.6 %shard_map.67 = (f32[264,256]{1,0:T(8,128)}, f32[256,256]{1,0:T(8,128)}, f32[8,256]{1,0:T(8,128)}) custom-call(f32[264,256]{1,0:T(8,128)} %copy-done.3, f32[264,256]{1,0:T(8,128)} %copy-done.6, f32[256,256]{1,0:T(8,128)} %fusion.13.sq_ref, f32[8,256]{1,0:T(8,128)} %broadcast_in_dim.19.sv_ref), custom_call_target="tpu_custom_call" | custom-call | tf_op jit(solution)/shard_map/pallas_call | solution.py:73
  29.3 0.0 collective-permute-start.1
  29.3 1.8 %collective-permute-done.1.got_ref = f32[264,256]{1,0:T(8,128)S(1)} collective-permute-done((f32[264,256]{1,0:T(8,128)}, f32[264,256]{1,0:T(8,128)S(1)}, u32[]{:S(2)}, u32[]{:S(2)}) %collective-permute-start.1) | collective-permute-done | bytes 270368 | tf_op jit(solution)/shard_map/ppermute | solution.py:165
  31.0 0.7 copy-done.7
  31.8 2.6 %shard_map.68 = (f32[264,256]{1,0:T(8,128)}, f32[256,256]{1,0:T(8,128)}, f32[8,256]{1,0:T(8,128)}) custom-call(f32[264,256]{1,0:T(8,128)} %get-tuple-element.17.own_ref, f32[264,256]{1,0:T(8,128)} %copy-done.7, f32[256,256]{1,0:T(8,128)} %get-tuple-element.18.sq_ref, f32[8,256]{1,0:T(8,128)} %get-tuple-element.19.sv_ref), custom_call_target="tpu_custom_call" | custom-call | tf_op jit(solution)/shard_map/pallas_call | solution.py:73
  34.3 1.7 %collective-permute-start.2 = (f32[264,256]{1,0:T(8,128)}, f32[264,256]{1,0:T(8,128)S(1)}, u32[]{:S(2)}, u32[]{:S(2)}) collective-permute-start(f32[264,256]{1,0:T(8,128)} %get-tuple-element.20.own_ref), channel_id=1, source_target_pairs={{0,2},{16,18},{1,3},{17,19},{2,0},{18,16},{3,1},{19,17},{4,6},{20,... | collective-permute-start | bytes 811016 | tf_op jit(solution)/shard_map/ppermute | solution.py:165
  36.0 7.0 %collective-permute-done.2.got_ref = f32[264,256]{1,0:T(8,128)S(1)} collective-permute-done((f32[264,256]{1,0:T(8,128)}, f32[264,256]{1,0:T(8,128)S(1)}, u32[]{:S(2)}, u32[]{:S(2)}) %collective-permute-start.2) | collective-permute-done | bytes 270368 | tf_op jit(solution)/shard_map/ppermute | solution.py:165
  43.1 0.7 copy-done.8
  43.8 2.5 %shard_map.69 = (f32[264,256]{1,0:T(8,128)}, f32[256,256]{1,0:T(8,128)}, f32[8,256]{1,0:T(8,128)}) custom-call(f32[264,256]{1,0:T(8,128)} %get-tuple-element.20.own_ref, f32[264,256]{1,0:T(8,128)} %copy-done.8, f32[256,256]{1,0:T(8,128)} %get-tuple-element.21.sq_ref, f32[8,256]{1,0:T(8,128)} %get-tuple-element.22.sv_ref), custom_call_target="tpu_custom_call" | custom-call | tf_op jit(solution)/shard_map/pallas_call | solution.py:73
  46.3 1.8 %collective-permute-start.3 = (f32[264,256]{1,0:T(8,128)}, f32[264,256]{1,0:T(8,128)S(1)}, u32[]{:S(2)}, u32[]{:S(2)}) collective-permute-start(f32[264,256]{1,0:T(8,128)} %get-tuple-element.23.own_ref), channel_id=1, source_target_pairs={{0,4},{16,20},{1,5},{17,21},{2,6},{18,22},{3,7},{19,23},{4,0},{20,... | collective-permute-start | bytes 811016 | tf_op jit(solution)/shard_map/ppermute | solution.py:165
  48.1 0.6 pad_maximum_fusion.refs_14_
  48.7 0.9 maximum_bitcast_fusion.refs_13_
  49.6 4.7 %collective-permute-done.3.got_ref = f32[264,256]{1,0:T(8,128)S(1)} collective-permute-done((f32[264,256]{1,0:T(8,128)}, f32[264,256]{1,0:T(8,128)S(1)}, u32[]{:S(2)}, u32[]{:S(2)}) %collective-permute-start.3) | collective-permute-done | bytes 270368 | tf_op jit(solution)/shard_map/ppermute | solution.py:165
  54.3 0.7 copy-done.5
  55.0 2.6 %shard_map.70 = (f32[264,256]{1,0:T(8,128)}, f32[256,256]{1,0:T(8,128)}, f32[8,256]{1,0:T(8,128)}) custom-call(f32[264,256]{1,0:T(8,128)} %get-tuple-element.23.own_ref, f32[264,256]{1,0:T(8,128)} %copy-done.5, f32[256,256]{1,0:T(8,128)} %get-tuple-element.24.sq_ref, f32[8,256]{1,0:T(8,128)} %get-tuple-element.25.sv_ref), custom_call_target="tpu_custom_call" | custom-call | tf_op jit(solution)/shard_map/pallas_call | solution.py:73
  57.5 0.7 slice.89
  58.2 2.8 %collective-permute-start.4 = (f32[8,256]{1,0:T(8,128)S(1)}, f32[8,256]{1,0:T(8,128)S(1)}, u32[]{:S(2)}, u32[]{:S(2)}) collective-permute-start(f32[8,256]{1,0:T(8,128)S(1)} %slice.89), channel_id=1, source_target_pairs={{0,8},{16,24},{1,9},{17,25},{2,10},{18,26},{3,11},{19,27},{4,12},{... | collective-permute-start | bytes 24584 | tf_op jit(solution)/shard_map/ppermute | solution.py:165
  61.0 1.8 %collective-permute-done.4.refs_0_ = f32[8,256]{1,0:T(8,128)S(1)} collective-permute-done((f32[8,256]{1,0:T(8,128)S(1)}, f32[8,256]{1,0:T(8,128)S(1)}, u32[]{:S(2)}, u32[]{:S(2)}) %collective-permute-start.4) | collective-permute-done | bytes 8224 | tf_op jit(solution)/shard_map/ppermute | solution.py:165
  62.8 0.6 copy-done.13
  63.4 6.6 %shard_map.71 = (f32[24,256]{1,0:T(8,128)}, f32[136,128]{1,0:T(8,128)}) custom-call(f32[8,256]{1,0:T(8,128)} %copy-done.13, f32[256,256]{1,0:T(8,128)} %get-tuple-element.27.refs_1_, f32[8,256]{1,0:T(8,128)} %get-tuple-element.28.refs_2_, f32[24,256]{1,0:T(8,128)} %bitcast.41, f32[24,2,128]{2,1,0:T(2,128)} %bitcast.42, bf16[12,2,256,256]{3,2,1,0:T(8,128)(2,1)} %bitcast.34, ...), custom_call_target="tpu_custom_call" | custom-call | tf_op jit(solution)/shard_map/pallas_call | solution.py:148
  69.9 0.0 copy-done.12
  69.9 1.3 %fusion.15 = f32[]{:T(128)} fusion(f32[24,256]{1,0:T(8,128)} %get-tuple-element.29, f32[1,24,256]{2,1,0:T(8,128)S(1)} %copy-done.12), kind=kLoop, calls=%fused_computation.27 | loop fusion | flops 12287 | bytes 49156 | tf_op jit(solution)/shard_map/reduce_sum | solution.py:195
  71.9 1.0 %and_select_fusion = f32[136,128]{1,0:T(8,128)S(1)} fusion(f32[136,128]{1,0:T(8,128)} %get-tuple-element.30, f32[]{:T(128)S(6)} %neg.3, pred[128]{0:T(512)(128)(4,1)S(1)} %iota_compare_fusion.2, pred[136]{0:T(512)(128)(4,1)S(1)} %iota_compare_fusion.1), kind=kLoop, calls=%fused_computation.25 | loop fusion | flops 34816 | bytes 139532 | tf_op jit(solution)/shard_map/jit(_where)/select_n | solution.py:199
  72.9 1.7 %collective-permute-start.5 = (f32[136,128]{1,0:T(8,128)S(1)}, f32[136,128]{1,0:T(8,128)S(1)}, u32[]{:S(2)}, u32[]{:S(2)}) collective-permute-start(f32[136,128]{1,0:T(8,128)S(1)} %and_select_fusion), channel_id=1, source_target_pairs={{0,16},{16,0},{1,17},{17,1},{2,18},{18,2},{3,19},{19,3},{4,20},{20... | collective-permute-start | bytes 208904 | tf_op jit(solution)/shard_map/ppermute | solution.py:165
  74.7 2.6 %collective-permute-done.5 = f32[136,128]{1,0:T(8,128)S(1)} collective-permute-done((f32[136,128]{1,0:T(8,128)S(1)}, f32[136,128]{1,0:T(8,128)S(1)}, u32[]{:S(2)}, u32[]{:S(2)}) %collective-permute-start.5) | collective-permute-done | bytes 69664 | tf_op jit(solution)/shard_map/ppermute | solution.py:165
  77.3 1.0 %fusion.21 = f32[136,128]{1,0:T(8,128)S(1)} fusion(f32[136,128]{1,0:T(8,128)S(1)} %collective-permute-done.5, f32[136,128]{1,0:T(8,128)} %get-tuple-element.30, f32[]{:T(128)S(6)} %neg.3, pred[128]{0:T(512)(128)(4,1)S(1)} %iota_compare_fusion.2, pred[136]{0:T(512)(128)(4,1)S(1)} %iota_compare_fusion.1), kind=kLoop, calls=%fused_computation.36 | loop fusion | flops 52224 | bytes 209164 | tf_op jit(solution)/shard_map/add | solution.py:202
  78.3 0.1 collective-permute-start.6
  78.3 1.2 %collective-permute-done.6 = f32[136,128]{1,0:T(8,128)S(1)} collective-permute-done((f32[136,128]{1,0:T(8,128)S(1)}, f32[136,128]{1,0:T(8,128)S(1)}, u32[]{:S(2)}, u32[]{:S(2)}) %collective-permute-start.6) | collective-permute-done | bytes 69664 | tf_op jit(solution)/shard_map/ppermute | solution.py:165
  79.6 1.7 %collective-permute-start.7 = (f32[136,128]{1,0:T(8,128)S(1)}, f32[136,128]{1,0:T(8,128)S(1)}, u32[]{:S(2)}, u32[]{:S(2)}) collective-permute-start(f32[136,128]{1,0:T(8,128)S(1)} %add.36), channel_id=1, source_target_pairs={{0,2},{16,18},{1,3},{17,19},{2,0},{18,16},{3,1},{19,17},{4,6},{20,... | collective-permute-start | bytes 208904 | tf_op jit(solution)/shard_map/ppermute | solution.py:165
  81.3 2.7 %collective-permute-done.7 = f32[136,128]{1,0:T(8,128)S(1)} collective-permute-done((f32[136,128]{1,0:T(8,128)S(1)}, f32[136,128]{1,0:T(8,128)S(1)}, u32[]{:S(2)}, u32[]{:S(2)}) %collective-permute-start.7) | collective-permute-done | bytes 69664 | tf_op jit(solution)/shard_map/ppermute | solution.py:165
  84.0 1.8 %collective-permute-start.8 = (f32[136,128]{1,0:T(8,128)S(1)}, f32[136,128]{1,0:T(8,128)S(1)}, u32[]{:S(2)}, u32[]{:S(2)}) collective-permute-start(f32[136,128]{1,0:T(8,128)S(1)} %add.37), channel_id=1, source_target_pairs={{0,4},{16,20},{1,5},{17,21},{2,6},{18,22},{3,7},{19,23},{4,0},{20,... | collective-permute-start | bytes 208904 | tf_op jit(solution)/shard_map/ppermute | solution.py:165
  85.8 2.6 %collective-permute-done.8 = f32[136,128]{1,0:T(8,128)S(1)} collective-permute-done((f32[136,128]{1,0:T(8,128)S(1)}, f32[136,128]{1,0:T(8,128)S(1)}, u32[]{:S(2)}, u32[]{:S(2)}) %collective-permute-start.8) | collective-permute-done | bytes 69664 | tf_op jit(solution)/shard_map/ppermute | solution.py:165
  88.4 2.8 %collective-permute-start.9 = (f32[136,128]{1,0:T(8,128)S(1)}, f32[136,128]{1,0:T(8,128)S(1)}, u32[]{:S(2)}, u32[]{:S(2)}) collective-permute-start(f32[136,128]{1,0:T(8,128)S(1)} %add.38), channel_id=1, source_target_pairs={{0,8},{16,24},{1,9},{17,25},{2,10},{18,26},{3,11},{19,27},{4,12},{... | collective-permute-start | bytes 208904 | tf_op jit(solution)/shard_map/ppermute | solution.py:165
  91.2 2.5 %collective-permute-done.9 = f32[136,128]{1,0:T(8,128)S(1)} collective-permute-done((f32[136,128]{1,0:T(8,128)S(1)}, f32[136,128]{1,0:T(8,128)S(1)}, u32[]{:S(2)}, u32[]{:S(2)}) %collective-permute-start.9) | collective-permute-done | bytes 69664 | tf_op jit(solution)/shard_map/ppermute | solution.py:165
  93.7 0.6 slice.98
  94.3 0.5 slice.99
  (29 shorter events, 0.2 us)
Async XLA Ops:
  0.6 2.9 %copy-start = (bf16[1,24,256,256]{3,2,1,0:T(8,128)(2,1)S(1)}, bf16[1,24,256,256]{3,2,1,0:T(8,128)(2,1)}, u32[]{:S(2)}) copy-start(bf16[1,24,256,256]{3,2,1,0:T(8,128)(2,1)} %param.4) | copy-start | bytes 9437188
  3.2 2.5 %copy-start.4 = (f32[24,256]{1,0:T(8,128)}, f32[24,256]{1,0:T(8,128)S(1)}, u32[]{:S(2)}) copy-start(f32[24,256]{1,0:T(8,128)S(1)} %multiply_reduce_fusion.refs_6_) | copy-start | bytes 73732
  6.2 4.9 %copy-start.1 = (f32[12,256,256]{2,1,0:T(8,128)S(1)}, f32[12,256,256]{2,1,0:T(8,128)}, u32[]{:S(2)}) copy-start(f32[12,256,256]{2,1,0:T(8,128)} %fusion.2) | copy-start | bytes 9437188
  6.2 5.1 %copy-start.9 = (f32[12,256]{1,0:T(8,128)}, f32[12,256]{1,0:T(8,128)S(1)}, u32[]{:S(2)}) copy-start(f32[12,256]{1,0:T(8,128)S(1)} %add.30.refs_8_) | copy-start | bytes 36868
  11.4 8.8 %copy-start.10 = (f32[6,256]{1,0:T(8,128)}, f32[6,256]{1,0:T(8,128)S(1)}, u32[]{:S(2)}) copy-start(f32[6,256]{1,0:T(8,128)S(1)} %add.31.refs_10_) | copy-start | bytes 18436
  13.7 32.6 %copy-start.2 = (f32[3,256,256]{2,1,0:T(8,128)}, f32[3,256,256]{2,1,0:T(8,128)S(1)}, u32[]{:S(2)}) copy-start(f32[3,256,256]{2,1,0:T(8,128)S(1)} %fusion.6.refs_11_) | copy-start | bytes 2359300
  15.3 34.2 %copy-start.11 = (f32[3,256]{1,0:T(4,128)}, f32[3,256]{1,0:T(4,128)S(1)}, u32[]{:S(2)}) copy-start(f32[3,256]{1,0:T(4,128)S(1)} %add.32.refs_12_) | copy-start | bytes 9220
  16.5 10.2 %copy-start.3 = (f32[264,256]{1,0:T(8,128)}, f32[264,256]{1,0:T(8,128)S(1)}, u32[]{:S(2)}) copy-start(f32[264,256]{1,0:T(8,128)S(1)} %maximum_maximum_fusion.own_ref) | copy-start | bytes 811012
  16.5 9.5 %collective-permute-start = (f32[264,256]{1,0:T(8,128)S(1)}, f32[264,256]{1,0:T(8,128)S(1)}, u32[]{:S(2)}, u32[]{:S(2)}) collective-permute-start(f32[264,256]{1,0:T(8,128)S(1)} %maximum_maximum_fusion.own_ref), channel_id=1, source_target_pairs={{0,16},{16,0},{1,17},{17,1},{2,18},{18,2},{3,19},{19,3},{4,20},{20... | collective-permute-start | bytes 811016 | tf_op jit(solution)/shard_map/ppermute | solution.py:165
  26.0 0.7 copy-start.6
  29.3 1.8 %collective-permute-start.1 = (f32[264,256]{1,0:T(8,128)}, f32[264,256]{1,0:T(8,128)S(1)}, u32[]{:S(2)}, u32[]{:S(2)}) collective-permute-start(f32[264,256]{1,0:T(8,128)} %get-tuple-element.17.own_ref), channel_id=1, source_target_pairs={{0,1},{16,17},{1,0},{17,16},{2,3},{18,19},{3,2},{19,18},{4,5},{20,... | collective-permute-start | bytes 811016 | tf_op jit(solution)/shard_map/ppermute | solution.py:165
  31.0 0.7 copy-start.7
  34.3 8.7 %collective-permute-start.2 = (f32[264,256]{1,0:T(8,128)}, f32[264,256]{1,0:T(8,128)S(1)}, u32[]{:S(2)}, u32[]{:S(2)}) collective-permute-start(f32[264,256]{1,0:T(8,128)} %get-tuple-element.20.own_ref), channel_id=1, source_target_pairs={{0,2},{16,18},{1,3},{17,19},{2,0},{18,16},{3,1},{19,17},{4,6},{20,... | collective-permute-start | bytes 811016 | tf_op jit(solution)/shard_map/ppermute | solution.py:165
  43.1 0.7 copy-start.8
  46.3 8.0 %collective-permute-start.3 = (f32[264,256]{1,0:T(8,128)}, f32[264,256]{1,0:T(8,128)S(1)}, u32[]{:S(2)}, u32[]{:S(2)}) collective-permute-start(f32[264,256]{1,0:T(8,128)} %get-tuple-element.23.own_ref), channel_id=1, source_target_pairs={{0,4},{16,20},{1,5},{17,21},{2,6},{18,22},{3,7},{19,23},{4,0},{20,... | collective-permute-start | bytes 811016 | tf_op jit(solution)/shard_map/ppermute | solution.py:165
  54.3 0.7 copy-start.5
  58.2 4.5 %collective-permute-start.4 = (f32[8,256]{1,0:T(8,128)S(1)}, f32[8,256]{1,0:T(8,128)S(1)}, u32[]{:S(2)}, u32[]{:S(2)}) collective-permute-start(f32[8,256]{1,0:T(8,128)S(1)} %slice.89), channel_id=1, source_target_pairs={{0,8},{16,24},{1,9},{17,25},{2,10},{18,26},{3,11},{19,27},{4,12},{... | collective-permute-start | bytes 24584 | tf_op jit(solution)/shard_map/ppermute | solution.py:165
  62.8 0.6 copy-start.13
  63.4 6.6 %copy-start.12 = (f32[1,24,256]{2,1,0:T(8,128)S(1)}, f32[1,24,256]{2,1,0:T(8,128)}, u32[]{:S(2)}) copy-start(f32[1,24,256]{2,1,0:T(8,128)} %param.7) | copy-start | bytes 73732
  72.9 4.4 %collective-permute-start.5 = (f32[136,128]{1,0:T(8,128)S(1)}, f32[136,128]{1,0:T(8,128)S(1)}, u32[]{:S(2)}, u32[]{:S(2)}) collective-permute-start(f32[136,128]{1,0:T(8,128)S(1)} %and_select_fusion), channel_id=1, source_target_pairs={{0,16},{16,0},{1,17},{17,1},{2,18},{18,2},{3,19},{19,3},{4,20},{20... | collective-permute-start | bytes 208904 | tf_op jit(solution)/shard_map/ppermute | solution.py:165
  78.3 1.3 %collective-permute-start.6 = (f32[136,128]{1,0:T(8,128)S(1)}, f32[136,128]{1,0:T(8,128)S(1)}, u32[]{:S(2)}, u32[]{:S(2)}) collective-permute-start(f32[136,128]{1,0:T(8,128)S(1)} %fusion.21), channel_id=1, source_target_pairs={{0,1},{16,17},{1,0},{17,16},{2,3},{18,19},{3,2},{19,18},{4,5},{20,... | collective-permute-start | bytes 208904 | tf_op jit(solution)/shard_map/ppermute | solution.py:165
  79.6 4.4 %collective-permute-start.7 = (f32[136,128]{1,0:T(8,128)S(1)}, f32[136,128]{1,0:T(8,128)S(1)}, u32[]{:S(2)}, u32[]{:S(2)}) collective-permute-start(f32[136,128]{1,0:T(8,128)S(1)} %add.36), channel_id=1, source_target_pairs={{0,2},{16,18},{1,3},{17,19},{2,0},{18,16},{3,1},{19,17},{4,6},{20,... | collective-permute-start | bytes 208904 | tf_op jit(solution)/shard_map/ppermute | solution.py:165
  84.0 4.4 %collective-permute-start.8 = (f32[136,128]{1,0:T(8,128)S(1)}, f32[136,128]{1,0:T(8,128)S(1)}, u32[]{:S(2)}, u32[]{:S(2)}) collective-permute-start(f32[136,128]{1,0:T(8,128)S(1)} %add.37), channel_id=1, source_target_pairs={{0,4},{16,20},{1,5},{17,21},{2,6},{18,22},{3,7},{19,23},{4,0},{20,... | collective-permute-start | bytes 208904 | tf_op jit(solution)/shard_map/ppermute | solution.py:165
  88.4 5.3 %collective-permute-start.9 = (f32[136,128]{1,0:T(8,128)S(1)}, f32[136,128]{1,0:T(8,128)S(1)}, u32[]{:S(2)}, u32[]{:S(2)}) collective-permute-start(f32[136,128]{1,0:T(8,128)S(1)} %add.38), channel_id=1, source_target_pairs={{0,8},{16,24},{1,9},{17,25},{2,10},{18,26},{3,11},{19,27},{4,12},{... | collective-permute-start | bytes 208904 | tf_op jit(solution)/shard_map/ppermute | solution.py:165
